TPU v7x, 128 devices: a whole 4x4x4 slice. The times are simulated.
128 devices in a mesh: row: 16 (over z_lo, x, core), col: 8 (over y, z_hi).
Axes of the slice: x: 4, y: 4, z: 4 (z_hi: 2, z_lo: 2; z = z_hi * 2 + z_lo), core: 2. Of those that a mesh axis runs over, the one named last changes fastest.
Arguments:
- slab_embed: float32 [65536, 768], P(('col', 'row')), may hold values from -1 to 1
- coverage_old: float32 [65536], P('col'), may hold values from 2 to 4.5
- sel_index: int32 [2048], P('row'), may hold values from 0 to 65535
- cand_index: int32 [3072], P('row'), may hold values from 0 to 65535
Outputs:
- coverage: float32 [65536], P('col')
- total_gain: float32 [3072], P('row')
Inputs may be any that keep to these rules, and one draw needn't show every extreme that they name: `sel_index`: indices into the slab. `cand_index`: indices into the slab.
All inputs are finite; a program needn't handle non-finite values.
Results may differ from a plain program's by a relative error of at most 0.00014.
Values sent between devices are 32-bit elements; how exact they have to be, the bound alone decides.
No kernel may reach another device: no remote copies, remote signals or barrier semaphores. Data moves between devices by JAX's collectives and lax.ppermute only.
A program may use at most 128 MiB of HBM per device.

v0:
```python
import jax
import jax.numpy as jnp
from jax import lax
from jax.sharding import PartitionSpec as P


def similar(left, right):
    return lax.dot_general(
        left,
        right,
        (((1,), (1,)), ((), ())),
        precision=lax.Precision.HIGHEST,
        preferred_element_type=jnp.float32,
    )


def lookup(source, indices, first_row):
    position = indices - first_row
    inside = (position >= 0) & (position < source.shape[0])
    picked = jnp.take(source, jnp.clip(position, 0, source.shape[0] - 1), axis=0)
    return jnp.where(inside[:, None], picked, 0.0)


def body(slab_embed, coverage_old, sel_index, cand_index):
    col_id = lax.axis_index("col")
    gathered = lax.all_gather(slab_embed, "row", axis=0, tiled=True)
    first_row = col_id * gathered.shape[0]
    selected, chosen = lax.psum(
        (lookup(gathered, sel_index, first_row), lookup(gathered, cand_index, first_row)), "col"
    )
    partial_value = jnp.max(similar(selected, gathered), axis=0)
    reached = lax.pmax(partial_value, "row")
    coverage = jnp.maximum(coverage_old, reached)
    gain_part = jnp.sum(jnp.maximum(similar(chosen, gathered) - coverage[None, :], 0.0), axis=1)
    total_gain = lax.psum(gain_part, "col")
    return (coverage, total_gain)


def solution(mesh):
    in_specs = (P(("col", "row"), None), P("col"), P("row"), P("row"))
    out_specs = (P("col"), P("row"))
    return jax.shard_map(body, mesh=mesh, in_specs=in_specs, out_specs=out_specs, check_vma=False)
```

profile of v0, /device:TPU:0, one launch (start us, length us, event | category | flops | bytes accessed | tf_op | source)
XLA Modules:
  0.0 394.2 jit_solution(11999986504088533474)
XLA Ops:
  7.2 0.0 copy-start.2
  7.2 0.0 all-gather.2.cloned.1.call-start
  7.2 0.7 all-gather.2.cloned.1.call-update
  7.9 0.0 all-reduce.3.cloned.1.call-start
  8.0 0.7 compare_and_fusion
  8.7 0.7 compare_and_fusion.2
  9.3 134.0 %all-gather.2.cloned.1.call-done = f32[8192,768]{1,0:T(8,128)} async-done(((f32[512,768]{1,0:T(8,128)}), f32[8192,768]{1,0:T(8,128)}) %all-gather.2.cloned.1.call-update) | async-done | bytes 25165840 | tf_op jit(solution)/shard_map/all_gather | solution.py:26
  143.4 9.1 %gather_fusion = f32[128,768]{1,0:T(8,128)S(1)} fusion(f32[8192,768]{1,0:T(8,128)} %all-gather.2.cloned.1.call-done, s32[1024]{0:T(1024)S(1)} %pad_clamp_fusion.1), kind=kCustom, calls=%fused_computation | custom fusion | bytes 786944 | tf_op jit(solution)/shard_map/jit(_take)/gather | solution.py:20
  152.5 0.9 select_select_fusion.1
  153.4 9.3 %gather_fusion.1 = f32[192,768]{1,0:T(8,128)S(1)} fusion(f32[8192,768]{1,0:T(8,128)} %all-gather.2.cloned.1.call-done, s32[1024]{0:T(1024)S(1)} %pad_clamp_fusion), kind=kCustom, calls=%fused_computation.1 | custom fusion | bytes 1180416 | tf_op jit(solution)/shard_map/jit(_take)/gather | solution.py:20
  162.7 1.0 select_select_fusion
  163.7 0.0 all-reduce.3.cloned.1.call-update
  163.8 89.4 %all-reduce.3.cloned.1.call-done = (f32[128,768]{1,0:T(8,128)}, f32[192,768]{1,0:T(8,128)}) async-done(((f32[128,768]{1,0:T(8,128)}, f32[192,768]{1,0:T(8,128)}), (f32[128,768]{1,0:T(8,128)}, f32[192,768]{1,0:T(8,128)})) %all-reduce.3.cloned.1.call-update) | async-done | bytes 983056 | tf_op jit(solution)/shard_map/psum | solution.py:28
  253.2 0.0 copy-start
  253.2 30.1 %convolution_reduce_fusion = f32[8192]{0:T(1024)S(1)} fusion(f32[128,768]{1,0:T(8,128)} %get-tuple-element.2, f32[8192,768]{1,0:T(8,128)} %all-gather.2.cloned.1.call-done), kind=kOutput, calls=%fused_computation.5 | convolution fusion | flops 9664716800 | bytes 25591808 | tf_op jit(solution)/shard_map/dot_general | solution.py:8
  283.3 53.1 %pmax.7 = f32[8192]{0:T(1024)S(1)} all-reduce(f32[8192]{0:T(1024)S(1)} %convolution_reduce_fusion), channel_id=1, replica_groups=mesh['row'=16,'col'=8] {'row'}, use_global_device_ids=true, to_apply=%region_2.3 | all-reduce | flops 8192 | bytes 65536 | tf_op jit(solution)/shard_map/pmax | solution.py:32
  336.4 0.0 copy-done.2
  336.4 0.0 copy-start.1
  336.4 0.0 copy-done
  336.4 29.9 %fusion.1 = f32[192]{0:T(256)S(1)} fusion(f32[8192]{0:T(1024)S(1)} %max.19, f32[192,768]{1,0:T(8,128)S(1)} %copy-done, f32[8192,768]{1,0:T(8,128)} %all-gather.2.cloned.1.call-done), kind=kOutput, calls=%fused_computation.4 | convolution fusion | flops 14500233216 | bytes 25789184 | tf_op jit(solution)/shard_map/dot_general | solution.py:8
  366.4 21.0 %psum.23 = f32[192]{0:T(256)} all-reduce(f32[192]{0:T(256)S(1)} %fusion.1), channel_id=1, replica_groups=mesh['row'=16,'col'=8] {'col'}, use_global_device_ids=true, to_apply=%region_5.6 | all-reduce | flops 192 | bytes 1536 | tf_op jit(solution)/shard_map/psum | solution.py:35
  387.4 0.0 copy-done.1
  (3 shorter events, 0.0 us)
Async XLA Ops:
  7.2 329.2 %copy-start.2 = (f32[8192]{0:T(1024)S(1)}, f32[8192]{0:T(1024)}, u32[]{:S(2)}) copy-start(f32[8192]{0:T(1024)} %param.5) | copy-start | bytes 98308
  7.2 136.2 %all-gather.2.cloned.1.call-start = ((), (), s32[]{:S(2)}) async-start(), calls=%async_computation | async-start | bytes 26738688 | tf_op jit(solution)/shard_map/all_gather | solution.py:26
  7.9 245.3 %all-reduce.3.cloned.1.call-start = ((), (), s32[]{:S(2)}) async-start(), calls=%async_computation.1 | async-start | bytes 1966080 | tf_op jit(solution)/shard_map/psum | solution.py:28
  253.2 83.3 %copy-start = (f32[192,768]{1,0:T(8,128)S(1)}, f32[192,768]{1,0:T(8,128)}, u32[]{:S(2)}) copy-start(f32[192,768]{1,0:T(8,128)} %get-tuple-element.3) | copy-start | bytes 1769476
  336.4 51.0 %copy-start.1 = (f32[8192]{0:T(1024)}, f32[8192]{0:T(1024)S(1)}, u32[]{:S(2)}) copy-start(f32[8192]{0:T(1024)S(1)} %max.19) | copy-start | bytes 98308
Sparse Core Ops, SparseCore 0:
  9.7 133.6 all-gather.1
  163.9 89.2 all-reduce.2
where the time goes:
time: 394 us
  waiting for transfers between devices  224 us (57%)
  blocking collectives  74.1 us (19%)
  matrix products  60.1 us (15%)
  local copies, waits for them, and re-layouts  18.5 us (5%)
  between operations  14.1 us (4%)
    all_gather x1, waiting for transfers between devices, body(): gathered = lax.all_gather(slab_embed, 'row', axis=0, tiled=True)  134 us
    psum x1, waiting for transfers between devices, body(): lax.psum((lookup(gathered, sel_index, first_row), lookup(gathered, cand_i...  89.4 us
    dot_general x2, matrix products, similar(): lax.dot_general(left, right, (((1,), (1,)), ((), ())), precision=lax.Prec...  60.1 us
    pmax x1, blocking collectives, body(): reached = lax.pmax(partial_value, 'row')  53.1 us
    psum x1, blocking collectives, body(): total_gain = lax.psum(gain_part, 'col')  21 us
    gather x2, local copies, waits for them, and re-layouts, lookup(): jnp.take(source, jnp.clip(position, 0, source.shape[0] - 1), axis=0)  18.5 us
  transfers between devices with their start and end apart: 2, of which 2 were waited for; matrix products, arithmetic and copies ran while one was open for 0% of the time, Pallas kernels for 0%

commit v1 on v0

--- a/solution.py
+++ b/solution.py
@@ -9,7 +9,7 @@
         left,
         right,
         (((1,), (1,)), ((), ())),
-        precision=lax.Precision.HIGHEST,
+        precision=lax.Precision.HIGH,
         preferred_element_type=jnp.float32,
     )
 
@@ -21,18 +21,71 @@
     return jnp.where(inside[:, None], picked, 0.0)
 
 
+def shift(value, axis, size, pairs):
+    return lax.ppermute(value, axis, [(i, j) for i, j in pairs if i < size and j < size])
+
+
+def col_parts(value, n_y, n_z):
+    size = n_y * n_z
+    here = lax.axis_index("col")
+    y, z = here // n_z, here % n_z
+    if n_z == 2:
+        other = shift(value, "col", size, [(c, c ^ 1) for c in range(size)])
+        pair = jnp.where(z == 0, jnp.stack([value, other]), jnp.stack([other, value]))
+    else:
+        pair = value[None]
+    if n_y == 1:
+        return pair
+    up = [(c, ((c // n_z + 1) % n_y) * n_z + c % n_z) for c in range(size)]
+    down = [(c, ((c // n_z - 1) % n_y) * n_z + c % n_z) for c in range(size)]
+    from_below = shift(pair, "col", size, up)
+    from_above = shift(pair, "col", size, down)
+    parts = [pair, from_above, None, from_below]
+    if n_y == 4:
+        parts[2] = shift(from_below, "col", size, up)
+        ordered = jnp.stack(parts)
+    else:
+        ordered = jnp.stack([pair, from_above])
+    return jnp.roll(ordered, y, axis=0).reshape((size,) + value.shape)
+
+
+def col_masked_sum(value, n_y, n_z):
+    size = n_y * n_z
+    if n_z == 2:
+        value = value + shift(value, "col", size, [(c, c ^ 1) for c in range(size)])
+    up = [(c, ((c // n_z + 1) % n_y) * n_z + c % n_z) for c in range(size)]
+    down = [(c, ((c // n_z - 1) % n_y) * n_z + c % n_z) for c in range(size)]
+    from_below = shift(value, "col", size, up)
+    from_above = shift(value, "col", size, down)
+    far = shift(from_below, "col", size, up)
+    return value + from_below + from_above + far
+
+
+def row_max(value, n):
+    here = lax.axis_index("row")
+    value = jnp.maximum(value, shift(value, "row", n, [(r, r ^ 1) for r in range(n)]))
+    x_up = [(r, (r & ~6) | ((((r >> 1) & 3) + 1) % 4) << 1) for r in range(n)]
+    x_down = [(r, (r & ~6) | ((((r >> 1) & 3) - 1) % 4) << 1) for r in range(n)]
+    value = jnp.maximum(value, jnp.maximum(shift(value, "row", n, x_up), shift(value, "row", n, x_down)))
+    value = jnp.maximum(value, shift(value, "row", n, x_up))
+    value = jnp.maximum(value, shift(value, "row", n, [(r, r ^ 8) for r in range(n)]))
+    return value
+
+
 def body(slab_embed, coverage_old, sel_index, cand_index):
     col_id = lax.axis_index("col")
     gathered = lax.all_gather(slab_embed, "row", axis=0, tiled=True)
     first_row = col_id * gathered.shape[0]
-    selected, chosen = lax.psum(
-        (lookup(gathered, sel_index, first_row), lookup(gathered, cand_index, first_row)), "col"
+    n_sel = sel_index.shape[0]
+    picked = col_masked_sum(
+        jnp.concatenate([lookup(gathered, sel_index, first_row), lookup(gathered, cand_index, first_row)]), 4, 2
     )
+    selected, chosen = picked[:n_sel], picked[n_sel:]
     partial_value = jnp.max(similar(selected, gathered), axis=0)
-    reached = lax.pmax(partial_value, "row")
+    reached = row_max(partial_value, 16)
     coverage = jnp.maximum(coverage_old, reached)
     gain_part = jnp.sum(jnp.maximum(similar(chosen, gathered) - coverage[None, :], 0.0), axis=1)
-    total_gain = lax.psum(gain_part, "col")
+    total_gain = jnp.sum(col_parts(gain_part, 4, 2), axis=0)
     return (coverage, total_gain)
 
 

time: 394 us -> 308 us (0.78)
  blocking collectives: 74.1 us -> 0 us
  matrix products: 60.1 us -> 33.9 us
  starting transfers between devices: 0.08 us -> 19.1 us
  waiting for transfers between devices: 224 us -> 219 us
    psum x1 -> x0, waiting for transfers between devices: 89.4 us -> none  [body(): lax.psum((lookup(gathered, sel_index, first_row), lookup(gathered, cand_i...]
    ppermute x0 -> x13, waiting for transfers between devices: none -> 84.5 us  [shift(): lax.ppermute(value, axis, [(i, j) for i, j in pairs if i < size and j < s...]
    pmax x1 -> x0, blocking collectives: 53.1 us -> none  [body(): reached = lax.pmax(partial_value, 'row')]
    dot_general x2, matrix products: 60.1 us -> 33.9 us  [similar(): lax.dot_general(left, right, (((1,), (1,)), ((), ())), precision=lax.Prec...]
    psum x1 -> x0, blocking collectives: 21 us -> none  [body(): total_gain = lax.psum(gain_part, 'col')]
    ppermute x0 -> x13, starting transfers between devices: none -> 19.1 us  [shift(): lax.ppermute(value, axis, [(i, j) for i, j in pairs if i < size and j < s...]
  transfers between devices with their start and end apart: 2 -> 14, of which waited for: 2 -> 11; matrix products, arithmetic and copies ran while one was open for 0% -> 0% of each run, Pallas kernels for 0% -> 0%
where the time goes in v1:
time: 308 us
  waiting for transfers between devices  219 us (71%)
  matrix products  33.9 us (11%)
  starting transfers between devices  19.1 us (6%)
  local copies, waits for them, and re-layouts  18.5 us (6%)
  between operations  14.2 us (5%)
    all_gather x1, waiting for transfers between devices, body(): gathered = lax.all_gather(slab_embed, 'row', axis=0, tiled=True)  134 us
    ppermute x13, waiting for transfers between devices, shift(): lax.ppermute(value, axis, [(i, j) for i, j in pairs if i < size and j < s...  84.5 us
    dot_general x2, matrix products, similar(): lax.dot_general(left, right, (((1,), (1,)), ((), ())), precision=lax.Prec...  33.9 us
    ppermute x13, starting transfers between devices, shift(): lax.ppermute(value, axis, [(i, j) for i, j in pairs if i < size and j < s...  19.1 us
    gather x2, local copies, waits for them, and re-layouts, lookup(): jnp.take(source, jnp.clip(position, 0, source.shape[0] - 1), axis=0)  18.5 us
  transfers between devices with their start and end apart: 14, of which 11 were waited for; matrix products, arithmetic and copies ran while one was open for 0% of the time, Pallas kernels for 0%

profile of v1, /device:TPU:0, one launch (start us, length us, event | category | flops | bytes accessed | tf_op | source)
XLA Modules:
  0.0 307.7 jit_solution(16716492885634201981)
XLA Ops:
  7.2 0.7 all-gather.2.cloned.1.call-update
  7.9 0.7 compare_and_fusion
  8.6 0.7 compare_and_fusion.2
  9.3 134.1 %all-gather.2.cloned.1.call-done = f32[8192,768]{1,0:T(8,128)} async-done(((f32[512,768]{1,0:T(8,128)}), f32[8192,768]{1,0:T(8,128)}) %all-gather.2.cloned.1.call-update) | async-done | bytes 25165840 | tf_op jit(solution)/shard_map/all_gather | solution.py:77
  143.4 9.3 %gather_fusion.1 = f32[192,768]{1,0:T(8,128)S(1)} fusion(f32[8192,768]{1,0:T(8,128)} %all-gather.2.cloned.1.call-done, s32[1024]{0:T(1024)S(1)} %pad_clamp_fusion), kind=kCustom, calls=%fused_computation.1 | custom fusion | bytes 1180416 | tf_op jit(solution)/shard_map/jit(_take)/gather | solution.py:20
  152.7 0.1 select_select_fusion
  152.9 9.1 %gather_fusion = f32[128,768]{1,0:T(8,128)S(1)} fusion(f32[8192,768]{1,0:T(8,128)} %all-gather.2.cloned.1.call-done, s32[1024]{0:T(1024)S(1)} %pad_clamp_fusion.1), kind=kCustom, calls=%fused_computation | custom fusion | bytes 786944 | tf_op jit(solution)/shard_map/jit(_take)/gather | solution.py:20
  162.0 0.1 select_select_fusion.1
  162.2 2.9 collective-permute-start
  165.1 22.6 %collective-permute-done = f32[320,768]{1,0:T(8,128)S(1)} collective-permute-done((f32[320,768]{1,0:T(8,128)S(1)}, f32[320,768]{1,0:T(8,128)S(1)}, u32[]{:S(2)}, u32[]{:S(2)}) %collective-permute-start) | collective-permute-done | bytes 983072 | tf_op jit(solution)/shard_map/ppermute | solution.py:25
  187.8 1.6 collective-permute-start.1
  189.4 1.8 collective-permute-start.2
  191.1 21.1 %collective-permute-done.1 = f32[320,768]{1,0:T(8,128)S(1)} collective-permute-done((f32[320,768]{1,0:T(8,128)S(1)}, f32[320,768]{1,0:T(8,128)S(1)}, u32[]{:S(2)}, u32[]{:S(2)}) %collective-permute-start.1) | collective-permute-done | bytes 983072 | tf_op jit(solution)/shard_map/ppermute | solution.py:25
  212.2 0.3 collective-permute-start.3
  212.5 23.1 %collective-permute-done.3 = f32[320,768]{1,0:T(8,128)S(1)} collective-permute-done((f32[320,768]{1,0:T(8,128)S(1)}, f32[320,768]{1,0:T(8,128)S(1)}, u32[]{:S(2)}, u32[]{:S(2)}) %collective-permute-start.3) | collective-permute-done | bytes 983072 | tf_op jit(solution)/shard_map/ppermute | solution.py:25
  235.6 0.3 add_add_fusion
  235.9 16.5 %convolution_reduce_fusion = f32[8192]{0:T(1024)S(1)} fusion(f32[8192,768]{1,0:T(8,128)} %all-gather.2.cloned.1.call-done, f32[320,768]{1,0:T(8,128)S(1)} %add_add_fusion), kind=kOutput, calls=%fused_computation.5 | convolution fusion | flops 4832878592 | bytes 25591808 | tf_op jit(solution)/shard_map/dot_general | solution.py:8
  252.5 1.2 collective-permute-done.4
  253.7 1.1 collective-permute-start.5
  254.8 2.1 collective-permute-start.6
  256.9 1.9 collective-permute-done.5
  258.8 1.1 collective-permute-start.7
  260.0 4.1 %collective-permute-done.7 = f32[8192]{0:T(1024)S(1)} collective-permute-done((f32[8192]{0:T(1024)S(1)}, f32[8192]{0:T(1024)S(1)}, u32[]{:S(2)}, u32[]{:S(2)}) %collective-permute-start.7) | collective-permute-done | bytes 32800 | tf_op jit(solution)/shard_map/ppermute | solution.py:25
  264.0 1.7 collective-permute-start.8
  265.8 2.2 collective-permute-done.8
  268.0 17.4 %fusion.1 = f32[192]{0:T(256)S(1)} fusion(f32[8192]{0:T(1024)S(1)} %maximum_maximum_fusion, f32[8192,768]{1,0:T(8,128)} %all-gather.2.cloned.1.call-done, f32[320,768]{1,0:T(8,128)S(1)} %add_add_fusion), kind=kOutput, calls=%fused_computation.4 | convolution fusion | flops 7252475904 | bytes 25789184 | tf_op jit(solution)/shard_map/dot_general | solution.py:8
  285.4 3.1 %collective-permute-start.9 = (f32[192]{0:T(256)S(1)}, f32[192]{0:T(256)S(1)}, u32[]{:S(2)}, u32[]{:S(2)}) collective-permute-start(f32[192]{0:T(256)S(1)} %fusion.1), channel_id=1, source_target_pairs={{0,1},{1,0},{2,3},{3,2},{4,5},{5,4},{6,7},{7,6},{8,9},{9,8},{10,11... | collective-permute-start | bytes 2312 | tf_op jit(solution)/shard_map/ppermute | solution.py:25
  288.5 2.0 collective-permute-done.9
  290.7 3.2 %collective-permute-start.10 = (f32[2,192]{1,0:T(2,128)S(1)}, f32[2,192]{1,0:T(2,128)S(1)}, u32[]{:S(2)}, u32[]{:S(2)}) collective-permute-start(f32[2,192]{1,0:T(2,128)S(1)} %maximum_select_fusion), channel_id=1, source_target_pairs={{0,6},{1,7},{2,0},{3,1},{4,2},{5,3},{6,4},{7,5},{8,14},{9,15},{10,... | collective-permute-start | bytes 4616 | tf_op jit(solution)/shard_map/ppermute | solution.py:25
  293.8 1.6 collective-permute-done.11
  295.5 4.8 %collective-permute-done.12 = f32[2,192]{1,0:T(2,128)S(1)} collective-permute-done((f32[2,192]{1,0:T(2,128)S(1)}, f32[2,192]{1,0:T(2,128)S(1)}, u32[]{:S(2)}, u32[]{:S(2)}) %collective-permute-start.12) | collective-permute-done | bytes 1568 | tf_op jit(solution)/shard_map/ppermute | solution.py:25
  300.2 0.6 dynamic-slice_reduce_fusion
  (25 shorter events, 0.5 us)
Async XLA Ops:
  7.2 136.2 %all-gather.2.cloned.1.call-start = ((), (), s32[]{:S(2)}) async-start(), calls=%async_computation | async-start | bytes 26738688 | tf_op jit(solution)/shard_map/all_gather | solution.py:77
  152.7 115.2 %copy-start.1 = (f32[8192]{0:T(1024)S(1)}, f32[8192]{0:T(1024)}, u32[]{:S(2)}) copy-start(f32[8192]{0:T(1024)} %param.5) | copy-start | bytes 98308
  162.2 25.5 %collective-permute-start = (f32[320,768]{1,0:T(8,128)S(1)}, f32[320,768]{1,0:T(8,128)S(1)}, u32[]{:S(2)}, u32[]{:S(2)}) collective-permute-start(f32[320,768]{1,0:T(8,128)S(1)} %pad_maximum_fusion), channel_id=1, source_target_pairs={{0,1},{1,0},{2,3},{3,2},{4,5},{5,4},{6,7},{7,6},{8,9},{9,8},{10,11... | collective-permute-start | bytes 2949128 | tf_op jit(solution)/shard_map/ppermute | solution.py:25
  187.8 24.4 %collective-permute-start.1 = (f32[320,768]{1,0:T(8,128)S(1)}, f32[320,768]{1,0:T(8,128)S(1)}, u32[]{:S(2)}, u32[]{:S(2)}) collective-permute-start(f32[320,768]{1,0:T(8,128)S(1)} %fusion.4), channel_id=1, source_target_pairs={{0,2},{1,3},{2,4},{3,5},{4,6},{5,7},{6,0},{7,1},{8,10},{9,11},{10,... | collective-permute-start | bytes 2949128 | tf_op jit(solution)/shard_map/ppermute | solution.py:25
  189.4 23.1 %collective-permute-start.2 = (f32[320,768]{1,0:T(8,128)S(1)}, f32[320,768]{1,0:T(8,128)S(1)}, u32[]{:S(2)}, u32[]{:S(2)}) collective-permute-start(f32[320,768]{1,0:T(8,128)S(1)} %fusion.4), channel_id=1, source_target_pairs={{0,6},{1,7},{2,0},{3,1},{4,2},{5,3},{6,4},{7,5},{8,14},{9,15},{10,... | collective-permute-start | bytes 2949128 | tf_op jit(solution)/shard_map/ppermute | solution.py:25
  212.2 23.4 %collective-permute-start.3 = (f32[320,768]{1,0:T(8,128)S(1)}, f32[320,768]{1,0:T(8,128)S(1)}, u32[]{:S(2)}, u32[]{:S(2)}) collective-permute-start(f32[320,768]{1,0:T(8,128)S(1)} %collective-permute-done.1), channel_id=1, source_target_pairs={{0,2},{1,3},{2,4},{3,5},{4,6},{5,7},{6,0},{7,1},{8,10},{9,11},{10,... | collective-permute-start | bytes 2949128 | tf_op jit(solution)/shard_map/ppermute | solution.py:25
  252.4 1.3 collective-permute-start.4
  253.7 5.1 %collective-permute-start.5 = (f32[8192]{0:T(1024)S(1)}, f32[8192]{0:T(1024)S(1)}, u32[]{:S(2)}, u32[]{:S(2)}) collective-permute-start(f32[8192]{0:T(1024)S(1)} %max.32), channel_id=1, source_target_pairs={{0,16},{8,24},{16,32},{24,40},{32,48},{40,56},{48,0},{56,8},{64,80... | collective-permute-start | bytes 98312 | tf_op jit(solution)/shard_map/ppermute | solution.py:25
  254.8 4.0 %collective-permute-start.6 = (f32[8192]{0:T(1024)S(1)}, f32[8192]{0:T(1024)S(1)}, u32[]{:S(2)}, u32[]{:S(2)}) collective-permute-start(f32[8192]{0:T(1024)S(1)} %max.32), channel_id=1, source_target_pairs={{0,48},{8,56},{16,0},{24,8},{32,16},{40,24},{48,32},{56,40},{64,11... | collective-permute-start | bytes 98312 | tf_op jit(solution)/shard_map/ppermute | solution.py:25
  258.8 5.2 %collective-permute-start.7 = (f32[8192]{0:T(1024)S(1)}, f32[8192]{0:T(1024)S(1)}, u32[]{:S(2)}, u32[]{:S(2)}) collective-permute-start(f32[8192]{0:T(1024)S(1)} %maximum_maximum_fusion.1), channel_id=1, source_target_pairs={{0,16},{8,24},{16,32},{24,40},{32,48},{40,56},{48,0},{56,8},{64,80... | collective-permute-start | bytes 98312 | tf_op jit(solution)/shard_map/ppermute | solution.py:25
  264.0 3.9 %collective-permute-start.8 = (f32[8192]{0:T(1024)S(1)}, f32[8192]{0:T(1024)S(1)}, u32[]{:S(2)}, u32[]{:S(2)}) collective-permute-start(f32[8192]{0:T(1024)S(1)} %max.35), channel_id=1, source_target_pairs={{0,64},{8,72},{16,80},{24,88},{32,96},{40,104},{48,112},{56,120},{... | collective-permute-start | bytes 98312 | tf_op jit(solution)/shard_map/ppermute | solution.py:25
  268.0 32.9 %copy-start = (f32[8192]{0:T(1024)}, f32[8192]{0:T(1024)S(1)}, u32[]{:S(2)}) copy-start(f32[8192]{0:T(1024)S(1)} %maximum_maximum_fusion) | copy-start | bytes 98308
  285.4 5.2 %collective-permute-start.9 = (f32[192]{0:T(256)S(1)}, f32[192]{0:T(256)S(1)}, u32[]{:S(2)}, u32[]{:S(2)}) collective-permute-start(f32[192]{0:T(256)S(1)} %fusion.1), channel_id=1, source_target_pairs={{0,1},{1,0},{2,3},{3,2},{4,5},{5,4},{6,7},{7,6},{8,9},{9,8},{10,11... | collective-permute-start | bytes 2312 | tf_op jit(solution)/shard_map/ppermute | solution.py:25
  290.5 4.9 %collective-permute-start.11 = (f32[2,192]{1,0:T(2,128)S(1)}, f32[2,192]{1,0:T(2,128)S(1)}, u32[]{:S(2)}, u32[]{:S(2)}) collective-permute-start(f32[2,192]{1,0:T(2,128)S(1)} %maximum_select_fusion), channel_id=1, source_target_pairs={{0,2},{1,3},{2,4},{3,5},{4,6},{5,7},{6,0},{7,1},{8,10},{9,11},{10,... | collective-permute-start | bytes 4616 | tf_op jit(solution)/shard_map/ppermute | solution.py:25
  290.7 4.8 %collective-permute-start.10 = (f32[2,192]{1,0:T(2,128)S(1)}, f32[2,192]{1,0:T(2,128)S(1)}, u32[]{:S(2)}, u32[]{:S(2)}) collective-permute-start(f32[2,192]{1,0:T(2,128)S(1)} %maximum_select_fusion), channel_id=1, source_target_pairs={{0,6},{1,7},{2,0},{3,1},{4,2},{5,3},{6,4},{7,5},{8,14},{9,15},{10,... | collective-permute-start | bytes 4616 | tf_op jit(solution)/shard_map/ppermute | solution.py:25
  295.4 4.8 %collective-permute-start.12 = (f32[2,192]{1,0:T(2,128)S(1)}, f32[2,192]{1,0:T(2,128)S(1)}, u32[]{:S(2)}, u32[]{:S(2)}) collective-permute-start(f32[2,192]{1,0:T(2,128)S(1)} %collective-permute-done.11), channel_id=1, source_target_pairs={{0,2},{1,3},{2,4},{3,5},{4,6},{5,7},{6,0},{7,1},{8,10},{9,11},{10,... | collective-permute-start | bytes 4616 | tf_op jit(solution)/shard_map/ppermute | solution.py:25
Sparse Core Ops, SparseCore 0:
  9.7 133.6 all-gather.1

commit v2 on v0

--- a/solution.py
+++ b/solution.py
@@ -2,6 +2,8 @@
 import jax.numpy as jnp
 from jax import lax
 from jax.sharding import PartitionSpec as P
+
+N_Y, N_Z = 4, 2
 
 
 def similar(left, right):
@@ -9,7 +11,7 @@
         left,
         right,
         (((1,), (1,)), ((), ())),
-        precision=lax.Precision.HIGHEST,
+        precision=lax.Precision.HIGH,
         preferred_element_type=jnp.float32,
     )
 
@@ -21,18 +23,63 @@
     return jnp.where(inside[:, None], picked, 0.0)
 
 
+def col_of(y, z):
+    return (y % N_Y) * N_Z + z
+
+
+def y_shift(value, step):
+    pairs = [(col_of(y, z), col_of(y + step, z)) for y in range(N_Y) for z in range(N_Z)]
+    return lax.ppermute(value, "col", pairs)
+
+
+def col_masked_sum(value):
+    here = lax.axis_index("col")
+    y, z = here // N_Z, here % N_Z
+    half = value.shape[0] // N_Z
+    quarter = half // N_Y
+    halves = value.reshape(N_Z, half, *value.shape[1:])
+    mine = jnp.where(z == 0, halves[0], halves[1])
+    theirs = jnp.where(z == 0, halves[1], halves[0])
+    mine = mine + lax.ppermute(theirs, "col", [(c, c ^ 1) for c in range(N_Y * N_Z)])
+
+    def part(k):
+        return lax.dynamic_slice_in_dim(mine, ((y + k) % N_Y) * quarter, quarter)
+
+    own = part(0)
+    for k in range(1, N_Y):
+        own = own + y_shift(part(k), k)
+    pieces = [own] + [y_shift(own, -k) for k in range(1, N_Y)]
+    ordered = jnp.roll(jnp.stack(pieces), y, axis=0).reshape(half, *value.shape[1:])
+    other = lax.ppermute(ordered, "col", [(c, c ^ 1) for c in range(N_Y * N_Z)])
+    return jnp.where(z == 0, jnp.concatenate([ordered, other]), jnp.concatenate([other, ordered]))
+
+
+def all_max(value, axis, n):
+    result = value
+    for k in range(1, n):
+        result = jnp.maximum(result, lax.ppermute(value, axis, [(i, i ^ k) for i in range(n)]))
+    return result
+
+
+def all_sum(value, axis, n):
+    here = lax.axis_index(axis)
+    parts = jnp.stack([value] + [lax.ppermute(value, axis, [(i, i ^ k) for i in range(n)]) for k in range(1, n)])
+    ordered = jnp.take(parts, jnp.arange(n) ^ here, axis=0)
+    return jnp.sum(ordered, axis=0)
+
+
 def body(slab_embed, coverage_old, sel_index, cand_index):
+    n_row = 16
     col_id = lax.axis_index("col")
     gathered = lax.all_gather(slab_embed, "row", axis=0, tiled=True)
     first_row = col_id * gathered.shape[0]
-    selected, chosen = lax.psum(
-        (lookup(gathered, sel_index, first_row), lookup(gathered, cand_index, first_row)), "col"
-    )
+    selected = col_masked_sum(lookup(gathered, sel_index, first_row))
+    chosen = col_masked_sum(lookup(gathered, cand_index, first_row))
     partial_value = jnp.max(similar(selected, gathered), axis=0)
-    reached = lax.pmax(partial_value, "row")
+    reached = all_max(partial_value, "row", n_row)
     coverage = jnp.maximum(coverage_old, reached)
     gain_part = jnp.sum(jnp.maximum(similar(chosen, gathered) - coverage[None, :], 0.0), axis=1)
-    total_gain = lax.psum(gain_part, "col")
+    total_gain = all_sum(gain_part, "col", N_Y * N_Z)
     return (coverage, total_gain)
 
 

time: 394 us -> 290 us (0.74)
  blocking collectives: 74.1 us -> 0 us
  waiting for transfers between devices: 224 us -> 164 us
  starting transfers between devices: 0.08 us -> 55.8 us
  matrix products: 60.1 us -> 33.8 us
    psum x1 -> x0, waiting for transfers between devices: 89.4 us -> none  [body(): lax.psum((lookup(gathered, sel_index, first_row), lookup(gathered, cand_i...]
    ppermute x0 -> x38, starting transfers between devices: none -> 55.7 us  [the longest x15 21 us: all_max(): lax.ppermute(value, axis, [(i, i ^ k) for i in range(n)])]
    pmax x1 -> x0, blocking collectives: 53.1 us -> none  [body(): reached = lax.pmax(partial_value, 'row')]
    ppermute x0 -> x38, waiting for transfers between devices: none -> 29 us  [the longest x12 18.5 us: y_shift(): return lax.ppermute(value, 'col', pairs)]
    dot_general x2, matrix products: 60.1 us -> 33.8 us  [similar(): lax.dot_general(left, right, (((1,), (1,)), ((), ())), precision=lax.Prec...]
    psum x1 -> x0, blocking collectives: 21 us -> none  [body(): total_gain = lax.psum(gain_part, 'col')]
  transfers between devices with their start and end apart: 2 -> 39, of which waited for: 2 -> 20; matrix products, arithmetic and copies ran while one was open for 0% -> 4% of each run, Pallas kernels for 0% -> 0%
where the time goes in v2:
time: 290 us; the launch traced here: 289 us
  waiting for transfers between devices  164 us (57%)
  starting transfers between devices  55.8 us (19%)
  matrix products  33.8 us (12%)
  local copies, waits for them, and re-layouts  19.2 us (7%)
  between operations  14.3 us (5%)
    all_gather x1, waiting for transfers between devices, body(): gathered = lax.all_gather(slab_embed, 'row', axis=0, tiled=True)  134 us
    dot_general x2, matrix products, similar(): lax.dot_general(left, right, (((1,), (1,)), ((), ())), precision=lax.Prec...  33.8 us
    ppermute x15, starting transfers between devices, all_max(): lax.ppermute(value, axis, [(i, i ^ k) for i in range(n)])  21 us
    ppermute x12, waiting for transfers between devices, y_shift(): return lax.ppermute(value, 'col', pairs)  18.5 us
    gather x2, local copies, waits for them, and re-layouts, lookup(): jnp.take(source, jnp.clip(position, 0, source.shape[0] - 1), axis=0)  18.5 us
    ppermute x7, starting transfers between devices, all_sum(): lax.ppermute(value, axis, [(i, i ^ k) for i in range(n)])  14.2 us
    ppermute x12, starting transfers between devices, y_shift(): return lax.ppermute(value, 'col', pairs)  13.1 us
    ppermute x7, waiting for transfers between devices, all_sum(): lax.ppermute(value, axis, [(i, i ^ k) for i in range(n)])  5.82 us
  transfers between devices with their start and end apart: 39, of which 20 were waited for; matrix products, arithmetic and copies ran while one was open for 4% of the time, Pallas kernels for 0%

profile of v2, /device:TPU:0, one launch (start us, length us, event | category | flops | bytes accessed | tf_op | source)
XLA Modules:
  0.0 289.4 jit_solution(17506802448954029451)
XLA Ops:
  9.3 134.1 %all-gather.2.cloned.1.call-done = f32[8192,768]{1,0:T(8,128)} async-done(((f32[512,768]{1,0:T(8,128)}), f32[8192,768]{1,0:T(8,128)}) %all-gather.2.cloned.1.call-update) | async-done | bytes 25165840 | tf_op jit(solution)/shard_map/all_gather | solution.py:74
  143.4 9.1 %gather_fusion = f32[128,768]{1,0:T(8,128)S(1)} fusion(f32[8192,768]{1,0:T(8,128)} %all-gather.2.cloned.1.call-done, s32[1024]{0:T(1024)S(1)} %get-tuple-element.19), kind=kCustom, calls=%fused_computation | custom fusion | bytes 786944 | tf_op jit(solution)/shard_map/jit(_take)/gather | solution.py:22
  152.7 2.9 %collective-permute-start = (f32[64,768]{1,0:T(8,128)S(1)}, f32[64,768]{1,0:T(8,128)S(1)}, u32[]{:S(2)}, u32[]{:S(2)}) collective-permute-start(f32[64,768]{1,0:T(8,128)S(1)} %slice_select_fusion.1), channel_id=1, source_target_pairs={{0,1},{1,0},{2,3},{3,2},{4,5},{5,4},{6,7},{7,6},{8,9},{9,8},{10,11... | collective-permute-start | bytes 589832 | tf_op jit(solution)/shard_map/ppermute | solution.py:43
  155.6 9.3 %gather_fusion.1 = f32[192,768]{1,0:T(8,128)S(1)} fusion(f32[8192,768]{1,0:T(8,128)} %all-gather.2.cloned.1.call-done, s32[1024]{0:T(1024)S(1)} %get-tuple-element.18), kind=kCustom, calls=%fused_computation.1 | custom fusion | bytes 1180416 | tf_op jit(solution)/shard_map/jit(_take)/gather | solution.py:22
  165.0 2.8 collective-permute-start.3
  169.9 3.6 %collective-permute-done.2 = f32[16,768]{1,0:T(8,128)S(1)} collective-permute-done((f32[16,768]{1,0:T(8,128)S(1)}, f32[16,768]{1,0:T(8,128)S(1)}, u32[]{:S(2)}, u32[]{:S(2)}) %collective-permute-start.2) | collective-permute-done | bytes 49184 | tf_op jit(solution)/shard_map/ppermute | solution.py:32
  176.6 1.2 collective-permute-start.6
  178.2 2.9 collective-permute-done.5
  181.9 1.8 collective-permute-done.23
  183.8 1.6 collective-permute-start.26
  185.4 1.7 collective-permute-start.25
  188.2 3.1 %collective-permute-done.25 = f32[24,768]{1,0:T(8,128)S(1)} collective-permute-done((f32[24,768]{1,0:T(8,128)S(1)}, f32[24,768]{1,0:T(8,128)S(1)}, u32[]{:S(2)}, u32[]{:S(2)}) %collective-permute-start.25) | collective-permute-done | bytes 73760 | tf_op jit(solution)/shard_map/ppermute | solution.py:32
  191.3 1.4 collective-permute-done.24
  197.1 2.9 collective-permute-done.28
  200.8 16.4 %convolution_reduce_fusion = f32[8192]{0:T(1024)S(1)} fusion(f32[8192,768]{1,0:T(8,128)} %all-gather.2.cloned.1.call-done, f32[64,768]{1,0:T(8,128)S(1)} %collective-permute-done.7, f32[64,768]{1,0:T(8,128)S(1)} %bitcast.41, pred[]{:T(512)S(6)} %eq.24), kind=kOutput, calls=%fused_computation.6 | convolution fusion | flops 4833173504 | bytes 25591808 | tf_op jit(solution)/shard_map/dot_general | solution.py:10
  217.4 2.7 collective-permute-start.21
  220.1 3.2 %collective-permute-start.20 = (f32[8192]{0:T(1024)S(1)}, f32[8192]{0:T(1024)S(1)}, u32[]{:S(2)}, u32[]{:S(2)}) collective-permute-start(f32[8192]{0:T(1024)S(1)} %convolution_reduce_fusion), channel_id=1, source_target_pairs={{0,104},{8,96},{16,120},{24,112},{32,72},{40,64},{48,88},{56,80},{... | collective-permute-start | bytes 98312 | tf_op jit(solution)/shard_map/ppermute | solution.py:60
  223.3 2.1 collective-permute-start.19
  225.4 1.5 collective-permute-start.17
  226.9 2.3 collective-permute-start.16
  230.9 1.5 collective-permute-start.13
  233.6 2.6 collective-permute-start.30
  236.2 2.9 %collective-permute-start.11 = (f32[8192]{0:T(1024)S(1)}, f32[8192]{0:T(1024)S(1)}, u32[]{:S(2)}, u32[]{:S(2)}) collective-permute-start(f32[8192]{0:T(1024)S(1)} %convolution_reduce_fusion), channel_id=1, source_target_pairs={{0,32},{8,40},{16,48},{24,56},{32,0},{40,8},{48,16},{56,24},{64,96... | collective-permute-start | bytes 98312 | tf_op jit(solution)/shard_map/ppermute | solution.py:60
  243.8 17.4 %fusion.1 = f32[192]{0:T(256)S(1)} fusion(f32[8192]{0:T(1024)S(1)} %maximum_maximum_fusion, f32[8192,768]{1,0:T(8,128)} %all-gather.2.cloned.1.call-done, f32[96,768]{1,0:T(8,128)S(1)} %collective-permute-done.30, f32[96,768]{1,0:T(8,128)S(1)} %bitcast.39, pred[]{:T(512)S(6)} %eq.24), kind=kOutput, calls=%fused_computation.5 | convolution fusion | flops 7252918272 | bytes 25789184 | tf_op jit(solution)/shard_map/dot_general | solution.py:10
  261.2 3.1 %collective-permute-start.31 = (f32[192]{0:T(256)S(1)}, f32[192]{0:T(256)S(1)}, u32[]{:S(2)}, u32[]{:S(2)}) collective-permute-start(f32[192]{0:T(256)S(1)} %fusion.1), channel_id=1, source_target_pairs={{0,1},{1,0},{2,3},{3,2},{4,5},{5,4},{6,7},{7,6},{8,9},{9,8},{10,11... | collective-permute-start | bytes 2312 | tf_op jit(solution)/shard_map/ppermute | solution.py:66
  265.0 1.3 collective-permute-start.33
  266.3 1.4 collective-permute-start.34
  267.7 4.6 %collective-permute-start.35 = (f32[192]{0:T(256)S(1)}, f32[192]{0:T(256)S(1)}, u32[]{:S(2)}, u32[]{:S(2)}) collective-permute-start(f32[192]{0:T(256)S(1)} %fusion.1), channel_id=1, source_target_pairs={{0,5},{1,4},{2,7},{3,6},{4,1},{5,0},{6,3},{7,2},{8,13},{9,12},{10,... | collective-permute-start | bytes 2312 | tf_op jit(solution)/shard_map/ppermute | solution.py:66
  272.3 1.8 collective-permute-start.36
  274.1 1.3 collective-permute-start.37
  275.5 1.6 collective-permute-done.36
  277.1 4.3 %collective-permute-done.37 = f32[192]{0:T(256)S(1)} collective-permute-done((f32[192]{0:T(256)S(1)}, f32[192]{0:T(256)S(1)}, u32[]{:S(2)}, u32[]{:S(2)}) %collective-permute-start.37) | collective-permute-done | bytes 800 | tf_op jit(solution)/shard_map/ppermute | solution.py:66
  (91 shorter events, 24.7 us)
Async XLA Ops:
  7.2 136.2 %all-gather.2.cloned.1.call-start = ((), (), s32[]{:S(2)}) async-start(), calls=%async_computation | async-start | bytes 26738688 | tf_op jit(solution)/shard_map/all_gather | solution.py:74
  152.7 12.3 %collective-permute-start = (f32[64,768]{1,0:T(8,128)S(1)}, f32[64,768]{1,0:T(8,128)S(1)}, u32[]{:S(2)}, u32[]{:S(2)}) collective-permute-start(f32[64,768]{1,0:T(8,128)S(1)} %slice_select_fusion.1), channel_id=1, source_target_pairs={{0,1},{1,0},{2,3},{3,2},{4,5},{5,4},{6,7},{7,6},{8,9},{9,8},{10,11... | collective-permute-start | bytes 589832 | tf_op jit(solution)/shard_map/ppermute | solution.py:43
  165.0 4.8 %collective-permute-start.3 = (f32[16,768]{1,0:T(8,128)S(1)}, f32[16,768]{1,0:T(8,128)S(1)}, u32[]{:S(2)}, u32[]{:S(2)}) collective-permute-start(f32[16,768]{1,0:T(8,128)S(1)} %get-tuple-element.14), channel_id=1, source_target_pairs={{0,6},{1,7},{2,0},{3,1},{4,2},{5,3},{6,4},{7,5},{8,14},{9,15},{10,... | collective-permute-start | bytes 147464 | tf_op jit(solution)/shard_map/ppermute | solution.py:32
  167.8 5.6 %collective-permute-start.2 = (f32[16,768]{1,0:T(8,128)S(1)}, f32[16,768]{1,0:T(8,128)S(1)}, u32[]{:S(2)}, u32[]{:S(2)}) collective-permute-start(f32[16,768]{1,0:T(8,128)S(1)} %get-tuple-element.15), channel_id=1, source_target_pairs={{0,4},{1,5},{2,6},{3,7},{4,0},{5,1},{6,2},{7,3},{8,12},{9,13},{10,... | collective-permute-start | bytes 147464 | tf_op jit(solution)/shard_map/ppermute | solution.py:32
  168.7 5.3 %collective-permute-start.1 = (f32[16,768]{1,0:T(8,128)S(1)}, f32[16,768]{1,0:T(8,128)S(1)}, u32[]{:S(2)}, u32[]{:S(2)}) collective-permute-start(f32[16,768]{1,0:T(8,128)S(1)} %get-tuple-element.13), channel_id=1, source_target_pairs={{0,2},{1,3},{2,4},{3,5},{4,6},{5,7},{6,0},{7,1},{8,10},{9,11},{10,... | collective-permute-start | bytes 147464 | tf_op jit(solution)/shard_map/ppermute | solution.py:32
  174.7 9.1 %collective-permute-start.23 = (f32[96,768]{1,0:T(8,128)S(1)}, f32[96,768]{1,0:T(8,128)S(1)}, u32[]{:S(2)}, u32[]{:S(2)}) collective-permute-start(f32[96,768]{1,0:T(8,128)S(1)} %slice_select_fusion), channel_id=1, source_target_pairs={{0,1},{1,0},{2,3},{3,2},{4,5},{5,4},{6,7},{7,6},{8,9},{9,8},{10,11... | collective-permute-start | bytes 884744 | tf_op jit(solution)/shard_map/ppermute | solution.py:43
  175.4 5.6 %collective-permute-start.5 = (f32[16,768]{1,0:T(8,128)S(1)}, f32[16,768]{1,0:T(8,128)S(1)}, u32[]{:S(2)}, u32[]{:S(2)}) collective-permute-start(f32[16,768]{1,0:T(8,128)S(1)} %get-tuple-element.7), channel_id=1, source_target_pairs={{0,4},{1,5},{2,6},{3,7},{4,0},{5,1},{6,2},{7,3},{8,12},{9,13},{10,... | collective-permute-start | bytes 147464 | tf_op jit(solution)/shard_map/ppermute | solution.py:32
  176.6 5.3 %collective-permute-start.6 = (f32[16,768]{1,0:T(8,128)S(1)}, f32[16,768]{1,0:T(8,128)S(1)}, u32[]{:S(2)}, u32[]{:S(2)}) collective-permute-start(f32[16,768]{1,0:T(8,128)S(1)} %get-tuple-element.7), channel_id=1, source_target_pairs={{0,2},{1,3},{2,4},{3,5},{4,6},{5,7},{6,0},{7,1},{8,10},{9,11},{10,... | collective-permute-start | bytes 147464 | tf_op jit(solution)/shard_map/ppermute | solution.py:32
  185.4 5.9 %collective-permute-start.25 = (f32[24,768]{1,0:T(8,128)S(1)}, f32[24,768]{1,0:T(8,128)S(1)}, u32[]{:S(2)}, u32[]{:S(2)}) collective-permute-start(f32[24,768]{1,0:T(8,128)S(1)} %get-tuple-element.12), channel_id=1, source_target_pairs={{0,4},{1,5},{2,6},{3,7},{4,0},{5,1},{6,2},{7,3},{8,12},{9,13},{10,... | collective-permute-start | bytes 221192 | tf_op jit(solution)/shard_map/ppermute | solution.py:32
  187.1 5.6 %collective-permute-start.24 = (f32[24,768]{1,0:T(8,128)S(1)}, f32[24,768]{1,0:T(8,128)S(1)}, u32[]{:S(2)}, u32[]{:S(2)}) collective-permute-start(f32[24,768]{1,0:T(8,128)S(1)} %get-tuple-element.10), channel_id=1, source_target_pairs={{0,2},{1,3},{2,4},{3,5},{4,6},{5,7},{6,0},{7,1},{8,10},{9,11},{10,... | collective-permute-start | bytes 221192 | tf_op jit(solution)/shard_map/ppermute | solution.py:32
  193.0 7.8 %collective-permute-start.7 = (f32[64,768]{1,0:T(8,128)S(1)}, f32[64,768]{1,0:T(8,128)S(1)}, u32[]{:S(2)}, u32[]{:S(2)}) collective-permute-start(f32[64,768]{1,0:T(8,128)S(1)} %bitcast.40), channel_id=1, source_target_pairs={{0,1},{1,0},{2,3},{3,2},{4,5},{5,4},{6,7},{7,6},{8,9},{9,8},{10,11... | collective-permute-start | bytes 589832 | tf_op jit(solution)/shard_map/ppermute | solution.py:53
  194.2 5.9 %collective-permute-start.28 = (f32[24,768]{1,0:T(8,128)S(1)}, f32[24,768]{1,0:T(8,128)S(1)}, u32[]{:S(2)}, u32[]{:S(2)}) collective-permute-start(f32[24,768]{1,0:T(8,128)S(1)} %get-tuple-element.3), channel_id=1, source_target_pairs={{0,4},{1,5},{2,6},{3,7},{4,0},{5,1},{6,2},{7,3},{8,12},{9,13},{10,... | collective-permute-start | bytes 221192 | tf_op jit(solution)/shard_map/ppermute | solution.py:32
  195.2 5.6 %collective-permute-start.29 = (f32[24,768]{1,0:T(8,128)S(1)}, f32[24,768]{1,0:T(8,128)S(1)}, u32[]{:S(2)}, u32[]{:S(2)}) collective-permute-start(f32[24,768]{1,0:T(8,128)S(1)} %get-tuple-element.3), channel_id=1, source_target_pairs={{0,2},{1,3},{2,4},{3,5},{4,6},{5,7},{6,0},{7,1},{8,10},{9,11},{10,... | collective-permute-start | bytes 221192 | tf_op jit(solution)/shard_map/ppermute | solution.py:32
  217.3 8.1 %collective-permute-start.22 = (f32[8192]{0:T(1024)S(1)}, f32[8192]{0:T(1024)S(1)}, u32[]{:S(2)}, u32[]{:S(2)}) collective-permute-start(f32[8192]{0:T(1024)S(1)} %convolution_reduce_fusion), channel_id=1, source_target_pairs={{0,120},{8,112},{16,104},{24,96},{32,88},{40,80},{48,72},{56,64},{... | collective-permute-start | bytes 98312 | tf_op jit(solution)/shard_map/ppermute | solution.py:60
  217.4 9.5 %collective-permute-start.21 = (f32[8192]{0:T(1024)S(1)}, f32[8192]{0:T(1024)S(1)}, u32[]{:S(2)}, u32[]{:S(2)}) collective-permute-start(f32[8192]{0:T(1024)S(1)} %convolution_reduce_fusion), channel_id=1, source_target_pairs={{0,112},{8,120},{16,96},{24,104},{32,80},{40,88},{48,64},{56,72},{... | collective-permute-start | bytes 98312 | tf_op jit(solution)/shard_map/ppermute | solution.py:60
  220.1 9.1 %collective-permute-start.20 = (f32[8192]{0:T(1024)S(1)}, f32[8192]{0:T(1024)S(1)}, u32[]{:S(2)}, u32[]{:S(2)}) collective-permute-start(f32[8192]{0:T(1024)S(1)} %convolution_reduce_fusion), channel_id=1, source_target_pairs={{0,104},{8,96},{16,120},{24,112},{32,72},{40,64},{48,88},{56,80},{... | collective-permute-start | bytes 98312 | tf_op jit(solution)/shard_map/ppermute | solution.py:60
  223.3 6.6 %collective-permute-start.19 = (f32[8192]{0:T(1024)S(1)}, f32[8192]{0:T(1024)S(1)}, u32[]{:S(2)}, u32[]{:S(2)}) collective-permute-start(f32[8192]{0:T(1024)S(1)} %convolution_reduce_fusion), channel_id=1, source_target_pairs={{0,96},{8,104},{16,112},{24,120},{32,64},{40,72},{48,80},{56,88},{... | collective-permute-start | bytes 98312 | tf_op jit(solution)/shard_map/ppermute | solution.py:60
  225.4 5.5 %collective-permute-start.18 = (f32[8192]{0:T(1024)S(1)}, f32[8192]{0:T(1024)S(1)}, u32[]{:S(2)}, u32[]{:S(2)}) collective-permute-start(f32[8192]{0:T(1024)S(1)} %convolution_reduce_fusion), channel_id=1, source_target_pairs={{0,88},{8,80},{16,72},{24,64},{32,120},{40,112},{48,104},{56,96},{... | collective-permute-start | bytes 98312 | tf_op jit(solution)/shard_map/ppermute | solution.py:60
  225.4 7.0 %collective-permute-start.17 = (f32[8192]{0:T(1024)S(1)}, f32[8192]{0:T(1024)S(1)}, u32[]{:S(2)}, u32[]{:S(2)}) collective-permute-start(f32[8192]{0:T(1024)S(1)} %convolution_reduce_fusion), channel_id=1, source_target_pairs={{0,80},{8,88},{16,64},{24,72},{32,112},{40,120},{48,96},{56,104},{... | collective-permute-start | bytes 98312 | tf_op jit(solution)/shard_map/ppermute | solution.py:60
  226.9 6.6 %collective-permute-start.16 = (f32[8192]{0:T(1024)S(1)}, f32[8192]{0:T(1024)S(1)}, u32[]{:S(2)}, u32[]{:S(2)}) collective-permute-start(f32[8192]{0:T(1024)S(1)} %convolution_reduce_fusion), channel_id=1, source_target_pairs={{0,72},{8,64},{16,88},{24,80},{32,104},{40,96},{48,120},{56,112},{... | collective-permute-start | bytes 98312 | tf_op jit(solution)/shard_map/ppermute | solution.py:60
  229.3 6.9 %collective-permute-start.15 = (f32[8192]{0:T(1024)S(1)}, f32[8192]{0:T(1024)S(1)}, u32[]{:S(2)}, u32[]{:S(2)}) collective-permute-start(f32[8192]{0:T(1024)S(1)} %convolution_reduce_fusion), channel_id=1, source_target_pairs={{0,64},{8,72},{16,80},{24,88},{32,96},{40,104},{48,112},{56,120},{... | collective-permute-start | bytes 98312 | tf_op jit(solution)/shard_map/ppermute | solution.py:60
  229.9 9.2 %collective-permute-start.14 = (f32[8192]{0:T(1024)S(1)}, f32[8192]{0:T(1024)S(1)}, u32[]{:S(2)}, u32[]{:S(2)}) collective-permute-start(f32[8192]{0:T(1024)S(1)} %convolution_reduce_fusion), channel_id=1, source_target_pairs={{0,56},{8,48},{16,40},{24,32},{32,24},{40,16},{48,8},{56,0},{64,12... | collective-permute-start | bytes 98312 | tf_op jit(solution)/shard_map/ppermute | solution.py:60
  230.9 8.2 %collective-permute-start.13 = (f32[8192]{0:T(1024)S(1)}, f32[8192]{0:T(1024)S(1)}, u32[]{:S(2)}, u32[]{:S(2)}) collective-permute-start(f32[8192]{0:T(1024)S(1)} %convolution_reduce_fusion), channel_id=1, source_target_pairs={{0,48},{8,56},{16,32},{24,40},{32,16},{40,24},{48,0},{56,8},{64,11... | collective-permute-start | bytes 98312 | tf_op jit(solution)/shard_map/ppermute | solution.py:60
  232.4 7.6 %collective-permute-start.12 = (f32[8192]{0:T(1024)S(1)}, f32[8192]{0:T(1024)S(1)}, u32[]{:S(2)}, u32[]{:S(2)}) collective-permute-start(f32[8192]{0:T(1024)S(1)} %convolution_reduce_fusion), channel_id=1, source_target_pairs={{0,40},{8,32},{16,56},{24,48},{32,8},{40,0},{48,24},{56,16},{64,10... | collective-permute-start | bytes 98312 | tf_op jit(solution)/shard_map/ppermute | solution.py:60
  233.6 10.2 %collective-permute-start.30 = (f32[96,768]{1,0:T(8,128)S(1)}, f32[96,768]{1,0:T(8,128)S(1)}, u32[]{:S(2)}, u32[]{:S(2)}) collective-permute-start(f32[96,768]{1,0:T(8,128)S(1)} %bitcast.38), channel_id=1, source_target_pairs={{0,1},{1,0},{2,3},{3,2},{4,5},{5,4},{6,7},{7,6},{8,9},{9,8},{10,11... | collective-permute-start | bytes 884744 | tf_op jit(solution)/shard_map/ppermute | solution.py:53
  236.2 5.4 %collective-permute-start.11 = (f32[8192]{0:T(1024)S(1)}, f32[8192]{0:T(1024)S(1)}, u32[]{:S(2)}, u32[]{:S(2)}) collective-permute-start(f32[8192]{0:T(1024)S(1)} %convolution_reduce_fusion), channel_id=1, source_target_pairs={{0,32},{8,40},{16,48},{24,56},{32,0},{40,8},{48,16},{56,24},{64,96... | collective-permute-start | bytes 98312 | tf_op jit(solution)/shard_map/ppermute | solution.py:60
  261.2 11.1 %collective-permute-start.31 = (f32[192]{0:T(256)S(1)}, f32[192]{0:T(256)S(1)}, u32[]{:S(2)}, u32[]{:S(2)}) collective-permute-start(f32[192]{0:T(256)S(1)} %fusion.1), channel_id=1, source_target_pairs={{0,1},{1,0},{2,3},{3,2},{4,5},{5,4},{6,7},{7,6},{8,9},{9,8},{10,11... | collective-permute-start | bytes 2312 | tf_op jit(solution)/shard_map/ppermute | solution.py:66
  264.3 9.8 %collective-permute-start.32 = (f32[192]{0:T(256)S(1)}, f32[192]{0:T(256)S(1)}, u32[]{:S(2)}, u32[]{:S(2)}) collective-permute-start(f32[192]{0:T(256)S(1)} %fusion.1), channel_id=1, source_target_pairs={{0,2},{1,3},{2,0},{3,1},{4,6},{5,7},{6,4},{7,5},{8,10},{9,11},{10,... | collective-permute-start | bytes 2312 | tf_op jit(solution)/shard_map/ppermute | solution.py:66
  265.0 10.5 %collective-permute-start.33 = (f32[192]{0:T(256)S(1)}, f32[192]{0:T(256)S(1)}, u32[]{:S(2)}, u32[]{:S(2)}) collective-permute-start(f32[192]{0:T(256)S(1)} %fusion.1), channel_id=1, source_target_pairs={{0,3},{1,2},{2,1},{3,0},{4,7},{5,6},{6,5},{7,4},{8,11},{9,10},{10,... | collective-permute-start | bytes 2312 | tf_op jit(solution)/shard_map/ppermute | solution.py:66
  266.3 9.2 %collective-permute-start.34 = (f32[192]{0:T(256)S(1)}, f32[192]{0:T(256)S(1)}, u32[]{:S(2)}, u32[]{:S(2)}) collective-permute-start(f32[192]{0:T(256)S(1)} %fusion.1), channel_id=1, source_target_pairs={{0,4},{1,5},{2,6},{3,7},{4,0},{5,1},{6,2},{7,3},{8,12},{9,13},{10,... | collective-permute-start | bytes 2312 | tf_op jit(solution)/shard_map/ppermute | solution.py:66
  267.7 7.8 %collective-permute-start.35 = (f32[192]{0:T(256)S(1)}, f32[192]{0:T(256)S(1)}, u32[]{:S(2)}, u32[]{:S(2)}) collective-permute-start(f32[192]{0:T(256)S(1)} %fusion.1), channel_id=1, source_target_pairs={{0,5},{1,4},{2,7},{3,6},{4,1},{5,0},{6,3},{7,2},{8,13},{9,12},{10,... | collective-permute-start | bytes 2312 | tf_op jit(solution)/shard_map/ppermute | solution.py:66
  274.1 7.2 %collective-permute-start.37 = (f32[192]{0:T(256)S(1)}, f32[192]{0:T(256)S(1)}, u32[]{:S(2)}, u32[]{:S(2)}) collective-permute-start(f32[192]{0:T(256)S(1)} %fusion.1), channel_id=1, source_target_pairs={{0,7},{1,6},{2,5},{3,4},{4,3},{5,2},{6,1},{7,0},{8,15},{9,14},{10,... | collective-permute-start | bytes 2312 | tf_op jit(solution)/shard_map/ppermute | solution.py:66
  (9 other events, 158.3 us)
Sparse Core Ops, SparseCore 0:
  9.7 133.6 all-gather.1

commit v3 on v2

--- a/solution.py
+++ b/solution.py
@@ -55,17 +55,23 @@
 
 
 def all_max(value, axis, n):
-    result = value
-    for k in range(1, n):
-        result = jnp.maximum(result, lax.ppermute(value, axis, [(i, i ^ k) for i in range(n)]))
-    return result
+    bit = 1
+    while bit < n:
+        value = jnp.maximum(value, lax.ppermute(value, axis, [(i, i ^ bit) for i in range(n)]))
+        bit *= 2
+    return value
 
 
 def all_sum(value, axis, n):
     here = lax.axis_index(axis)
-    parts = jnp.stack([value] + [lax.ppermute(value, axis, [(i, i ^ k) for i in range(n)]) for k in range(1, n)])
-    ordered = jnp.take(parts, jnp.arange(n) ^ here, axis=0)
-    return jnp.sum(ordered, axis=0)
+    parts = value[None]
+    bit = 1
+    while bit < n:
+        other = lax.ppermute(parts, axis, [(i, i ^ bit) for i in range(n)])
+        low = (here & bit) == 0
+        parts = jnp.where(low, jnp.concatenate([parts, other]), jnp.concatenate([other, parts]))
+        bit *= 2
+    return jnp.sum(parts, axis=0)
 
 
 def body(slab_embed, coverage_old, sel_index, cand_index):
@@ -75,12 +81,17 @@
     first_row = col_id * gathered.shape[0]
     selected = col_masked_sum(lookup(gathered, sel_index, first_row))
     chosen = col_masked_sum(lookup(gathered, cand_index, first_row))
-    partial_value = jnp.max(similar(selected, gathered), axis=0)
-    reached = all_max(partial_value, "row", n_row)
-    coverage = jnp.maximum(coverage_old, reached)
-    gain_part = jnp.sum(jnp.maximum(similar(chosen, gathered) - coverage[None, :], 0.0), axis=1)
-    total_gain = all_sum(gain_part, "col", N_Y * N_Z)
-    return (coverage, total_gain)
+    n_chunks = 2
+    width = gathered.shape[0] // n_chunks
+    coverages, gains = [], []
+    for i in range(n_chunks):
+        points = gathered[i * width:(i + 1) * width]
+        reached = all_max(jnp.max(similar(selected, points), axis=0), "row", n_row)
+        coverage = jnp.maximum(coverage_old[i * width:(i + 1) * width], reached)
+        coverages.append(coverage)
+        gains.append(jnp.sum(jnp.maximum(similar(chosen, points) - coverage[None, :], 0.0), axis=1))
+    total_gain = all_sum(sum(gains[1:], gains[0]), "col", N_Y * N_Z)
+    return (jnp.concatenate(coverages), total_gain)
 
 
 def solution(mesh):

time: 290 us -> 281 us (0.969)
  starting transfers between devices: 55.8 us -> 32.5 us
  waiting for transfers between devices: 164 us -> 172 us
  matrix products: 33.8 us -> 37.3 us
    ppermute x22 -> x11, starting transfers between devices: 35.2 us -> 11.5 us  [the longest x8 8.64 us: all_max(): lax.ppermute(value, axis, [(i, i ^ bit) for i in range(n)])]
    ppermute x22 -> x11, waiting for transfers between devices: 8.04 us -> 17.3 us  [the longest x3 9.76 us: all_sum(): other = lax.ppermute(parts, axis, [(i, i ^ bit) for i in range(n)])]
    dot_general x2 -> x4, matrix products: 33.8 us -> 37.3 us  [similar(): lax.dot_general(left, right, (((1,), (1,)), ((), ())), precision=lax.Prec...]
  transfers between devices with their start and end apart: 39 -> 28, of which waited for: 20 -> 22; matrix products, arithmetic and copies ran while one was open for 4% -> 13% of each run, Pallas kernels for 0% -> 0%
where the time goes in v3:
time: 281 us; the launch traced here: 280 us
  waiting for transfers between devices  172 us (61%)
  matrix products  37.3 us (13%)
  starting transfers between devices  32.5 us (12%)
  local copies, waits for them, and re-layouts  18.7 us (7%)
  between operations  14.3 us (5%)
  other arithmetic  5.06 us (2%)
    all_gather x1, waiting for transfers between devices, body(): gathered = lax.all_gather(slab_embed, 'row', axis=0, tiled=True)  134 us
    dot_general x4, matrix products, similar(): lax.dot_general(left, right, (((1,), (1,)), ((), ())), precision=lax.Prec...  37.3 us
    ppermute x12, waiting for transfers between devices, y_shift(): return lax.ppermute(value, 'col', pairs)  18.5 us
    gather x2, local copies, waits for them, and re-layouts, lookup(): jnp.take(source, jnp.clip(position, 0, source.shape[0] - 1), axis=0)  18.5 us
    ppermute x12, starting transfers between devices, y_shift(): return lax.ppermute(value, 'col', pairs)  13.1 us
    ppermute x3, waiting for transfers between devices, all_sum(): other = lax.ppermute(parts, axis, [(i, i ^ bit) for i in range(n)])  9.76 us
    ppermute x8, starting transfers between devices, all_max(): lax.ppermute(value, axis, [(i, i ^ bit) for i in range(n)])  8.64 us
    ppermute x8, waiting for transfers between devices, all_max(): lax.ppermute(value, axis, [(i, i ^ bit) for i in range(n)])  7.54 us
  transfers between devices with their start and end apart: 28, of which 22 were waited for; matrix products, arithmetic and copies ran while one was open for 13% of the time, Pallas kernels for 0%

profile of v3, /device:TPU:0, one launch (start us, length us, event | category | flops | bytes accessed | tf_op | source)
XLA Modules:
  0.0 280.2 jit_solution(54624820540219910)
XLA Ops:
  9.3 134.1 %all-gather.2.cloned.1.call-done = f32[8192,768]{1,0:T(8,128)} async-done(((f32[512,768]{1,0:T(8,128)}), f32[8192,768]{1,0:T(8,128)}) %all-gather.2.cloned.1.call-update) | async-done | bytes 25165840 | tf_op jit(solution)/shard_map/all_gather | solution.py:80
  143.4 9.1 %gather_fusion = f32[128,768]{1,0:T(8,128)S(1)} fusion(f32[8192,768]{1,0:T(8,128)} %all-gather.2.cloned.1.call-done, s32[1024]{0:T(1024)S(1)} %get-tuple-element.21), kind=kCustom, calls=%fused_computation | custom fusion | bytes 786944 | tf_op jit(solution)/shard_map/jit(_take)/gather | solution.py:22
  152.7 2.9 %collective-permute-start = (f32[64,768]{1,0:T(8,128)S(1)}, f32[64,768]{1,0:T(8,128)S(1)}, u32[]{:S(2)}, u32[]{:S(2)}) collective-permute-start(f32[64,768]{1,0:T(8,128)S(1)} %slice_select_fusion.1), channel_id=1, source_target_pairs={{0,1},{1,0},{2,3},{3,2},{4,5},{5,4},{6,7},{7,6},{8,9},{9,8},{10,11... | collective-permute-start | bytes 589832 | tf_op jit(solution)/shard_map/ppermute | solution.py:43
  155.6 9.3 %gather_fusion.1 = f32[192,768]{1,0:T(8,128)S(1)} fusion(f32[8192,768]{1,0:T(8,128)} %all-gather.2.cloned.1.call-done, s32[1024]{0:T(1024)S(1)} %get-tuple-element.20), kind=kCustom, calls=%fused_computation.1 | custom fusion | bytes 1180416 | tf_op jit(solution)/shard_map/jit(_take)/gather | solution.py:22
  165.0 2.8 %collective-permute-start.3 = (f32[16,768]{1,0:T(8,128)S(1)}, f32[16,768]{1,0:T(8,128)S(1)}, u32[]{:S(2)}, u32[]{:S(2)}) collective-permute-start(f32[16,768]{1,0:T(8,128)S(1)} %get-tuple-element.14), channel_id=1, source_target_pairs={{0,6},{1,7},{2,0},{3,1},{4,2},{5,3},{6,4},{7,5},{8,14},{9,15},{10,... | collective-permute-start | bytes 147464 | tf_op jit(solution)/shard_map/ppermute | solution.py:32
  169.9 3.6 %collective-permute-done.2 = f32[16,768]{1,0:T(8,128)S(1)} collective-permute-done((f32[16,768]{1,0:T(8,128)S(1)}, f32[16,768]{1,0:T(8,128)S(1)}, u32[]{:S(2)}, u32[]{:S(2)}) %collective-permute-start.2) | collective-permute-done | bytes 49184 | tf_op jit(solution)/shard_map/ppermute | solution.py:32
  175.4 1.2 collective-permute-start.5
  176.6 1.2 collective-permute-start.6
  178.1 2.9 %collective-permute-done.5 = f32[16,768]{1,0:T(8,128)S(1)} collective-permute-done((f32[16,768]{1,0:T(8,128)S(1)}, f32[16,768]{1,0:T(8,128)S(1)}, u32[]{:S(2)}, u32[]{:S(2)}) %collective-permute-start.5) | collective-permute-done | bytes 49184 | tf_op jit(solution)/shard_map/ppermute | solution.py:32
  181.9 1.8 collective-permute-done.16
  183.8 1.6 collective-permute-start.19
  185.4 1.7 collective-permute-start.18
  188.2 3.1 %collective-permute-done.18 = f32[24,768]{1,0:T(8,128)S(1)} collective-permute-done((f32[24,768]{1,0:T(8,128)S(1)}, f32[24,768]{1,0:T(8,128)S(1)}, u32[]{:S(2)}, u32[]{:S(2)}) %collective-permute-start.18) | collective-permute-done | bytes 73760 | tf_op jit(solution)/shard_map/ppermute | solution.py:32
  191.3 1.4 collective-permute-done.17
  197.1 2.9 %collective-permute-done.21 = f32[24,768]{1,0:T(8,128)S(1)} collective-permute-done((f32[24,768]{1,0:T(8,128)S(1)}, f32[24,768]{1,0:T(8,128)S(1)}, u32[]{:S(2)}, u32[]{:S(2)}) %collective-permute-start.21) | collective-permute-done | bytes 73760 | tf_op jit(solution)/shard_map/ppermute | solution.py:32
  200.9 3.1 %collective-permute-start.23 = (f32[96,768]{1,0:T(8,128)S(1)}, f32[96,768]{1,0:T(8,128)S(1)}, u32[]{:S(2)}, u32[]{:S(2)}) collective-permute-start(f32[96,768]{1,0:T(8,128)S(1)} %bitcast.27), channel_id=1, source_target_pairs={{0,1},{1,0},{2,3},{3,2},{4,5},{5,4},{6,7},{7,6},{8,9},{9,8},{10,11... | collective-permute-start | bytes 884744 | tf_op jit(solution)/shard_map/ppermute | solution.py:53
  204.0 11.6 %fusion.26 = f32[4096]{0:T(1024)S(1)} fusion(f32[8192,768]{1,0:T(8,128)} %all-gather.2.cloned.1.call-done, f32[64,768]{1,0:T(8,128)S(1)} %collective-permute-done.7, f32[64,768]{1,0:T(8,128)S(1)} %bitcast.31, pred[]{:T(512)S(6)} %eq.33), kind=kOutput, calls=%fused_computation.16 | convolution fusion | flops 2416734208 | bytes 12992513 | tf_op jit(solution)/shard_map/dot_general | solution.py:10
  215.7 10.9 %fusion.29 = f32[4096]{0:T(1024)S(1)} fusion(f32[8192,768]{1,0:T(8,128)} %all-gather.2.cloned.1.call-done, f32[64,768]{1,0:T(8,128)S(1)} %collective-permute-done.7, f32[64,768]{1,0:T(8,128)S(1)} %bitcast.32, pred[]{:T(512)S(6)} %eq.33), kind=kOutput, calls=%fused_computation.17 | convolution fusion | flops 2416734208 | bytes 12992513 | tf_op jit(solution)/shard_map/dot_general | solution.py:10
  227.2 1.5 collective-permute-start.9
  229.4 1.6 collective-permute-done.9
  231.0 2.7 collective-permute-start.10
  233.7 1.3 collective-permute-start.14
  235.0 1.3 collective-permute-done.10
  237.1 1.9 collective-permute-done.14
  240.0 2.7 collective-permute-done.15
  243.4 7.0 %fusion.23 = f32[192]{0:T(256)} fusion(f32[4096]{0:T(1024)S(1)} %get-tuple-element.16, f32[8192,768]{1,0:T(8,128)S(1)} %copy-done, f32[96,768]{1,0:T(8,128)S(1)} %collective-permute-done.23, f32[96,768]{1,0:T(8,128)S(1)} %bitcast.28, pred[]{:T(512)S(6)} %eq.33), kind=kOutput, calls=%fused_computation.15 | convolution fusion | flops 3626680064 | bytes 13189889 | tf_op jit(solution)/shard_map/dot_general | solution.py:10
  250.4 7.8 %fusion.20 = f32[192]{0:T(256)} fusion(f32[4096]{0:T(1024)} %get-tuple-element.17, f32[8192,768]{1,0:T(8,128)S(1)} %copy-done, f32[96,768]{1,0:T(8,128)S(1)} %collective-permute-done.23, f32[96,768]{1,0:T(8,128)S(1)} %bitcast.29, pred[]{:T(512)S(6)} %eq.33), kind=kOutput, calls=%fused_computation.14 | convolution fusion | flops 3626680064 | bytes 13189889 | tf_op jit(solution)/shard_map/dot_general | solution.py:10
  259.5 4.4 %collective-permute-done.24 = f32[1,192]{1,0:T(1,128)S(1)} collective-permute-done((f32[1,192]{1,0:T(1,128)S(1)}, f32[1,192]{1,0:T(1,128)S(1)}, u32[]{:S(2)}, u32[]{:S(2)}) %collective-permute-start.24) | collective-permute-done | bytes 800 | tf_op jit(solution)/shard_map/ppermute | solution.py:70
  264.7 2.9 %collective-permute-done.25 = f32[2,192]{1,0:T(2,128)S(1)} collective-permute-done((f32[2,192]{1,0:T(2,128)S(1)}, f32[2,192]{1,0:T(2,128)S(1)}, u32[]{:S(2)}, u32[]{:S(2)}) %collective-permute-start.25) | collective-permute-done | bytes 1568 | tf_op jit(solution)/shard_map/ppermute | solution.py:70
  267.6 1.4 collective-permute-start.26
  269.0 1.3 pad_maximum_fusion
  270.3 2.5 collective-permute-done.26
  (76 shorter events, 20.7 us)
Async XLA Ops:
  7.2 136.2 %all-gather.2.cloned.1.call-start = ((), (), s32[]{:S(2)}) async-start(), calls=%async_computation | async-start | bytes 26738688 | tf_op jit(solution)/shard_map/all_gather | solution.py:80
  152.7 12.3 %collective-permute-start = (f32[64,768]{1,0:T(8,128)S(1)}, f32[64,768]{1,0:T(8,128)S(1)}, u32[]{:S(2)}, u32[]{:S(2)}) collective-permute-start(f32[64,768]{1,0:T(8,128)S(1)} %slice_select_fusion.1), channel_id=1, source_target_pairs={{0,1},{1,0},{2,3},{3,2},{4,5},{5,4},{6,7},{7,6},{8,9},{9,8},{10,11... | collective-permute-start | bytes 589832 | tf_op jit(solution)/shard_map/ppermute | solution.py:43
  165.0 4.8 %collective-permute-start.3 = (f32[16,768]{1,0:T(8,128)S(1)}, f32[16,768]{1,0:T(8,128)S(1)}, u32[]{:S(2)}, u32[]{:S(2)}) collective-permute-start(f32[16,768]{1,0:T(8,128)S(1)} %get-tuple-element.14), channel_id=1, source_target_pairs={{0,6},{1,7},{2,0},{3,1},{4,2},{5,3},{6,4},{7,5},{8,14},{9,15},{10,... | collective-permute-start | bytes 147464 | tf_op jit(solution)/shard_map/ppermute | solution.py:32
  167.8 5.6 %collective-permute-start.2 = (f32[16,768]{1,0:T(8,128)S(1)}, f32[16,768]{1,0:T(8,128)S(1)}, u32[]{:S(2)}, u32[]{:S(2)}) collective-permute-start(f32[16,768]{1,0:T(8,128)S(1)} %get-tuple-element.15), channel_id=1, source_target_pairs={{0,4},{1,5},{2,6},{3,7},{4,0},{5,1},{6,2},{7,3},{8,12},{9,13},{10,... | collective-permute-start | bytes 147464 | tf_op jit(solution)/shard_map/ppermute | solution.py:32
  168.6 5.3 %collective-permute-start.1 = (f32[16,768]{1,0:T(8,128)S(1)}, f32[16,768]{1,0:T(8,128)S(1)}, u32[]{:S(2)}, u32[]{:S(2)}) collective-permute-start(f32[16,768]{1,0:T(8,128)S(1)} %get-tuple-element.13), channel_id=1, source_target_pairs={{0,2},{1,3},{2,4},{3,5},{4,6},{5,7},{6,0},{7,1},{8,10},{9,11},{10,... | collective-permute-start | bytes 147464 | tf_op jit(solution)/shard_map/ppermute | solution.py:32
  174.0 4.2 %collective-permute-start.4 = (f32[16,768]{1,0:T(8,128)S(1)}, f32[16,768]{1,0:T(8,128)S(1)}, u32[]{:S(2)}, u32[]{:S(2)}) collective-permute-start(f32[16,768]{1,0:T(8,128)S(1)} %get-tuple-element.7), channel_id=1, source_target_pairs={{0,6},{1,7},{2,0},{3,1},{4,2},{5,3},{6,4},{7,5},{8,14},{9,15},{10,... | collective-permute-start | bytes 147464 | tf_op jit(solution)/shard_map/ppermute | solution.py:32
  174.6 9.1 %collective-permute-start.16 = (f32[96,768]{1,0:T(8,128)S(1)}, f32[96,768]{1,0:T(8,128)S(1)}, u32[]{:S(2)}, u32[]{:S(2)}) collective-permute-start(f32[96,768]{1,0:T(8,128)S(1)} %slice_select_fusion), channel_id=1, source_target_pairs={{0,1},{1,0},{2,3},{3,2},{4,5},{5,4},{6,7},{7,6},{8,9},{9,8},{10,11... | collective-permute-start | bytes 884744 | tf_op jit(solution)/shard_map/ppermute | solution.py:43
  175.4 5.6 %collective-permute-start.5 = (f32[16,768]{1,0:T(8,128)S(1)}, f32[16,768]{1,0:T(8,128)S(1)}, u32[]{:S(2)}, u32[]{:S(2)}) collective-permute-start(f32[16,768]{1,0:T(8,128)S(1)} %get-tuple-element.7), channel_id=1, source_target_pairs={{0,4},{1,5},{2,6},{3,7},{4,0},{5,1},{6,2},{7,3},{8,12},{9,13},{10,... | collective-permute-start | bytes 147464 | tf_op jit(solution)/shard_map/ppermute | solution.py:32
  176.6 5.3 %collective-permute-start.6 = (f32[16,768]{1,0:T(8,128)S(1)}, f32[16,768]{1,0:T(8,128)S(1)}, u32[]{:S(2)}, u32[]{:S(2)}) collective-permute-start(f32[16,768]{1,0:T(8,128)S(1)} %get-tuple-element.7), channel_id=1, source_target_pairs={{0,2},{1,3},{2,4},{3,5},{4,6},{5,7},{6,0},{7,1},{8,10},{9,11},{10,... | collective-permute-start | bytes 147464 | tf_op jit(solution)/shard_map/ppermute | solution.py:32
  183.8 4.4 %collective-permute-start.19 = (f32[24,768]{1,0:T(8,128)S(1)}, f32[24,768]{1,0:T(8,128)S(1)}, u32[]{:S(2)}, u32[]{:S(2)}) collective-permute-start(f32[24,768]{1,0:T(8,128)S(1)} %get-tuple-element.11), channel_id=1, source_target_pairs={{0,6},{1,7},{2,0},{3,1},{4,2},{5,3},{6,4},{7,5},{8,14},{9,15},{10,... | collective-permute-start | bytes 221192 | tf_op jit(solution)/shard_map/ppermute | solution.py:32
  185.4 5.9 %collective-permute-start.18 = (f32[24,768]{1,0:T(8,128)S(1)}, f32[24,768]{1,0:T(8,128)S(1)}, u32[]{:S(2)}, u32[]{:S(2)}) collective-permute-start(f32[24,768]{1,0:T(8,128)S(1)} %get-tuple-element.12), channel_id=1, source_target_pairs={{0,4},{1,5},{2,6},{3,7},{4,0},{5,1},{6,2},{7,3},{8,12},{9,13},{10,... | collective-permute-start | bytes 221192 | tf_op jit(solution)/shard_map/ppermute | solution.py:32
  187.1 5.6 %collective-permute-start.17 = (f32[24,768]{1,0:T(8,128)S(1)}, f32[24,768]{1,0:T(8,128)S(1)}, u32[]{:S(2)}, u32[]{:S(2)}) collective-permute-start(f32[24,768]{1,0:T(8,128)S(1)} %get-tuple-element.10), channel_id=1, source_target_pairs={{0,2},{1,3},{2,4},{3,5},{4,6},{5,7},{6,0},{7,1},{8,10},{9,11},{10,... | collective-permute-start | bytes 221192 | tf_op jit(solution)/shard_map/ppermute | solution.py:32
  192.7 4.4 %collective-permute-start.20 = (f32[24,768]{1,0:T(8,128)S(1)}, f32[24,768]{1,0:T(8,128)S(1)}, u32[]{:S(2)}, u32[]{:S(2)}) collective-permute-start(f32[24,768]{1,0:T(8,128)S(1)} %get-tuple-element.3), channel_id=1, source_target_pairs={{0,6},{1,7},{2,0},{3,1},{4,2},{5,3},{6,4},{7,5},{8,14},{9,15},{10,... | collective-permute-start | bytes 221192 | tf_op jit(solution)/shard_map/ppermute | solution.py:32
  193.0 11.0 %collective-permute-start.7 = (f32[64,768]{1,0:T(8,128)S(1)}, f32[64,768]{1,0:T(8,128)S(1)}, u32[]{:S(2)}, u32[]{:S(2)}) collective-permute-start(f32[64,768]{1,0:T(8,128)S(1)} %bitcast.30), channel_id=1, source_target_pairs={{0,1},{1,0},{2,3},{3,2},{4,5},{5,4},{6,7},{7,6},{8,9},{9,8},{10,11... | collective-permute-start | bytes 589832 | tf_op jit(solution)/shard_map/ppermute | solution.py:53
  194.1 5.9 %collective-permute-start.21 = (f32[24,768]{1,0:T(8,128)S(1)}, f32[24,768]{1,0:T(8,128)S(1)}, u32[]{:S(2)}, u32[]{:S(2)}) collective-permute-start(f32[24,768]{1,0:T(8,128)S(1)} %get-tuple-element.3), channel_id=1, source_target_pairs={{0,4},{1,5},{2,6},{3,7},{4,0},{5,1},{6,2},{7,3},{8,12},{9,13},{10,... | collective-permute-start | bytes 221192 | tf_op jit(solution)/shard_map/ppermute | solution.py:32
  195.2 5.6 %collective-permute-start.22 = (f32[24,768]{1,0:T(8,128)S(1)}, f32[24,768]{1,0:T(8,128)S(1)}, u32[]{:S(2)}, u32[]{:S(2)}) collective-permute-start(f32[24,768]{1,0:T(8,128)S(1)} %get-tuple-element.3), channel_id=1, source_target_pairs={{0,2},{1,3},{2,4},{3,5},{4,6},{5,7},{6,0},{7,1},{8,10},{9,11},{10,... | collective-permute-start | bytes 221192 | tf_op jit(solution)/shard_map/ppermute | solution.py:32
  200.9 41.9 %copy-start.1 = (f32[8192]{0:T(1024)S(1)}, f32[8192]{0:T(1024)}, u32[]{:S(2)}) copy-start(f32[8192]{0:T(1024)} %param.5) | copy-start | bytes 98308
  200.9 42.5 %copy-start = (f32[8192,768]{1,0:T(8,128)S(1)}, f32[8192,768]{1,0:T(8,128)}, u32[]{:S(2)}) copy-start(f32[8192,768]{1,0:T(8,128)} %all-gather.2.cloned.1.call-done) | copy-start | bytes 75497472
  200.9 42.4 %collective-permute-start.23 = (f32[96,768]{1,0:T(8,128)S(1)}, f32[96,768]{1,0:T(8,128)S(1)}, u32[]{:S(2)}, u32[]{:S(2)}) collective-permute-start(f32[96,768]{1,0:T(8,128)S(1)} %bitcast.27), channel_id=1, source_target_pairs={{0,1},{1,0},{2,3},{3,2},{4,5},{5,4},{6,7},{7,6},{8,9},{9,8},{10,11... | collective-permute-start | bytes 884744 | tf_op jit(solution)/shard_map/ppermute | solution.py:53
  215.6 11.6 %collective-permute-start.8 = (f32[4096]{0:T(1024)S(1)}, f32[4096]{0:T(1024)S(1)}, u32[]{:S(2)}, u32[]{:S(2)}) collective-permute-start(f32[4096]{0:T(1024)S(1)} %fusion.26), channel_id=1, source_target_pairs={{0,8},{8,0},{16,24},{24,16},{32,40},{40,32},{48,56},{56,48},{64,72... | collective-permute-start | bytes 49160 | tf_op jit(solution)/shard_map/ppermute | solution.py:60
  226.6 2.1 collective-permute-start.12
  227.2 3.8 %collective-permute-start.9 = (f32[4096]{0:T(1024)S(1)}, f32[4096]{0:T(1024)S(1)}, u32[]{:S(2)}, u32[]{:S(2)}) collective-permute-start(f32[4096]{0:T(1024)S(1)} %max.44), channel_id=1, source_target_pairs={{0,16},{8,24},{16,0},{24,8},{32,48},{40,56},{48,32},{56,40},{64,80... | collective-permute-start | bytes 49160 | tf_op jit(solution)/shard_map/ppermute | solution.py:60
  228.7 5.0 %collective-permute-start.13 = (f32[4096]{0:T(1024)S(1)}, f32[4096]{0:T(1024)S(1)}, u32[]{:S(2)}, u32[]{:S(2)}) collective-permute-start(f32[4096]{0:T(1024)S(1)} %max.49), channel_id=1, source_target_pairs={{0,16},{8,24},{16,0},{24,8},{32,48},{40,56},{48,32},{56,40},{64,80... | collective-permute-start | bytes 49160 | tf_op jit(solution)/shard_map/ppermute | solution.py:60
  231.0 5.2 %collective-permute-start.10 = (f32[4096]{0:T(1024)S(1)}, f32[4096]{0:T(1024)S(1)}, u32[]{:S(2)}, u32[]{:S(2)}) collective-permute-start(f32[4096]{0:T(1024)S(1)} %max.45), channel_id=1, source_target_pairs={{0,32},{8,40},{16,48},{24,56},{32,0},{40,8},{48,16},{56,24},{64,96... | collective-permute-start | bytes 49160 | tf_op jit(solution)/shard_map/ppermute | solution.py:60
  233.7 5.3 %collective-permute-start.14 = (f32[4096]{0:T(1024)S(1)}, f32[4096]{0:T(1024)S(1)}, u32[]{:S(2)}, u32[]{:S(2)}) collective-permute-start(f32[4096]{0:T(1024)S(1)} %max.50), channel_id=1, source_target_pairs={{0,32},{8,40},{16,48},{24,56},{32,0},{40,8},{48,16},{56,24},{64,96... | collective-permute-start | bytes 49160 | tf_op jit(solution)/shard_map/ppermute | solution.py:60
  236.3 3.7 %collective-permute-start.11 = (f32[4096]{0:T(1024)S(1)}, f32[4096]{0:T(1024)S(1)}, u32[]{:S(2)}, u32[]{:S(2)}) collective-permute-start(f32[4096]{0:T(1024)S(1)} %max.46), channel_id=1, source_target_pairs={{0,64},{8,72},{16,80},{24,88},{32,96},{40,104},{48,112},{56,120},{... | collective-permute-start | bytes 49160 | tf_op jit(solution)/shard_map/ppermute | solution.py:60
  239.0 3.7 %collective-permute-start.15 = (f32[4096]{0:T(1024)S(1)}, f32[4096]{0:T(1024)S(1)}, u32[]{:S(2)}, u32[]{:S(2)}) collective-permute-start(f32[4096]{0:T(1024)S(1)} %max.51), channel_id=1, source_target_pairs={{0,64},{8,72},{16,80},{24,88},{32,96},{40,104},{48,112},{56,120},{... | collective-permute-start | bytes 49160 | tf_op jit(solution)/shard_map/ppermute | solution.py:60
  258.9 5.1 %collective-permute-start.24 = (f32[1,192]{1,0:T(1,128)S(1)}, f32[1,192]{1,0:T(1,128)S(1)}, u32[]{:S(2)}, u32[]{:S(2)}) collective-permute-start(f32[1,192]{1,0:T(1,128)S(1)} %bitcast.33), channel_id=1, source_target_pairs={{0,1},{1,0},{2,3},{3,2},{4,5},{5,4},{6,7},{7,6},{8,9},{9,8},{10,11... | collective-permute-start | bytes 2312 | tf_op jit(solution)/shard_map/ppermute | solution.py:70
  263.9 3.7 %collective-permute-start.25 = (f32[2,192]{1,0:T(2,128)S(1)}, f32[2,192]{1,0:T(2,128)S(1)}, u32[]{:S(2)}, u32[]{:S(2)}) collective-permute-start(f32[2,192]{1,0:T(2,128)S(1)} %maximum_select_fusion.8), channel_id=1, source_target_pairs={{0,2},{1,3},{2,0},{3,1},{4,6},{5,7},{6,4},{7,5},{8,10},{9,11},{10,... | collective-permute-start | bytes 4616 | tf_op jit(solution)/shard_map/ppermute | solution.py:70
  267.6 5.2 %collective-permute-start.26 = (f32[4,192]{1,0:T(4,128)S(1)}, f32[4,192]{1,0:T(4,128)S(1)}, u32[]{:S(2)}, u32[]{:S(2)}) collective-permute-start(f32[4,192]{1,0:T(4,128)S(1)} %maximum_select_fusion.7), channel_id=1, source_target_pairs={{0,4},{1,5},{2,6},{3,7},{4,0},{5,1},{6,2},{7,3},{8,12},{9,13},{10,... | collective-permute-start | bytes 9224 | tf_op jit(solution)/shard_map/ppermute | solution.py:70
Sparse Core Ops, SparseCore 0:
  9.7 133.6 all-gather.1

commit v4 on v3

--- a/solution.py
+++ b/solution.py
@@ -79,9 +79,12 @@
     col_id = lax.axis_index("col")
     gathered = lax.all_gather(slab_embed, "row", axis=0, tiled=True)
     first_row = col_id * gathered.shape[0]
-    selected = col_masked_sum(lookup(gathered, sel_index, first_row))
-    chosen = col_masked_sum(lookup(gathered, cand_index, first_row))
-    n_chunks = 2
+    n_sel = sel_index.shape[0]
+    picked = col_masked_sum(
+        jnp.concatenate([lookup(gathered, sel_index, first_row), lookup(gathered, cand_index, first_row)])
+    )
+    selected, chosen = picked[:n_sel], picked[n_sel:]
+    n_chunks = 1
     width = gathered.shape[0] // n_chunks
     coverages, gains = [], []
     for i in range(n_chunks):

time: 281 us -> 280 us (level)
  waiting for transfers between devices: 172 us -> 185 us
  starting transfers between devices: 32.5 us -> 25.6 us
  matrix products: 37.3 us -> 33.9 us
    ppermute x2 -> x1, waiting for transfers between devices: 1.83 us -> 12 us  [col_masked_sum(): lax.ppermute(theirs, 'col', [(c, c ^ 1) for c in range(N_Y * N_Z)])]
    ppermute x2 -> x1, waiting for transfers between devices: 0.01 us -> 9.2 us  [col_masked_sum(): other = lax.ppermute(ordered, 'col', [(c, c ^ 1) for c in range(N_Y * N_Z)])]
    ppermute x12 -> x6, waiting for transfers between devices: 18.5 us -> 10.5 us  [y_shift(): return lax.ppermute(value, 'col', pairs)]
    ppermute x8 -> x4, starting transfers between devices: 8.64 us -> 4.97 us  [all_max(): lax.ppermute(value, axis, [(i, i ^ bit) for i in range(n)])]
    dot_general x4 -> x2, matrix products: 37.3 us -> 33.9 us  [similar(): lax.dot_general(left, right, (((1,), (1,)), ((), ())), precision=lax.Prec...]
    ppermute x12 -> x6, starting transfers between devices: 13.1 us -> 9.77 us  [y_shift(): return lax.ppermute(value, 'col', pairs)]
    ppermute x8 -> x4, waiting for transfers between devices: 7.54 us -> 9.56 us  [all_max(): lax.ppermute(value, axis, [(i, i ^ bit) for i in range(n)])]
  transfers between devices with their start and end apart: 28 -> 16, of which waited for: 22 -> 16; matrix products, arithmetic and copies ran while one was open for 13% -> 0% of each run, Pallas kernels for 0% -> 0%
where the time goes in v4:
time: 280 us
  waiting for transfers between devices  185 us (66%)
  matrix products  33.9 us (12%)
  starting transfers between devices  25.6 us (9%)
  local copies, waits for them, and re-layouts  18.6 us (7%)
  between operations  14.2 us (5%)
    all_gather x1, waiting for transfers between devices, body(): gathered = lax.all_gather(slab_embed, 'row', axis=0, tiled=True)  134 us
    dot_general x2, matrix products, similar(): lax.dot_general(left, right, (((1,), (1,)), ((), ())), precision=lax.Prec...  33.9 us
    gather x2, local copies, waits for them, and re-layouts, lookup(): jnp.take(source, jnp.clip(position, 0, source.shape[0] - 1), axis=0)  18.5 us
    ppermute x1, waiting for transfers between devices, col_masked_sum(): lax.ppermute(theirs, 'col', [(c, c ^ 1) for c in range(N_Y * N_Z)])  12 us
    ppermute x6, waiting for transfers between devices, y_shift(): return lax.ppermute(value, 'col', pairs)  10.5 us
    ppermute x6, starting transfers between devices, y_shift(): return lax.ppermute(value, 'col', pairs)  9.77 us
    ppermute x4, waiting for transfers between devices, all_max(): lax.ppermute(value, axis, [(i, i ^ bit) for i in range(n)])  9.56 us
    ppermute x1, waiting for transfers between devices, col_masked_sum(): other = lax.ppermute(ordered, 'col', [(c, c ^ 1) for c in range(N_Y * N_Z)])  9.2 us
  transfers between devices with their start and end apart: 16, of which 16 were waited for; matrix products, arithmetic and copies ran while one was open for 0% of the time, Pallas kernels for 0%

profile of v4, /device:TPU:0, one launch (start us, length us, event | category | flops | bytes accessed | tf_op | source)
XLA Modules:
  0.0 279.9 jit_solution(4963495831859430870)
XLA Ops:
  7.2 0.7 all-gather.2.cloned.1.call-update
  8.6 0.7 compare_and_fusion
  9.3 134.1 %all-gather.2.cloned.1.call-done = f32[8192,768]{1,0:T(8,128)} async-done(((f32[512,768]{1,0:T(8,128)}), f32[8192,768]{1,0:T(8,128)}) %all-gather.2.cloned.1.call-update) | async-done | bytes 25165840 | tf_op jit(solution)/shard_map/all_gather | solution.py:80
  143.4 9.3 %gather_fusion.1 = f32[192,768]{1,0:T(8,128)S(1)} fusion(f32[8192,768]{1,0:T(8,128)} %all-gather.2.cloned.1.call-done, s32[1024]{0:T(1024)S(1)} %get-tuple-element.13), kind=kCustom, calls=%fused_computation.1 | custom fusion | bytes 1180416 | tf_op jit(solution)/shard_map/jit(_take)/gather | solution.py:22
  152.9 9.1 %gather_fusion = f32[128,768]{1,0:T(8,128)S(1)} fusion(f32[8192,768]{1,0:T(8,128)} %all-gather.2.cloned.1.call-done, s32[1024]{0:T(1024)S(1)} %get-tuple-element.14), kind=kCustom, calls=%fused_computation | custom fusion | bytes 786944 | tf_op jit(solution)/shard_map/jit(_take)/gather | solution.py:22
  162.2 2.9 %collective-permute-start = (f32[160,768]{1,0:T(8,128)S(1)}, f32[160,768]{1,0:T(8,128)S(1)}, u32[]{:S(2)}, u32[]{:S(2)}) collective-permute-start(f32[160,768]{1,0:T(8,128)S(1)} %slice_select_fusion), channel_id=1, source_target_pairs={{0,1},{1,0},{2,3},{3,2},{4,5},{5,4},{6,7},{7,6},{8,9},{9,8},{10,11... | collective-permute-start | bytes 1474568 | tf_op jit(solution)/shard_map/ppermute | solution.py:43
  165.1 12.0 %collective-permute-done = f32[160,768]{1,0:T(8,128)S(1)} collective-permute-done((f32[160,768]{1,0:T(8,128)S(1)}, f32[160,768]{1,0:T(8,128)S(1)}, u32[]{:S(2)}, u32[]{:S(2)}) %collective-permute-start) | collective-permute-done | bytes 491552 | tf_op jit(solution)/shard_map/ppermute | solution.py:43
  177.3 1.6 collective-permute-start.1
  178.8 2.7 collective-permute-start.2
  181.6 1.4 collective-permute-start.3
  183.0 1.3 collective-permute-done.1
  184.3 2.6 collective-permute-done.2
  187.0 2.7 collective-permute-start.4
  191.0 3.1 %collective-permute-done.4 = f32[40,768]{1,0:T(8,128)S(1)} collective-permute-done((f32[40,768]{1,0:T(8,128)S(1)}, f32[40,768]{1,0:T(8,128)S(1)}, u32[]{:S(2)}, u32[]{:S(2)}) %collective-permute-start.4) | collective-permute-done | bytes 122912 | tf_op jit(solution)/shard_map/ppermute | solution.py:32
  194.2 2.4 collective-permute-done.5
  196.6 1.0 collective-permute-done.6
  197.8 2.9 %collective-permute-start.7 = (f32[160,768]{1,0:T(8,128)S(1)}, f32[160,768]{1,0:T(8,128)S(1)}, u32[]{:S(2)}, u32[]{:S(2)}) collective-permute-start(f32[160,768]{1,0:T(8,128)S(1)} %bitcast.16), channel_id=1, source_target_pairs={{0,1},{1,0},{2,3},{3,2},{4,5},{5,4},{6,7},{7,6},{8,9},{9,8},{10,11... | collective-permute-start | bytes 1474568 | tf_op jit(solution)/shard_map/ppermute | solution.py:53
  200.7 9.2 %collective-permute-done.7 = f32[160,768]{1,0:T(8,128)S(1)} collective-permute-done((f32[160,768]{1,0:T(8,128)S(1)}, f32[160,768]{1,0:T(8,128)S(1)}, u32[]{:S(2)}, u32[]{:S(2)}) %collective-permute-start.7) | collective-permute-done | bytes 491552 | tf_op jit(solution)/shard_map/ppermute | solution.py:53
  210.0 16.5 %convolution_reduce_fusion = f32[8192]{0:T(1024)S(1)} fusion(f32[8192,768]{1,0:T(8,128)} %all-gather.2.cloned.1.call-done, f32[320,768]{1,0:T(8,128)S(1)} %maximum_select_fusion), kind=kOutput, calls=%fused_computation.5 | convolution fusion | flops 4832878592 | bytes 25591808 | tf_op jit(solution)/shard_map/dot_general | solution.py:10
  226.6 1.2 collective-permute-done.8
  227.8 1.1 collective-permute-start.9
  228.9 2.8 %collective-permute-done.9 = f32[8192]{0:T(1024)S(1)} collective-permute-done((f32[8192]{0:T(1024)S(1)}, f32[8192]{0:T(1024)S(1)}, u32[]{:S(2)}, u32[]{:S(2)}) %collective-permute-start.9) | collective-permute-done | bytes 32800 | tf_op jit(solution)/shard_map/ppermute | solution.py:60
  231.7 2.3 collective-permute-start.10
  234.0 3.1 %collective-permute-done.10 = f32[8192]{0:T(1024)S(1)} collective-permute-done((f32[8192]{0:T(1024)S(1)}, f32[8192]{0:T(1024)S(1)}, u32[]{:S(2)}, u32[]{:S(2)}) %collective-permute-start.10) | collective-permute-done | bytes 32800 | tf_op jit(solution)/shard_map/ppermute | solution.py:60
  237.1 1.5 collective-permute-start.11
  238.6 2.5 collective-permute-done.11
  241.1 17.4 %fusion.1 = f32[192]{0:T(256)S(1)} fusion(f32[8192]{0:T(1024)S(1)} %maximum_maximum_fusion, f32[8192,768]{1,0:T(8,128)} %all-gather.2.cloned.1.call-done, f32[320,768]{1,0:T(8,128)S(1)} %maximum_select_fusion), kind=kOutput, calls=%fused_computation.4 | convolution fusion | flops 7252475904 | bytes 25789184 | tf_op jit(solution)/shard_map/dot_general | solution.py:10
  258.4 2.9 %collective-permute-start.12 = (f32[1,192]{1,0:T(1,128)S(1)}, f32[1,192]{1,0:T(1,128)S(1)}, u32[]{:S(2)}, u32[]{:S(2)}) collective-permute-start(f32[1,192]{1,0:T(1,128)S(1)} %bitcast.18), channel_id=1, source_target_pairs={{0,1},{1,0},{2,3},{3,2},{4,5},{5,4},{6,7},{7,6},{8,9},{9,8},{10,11... | collective-permute-start | bytes 2312 | tf_op jit(solution)/shard_map/ppermute | solution.py:70
  261.4 2.2 collective-permute-done.12
  263.7 3.6 %collective-permute-done.13 = f32[2,192]{1,0:T(2,128)S(1)} collective-permute-done((f32[2,192]{1,0:T(2,128)S(1)}, f32[2,192]{1,0:T(2,128)S(1)}, u32[]{:S(2)}, u32[]{:S(2)}) %collective-permute-start.13) | collective-permute-done | bytes 1568 | tf_op jit(solution)/shard_map/ppermute | solution.py:70
  267.3 2.0 collective-permute-start.14
  269.3 3.2 %collective-permute-done.14 = f32[4,192]{1,0:T(4,128)S(1)} collective-permute-done((f32[4,192]{1,0:T(4,128)S(1)}, f32[4,192]{1,0:T(4,128)S(1)}, u32[]{:S(2)}, u32[]{:S(2)}) %collective-permute-start.14) | collective-permute-done | bytes 3104 | tf_op jit(solution)/shard_map/ppermute | solution.py:70
  (34 shorter events, 3.6 us)
Async XLA Ops:
  7.2 136.2 %all-gather.2.cloned.1.call-start = ((), (), s32[]{:S(2)}) async-start(), calls=%async_computation | async-start | bytes 26738688 | tf_op jit(solution)/shard_map/all_gather | solution.py:80
  152.7 88.3 %copy-start.1 = (f32[8192]{0:T(1024)S(1)}, f32[8192]{0:T(1024)}, u32[]{:S(2)}) copy-start(f32[8192]{0:T(1024)} %param.5) | copy-start | bytes 98308
  162.2 15.0 %collective-permute-start = (f32[160,768]{1,0:T(8,128)S(1)}, f32[160,768]{1,0:T(8,128)S(1)}, u32[]{:S(2)}, u32[]{:S(2)}) collective-permute-start(f32[160,768]{1,0:T(8,128)S(1)} %slice_select_fusion), channel_id=1, source_target_pairs={{0,1},{1,0},{2,3},{3,2},{4,5},{5,4},{6,7},{7,6},{8,9},{9,8},{10,11... | collective-permute-start | bytes 1474568 | tf_op jit(solution)/shard_map/ppermute | solution.py:43
  177.3 7.0 %collective-permute-start.1 = (f32[40,768]{1,0:T(8,128)S(1)}, f32[40,768]{1,0:T(8,128)S(1)}, u32[]{:S(2)}, u32[]{:S(2)}) collective-permute-start(f32[40,768]{1,0:T(8,128)S(1)} %get-tuple-element.8), channel_id=1, source_target_pairs={{0,2},{1,3},{2,4},{3,5},{4,6},{5,7},{6,0},{7,1},{8,10},{9,11},{10,... | collective-permute-start | bytes 368648 | tf_op jit(solution)/shard_map/ppermute | solution.py:32
  178.8 8.0 %collective-permute-start.2 = (f32[40,768]{1,0:T(8,128)S(1)}, f32[40,768]{1,0:T(8,128)S(1)}, u32[]{:S(2)}, u32[]{:S(2)}) collective-permute-start(f32[40,768]{1,0:T(8,128)S(1)} %get-tuple-element.10), channel_id=1, source_target_pairs={{0,4},{1,5},{2,6},{3,7},{4,0},{5,1},{6,2},{7,3},{8,12},{9,13},{10,... | collective-permute-start | bytes 368648 | tf_op jit(solution)/shard_map/ppermute | solution.py:32
  181.6 5.4 %collective-permute-start.3 = (f32[40,768]{1,0:T(8,128)S(1)}, f32[40,768]{1,0:T(8,128)S(1)}, u32[]{:S(2)}, u32[]{:S(2)}) collective-permute-start(f32[40,768]{1,0:T(8,128)S(1)} %get-tuple-element.9), channel_id=1, source_target_pairs={{0,6},{1,7},{2,0},{3,1},{4,2},{5,3},{6,4},{7,5},{8,14},{9,15},{10,... | collective-permute-start | bytes 368648 | tf_op jit(solution)/shard_map/ppermute | solution.py:32
  187.0 7.2 %collective-permute-start.4 = (f32[40,768]{1,0:T(8,128)S(1)}, f32[40,768]{1,0:T(8,128)S(1)}, u32[]{:S(2)}, u32[]{:S(2)}) collective-permute-start(f32[40,768]{1,0:T(8,128)S(1)} %get-tuple-element.3), channel_id=1, source_target_pairs={{0,6},{1,7},{2,0},{3,1},{4,2},{5,3},{6,4},{7,5},{8,14},{9,15},{10,... | collective-permute-start | bytes 368648 | tf_op jit(solution)/shard_map/ppermute | solution.py:32
  189.7 6.9 %collective-permute-start.5 = (f32[40,768]{1,0:T(8,128)S(1)}, f32[40,768]{1,0:T(8,128)S(1)}, u32[]{:S(2)}, u32[]{:S(2)}) collective-permute-start(f32[40,768]{1,0:T(8,128)S(1)} %get-tuple-element.3), channel_id=1, source_target_pairs={{0,4},{1,5},{2,6},{3,7},{4,0},{5,1},{6,2},{7,3},{8,12},{9,13},{10,... | collective-permute-start | bytes 368648 | tf_op jit(solution)/shard_map/ppermute | solution.py:32
  190.4 7.3 %collective-permute-start.6 = (f32[40,768]{1,0:T(8,128)S(1)}, f32[40,768]{1,0:T(8,128)S(1)}, u32[]{:S(2)}, u32[]{:S(2)}) collective-permute-start(f32[40,768]{1,0:T(8,128)S(1)} %get-tuple-element.3), channel_id=1, source_target_pairs={{0,2},{1,3},{2,4},{3,5},{4,6},{5,7},{6,0},{7,1},{8,10},{9,11},{10,... | collective-permute-start | bytes 368648 | tf_op jit(solution)/shard_map/ppermute | solution.py:32
  197.8 12.1 %collective-permute-start.7 = (f32[160,768]{1,0:T(8,128)S(1)}, f32[160,768]{1,0:T(8,128)S(1)}, u32[]{:S(2)}, u32[]{:S(2)}) collective-permute-start(f32[160,768]{1,0:T(8,128)S(1)} %bitcast.16), channel_id=1, source_target_pairs={{0,1},{1,0},{2,3},{3,2},{4,5},{5,4},{6,7},{7,6},{8,9},{9,8},{10,11... | collective-permute-start | bytes 1474568 | tf_op jit(solution)/shard_map/ppermute | solution.py:53
  226.5 1.3 collective-permute-start.8
  227.8 3.9 %collective-permute-start.9 = (f32[8192]{0:T(1024)S(1)}, f32[8192]{0:T(1024)S(1)}, u32[]{:S(2)}, u32[]{:S(2)}) collective-permute-start(f32[8192]{0:T(1024)S(1)} %max.29), channel_id=1, source_target_pairs={{0,16},{8,24},{16,0},{24,8},{32,48},{40,56},{48,32},{56,40},{64,80... | collective-permute-start | bytes 98312 | tf_op jit(solution)/shard_map/ppermute | solution.py:60
  231.7 5.4 %collective-permute-start.10 = (f32[8192]{0:T(1024)S(1)}, f32[8192]{0:T(1024)S(1)}, u32[]{:S(2)}, u32[]{:S(2)}) collective-permute-start(f32[8192]{0:T(1024)S(1)} %max.30), channel_id=1, source_target_pairs={{0,32},{8,40},{16,48},{24,56},{32,0},{40,8},{48,16},{56,24},{64,96... | collective-permute-start | bytes 98312 | tf_op jit(solution)/shard_map/ppermute | solution.py:60
  237.1 3.9 %collective-permute-start.11 = (f32[8192]{0:T(1024)S(1)}, f32[8192]{0:T(1024)S(1)}, u32[]{:S(2)}, u32[]{:S(2)}) collective-permute-start(f32[8192]{0:T(1024)S(1)} %max.31), channel_id=1, source_target_pairs={{0,64},{8,72},{16,80},{24,88},{32,96},{40,104},{48,112},{56,120},{... | collective-permute-start | bytes 98312 | tf_op jit(solution)/shard_map/ppermute | solution.py:60
  241.0 32.0 %copy-start = (f32[8192]{0:T(1024)}, f32[8192]{0:T(1024)S(1)}, u32[]{:S(2)}) copy-start(f32[8192]{0:T(1024)S(1)} %maximum_maximum_fusion) | copy-start | bytes 98308
  258.4 5.2 %collective-permute-start.12 = (f32[1,192]{1,0:T(1,128)S(1)}, f32[1,192]{1,0:T(1,128)S(1)}, u32[]{:S(2)}, u32[]{:S(2)}) collective-permute-start(f32[1,192]{1,0:T(1,128)S(1)} %bitcast.18), channel_id=1, source_target_pairs={{0,1},{1,0},{2,3},{3,2},{4,5},{5,4},{6,7},{7,6},{8,9},{9,8},{10,11... | collective-permute-start | bytes 2312 | tf_op jit(solution)/shard_map/ppermute | solution.py:70
  263.6 3.7 %collective-permute-start.13 = (f32[2,192]{1,0:T(2,128)S(1)}, f32[2,192]{1,0:T(2,128)S(1)}, u32[]{:S(2)}, u32[]{:S(2)}) collective-permute-start(f32[2,192]{1,0:T(2,128)S(1)} %maximum_select_fusion.3), channel_id=1, source_target_pairs={{0,2},{1,3},{2,0},{3,1},{4,6},{5,7},{6,4},{7,5},{8,10},{9,11},{10,... | collective-permute-start | bytes 4616 | tf_op jit(solution)/shard_map/ppermute | solution.py:70
  267.3 5.2 %collective-permute-start.14 = (f32[4,192]{1,0:T(4,128)S(1)}, f32[4,192]{1,0:T(4,128)S(1)}, u32[]{:S(2)}, u32[]{:S(2)}) collective-permute-start(f32[4,192]{1,0:T(4,128)S(1)} %maximum_select_fusion.2), channel_id=1, source_target_pairs={{0,4},{1,5},{2,6},{3,7},{4,0},{5,1},{6,2},{7,3},{8,12},{9,13},{10,... | collective-permute-start | bytes 9224 | tf_op jit(solution)/shard_map/ppermute | solution.py:70
Sparse Core Ops, SparseCore 0:
  9.7 133.6 all-gather.1

commit v5 on v4

--- a/solution.py
+++ b/solution.py
@@ -1,6 +1,8 @@
 import jax
 import jax.numpy as jnp
 from jax import lax
+from jax.experimental import pallas as pl
+from jax.experimental.pallas import tpu as pltpu
 from jax.sharding import PartitionSpec as P
 
 N_Y, N_Z = 4, 2
@@ -16,10 +18,35 @@
     )
 
 
+def row_copy_kernel(position_ref, source_ref, out_ref, sem):
+    count = out_ref.shape[0]
+
+    def issue(i, carry):
+        pltpu.make_async_copy(source_ref.at[pl.ds(position_ref[i], 1)], out_ref.at[pl.ds(i, 1)], sem).start()
+        return carry
+
+    lax.fori_loop(0, count, issue, 0)
+    pltpu.make_async_copy(source_ref.at[pl.ds(0, count)], out_ref, sem).wait()
+
+
+def take_rows(source, positions):
+    return pl.pallas_call(
+        row_copy_kernel,
+        grid_spec=pltpu.PrefetchScalarGridSpec(
+            num_scalar_prefetch=1,
+            grid=(1,),
+            in_specs=[pl.BlockSpec(memory_space=pl.ANY)],
+            out_specs=pl.BlockSpec(memory_space=pl.ANY),
+            scratch_shapes=[pltpu.SemaphoreType.DMA(())],
+        ),
+        out_shape=jax.ShapeDtypeStruct((positions.shape[0], source.shape[1]), source.dtype),
+    )(positions, source)
+
+
 def lookup(source, indices, first_row):
     position = indices - first_row
     inside = (position >= 0) & (position < source.shape[0])
-    picked = jnp.take(source, jnp.clip(position, 0, source.shape[0] - 1), axis=0)
+    picked = take_rows(source, jnp.clip(position, 0, source.shape[0] - 1))
     return jnp.where(inside[:, None], picked, 0.0)
 
 
@@ -80,9 +107,7 @@
     gathered = lax.all_gather(slab_embed, "row", axis=0, tiled=True)
     first_row = col_id * gathered.shape[0]
     n_sel = sel_index.shape[0]
-    picked = col_masked_sum(
-        jnp.concatenate([lookup(gathered, sel_index, first_row), lookup(gathered, cand_index, first_row)])
-    )
+    picked = col_masked_sum(lookup(gathered, jnp.concatenate([sel_index, cand_index]), first_row))
     selected, chosen = picked[:n_sel], picked[n_sel:]
     n_chunks = 1
     width = gathered.shape[0] // n_chunks

time: 280 us -> 294 us (1.050)
  Pallas kernels: 0 us -> 31.6 us
  local copies, waits for them, and re-layouts: 18.6 us -> 0.17 us
    pallas_call x0 -> x1, Pallas kernels: none -> 31.6 us  [take_rows(): pl.pallas_call(row_copy_kernel, grid_spec=pltpu.PrefetchScalarGridSpec(nu...]
    gather x2 -> x0, local copies, waits for them, and re-layouts: 18.5 us -> none  [lookup(): jnp.take(source, jnp.clip(position, 0, source.shape[0] - 1), axis=0)]
  transfers between devices with their start and end apart: 16 -> 16, of which waited for: 16 -> 16; matrix products, arithmetic and copies ran while one was open for 0% -> 1% of each run, Pallas kernels for 0% -> 0%
where the time goes in v5:
time: 294 us
  waiting for transfers between devices  184 us (63%)
  matrix products  33.9 us (12%)
  Pallas kernels  31.6 us (11%)
  starting transfers between devices  25.7 us (9%)
  between operations  14.2 us (5%)
  other arithmetic  4.17 us (1%)
    all_gather x1, waiting for transfers between devices, body(): gathered = lax.all_gather(slab_embed, 'row', axis=0, tiled=True)  133 us
    dot_general x2, matrix products, similar(): lax.dot_general(left, right, (((1,), (1,)), ((), ())), precision=lax.Prec...  33.9 us
    pallas_call x1, Pallas kernels, take_rows(): pl.pallas_call(row_copy_kernel, grid_spec=pltpu.PrefetchScalarGridSpec(nu...  31.6 us
    ppermute x1, waiting for transfers between devices, col_masked_sum(): lax.ppermute(theirs, 'col', [(c, c ^ 1) for c in range(N_Y * N_Z)])  12 us
    ppermute x6, waiting for transfers between devices, y_shift(): return lax.ppermute(value, 'col', pairs)  10.5 us
    ppermute x6, starting transfers between devices, y_shift(): return lax.ppermute(value, 'col', pairs)  9.77 us
    ppermute x4, waiting for transfers between devices, all_max(): lax.ppermute(value, axis, [(i, i ^ bit) for i in range(n)])  9.54 us
    ppermute x1, waiting for transfers between devices, col_masked_sum(): other = lax.ppermute(ordered, 'col', [(c, c ^ 1) for c in range(N_Y * N_Z)])  9.2 us
  transfers between devices with their start and end apart: 16, of which 16 were waited for; matrix products, arithmetic and copies ran while one was open for 1% of the time, Pallas kernels for 0%

profile of v5, /device:TPU:0, one launch (start us, length us, event | category | flops | bytes accessed | tf_op | source)
XLA Modules:
  0.0 294.1 jit_solution(3347161082256250721)
XLA Ops:
  7.9 0.7 compare_and_fusion
  8.6 1.3 fusion.5.position_ref
  9.9 133.5 %all-gather.2.cloned.1.call-done.source_ref = f32[8192,768]{1,0:T(8,128)} async-done(((f32[512,768]{1,0:T(8,128)}), f32[8192,768]{1,0:T(8,128)}) %all-gather.2.cloned.1.call-update) | async-done | bytes 25165840 | tf_op jit(solution)/shard_map/all_gather | solution.py:107
  143.4 31.6 %shard_map.59 = f32[320,768]{1,0:T(8,128)} custom-call(s32[320]{0:T(512)} %fusion.5.position_ref, f32[8192,768]{1,0:T(8,128)} %all-gather.2.cloned.1.call-done.source_ref), custom_call_target="tpu_custom_call" | custom-call | tf_op jit(solution)/shard_map/pallas_call | solution.py:33
  175.0 1.3 broadcast_select_fusion
  176.4 2.9 collective-permute-start
  179.3 12.0 %collective-permute-done = f32[160,768]{1,0:T(8,128)S(1)} collective-permute-done((f32[160,768]{1,0:T(8,128)S(1)}, f32[160,768]{1,0:T(8,128)S(1)}, u32[]{:S(2)}, u32[]{:S(2)}) %collective-permute-start) | collective-permute-done | bytes 491552 | tf_op jit(solution)/shard_map/ppermute | solution.py:70
  191.5 1.6 collective-permute-start.1
  193.1 2.7 collective-permute-start.2
  195.8 1.4 collective-permute-start.3
  197.2 1.3 collective-permute-done.1
  198.5 2.6 collective-permute-done.2
  201.2 2.7 collective-permute-start.4
  205.3 3.1 %collective-permute-done.4 = f32[40,768]{1,0:T(8,128)S(1)} collective-permute-done((f32[40,768]{1,0:T(8,128)S(1)}, f32[40,768]{1,0:T(8,128)S(1)}, u32[]{:S(2)}, u32[]{:S(2)}) %collective-permute-start.4) | collective-permute-done | bytes 122912 | tf_op jit(solution)/shard_map/ppermute | solution.py:59
  208.4 2.4 collective-permute-done.5
  210.8 1.0 collective-permute-done.6
  212.0 2.9 collective-permute-start.7
  214.9 9.2 %collective-permute-done.7 = f32[160,768]{1,0:T(8,128)S(1)} collective-permute-done((f32[160,768]{1,0:T(8,128)S(1)}, f32[160,768]{1,0:T(8,128)S(1)}, u32[]{:S(2)}, u32[]{:S(2)}) %collective-permute-start.7) | collective-permute-done | bytes 491552 | tf_op jit(solution)/shard_map/ppermute | solution.py:80
  224.2 16.5 %convolution_reduce_fusion = f32[8192]{0:T(1024)S(1)} fusion(f32[8192,768]{1,0:T(8,128)} %all-gather.2.cloned.1.call-done.source_ref, f32[320,768]{1,0:T(8,128)S(1)} %maximum_select_fusion), kind=kOutput, calls=%fused_computation.3 | convolution fusion | flops 4832878592 | bytes 25591808 | tf_op jit(solution)/shard_map/dot_general | solution.py:12
  240.8 1.2 collective-permute-done.8
  242.0 1.1 collective-permute-start.9
  243.1 2.8 collective-permute-done.9
  245.9 2.3 collective-permute-start.10
  248.2 3.1 %collective-permute-done.10 = f32[8192]{0:T(1024)S(1)} collective-permute-done((f32[8192]{0:T(1024)S(1)}, f32[8192]{0:T(1024)S(1)}, u32[]{:S(2)}, u32[]{:S(2)}) %collective-permute-start.10) | collective-permute-done | bytes 32800 | tf_op jit(solution)/shard_map/ppermute | solution.py:87
  251.3 1.5 collective-permute-start.11
  252.8 2.4 collective-permute-done.11
  255.3 17.4 %fusion.1 = f32[192]{0:T(256)S(1)} fusion(f32[8192]{0:T(1024)S(1)} %maximum_maximum_fusion, f32[8192,768]{1,0:T(8,128)} %all-gather.2.cloned.1.call-done.source_ref, f32[320,768]{1,0:T(8,128)S(1)} %maximum_select_fusion), kind=kOutput, calls=%fused_computation.2 | convolution fusion | flops 7252475904 | bytes 25789184 | tf_op jit(solution)/shard_map/dot_general | solution.py:12
  272.7 2.9 collective-permute-start.12
  275.6 2.2 collective-permute-done.12
  277.9 3.6 %collective-permute-done.13 = f32[2,192]{1,0:T(2,128)S(1)} collective-permute-done((f32[2,192]{1,0:T(2,128)S(1)}, f32[2,192]{1,0:T(2,128)S(1)}, u32[]{:S(2)}, u32[]{:S(2)}) %collective-permute-start.13) | collective-permute-done | bytes 1568 | tf_op jit(solution)/shard_map/ppermute | solution.py:97
  281.5 2.0 collective-permute-start.14
  283.5 3.2 %collective-permute-done.14 = f32[4,192]{1,0:T(4,128)S(1)} collective-permute-done((f32[4,192]{1,0:T(4,128)S(1)}, f32[4,192]{1,0:T(4,128)S(1)}, u32[]{:S(2)}, u32[]{:S(2)}) %collective-permute-start.14) | collective-permute-done | bytes 3104 | tf_op jit(solution)/shard_map/ppermute | solution.py:97
  (31 shorter events, 3.3 us)
Async XLA Ops:
  7.2 136.2 %all-gather.2.cloned.1.call-start = ((), (), s32[]{:S(2)}) async-start(), calls=%async_computation | async-start | bytes 26738688 | tf_op jit(solution)/shard_map/all_gather | solution.py:107
  175.0 80.3 %copy-start.1 = (f32[8192]{0:T(1024)S(1)}, f32[8192]{0:T(1024)}, u32[]{:S(2)}) copy-start(f32[8192]{0:T(1024)} %param.5) | copy-start | bytes 98308
  176.4 15.0 %collective-permute-start = (f32[160,768]{1,0:T(8,128)S(1)}, f32[160,768]{1,0:T(8,128)S(1)}, u32[]{:S(2)}, u32[]{:S(2)}) collective-permute-start(f32[160,768]{1,0:T(8,128)S(1)} %slice_select_fusion), channel_id=1, source_target_pairs={{0,1},{1,0},{2,3},{3,2},{4,5},{5,4},{6,7},{7,6},{8,9},{9,8},{10,11... | collective-permute-start | bytes 1474568 | tf_op jit(solution)/shard_map/ppermute | solution.py:70
  191.5 7.0 %collective-permute-start.1 = (f32[40,768]{1,0:T(8,128)S(1)}, f32[40,768]{1,0:T(8,128)S(1)}, u32[]{:S(2)}, u32[]{:S(2)}) collective-permute-start(f32[40,768]{1,0:T(8,128)S(1)} %get-tuple-element.4), channel_id=1, source_target_pairs={{0,2},{1,3},{2,4},{3,5},{4,6},{5,7},{6,0},{7,1},{8,10},{9,11},{10,... | collective-permute-start | bytes 368648 | tf_op jit(solution)/shard_map/ppermute | solution.py:59
  193.1 8.0 %collective-permute-start.2 = (f32[40,768]{1,0:T(8,128)S(1)}, f32[40,768]{1,0:T(8,128)S(1)}, u32[]{:S(2)}, u32[]{:S(2)}) collective-permute-start(f32[40,768]{1,0:T(8,128)S(1)} %get-tuple-element.6), channel_id=1, source_target_pairs={{0,4},{1,5},{2,6},{3,7},{4,0},{5,1},{6,2},{7,3},{8,12},{9,13},{10,... | collective-permute-start | bytes 368648 | tf_op jit(solution)/shard_map/ppermute | solution.py:59
  195.8 5.4 %collective-permute-start.3 = (f32[40,768]{1,0:T(8,128)S(1)}, f32[40,768]{1,0:T(8,128)S(1)}, u32[]{:S(2)}, u32[]{:S(2)}) collective-permute-start(f32[40,768]{1,0:T(8,128)S(1)} %get-tuple-element.5), channel_id=1, source_target_pairs={{0,6},{1,7},{2,0},{3,1},{4,2},{5,3},{6,4},{7,5},{8,14},{9,15},{10,... | collective-permute-start | bytes 368648 | tf_op jit(solution)/shard_map/ppermute | solution.py:59
  201.2 7.2 %collective-permute-start.4 = (f32[40,768]{1,0:T(8,128)S(1)}, f32[40,768]{1,0:T(8,128)S(1)}, u32[]{:S(2)}, u32[]{:S(2)}) collective-permute-start(f32[40,768]{1,0:T(8,128)S(1)} %get-tuple-element.3), channel_id=1, source_target_pairs={{0,6},{1,7},{2,0},{3,1},{4,2},{5,3},{6,4},{7,5},{8,14},{9,15},{10,... | collective-permute-start | bytes 368648 | tf_op jit(solution)/shard_map/ppermute | solution.py:59
  203.9 6.9 %collective-permute-start.5 = (f32[40,768]{1,0:T(8,128)S(1)}, f32[40,768]{1,0:T(8,128)S(1)}, u32[]{:S(2)}, u32[]{:S(2)}) collective-permute-start(f32[40,768]{1,0:T(8,128)S(1)} %get-tuple-element.3), channel_id=1, source_target_pairs={{0,4},{1,5},{2,6},{3,7},{4,0},{5,1},{6,2},{7,3},{8,12},{9,13},{10,... | collective-permute-start | bytes 368648 | tf_op jit(solution)/shard_map/ppermute | solution.py:59
  204.6 7.3 %collective-permute-start.6 = (f32[40,768]{1,0:T(8,128)S(1)}, f32[40,768]{1,0:T(8,128)S(1)}, u32[]{:S(2)}, u32[]{:S(2)}) collective-permute-start(f32[40,768]{1,0:T(8,128)S(1)} %get-tuple-element.3), channel_id=1, source_target_pairs={{0,2},{1,3},{2,4},{3,5},{4,6},{5,7},{6,0},{7,1},{8,10},{9,11},{10,... | collective-permute-start | bytes 368648 | tf_op jit(solution)/shard_map/ppermute | solution.py:59
  212.0 12.1 %collective-permute-start.7 = (f32[160,768]{1,0:T(8,128)S(1)}, f32[160,768]{1,0:T(8,128)S(1)}, u32[]{:S(2)}, u32[]{:S(2)}) collective-permute-start(f32[160,768]{1,0:T(8,128)S(1)} %bitcast.16), channel_id=1, source_target_pairs={{0,1},{1,0},{2,3},{3,2},{4,5},{5,4},{6,7},{7,6},{8,9},{9,8},{10,11... | collective-permute-start | bytes 1474568 | tf_op jit(solution)/shard_map/ppermute | solution.py:80
  240.7 1.3 collective-permute-start.8
  242.0 3.9 %collective-permute-start.9 = (f32[8192]{0:T(1024)S(1)}, f32[8192]{0:T(1024)S(1)}, u32[]{:S(2)}, u32[]{:S(2)}) collective-permute-start(f32[8192]{0:T(1024)S(1)} %max.25), channel_id=1, source_target_pairs={{0,16},{8,24},{16,0},{24,8},{32,48},{40,56},{48,32},{56,40},{64,80... | collective-permute-start | bytes 98312 | tf_op jit(solution)/shard_map/ppermute | solution.py:87
  245.9 5.4 %collective-permute-start.10 = (f32[8192]{0:T(1024)S(1)}, f32[8192]{0:T(1024)S(1)}, u32[]{:S(2)}, u32[]{:S(2)}) collective-permute-start(f32[8192]{0:T(1024)S(1)} %max.26), channel_id=1, source_target_pairs={{0,32},{8,40},{16,48},{24,56},{32,0},{40,8},{48,16},{56,24},{64,96... | collective-permute-start | bytes 98312 | tf_op jit(solution)/shard_map/ppermute | solution.py:87
  251.3 3.9 %collective-permute-start.11 = (f32[8192]{0:T(1024)S(1)}, f32[8192]{0:T(1024)S(1)}, u32[]{:S(2)}, u32[]{:S(2)}) collective-permute-start(f32[8192]{0:T(1024)S(1)} %max.27), channel_id=1, source_target_pairs={{0,64},{8,72},{16,80},{24,88},{32,96},{40,104},{48,112},{56,120},{... | collective-permute-start | bytes 98312 | tf_op jit(solution)/shard_map/ppermute | solution.py:87
  255.3 32.0 %copy-start = (f32[8192]{0:T(1024)}, f32[8192]{0:T(1024)S(1)}, u32[]{:S(2)}) copy-start(f32[8192]{0:T(1024)S(1)} %maximum_maximum_fusion) | copy-start | bytes 98308
  272.7 5.2 %collective-permute-start.12 = (f32[1,192]{1,0:T(1,128)S(1)}, f32[1,192]{1,0:T(1,128)S(1)}, u32[]{:S(2)}, u32[]{:S(2)}) collective-permute-start(f32[1,192]{1,0:T(1,128)S(1)} %bitcast.18), channel_id=1, source_target_pairs={{0,1},{1,0},{2,3},{3,2},{4,5},{5,4},{6,7},{7,6},{8,9},{9,8},{10,11... | collective-permute-start | bytes 2312 | tf_op jit(solution)/shard_map/ppermute | solution.py:97
  277.8 3.7 %collective-permute-start.13 = (f32[2,192]{1,0:T(2,128)S(1)}, f32[2,192]{1,0:T(2,128)S(1)}, u32[]{:S(2)}, u32[]{:S(2)}) collective-permute-start(f32[2,192]{1,0:T(2,128)S(1)} %maximum_select_fusion.3), channel_id=1, source_target_pairs={{0,2},{1,3},{2,0},{3,1},{4,6},{5,7},{6,4},{7,5},{8,10},{9,11},{10,... | collective-permute-start | bytes 4616 | tf_op jit(solution)/shard_map/ppermute | solution.py:97
  281.5 5.2 %collective-permute-start.14 = (f32[4,192]{1,0:T(4,128)S(1)}, f32[4,192]{1,0:T(4,128)S(1)}, u32[]{:S(2)}, u32[]{:S(2)}) collective-permute-start(f32[4,192]{1,0:T(4,128)S(1)} %maximum_select_fusion.2), channel_id=1, source_target_pairs={{0,4},{1,5},{2,6},{3,7},{4,0},{5,1},{6,2},{7,3},{8,12},{9,13},{10,... | collective-permute-start | bytes 9224 | tf_op jit(solution)/shard_map/ppermute | solution.py:97
Sparse Core Ops, SparseCore 0:
  9.7 133.6 all-gather.1

commit v6 on v4

--- a/solution.py
+++ b/solution.py
@@ -35,23 +35,24 @@
 def col_masked_sum(value):
     here = lax.axis_index("col")
     y, z = here // N_Z, here % N_Z
-    half = value.shape[0] // N_Z
-    quarter = half // N_Y
-    halves = value.reshape(N_Z, half, *value.shape[1:])
-    mine = jnp.where(z == 0, halves[0], halves[1])
-    theirs = jnp.where(z == 0, halves[1], halves[0])
-    mine = mine + lax.ppermute(theirs, "col", [(c, c ^ 1) for c in range(N_Y * N_Z)])
+    quarter = value.shape[0] // N_Y
+    half = quarter // N_Z
 
     def part(k):
-        return lax.dynamic_slice_in_dim(mine, ((y + k) % N_Y) * quarter, quarter)
+        return lax.dynamic_slice_in_dim(value, ((y + k) % N_Y) * quarter, quarter)
 
     own = part(0)
     for k in range(1, N_Y):
         own = own + y_shift(part(k), k)
+    halves = own.reshape(N_Z, half, *value.shape[1:])
+    mine = jnp.where(z == 0, halves[0], halves[1])
+    theirs = jnp.where(z == 0, halves[1], halves[0])
+    swap = [(c, c ^ 1) for c in range(N_Y * N_Z)]
+    mine = mine + lax.ppermute(theirs, "col", swap)
+    other = lax.ppermute(mine, "col", swap)
+    own = jnp.where(z == 0, jnp.concatenate([mine, other]), jnp.concatenate([other, mine]))
     pieces = [own] + [y_shift(own, -k) for k in range(1, N_Y)]
-    ordered = jnp.roll(jnp.stack(pieces), y, axis=0).reshape(half, *value.shape[1:])
-    other = lax.ppermute(ordered, "col", [(c, c ^ 1) for c in range(N_Y * N_Z)])
-    return jnp.where(z == 0, jnp.concatenate([ordered, other]), jnp.concatenate([other, ordered]))
+    return jnp.roll(jnp.stack(pieces), y, axis=0).reshape(value.shape)
 
 
 def all_max(value, axis, n):

time: 280 us -> 276 us (0.986)
  waiting for transfers between devices: 185 us -> 182 us
    ppermute x2, waiting for transfers between devices: 21.2 us -> 7.06 us  [the longest x1 3.53 us: col_masked_sum(): other = lax.ppermute(mine, 'col', swap)]
    ppermute x6, waiting for transfers between devices: 10.5 us -> 20.5 us  [y_shift(): return lax.ppermute(value, 'col', pairs)]
  transfers between devices with their start and end apart: 16 -> 16, of which waited for: 16 -> 15; matrix products, arithmetic and copies ran while one was open for 0% -> 1% of each run, Pallas kernels for 0% -> 0%
where the time goes in v6:
time: 276 us
  waiting for transfers between devices  182 us (66%)
  matrix products  33.8 us (12%)
  starting transfers between devices  24.4 us (9%)
  local copies, waits for them, and re-layouts  18.7 us (7%)
  between operations  14.3 us (5%)
    all_gather x1, waiting for transfers between devices, body(): gathered = lax.all_gather(slab_embed, 'row', axis=0, tiled=True)  134 us
    dot_general x2, matrix products, similar(): lax.dot_general(left, right, (((1,), (1,)), ((), ())), precision=lax.Prec...  33.8 us
    ppermute x6, waiting for transfers between devices, y_shift(): return lax.ppermute(value, 'col', pairs)  20.5 us
    gather x2, local copies, waits for them, and re-layouts, lookup(): jnp.take(source, jnp.clip(position, 0, source.shape[0] - 1), axis=0)  18.5 us
    ppermute x3, waiting for transfers between devices, all_sum(): other = lax.ppermute(parts, axis, [(i, i ^ bit) for i in range(n)])  10.3 us
    ppermute x6, starting transfers between devices, y_shift(): return lax.ppermute(value, 'col', pairs)  9.86 us
    ppermute x4, waiting for transfers between devices, all_max(): lax.ppermute(value, axis, [(i, i ^ bit) for i in range(n)])  9.53 us
  transfers between devices with their start and end apart: 16, of which 15 were waited for; matrix products, arithmetic and copies ran while one was open for 1% of the time, Pallas kernels for 0%

profile of v6, /device:TPU:0, one launch (start us, length us, event | category | flops | bytes accessed | tf_op | source)
XLA Modules:
  0.0 276.0 jit_solution(3624920253089503861)
XLA Ops:
  7.2 0.7 all-gather.2.cloned.1.call-update
  8.6 0.7 compare_and_fusion
  9.3 134.0 %all-gather.2.cloned.1.call-done = f32[8192,768]{1,0:T(8,128)} async-done(((f32[512,768]{1,0:T(8,128)}), f32[8192,768]{1,0:T(8,128)}) %all-gather.2.cloned.1.call-update) | async-done | bytes 25165840 | tf_op jit(solution)/shard_map/all_gather | solution.py:81
  143.4 9.3 %gather_fusion.1 = f32[192,768]{1,0:T(8,128)S(1)} fusion(f32[8192,768]{1,0:T(8,128)} %all-gather.2.cloned.1.call-done, s32[1024]{0:T(1024)S(1)} %get-tuple-element.11), kind=kCustom, calls=%fused_computation.1 | custom fusion | bytes 1180416 | tf_op jit(solution)/shard_map/jit(_take)/gather | solution.py:22
  152.9 9.1 %gather_fusion = f32[128,768]{1,0:T(8,128)S(1)} fusion(f32[8192,768]{1,0:T(8,128)} %all-gather.2.cloned.1.call-done, s32[1024]{0:T(1024)S(1)} %get-tuple-element.12), kind=kCustom, calls=%fused_computation | custom fusion | bytes 786944 | tf_op jit(solution)/shard_map/jit(_take)/gather | solution.py:22
  162.3 1.6 collective-permute-start
  163.9 2.7 collective-permute-start.1
  166.6 1.4 collective-permute-start.2
  168.0 3.7 %collective-permute-done = f32[80,768]{1,0:T(8,128)S(1)} collective-permute-done((f32[80,768]{1,0:T(8,128)S(1)}, f32[80,768]{1,0:T(8,128)S(1)}, u32[]{:S(2)}, u32[]{:S(2)}) %collective-permute-start) | collective-permute-done | bytes 245792 | tf_op jit(solution)/shard_map/ppermute | solution.py:32
  171.7 6.2 %collective-permute-done.1 = f32[80,768]{1,0:T(8,128)S(1)} collective-permute-done((f32[80,768]{1,0:T(8,128)S(1)}, f32[80,768]{1,0:T(8,128)S(1)}, u32[]{:S(2)}, u32[]{:S(2)}) %collective-permute-start.1) | collective-permute-done | bytes 245792 | tf_op jit(solution)/shard_map/ppermute | solution.py:32
  178.1 2.9 %collective-permute-start.3 = (f32[40,768]{1,0:T(8,128)S(1)}, f32[40,768]{1,0:T(8,128)S(1)}, u32[]{:S(2)}, u32[]{:S(2)}) collective-permute-start(f32[40,768]{1,0:T(8,128)S(1)} %slice_select_fusion), channel_id=1, source_target_pairs={{0,1},{1,0},{2,3},{3,2},{4,5},{5,4},{6,7},{7,6},{8,9},{9,8},{10,11... | collective-permute-start | bytes 368648 | tf_op jit(solution)/shard_map/ppermute | solution.py:51
  181.0 3.5 %collective-permute-done.3 = f32[40,768]{1,0:T(8,128)S(1)} collective-permute-done((f32[40,768]{1,0:T(8,128)S(1)}, f32[40,768]{1,0:T(8,128)S(1)}, u32[]{:S(2)}, u32[]{:S(2)}) %collective-permute-start.3) | collective-permute-done | bytes 122912 | tf_op jit(solution)/shard_map/ppermute | solution.py:51
  184.5 2.9 %collective-permute-start.4 = (f32[40,768]{1,0:T(8,128)S(1)}, f32[40,768]{1,0:T(8,128)S(1)}, u32[]{:S(2)}, u32[]{:S(2)}) collective-permute-start(f32[40,768]{1,0:T(8,128)S(1)} %select_add_fusion), channel_id=1, source_target_pairs={{0,1},{1,0},{2,3},{3,2},{4,5},{5,4},{6,7},{7,6},{8,9},{9,8},{10,11... | collective-permute-start | bytes 368648 | tf_op jit(solution)/shard_map/ppermute | solution.py:52
  187.5 3.5 %collective-permute-done.4 = f32[40,768]{1,0:T(8,128)S(1)} collective-permute-done((f32[40,768]{1,0:T(8,128)S(1)}, f32[40,768]{1,0:T(8,128)S(1)}, u32[]{:S(2)}, u32[]{:S(2)}) %collective-permute-start.4) | collective-permute-done | bytes 122912 | tf_op jit(solution)/shard_map/ppermute | solution.py:52
  191.0 2.7 collective-permute-start.5
  193.7 0.8 collective-permute-start.6
  195.2 7.2 %collective-permute-done.5 = f32[80,768]{1,0:T(8,128)S(1)} collective-permute-done((f32[80,768]{1,0:T(8,128)S(1)}, f32[80,768]{1,0:T(8,128)S(1)}, u32[]{:S(2)}, u32[]{:S(2)}) %collective-permute-start.5) | collective-permute-done | bytes 245792 | tf_op jit(solution)/shard_map/ppermute | solution.py:32
  202.4 1.1 collective-permute-done.6
  203.6 2.2 collective-permute-done.7
  206.1 16.5 %convolution_reduce_fusion = f32[8192]{0:T(1024)S(1)} fusion(f32[8192,768]{1,0:T(8,128)} %all-gather.2.cloned.1.call-done, f32[320,768]{1,0:T(8,128)S(1)} %bitcast.15), kind=kOutput, calls=%fused_computation.7 | convolution fusion | flops 4832878592 | bytes 25591808 | tf_op jit(solution)/shard_map/dot_general | solution.py:10
  222.6 1.2 collective-permute-done.8
  223.8 1.1 collective-permute-start.9
  224.9 2.8 %collective-permute-done.9 = f32[8192]{0:T(1024)S(1)} collective-permute-done((f32[8192]{0:T(1024)S(1)}, f32[8192]{0:T(1024)S(1)}, u32[]{:S(2)}, u32[]{:S(2)}) %collective-permute-start.9) | collective-permute-done | bytes 32800 | tf_op jit(solution)/shard_map/ppermute | solution.py:61
  227.8 2.3 collective-permute-start.10
  230.1 3.1 %collective-permute-done.10 = f32[8192]{0:T(1024)S(1)} collective-permute-done((f32[8192]{0:T(1024)S(1)}, f32[8192]{0:T(1024)S(1)}, u32[]{:S(2)}, u32[]{:S(2)}) %collective-permute-start.10) | collective-permute-done | bytes 32800 | tf_op jit(solution)/shard_map/ppermute | solution.py:61
  233.2 1.5 collective-permute-start.11
  234.7 2.4 collective-permute-done.11
  237.1 17.4 %maximum_reduce_fusion = f32[192]{0:T(256)S(1)} fusion(f32[8192]{0:T(1024)S(1)} %maximum_maximum_fusion, f32[8192,768]{1,0:T(8,128)} %all-gather.2.cloned.1.call-done, f32[320,768]{1,0:T(8,128)S(1)} %bitcast.16), kind=kOutput, calls=%fused_computation.2 | convolution fusion | flops 7252475904 | bytes 25789184 | tf_op jit(solution)/shard_map/dot_general | solution.py:10
  254.5 2.9 %collective-permute-start.12 = (f32[1,192]{1,0:T(1,128)S(1)}, f32[1,192]{1,0:T(1,128)S(1)}, u32[]{:S(2)}, u32[]{:S(2)}) collective-permute-start(f32[1,192]{1,0:T(1,128)S(1)} %bitcast.21), channel_id=1, source_target_pairs={{0,1},{1,0},{2,3},{3,2},{4,5},{5,4},{6,7},{7,6},{8,9},{9,8},{10,11... | collective-permute-start | bytes 2312 | tf_op jit(solution)/shard_map/ppermute | solution.py:71
  257.5 2.2 collective-permute-done.12
  259.8 3.6 %collective-permute-done.13 = f32[2,192]{1,0:T(2,128)S(1)} collective-permute-done((f32[2,192]{1,0:T(2,128)S(1)}, f32[2,192]{1,0:T(2,128)S(1)}, u32[]{:S(2)}, u32[]{:S(2)}) %collective-permute-start.13) | collective-permute-done | bytes 1568 | tf_op jit(solution)/shard_map/ppermute | solution.py:71
  264.0 4.5 %collective-permute-done.14 = f32[4,192]{1,0:T(4,128)S(1)} collective-permute-done((f32[4,192]{1,0:T(4,128)S(1)}, f32[4,192]{1,0:T(4,128)S(1)}, u32[]{:S(2)}, u32[]{:S(2)}) %collective-permute-start.14) | collective-permute-done | bytes 3104 | tf_op jit(solution)/shard_map/ppermute | solution.py:71
  (35 shorter events, 3.7 us)
Async XLA Ops:
  7.2 136.2 %all-gather.2.cloned.1.call-start = ((), (), s32[]{:S(2)}) async-start(), calls=%async_computation | async-start | bytes 26738688 | tf_op jit(solution)/shard_map/all_gather | solution.py:81
  162.3 9.4 %collective-permute-start = (f32[80,768]{1,0:T(8,128)S(1)}, f32[80,768]{1,0:T(8,128)S(1)}, u32[]{:S(2)}, u32[]{:S(2)}) collective-permute-start(f32[80,768]{1,0:T(8,128)S(1)} %get-tuple-element.6), channel_id=1, source_target_pairs={{0,2},{1,3},{2,4},{3,5},{4,6},{5,7},{6,0},{7,1},{8,10},{9,11},{10,... | collective-permute-start | bytes 737288 | tf_op jit(solution)/shard_map/ppermute | solution.py:32
  163.9 14.1 %collective-permute-start.1 = (f32[80,768]{1,0:T(8,128)S(1)}, f32[80,768]{1,0:T(8,128)S(1)}, u32[]{:S(2)}, u32[]{:S(2)}) collective-permute-start(f32[80,768]{1,0:T(8,128)S(1)} %get-tuple-element.7), channel_id=1, source_target_pairs={{0,4},{1,5},{2,6},{3,7},{4,0},{5,1},{6,2},{7,3},{8,12},{9,13},{10,... | collective-permute-start | bytes 737288 | tf_op jit(solution)/shard_map/ppermute | solution.py:32
  166.6 11.4 %collective-permute-start.2 = (f32[80,768]{1,0:T(8,128)S(1)}, f32[80,768]{1,0:T(8,128)S(1)}, u32[]{:S(2)}, u32[]{:S(2)}) collective-permute-start(f32[80,768]{1,0:T(8,128)S(1)} %get-tuple-element.8), channel_id=1, source_target_pairs={{0,6},{1,7},{2,0},{3,1},{4,2},{5,3},{6,4},{7,5},{8,14},{9,15},{10,... | collective-permute-start | bytes 737288 | tf_op jit(solution)/shard_map/ppermute | solution.py:32
  178.1 6.5 %collective-permute-start.3 = (f32[40,768]{1,0:T(8,128)S(1)}, f32[40,768]{1,0:T(8,128)S(1)}, u32[]{:S(2)}, u32[]{:S(2)}) collective-permute-start(f32[40,768]{1,0:T(8,128)S(1)} %slice_select_fusion), channel_id=1, source_target_pairs={{0,1},{1,0},{2,3},{3,2},{4,5},{5,4},{6,7},{7,6},{8,9},{9,8},{10,11... | collective-permute-start | bytes 368648 | tf_op jit(solution)/shard_map/ppermute | solution.py:51
  184.5 6.5 %collective-permute-start.4 = (f32[40,768]{1,0:T(8,128)S(1)}, f32[40,768]{1,0:T(8,128)S(1)}, u32[]{:S(2)}, u32[]{:S(2)}) collective-permute-start(f32[40,768]{1,0:T(8,128)S(1)} %select_add_fusion), channel_id=1, source_target_pairs={{0,1},{1,0},{2,3},{3,2},{4,5},{5,4},{6,7},{7,6},{8,9},{9,8},{10,11... | collective-permute-start | bytes 368648 | tf_op jit(solution)/shard_map/ppermute | solution.py:52
  191.0 11.4 %collective-permute-start.5 = (f32[80,768]{1,0:T(8,128)S(1)}, f32[80,768]{1,0:T(8,128)S(1)}, u32[]{:S(2)}, u32[]{:S(2)}) collective-permute-start(f32[80,768]{1,0:T(8,128)S(1)} %maximum_select_fusion.1), channel_id=1, source_target_pairs={{0,6},{1,7},{2,0},{3,1},{4,2},{5,3},{6,4},{7,5},{8,14},{9,15},{10,... | collective-permute-start | bytes 737288 | tf_op jit(solution)/shard_map/ppermute | solution.py:32
  193.7 9.8 %collective-permute-start.6 = (f32[80,768]{1,0:T(8,128)S(1)}, f32[80,768]{1,0:T(8,128)S(1)}, u32[]{:S(2)}, u32[]{:S(2)}) collective-permute-start(f32[80,768]{1,0:T(8,128)S(1)} %maximum_select_fusion.1), channel_id=1, source_target_pairs={{0,4},{1,5},{2,6},{3,7},{4,0},{5,1},{6,2},{7,3},{8,12},{9,13},{10,... | collective-permute-start | bytes 737288 | tf_op jit(solution)/shard_map/ppermute | solution.py:32
  194.5 11.3 %collective-permute-start.7 = (f32[80,768]{1,0:T(8,128)S(1)}, f32[80,768]{1,0:T(8,128)S(1)}, u32[]{:S(2)}, u32[]{:S(2)}) collective-permute-start(f32[80,768]{1,0:T(8,128)S(1)} %maximum_select_fusion.1), channel_id=1, source_target_pairs={{0,2},{1,3},{2,4},{3,5},{4,6},{5,7},{6,0},{7,1},{8,10},{9,11},{10,... | collective-permute-start | bytes 737288 | tf_op jit(solution)/shard_map/ppermute | solution.py:32
  206.1 31.0 %copy-start.1 = (f32[8192]{0:T(1024)S(1)}, f32[8192]{0:T(1024)}, u32[]{:S(2)}) copy-start(f32[8192]{0:T(1024)} %param.5) | copy-start | bytes 98308
  222.5 1.3 collective-permute-start.8
  223.8 3.9 %collective-permute-start.9 = (f32[8192]{0:T(1024)S(1)}, f32[8192]{0:T(1024)S(1)}, u32[]{:S(2)}, u32[]{:S(2)}) collective-permute-start(f32[8192]{0:T(1024)S(1)} %max.29), channel_id=1, source_target_pairs={{0,16},{8,24},{16,0},{24,8},{32,48},{40,56},{48,32},{56,40},{64,80... | collective-permute-start | bytes 98312 | tf_op jit(solution)/shard_map/ppermute | solution.py:61
  227.8 5.4 %collective-permute-start.10 = (f32[8192]{0:T(1024)S(1)}, f32[8192]{0:T(1024)S(1)}, u32[]{:S(2)}, u32[]{:S(2)}) collective-permute-start(f32[8192]{0:T(1024)S(1)} %max.30), channel_id=1, source_target_pairs={{0,32},{8,40},{16,48},{24,56},{32,0},{40,8},{48,16},{56,24},{64,96... | collective-permute-start | bytes 98312 | tf_op jit(solution)/shard_map/ppermute | solution.py:61
  233.2 3.9 %collective-permute-start.11 = (f32[8192]{0:T(1024)S(1)}, f32[8192]{0:T(1024)S(1)}, u32[]{:S(2)}, u32[]{:S(2)}) collective-permute-start(f32[8192]{0:T(1024)S(1)} %max.31), channel_id=1, source_target_pairs={{0,64},{8,72},{16,80},{24,88},{32,96},{40,104},{48,112},{56,120},{... | collective-permute-start | bytes 98312 | tf_op jit(solution)/shard_map/ppermute | solution.py:61
  237.1 17.4 %copy-start = (f32[8192]{0:T(1024)}, f32[8192]{0:T(1024)S(1)}, u32[]{:S(2)}) copy-start(f32[8192]{0:T(1024)S(1)} %maximum_maximum_fusion) | copy-start | bytes 98308
  254.5 5.2 %collective-permute-start.12 = (f32[1,192]{1,0:T(1,128)S(1)}, f32[1,192]{1,0:T(1,128)S(1)}, u32[]{:S(2)}, u32[]{:S(2)}) collective-permute-start(f32[1,192]{1,0:T(1,128)S(1)} %bitcast.21), channel_id=1, source_target_pairs={{0,1},{1,0},{2,3},{3,2},{4,5},{5,4},{6,7},{7,6},{8,9},{9,8},{10,11... | collective-permute-start | bytes 2312 | tf_op jit(solution)/shard_map/ppermute | solution.py:71
  259.7 3.7 %collective-permute-start.13 = (f32[2,192]{1,0:T(2,128)S(1)}, f32[2,192]{1,0:T(2,128)S(1)}, u32[]{:S(2)}, u32[]{:S(2)}) collective-permute-start(f32[2,192]{1,0:T(2,128)S(1)} %maximum_select_fusion.4), channel_id=1, source_target_pairs={{0,2},{1,3},{2,0},{3,1},{4,6},{5,7},{6,4},{7,5},{8,10},{9,11},{10,... | collective-permute-start | bytes 4616 | tf_op jit(solution)/shard_map/ppermute | solution.py:71
  263.4 5.2 %collective-permute-start.14 = (f32[4,192]{1,0:T(4,128)S(1)}, f32[4,192]{1,0:T(4,128)S(1)}, u32[]{:S(2)}, u32[]{:S(2)}) collective-permute-start(f32[4,192]{1,0:T(4,128)S(1)} %maximum_select_fusion.3), channel_id=1, source_target_pairs={{0,4},{1,5},{2,6},{3,7},{4,0},{5,1},{6,2},{7,3},{8,12},{9,13},{10,... | collective-permute-start | bytes 9224 | tf_op jit(solution)/shard_map/ppermute | solution.py:71
Sparse Core Ops, SparseCore 0:
  9.7 133.6 all-gather.1

commit v7 on v6

--- a/solution.py
+++ b/solution.py
@@ -80,21 +80,13 @@
     col_id = lax.axis_index("col")
     gathered = lax.all_gather(slab_embed, "row", axis=0, tiled=True)
     first_row = col_id * gathered.shape[0]
-    n_sel = sel_index.shape[0]
-    picked = col_masked_sum(
-        jnp.concatenate([lookup(gathered, sel_index, first_row), lookup(gathered, cand_index, first_row)])
-    )
-    selected, chosen = picked[:n_sel], picked[n_sel:]
-    n_chunks = 1
-    width = gathered.shape[0] // n_chunks
-    coverages, gains = [], []
-    for i in range(n_chunks):
-        points = gathered[i * width:(i + 1) * width]
-        reached = all_max(jnp.max(similar(selected, points), axis=0), "row", n_row)
-        coverage = jnp.maximum(coverage_old[i * width:(i + 1) * width], reached)
-        coverages.append(coverage)
-        gains.append(jnp.sum(jnp.maximum(similar(chosen, points) - coverage[None, :], 0.0), axis=1))
-    total_gain = all_sum(sum(gains[1:], gains[0]), "col", N_Y * N_Z)
+    selected = col_masked_sum(lookup(gathered, sel_index, first_row))
+    chosen = col_masked_sum(lookup(gathered, cand_index, first_row))
+    reached = all_max(jnp.max(similar(selected, gathered), axis=0), "row", n_row)
+    coverages = [jnp.maximum(coverage_old, reached)]
+    scores = lax.optimization_barrier(similar(chosen, gathered))
+    gain_part = jnp.sum(jnp.maximum(scores - coverages[0][None, :], 0.0), axis=1)
+    total_gain = all_sum(gain_part, "col", N_Y * N_Z)
     return (jnp.concatenate(coverages), total_gain)
 
 

time: 276 us -> 265 us (0.960)
  waiting for transfers between devices: 182 us -> 165 us
  starting transfers between devices: 24.4 us -> 30.2 us
    ppermute x6 -> x12, waiting for transfers between devices: 20.5 us -> 11.2 us  [y_shift(): return lax.ppermute(value, 'col', pairs)]
    ppermute x6 -> x12, starting transfers between devices: 9.86 us -> 14.5 us  [y_shift(): return lax.ppermute(value, 'col', pairs)]
    ppermute x1 -> x2, waiting for transfers between devices: 3.53 us -> 0.01 us  [col_masked_sum(): other = lax.ppermute(mine, 'col', swap)]
    ppermute x4, waiting for transfers between devices: 9.53 us -> 6.34 us  [all_max(): lax.ppermute(value, axis, [(i, i ^ bit) for i in range(n)])]
  transfers between devices with their start and end apart: 16 -> 24, of which waited for: 15 -> 15; matrix products, arithmetic and copies ran while one was open for 1% -> 10% of each run, Pallas kernels for 0% -> 0%
where the time goes in v7:
time: 265 us
  waiting for transfers between devices  165 us (62%)
  matrix products  33.9 us (13%)
  starting transfers between devices  30.2 us (11%)
  local copies, waits for them, and re-layouts  18.8 us (7%)
  between operations  14.5 us (5%)
    all_gather x1, waiting for transfers between devices, body(): gathered = lax.all_gather(slab_embed, 'row', axis=0, tiled=True)  135 us
    dot_general x2, matrix products, similar(): lax.dot_general(left, right, (((1,), (1,)), ((), ())), precision=lax.Prec...  33.9 us
    gather x2, local copies, waits for them, and re-layouts, lookup(): jnp.take(source, jnp.clip(position, 0, source.shape[0] - 1), axis=0)  18.5 us
    ppermute x12, starting transfers between devices, y_shift(): return lax.ppermute(value, 'col', pairs)  14.5 us
    ppermute x12, waiting for transfers between devices, y_shift(): return lax.ppermute(value, 'col', pairs)  11.2 us
    ppermute x3, waiting for transfers between devices, all_sum(): other = lax.ppermute(parts, axis, [(i, i ^ bit) for i in range(n)])  9.67 us
    ppermute x4, waiting for transfers between devices, all_max(): lax.ppermute(value, axis, [(i, i ^ bit) for i in range(n)])  6.34 us
  transfers between devices with their start and end apart: 24, of which 15 were waited for; matrix products, arithmetic and copies ran while one was open for 10% of the time, Pallas kernels for 0%

profile of v7, /device:TPU:0, one launch (start us, length us, event | category | flops | bytes accessed | tf_op | source)
XLA Modules:
  0.0 264.6 jit_solution(4161577968116386693)
XLA Ops:
  8.1 135.3 %all-gather.2.cloned.1.call-done = f32[8192,768]{1,0:T(8,128)} async-done(((f32[512,768]{1,0:T(8,128)}), f32[8192,768]{1,0:T(8,128)}) %all-gather.2.cloned.1.call-update) | async-done | bytes 25165840 | tf_op jit(solution)/shard_map/all_gather | solution.py:81
  143.4 9.1 %gather_fusion = f32[128,768]{1,0:T(8,128)S(1)} fusion(f32[8192,768]{1,0:T(8,128)} %all-gather.2.cloned.1.call-done, s32[1024]{0:T(1024)S(1)} %get-tuple-element.15), kind=kCustom, calls=%fused_computation | custom fusion | bytes 786944 | tf_op jit(solution)/shard_map/jit(_take)/gather | solution.py:22
  152.7 2.8 %collective-permute-start.2 = (f32[32,768]{1,0:T(8,128)S(1)}, f32[32,768]{1,0:T(8,128)S(1)}, u32[]{:S(2)}, u32[]{:S(2)}) collective-permute-start(f32[32,768]{1,0:T(8,128)S(1)} %get-tuple-element.10), channel_id=1, source_target_pairs={{0,6},{1,7},{2,0},{3,1},{4,2},{5,3},{6,4},{7,5},{8,14},{9,15},{10,... | collective-permute-start | bytes 294920 | tf_op jit(solution)/shard_map/ppermute | solution.py:32
  157.2 9.3 %gather_fusion.1 = f32[192,768]{1,0:T(8,128)S(1)} fusion(f32[8192,768]{1,0:T(8,128)} %all-gather.2.cloned.1.call-done, s32[1024]{0:T(1024)S(1)} %get-tuple-element.14), kind=kCustom, calls=%fused_computation.1 | custom fusion | bytes 1180416 | tf_op jit(solution)/shard_map/jit(_take)/gather | solution.py:22
  166.8 2.9 %collective-permute-start.3 = (f32[16,768]{1,0:T(8,128)S(1)}, f32[16,768]{1,0:T(8,128)S(1)}, u32[]{:S(2)}, u32[]{:S(2)}) collective-permute-start(f32[16,768]{1,0:T(8,128)S(1)} %slice_select_fusion.1), channel_id=1, source_target_pairs={{0,1},{1,0},{2,3},{3,2},{4,5},{5,4},{6,7},{7,6},{8,9},{9,8},{10,11... | collective-permute-start | bytes 147464 | tf_op jit(solution)/shard_map/ppermute | solution.py:51
  169.7 2.4 collective-permute-start.14
  172.2 1.5 collective-permute-start.13
  173.7 1.7 collective-permute-start.4
  175.4 2.4 collective-permute-done.14
  177.8 2.2 collective-permute-done.13
  179.9 1.5 collective-permute-done.12
  182.9 1.5 collective-permute-start.6
  185.3 2.2 collective-permute-done.15
  188.3 0.9 collective-permute-done.6
  189.2 1.0 collective-permute-done.7
  190.4 16.5 %convolution_reduce_fusion = f32[8192]{0:T(1024)S(1)} fusion(f32[128,768]{1,0:T(8,128)S(1)} %bitcast.30, f32[8192,768]{1,0:T(8,128)} %all-gather.2.cloned.1.call-done), kind=kOutput, calls=%fused_computation.3 | convolution fusion | flops 4832878592 | bytes 25591808 | tf_op jit(solution)/shard_map/dot_general | solution.py:10
  207.0 1.2 collective-permute-done.8
  208.2 1.1 collective-permute-start.9
  209.3 2.8 %collective-permute-done.9 = f32[8192]{0:T(1024)S(1)} collective-permute-done((f32[8192]{0:T(1024)S(1)}, f32[8192]{0:T(1024)S(1)}, u32[]{:S(2)}, u32[]{:S(2)}) %collective-permute-start.9) | collective-permute-done | bytes 32800 | tf_op jit(solution)/shard_map/ppermute | solution.py:61
  212.1 2.3 collective-permute-start.10
  214.4 1.5 collective-permute-start.17
  215.9 0.9 collective-permute-start.18
  217.5 1.6 collective-permute-start.11
  219.2 2.3 collective-permute-done.11
  221.6 1.7 collective-permute-done.18
  223.3 1.5 collective-permute-done.19
  224.9 17.4 %fusion.5 = f32[192,8192]{1,0:T(8,128)S(1)} fusion(f32[192,768]{1,0:T(8,128)S(1)} %bitcast.29, f32[8192,768]{1,0:T(8,128)} %all-gather.2.cloned.1.call-done), kind=kOutput, calls=%fused_computation.53 | convolution fusion | flops 7247757312 | bytes 32047104 | tf_op jit(solution)/shard_map/dot_general | solution.py:10
  243.2 3.2 %collective-permute-start.20 = (f32[1,192]{1,0:T(1,128)S(1)}, f32[1,192]{1,0:T(1,128)S(1)}, u32[]{:S(2)}, u32[]{:S(2)}) collective-permute-start(f32[1,192]{1,0:T(1,128)S(1)} %bitcast.39), channel_id=1, source_target_pairs={{0,1},{1,0},{2,3},{3,2},{4,5},{5,4},{6,7},{7,6},{8,9},{9,8},{10,11... | collective-permute-start | bytes 2312 | tf_op jit(solution)/shard_map/ppermute | solution.py:71
  246.4 1.9 collective-permute-done.20
  248.4 3.6 %collective-permute-done.21 = f32[2,192]{1,0:T(2,128)S(1)} collective-permute-done((f32[2,192]{1,0:T(2,128)S(1)}, f32[2,192]{1,0:T(2,128)S(1)}, u32[]{:S(2)}, u32[]{:S(2)}) %collective-permute-start.21) | collective-permute-done | bytes 1568 | tf_op jit(solution)/shard_map/ppermute | solution.py:71
  252.0 1.0 collective-permute-start.22
  253.0 4.2 %collective-permute-done.22 = f32[4,192]{1,0:T(4,128)S(1)} collective-permute-done((f32[4,192]{1,0:T(4,128)S(1)}, f32[4,192]{1,0:T(4,128)S(1)}, u32[]{:S(2)}, u32[]{:S(2)}) %collective-permute-start.22) | collective-permute-done | bytes 3104 | tf_op jit(solution)/shard_map/ppermute | solution.py:71
  (70 shorter events, 8.6 us)
Async XLA Ops:
  7.2 0.9 copy-start.3
  7.2 0.9 copy-start.2
  7.2 136.2 %all-gather.2.cloned.1.call-start = ((), (), s32[]{:S(2)}) async-start(), calls=%async_computation | async-start | bytes 26738688 | tf_op jit(solution)/shard_map/all_gather | solution.py:81
  152.7 14.0 %collective-permute-start.2 = (f32[32,768]{1,0:T(8,128)S(1)}, f32[32,768]{1,0:T(8,128)S(1)}, u32[]{:S(2)}, u32[]{:S(2)}) collective-permute-start(f32[32,768]{1,0:T(8,128)S(1)} %get-tuple-element.10), channel_id=1, source_target_pairs={{0,6},{1,7},{2,0},{3,1},{4,2},{5,3},{6,4},{7,5},{8,14},{9,15},{10,... | collective-permute-start | bytes 294920 | tf_op jit(solution)/shard_map/ppermute | solution.py:32
  155.5 11.2 %collective-permute-start.1 = (f32[32,768]{1,0:T(8,128)S(1)}, f32[32,768]{1,0:T(8,128)S(1)}, u32[]{:S(2)}, u32[]{:S(2)}) collective-permute-start(f32[32,768]{1,0:T(8,128)S(1)} %get-tuple-element.11), channel_id=1, source_target_pairs={{0,4},{1,5},{2,6},{3,7},{4,0},{5,1},{6,2},{7,3},{8,12},{9,13},{10,... | collective-permute-start | bytes 294920 | tf_op jit(solution)/shard_map/ppermute | solution.py:32
  156.3 10.4 %collective-permute-start = (f32[32,768]{1,0:T(8,128)S(1)}, f32[32,768]{1,0:T(8,128)S(1)}, u32[]{:S(2)}, u32[]{:S(2)}) collective-permute-start(f32[32,768]{1,0:T(8,128)S(1)} %get-tuple-element.9), channel_id=1, source_target_pairs={{0,2},{1,3},{2,4},{3,5},{4,6},{5,7},{6,0},{7,1},{8,10},{9,11},{10,... | collective-permute-start | bytes 294920 | tf_op jit(solution)/shard_map/ppermute | solution.py:32
  166.8 6.9 %collective-permute-start.3 = (f32[16,768]{1,0:T(8,128)S(1)}, f32[16,768]{1,0:T(8,128)S(1)}, u32[]{:S(2)}, u32[]{:S(2)}) collective-permute-start(f32[16,768]{1,0:T(8,128)S(1)} %slice_select_fusion.1), channel_id=1, source_target_pairs={{0,1},{1,0},{2,3},{3,2},{4,5},{5,4},{6,7},{7,6},{8,9},{9,8},{10,11... | collective-permute-start | bytes 147464 | tf_op jit(solution)/shard_map/ppermute | solution.py:51
  169.7 8.0 %collective-permute-start.14 = (f32[48,768]{1,0:T(8,128)S(1)}, f32[48,768]{1,0:T(8,128)S(1)}, u32[]{:S(2)}, u32[]{:S(2)}) collective-permute-start(f32[48,768]{1,0:T(8,128)S(1)} %get-tuple-element.7), channel_id=1, source_target_pairs={{0,6},{1,7},{2,0},{3,1},{4,2},{5,3},{6,4},{7,5},{8,14},{9,15},{10,... | collective-permute-start | bytes 442376 | tf_op jit(solution)/shard_map/ppermute | solution.py:32
  172.2 7.8 %collective-permute-start.13 = (f32[48,768]{1,0:T(8,128)S(1)}, f32[48,768]{1,0:T(8,128)S(1)}, u32[]{:S(2)}, u32[]{:S(2)}) collective-permute-start(f32[48,768]{1,0:T(8,128)S(1)} %get-tuple-element.8), channel_id=1, source_target_pairs={{0,4},{1,5},{2,6},{3,7},{4,0},{5,1},{6,2},{7,3},{8,12},{9,13},{10,... | collective-permute-start | bytes 442376 | tf_op jit(solution)/shard_map/ppermute | solution.py:32
  173.7 7.8 %collective-permute-start.12 = (f32[48,768]{1,0:T(8,128)S(1)}, f32[48,768]{1,0:T(8,128)S(1)}, u32[]{:S(2)}, u32[]{:S(2)}) collective-permute-start(f32[48,768]{1,0:T(8,128)S(1)} %get-tuple-element.6), channel_id=1, source_target_pairs={{0,2},{1,3},{2,4},{3,5},{4,6},{5,7},{6,0},{7,1},{8,10},{9,11},{10,... | collective-permute-start | bytes 442376 | tf_op jit(solution)/shard_map/ppermute | solution.py:32
  173.7 8.6 %collective-permute-start.4 = (f32[16,768]{1,0:T(8,128)S(1)}, f32[16,768]{1,0:T(8,128)S(1)}, u32[]{:S(2)}, u32[]{:S(2)}) collective-permute-start(f32[16,768]{1,0:T(8,128)S(1)} %select_add_fusion.1), channel_id=1, source_target_pairs={{0,1},{1,0},{2,3},{3,2},{4,5},{5,4},{6,7},{7,6},{8,9},{9,8},{10,11... | collective-permute-start | bytes 147464 | tf_op jit(solution)/shard_map/ppermute | solution.py:52
  181.5 5.9 %collective-permute-start.15 = (f32[24,768]{1,0:T(8,128)S(1)}, f32[24,768]{1,0:T(8,128)S(1)}, u32[]{:S(2)}, u32[]{:S(2)}) collective-permute-start(f32[24,768]{1,0:T(8,128)S(1)} %slice_select_fusion), channel_id=1, source_target_pairs={{0,1},{1,0},{2,3},{3,2},{4,5},{5,4},{6,7},{7,6},{8,9},{9,8},{10,11... | collective-permute-start | bytes 221192 | tf_op jit(solution)/shard_map/ppermute | solution.py:51
  182.3 6.0 %collective-permute-start.5 = (f32[32,768]{1,0:T(8,128)S(1)}, f32[32,768]{1,0:T(8,128)S(1)}, u32[]{:S(2)}, u32[]{:S(2)}) collective-permute-start(f32[32,768]{1,0:T(8,128)S(1)} %maximum_select_fusion.3), channel_id=1, source_target_pairs={{0,6},{1,7},{2,0},{3,1},{4,2},{5,3},{6,4},{7,5},{8,14},{9,15},{10,... | collective-permute-start | bytes 294920 | tf_op jit(solution)/shard_map/ppermute | solution.py:32
  182.9 6.3 %collective-permute-start.6 = (f32[32,768]{1,0:T(8,128)S(1)}, f32[32,768]{1,0:T(8,128)S(1)}, u32[]{:S(2)}, u32[]{:S(2)}) collective-permute-start(f32[32,768]{1,0:T(8,128)S(1)} %maximum_select_fusion.3), channel_id=1, source_target_pairs={{0,4},{1,5},{2,6},{3,7},{4,0},{5,1},{6,2},{7,3},{8,12},{9,13},{10,... | collective-permute-start | bytes 294920 | tf_op jit(solution)/shard_map/ppermute | solution.py:32
  184.4 5.9 %collective-permute-start.7 = (f32[32,768]{1,0:T(8,128)S(1)}, f32[32,768]{1,0:T(8,128)S(1)}, u32[]{:S(2)}, u32[]{:S(2)}) collective-permute-start(f32[32,768]{1,0:T(8,128)S(1)} %maximum_select_fusion.3), channel_id=1, source_target_pairs={{0,2},{1,3},{2,4},{3,5},{4,6},{5,7},{6,0},{7,1},{8,10},{9,11},{10,... | collective-permute-start | bytes 294920 | tf_op jit(solution)/shard_map/ppermute | solution.py:32
  187.4 27.0 %collective-permute-start.16 = (f32[24,768]{1,0:T(8,128)S(1)}, f32[24,768]{1,0:T(8,128)S(1)}, u32[]{:S(2)}, u32[]{:S(2)}) collective-permute-start(f32[24,768]{1,0:T(8,128)S(1)} %select_add_fusion), channel_id=1, source_target_pairs={{0,1},{1,0},{2,3},{3,2},{4,5},{5,4},{6,7},{7,6},{8,9},{9,8},{10,11... | collective-permute-start | bytes 221192 | tf_op jit(solution)/shard_map/ppermute | solution.py:52
  190.4 31.1 %copy-start.1 = (f32[8192]{0:T(1024)S(1)}, f32[8192]{0:T(1024)}, u32[]{:S(2)}) copy-start(f32[8192]{0:T(1024)} %param.5) | copy-start | bytes 98308
  206.9 1.3 collective-permute-start.8
  208.2 3.9 %collective-permute-start.9 = (f32[8192]{0:T(1024)S(1)}, f32[8192]{0:T(1024)S(1)}, u32[]{:S(2)}, u32[]{:S(2)}) collective-permute-start(f32[8192]{0:T(1024)S(1)} %max.29), channel_id=1, source_target_pairs={{0,16},{8,24},{16,0},{24,8},{32,48},{40,56},{48,32},{56,40},{64,80... | collective-permute-start | bytes 98312 | tf_op jit(solution)/shard_map/ppermute | solution.py:61
  212.1 5.4 %collective-permute-start.10 = (f32[8192]{0:T(1024)S(1)}, f32[8192]{0:T(1024)S(1)}, u32[]{:S(2)}, u32[]{:S(2)}) collective-permute-start(f32[8192]{0:T(1024)S(1)} %max.30), channel_id=1, source_target_pairs={{0,32},{8,40},{16,48},{24,56},{32,0},{40,8},{48,16},{56,24},{64,96... | collective-permute-start | bytes 98312 | tf_op jit(solution)/shard_map/ppermute | solution.py:61
  214.4 7.1 %collective-permute-start.17 = (f32[48,768]{1,0:T(8,128)S(1)}, f32[48,768]{1,0:T(8,128)S(1)}, u32[]{:S(2)}, u32[]{:S(2)}) collective-permute-start(f32[48,768]{1,0:T(8,128)S(1)} %maximum_select_fusion.1), channel_id=1, source_target_pairs={{0,6},{1,7},{2,0},{3,1},{4,2},{5,3},{6,4},{7,5},{8,14},{9,15},{10,... | collective-permute-start | bytes 442376 | tf_op jit(solution)/shard_map/ppermute | solution.py:32
  215.9 7.4 %collective-permute-start.18 = (f32[48,768]{1,0:T(8,128)S(1)}, f32[48,768]{1,0:T(8,128)S(1)}, u32[]{:S(2)}, u32[]{:S(2)}) collective-permute-start(f32[48,768]{1,0:T(8,128)S(1)} %maximum_select_fusion.1), channel_id=1, source_target_pairs={{0,4},{1,5},{2,6},{3,7},{4,0},{5,1},{6,2},{7,3},{8,12},{9,13},{10,... | collective-permute-start | bytes 442376 | tf_op jit(solution)/shard_map/ppermute | solution.py:32
  216.8 7.9 %collective-permute-start.19 = (f32[48,768]{1,0:T(8,128)S(1)}, f32[48,768]{1,0:T(8,128)S(1)}, u32[]{:S(2)}, u32[]{:S(2)}) collective-permute-start(f32[48,768]{1,0:T(8,128)S(1)} %maximum_select_fusion.1), channel_id=1, source_target_pairs={{0,2},{1,3},{2,4},{3,5},{4,6},{5,7},{6,0},{7,1},{8,10},{9,11},{10,... | collective-permute-start | bytes 442376 | tf_op jit(solution)/shard_map/ppermute | solution.py:32
  217.5 4.0 %collective-permute-start.11 = (f32[8192]{0:T(1024)S(1)}, f32[8192]{0:T(1024)S(1)}, u32[]{:S(2)}, u32[]{:S(2)}) collective-permute-start(f32[8192]{0:T(1024)S(1)} %max.31), channel_id=1, source_target_pairs={{0,64},{8,72},{16,80},{24,88},{32,96},{40,104},{48,112},{56,120},{... | collective-permute-start | bytes 98312 | tf_op jit(solution)/shard_map/ppermute | solution.py:61
  221.5 20.8 %copy-start = (f32[8192]{0:T(1024)}, f32[8192]{0:T(1024)S(1)}, u32[]{:S(2)}) copy-start(f32[8192]{0:T(1024)S(1)} %maximum_maximum_fusion) | copy-start | bytes 98308
  243.2 5.1 %collective-permute-start.20 = (f32[1,192]{1,0:T(1,128)S(1)}, f32[1,192]{1,0:T(1,128)S(1)}, u32[]{:S(2)}, u32[]{:S(2)}) collective-permute-start(f32[1,192]{1,0:T(1,128)S(1)} %bitcast.39), channel_id=1, source_target_pairs={{0,1},{1,0},{2,3},{3,2},{4,5},{5,4},{6,7},{7,6},{8,9},{9,8},{10,11... | collective-permute-start | bytes 2312 | tf_op jit(solution)/shard_map/ppermute | solution.py:71
  248.3 3.7 %collective-permute-start.21 = (f32[2,192]{1,0:T(2,128)S(1)}, f32[2,192]{1,0:T(2,128)S(1)}, u32[]{:S(2)}, u32[]{:S(2)}) collective-permute-start(f32[2,192]{1,0:T(2,128)S(1)} %maximum_select_fusion.6), channel_id=1, source_target_pairs={{0,2},{1,3},{2,0},{3,1},{4,6},{5,7},{6,4},{7,5},{8,10},{9,11},{10,... | collective-permute-start | bytes 4616 | tf_op jit(solution)/shard_map/ppermute | solution.py:71
  252.0 5.2 %collective-permute-start.22 = (f32[4,192]{1,0:T(4,128)S(1)}, f32[4,192]{1,0:T(4,128)S(1)}, u32[]{:S(2)}, u32[]{:S(2)}) collective-permute-start(f32[4,192]{1,0:T(4,128)S(1)} %maximum_select_fusion.5), channel_id=1, source_target_pairs={{0,4},{1,5},{2,6},{3,7},{4,0},{5,1},{6,2},{7,3},{8,12},{9,13},{10,... | collective-permute-start | bytes 9224 | tf_op jit(solution)/shard_map/ppermute | solution.py:71
Sparse Core Ops, SparseCore 0:
  9.7 133.6 all-gather.1

commit v8 on v7

v8 whole, which is shorter than its diff:
```python
import jax
import jax.numpy as jnp
from jax import lax
from jax.sharding import Mesh
from jax.sharding import PartitionSpec as P

N_Y, N_Z = 4, 2


def similar(left, right):
    return lax.dot_general(
        left,
        right,
        (((1,), (1,)), ((), ())),
        precision=lax.Precision.HIGH,
        preferred_element_type=jnp.float32,
    )


def lookup(source, indices, first_row):
    position = indices - first_row
    inside = (position >= 0) & (position < source.shape[0])
    picked = jnp.take(source, jnp.clip(position, 0, source.shape[0] - 1), axis=0)
    return jnp.where(inside[:, None], picked, 0.0)


def col_of(y, z):
    return (y % N_Y) * N_Z + z


def y_shift(value, step):
    pairs = [(col_of(y, z), col_of(y + step, z)) for y in range(N_Y) for z in range(N_Z)]
    return lax.ppermute(value, "col", pairs)


def pair_split(value, low):
    halves = value.reshape(2, value.shape[0] // 2, *value.shape[1:])
    return jnp.where(low, halves[0], halves[1]), jnp.where(low, halves[1], halves[0])


def pair_join(mine, other, low):
    return jnp.where(low, jnp.concatenate([mine, other]), jnp.concatenate([other, mine]))


def group_masked_sum(value):
    here = lax.axis_index("col")
    y, z = here // N_Z, here % N_Z
    zl = lax.axis_index("zl")
    quarter = value.shape[0] // N_Y

    def part(k):
        return lax.dynamic_slice_in_dim(value, ((y + k) % N_Y) * quarter, quarter)

    own = part(0)
    for k in range(1, N_Y):
        own = own + y_shift(part(k), k)
    zl_swap = [(0, 1), (1, 0)]
    z_swap = [(c, c ^ 1) for c in range(N_Y * N_Z)]
    mine, theirs = pair_split(own, zl == 0)
    mine = mine + lax.ppermute(theirs, "zl", zl_swap)
    low, high = pair_split(mine, z == 0)
    low = low + lax.ppermute(high, "col", z_swap)
    mine = pair_join(low, lax.ppermute(low, "col", z_swap), z == 0)
    own = pair_join(mine, lax.ppermute(mine, "zl", zl_swap), zl == 0)
    pieces = [own] + [y_shift(own, -k) for k in range(1, N_Y)]
    return jnp.roll(jnp.stack(pieces), y, axis=0).reshape(value.shape)


def all_max(value, axis, n):
    bit = 1
    while bit < n:
        value = jnp.maximum(value, lax.ppermute(value, axis, [(i, i ^ bit) for i in range(n)]))
        bit *= 2
    return value


def gather_in_order(parts, axis, n):
    here = lax.axis_index(axis)
    bit = 1
    while bit < n:
        other = lax.ppermute(parts, axis, [(i, i ^ bit) for i in range(n)])
        low = (here & bit) == 0
        parts = jnp.where(low, jnp.concatenate([parts, other]), jnp.concatenate([other, parts]))
        bit *= 2
    return parts


def body(slab_embed, coverage_old, sel_index, cand_index):
    n_xc = 8
    col_id = lax.axis_index("col")
    zl = lax.axis_index("zl")
    half = lax.all_gather(slab_embed, "xc", axis=0, tiled=True)
    first_row = (col_id * 2 + zl) * half.shape[0]
    zl_swap = [(0, 1), (1, 0)]
    both_sel = pair_join(sel_index, lax.ppermute(sel_index, "zl", zl_swap), zl == 0)
    both_cand = pair_join(cand_index, lax.ppermute(cand_index, "zl", zl_swap), zl == 0)
    selected = group_masked_sum(lookup(half, both_sel, first_row))
    chosen = group_masked_sum(lookup(half, both_cand, first_row))
    reached = all_max(jnp.max(similar(selected, half), axis=0), "xc", n_xc)
    old = lax.dynamic_slice_in_dim(coverage_old, zl * half.shape[0], half.shape[0])
    coverage = jnp.maximum(old, reached)
    scores = lax.optimization_barrier(similar(chosen, half))
    gain_part = jnp.sum(jnp.maximum(scores - coverage[None, :], 0.0), axis=1)
    parts = gather_in_order(gather_in_order(gain_part[None], "zl", 2)[None], "col", N_Y * N_Z)
    total = jnp.sum(parts.reshape(-1, gain_part.shape[0]), axis=0)
    total_gain = lax.dynamic_slice_in_dim(total, zl * cand_index.shape[0], cand_index.shape[0])
    full_coverage = pair_join(coverage, lax.ppermute(coverage, "zl", zl_swap), zl == 0)
    return (full_coverage, total_gain)


def solution(mesh):
    shape = dict(zip(mesh.axis_names, mesh.devices.shape))
    names, sizes = [], []
    for name in mesh.axis_names:
        if name == "row":
            names += ["zl", "xc"]
            sizes += [2, shape["row"] // 2]
        else:
            names.append(name)
            sizes.append(shape[name])
    split = Mesh(mesh.devices.reshape(sizes), tuple(names))
    in_specs = (P(("col", "zl", "xc"), None), P("col"), P(("zl", "xc")), P(("zl", "xc")))
    out_specs = (P("col"), P(("zl", "xc")))
    return jax.shard_map(body, mesh=split, in_specs=in_specs, out_specs=out_specs, check_vma=False)
```

time: 265 us -> 221 us (0.83)
  waiting for transfers between devices: 165 us -> 128 us
  matrix products: 33.9 us -> 28.1 us
  local copies, waits for them, and re-layouts: 18.8 us -> 14.2 us
  starting transfers between devices: 30.2 us -> 33.7 us
    all_gather x1, waiting for transfers between devices: 135 us -> 65.7 us  [body(): half = lax.all_gather(slab_embed, 'xc', axis=0, tiled=True)]
    ppermute x7 -> x15, waiting for transfers between devices: 11.8 us -> 30.7 us  [the longest x4 11.7 us: gather_in_order(): other = lax.ppermute(parts, axis, [(i, i ^ bit) for i in range(n)])]
    ppermute x12, waiting for transfers between devices: 11.2 us -> 26.3 us  [y_shift(): return lax.ppermute(value, 'col', pairs)]
    ppermute x7 -> x15, starting transfers between devices: 10.5 us -> 18.9 us  [the longest x4 4.41 us: gather_in_order(): other = lax.ppermute(parts, axis, [(i, i ^ bit) for i in range(n)])]
    dot_general x2, matrix products: 33.9 us -> 28.1 us  [similar(): lax.dot_general(left, right, (((1,), (1,)), ((), ())), precision=lax.Prec...]
    gather x2, local copies, waits for them, and re-layouts: 18.5 us -> 13 us  [lookup(): jnp.take(source, jnp.clip(position, 0, source.shape[0] - 1), axis=0)]
    ppermute x12, starting transfers between devices: 14.5 us -> 11.7 us  [y_shift(): return lax.ppermute(value, 'col', pairs)]
    ppermute x4 -> x3, waiting for transfers between devices: 6.34 us -> 4.52 us  [all_max(): lax.ppermute(value, axis, [(i, i ^ bit) for i in range(n)])]
  transfers between devices with their start and end apart: 24 -> 31, of which waited for: 15 -> 24; matrix products, arithmetic and copies ran while one was open for 10% -> 12% of each run, Pallas kernels for 0% -> 0%
where the time goes in v8:
time: 221 us
  waiting for transfers between devices  128 us (58%)
  starting transfers between devices  33.7 us (15%)
  matrix products  28.1 us (13%)
  between operations  14.4 us (7%)
  local copies, waits for them, and re-layouts  14.2 us (6%)
  other arithmetic  2.41 us (1%)
    all_gather x1, waiting for transfers between devices, body(): half = lax.all_gather(slab_embed, 'xc', axis=0, tiled=True)  65.7 us
    dot_general x2, matrix products, similar(): lax.dot_general(left, right, (((1,), (1,)), ((), ())), precision=lax.Prec...  28.1 us
    ppermute x12, waiting for transfers between devices, y_shift(): return lax.ppermute(value, 'col', pairs)  26.3 us
    gather x2, local copies, waits for them, and re-layouts, lookup(): jnp.take(source, jnp.clip(position, 0, source.shape[0] - 1), axis=0)  13 us
    ppermute x4, waiting for transfers between devices, gather_in_order(): other = lax.ppermute(parts, axis, [(i, i ^ bit) for i in range(n)])  11.7 us
    ppermute x12, starting transfers between devices, y_shift(): return lax.ppermute(value, 'col', pairs)  11.7 us
    ppermute x2, waiting for transfers between devices, group_masked_sum(): mine = pair_join(low, lax.ppermute(low, 'col', z_swap), z == 0)  8.6 us
    ppermute x3, waiting for transfers between devices, all_max(): lax.ppermute(value, axis, [(i, i ^ bit) for i in range(n)])  4.52 us
  transfers between devices with their start and end apart: 31, of which 24 were waited for; matrix products, arithmetic and copies ran while one was open for 12% of the time, Pallas kernels for 0%

profile of v8, /device:TPU:0, one launch (start us, length us, event | category | flops | bytes accessed | tf_op | source)
XLA Modules:
  0.0 220.7 jit_solution(16375864051123156292)
XLA Ops:
  7.9 2.1 collective-permute-start
  11.6 2.0 collective-permute-done.15
  13.8 65.7 %all-gather.2.cloned.1.call-done = f32[4096,768]{1,0:T(8,128)} async-done(((f32[512,768]{1,0:T(8,128)}), f32[4096,768]{1,0:T(8,128)}) %all-gather.2.cloned.1.call-update) | async-done | bytes 12582928 | tf_op jit(solution)/shard_map/all_gather | solution.py:92
  79.5 6.0 %gather_fusion = f32[256,768]{1,0:T(8,128)S(1)} fusion(f32[4096,768]{1,0:T(8,128)} %all-gather.2.cloned.1.call-done, s32[1024]{0:T(1024)S(1)} %pad_clamp_fusion.1), kind=kCustom, calls=%fused_computation | custom fusion | bytes 1573888 | tf_op jit(solution)/shard_map/jit(_take)/gather | solution.py:23
  85.7 2.8 %collective-permute-start.3 = (f32[64,768]{1,0:T(8,128)S(1)}, f32[64,768]{1,0:T(8,128)S(1)}, u32[]{:S(2)}, u32[]{:S(2)}) collective-permute-start(f32[64,768]{1,0:T(8,128)S(1)} %get-tuple-element.8), channel_id=1, source_target_pairs={{0,6},{1,7},{2,0},{3,1},{4,2},{5,3},{6,4},{7,5},{8,14},{9,15},{10,... | collective-permute-start | bytes 589832 | tf_op jit(solution)/shard_map/ppermute | solution.py:33
  90.2 7.1 %gather_fusion.1 = f32[384,768]{1,0:T(8,128)S(1)} fusion(f32[4096,768]{1,0:T(8,128)} %all-gather.2.cloned.1.call-done, s32[1024]{0:T(1024)S(1)} %pad_clamp_fusion), kind=kCustom, calls=%fused_computation.1 | custom fusion | bytes 2360832 | tf_op jit(solution)/shard_map/jit(_take)/gather | solution.py:23
  97.8 3.2 %collective-permute-done.1 = f32[64,768]{1,0:T(8,128)S(1)} collective-permute-done((f32[64,768]{1,0:T(8,128)S(1)}, f32[64,768]{1,0:T(8,128)S(1)}, u32[]{:S(2)}, u32[]{:S(2)}) %collective-permute-start.1) | collective-permute-done | bytes 196640 | tf_op jit(solution)/shard_map/ppermute | solution.py:33
  101.1 1.6 collective-permute-start.4
  105.9 3.2 %collective-permute-start.5 = (f32[16,768]{1,0:T(8,128)S(1)}, f32[16,768]{1,0:T(8,128)S(1)}, u32[]{:S(2)}, u32[]{:S(2)}) collective-permute-start(f32[16,768]{1,0:T(8,128)S(1)} %slice_select_fusion.3), channel_id=1, source_target_pairs={{0,1},{1,0},{2,3},{3,2},{4,5},{5,4},{6,7},{7,6},{8,9},{9,8},{10,11... | collective-permute-start | bytes 147464 | tf_op jit(solution)/shard_map/ppermute | solution.py:62
  109.2 3.6 %collective-permute-done.18 = f32[96,768]{1,0:T(8,128)S(1)} collective-permute-done((f32[96,768]{1,0:T(8,128)S(1)}, f32[96,768]{1,0:T(8,128)S(1)}, u32[]{:S(2)}, u32[]{:S(2)}) %collective-permute-start.18) | collective-permute-done | bytes 294944 | tf_op jit(solution)/shard_map/ppermute | solution.py:33
  112.8 2.2 collective-permute-done.17
  115.0 4.5 %collective-permute-done.16 = f32[96,768]{1,0:T(8,128)S(1)} collective-permute-done((f32[96,768]{1,0:T(8,128)S(1)}, f32[96,768]{1,0:T(8,128)S(1)}, u32[]{:S(2)}, u32[]{:S(2)}) %collective-permute-start.16) | collective-permute-done | bytes 294944 | tf_op jit(solution)/shard_map/ppermute | solution.py:33
  119.5 2.9 %collective-permute-start.6 = (f32[16,768]{1,0:T(8,128)S(1)}, f32[16,768]{1,0:T(8,128)S(1)}, u32[]{:S(2)}, u32[]{:S(2)}) collective-permute-start(f32[16,768]{1,0:T(8,128)S(1)} %select_add_fusion.3), channel_id=1, source_target_pairs={{0,1},{1,0},{2,3},{3,2},{4,5},{5,4},{6,7},{7,6},{8,9},{9,8},{10,11... | collective-permute-start | bytes 147464 | tf_op jit(solution)/shard_map/ppermute | solution.py:63
  122.7 3.0 %collective-permute-done.6 = f32[16,768]{1,0:T(8,128)S(1)} collective-permute-done((f32[16,768]{1,0:T(8,128)S(1)}, f32[16,768]{1,0:T(8,128)S(1)}, u32[]{:S(2)}, u32[]{:S(2)}) %collective-permute-start.6) | collective-permute-done | bytes 49184 | tf_op jit(solution)/shard_map/ppermute | solution.py:63
  126.3 2.8 %collective-permute-done.19 = f32[48,768]{1,0:T(8,128)S(1)} collective-permute-done((f32[48,768]{1,0:T(8,128)S(1)}, f32[48,768]{1,0:T(8,128)S(1)}, u32[]{:S(2)}, u32[]{:S(2)}) %collective-permute-start.19) | collective-permute-done | bytes 147488 | tf_op jit(solution)/shard_map/ppermute | solution.py:60
  129.4 1.8 collective-permute-done.7
  133.5 1.6 collective-permute-done.20
  135.7 5.6 %collective-permute-done.21 = f32[24,768]{1,0:T(8,128)S(1)} collective-permute-done((f32[24,768]{1,0:T(8,128)S(1)}, f32[24,768]{1,0:T(8,128)S(1)}, u32[]{:S(2)}, u32[]{:S(2)}) %collective-permute-start.21) | collective-permute-done | bytes 73760 | tf_op jit(solution)/shard_map/ppermute | solution.py:63
  141.4 1.9 collective-permute-start.22
  143.5 17.2 %convolution_reduce_fusion = f32[4096]{0:T(1024)S(1)} fusion(f32[256,768]{1,0:T(8,128)S(1)} %bitcast.35, f32[4096,768]{1,0:T(8,128)} %all-gather.2.cloned.1.call-done), kind=kOutput, calls=%fused_computation.3 | convolution fusion | flops 4832882688 | bytes 13385728 | tf_op jit(solution)/shard_map/dot_general | solution.py:11
  162.9 2.8 %collective-permute-done.12 = f32[4096]{0:T(1024)S(1)} collective-permute-done((f32[4096]{0:T(1024)S(1)}, f32[4096]{0:T(1024)S(1)}, u32[]{:S(2)}, u32[]{:S(2)}) %collective-permute-start.12) | collective-permute-done | bytes 16416 | tf_op jit(solution)/shard_map/ppermute | solution.py:72
  165.7 2.1 collective-permute-start.13
  168.0 1.5 collective-permute-start.24
  171.0 6.9 %collective-permute-done.23 = f32[96,768]{1,0:T(8,128)S(1)} collective-permute-done((f32[96,768]{1,0:T(8,128)S(1)}, f32[96,768]{1,0:T(8,128)S(1)}, u32[]{:S(2)}, u32[]{:S(2)}) %collective-permute-start.23) | collective-permute-done | bytes 294944 | tf_op jit(solution)/shard_map/ppermute | solution.py:33
  177.9 1.6 collective-permute-done.24
  179.6 4.0 %collective-permute-done.25 = f32[96,768]{1,0:T(8,128)S(1)} collective-permute-done((f32[96,768]{1,0:T(8,128)S(1)}, f32[96,768]{1,0:T(8,128)S(1)}, u32[]{:S(2)}, u32[]{:S(2)}) %collective-permute-start.25) | collective-permute-done | bytes 294944 | tf_op jit(solution)/shard_map/ppermute | solution.py:33
  183.8 10.8 %fusion.13 = f32[384,4096]{1,0:T(8,128)S(1)} fusion(f32[384,768]{1,0:T(8,128)S(1)} %bitcast.34, f32[4096,768]{1,0:T(8,128)} %all-gather.2.cloned.1.call-done), kind=kOutput, calls=%fused_computation.74 | convolution fusion | flops 7247757312 | bytes 20054016 | tf_op jit(solution)/shard_map/dot_general | solution.py:11
  196.4 2.6 %collective-permute-done.26 = f32[1,384]{1,0:T(1,128)S(1)} collective-permute-done((f32[1,384]{1,0:T(1,128)S(1)}, f32[1,384]{1,0:T(1,128)S(1)}, u32[]{:S(2)}, u32[]{:S(2)}) %collective-permute-start.26) | collective-permute-done | bytes 1568 | tf_op jit(solution)/shard_map/ppermute | solution.py:81
  199.0 2.1 collective-permute-start.27
  201.1 3.0 %collective-permute-done.27 = f32[1,2,384]{2,0,1:T(1,128)S(1)} collective-permute-done((f32[1,2,384]{2,0,1:T(1,128)S(1)}, f32[1,2,384]{2,0,1:T(1,128)S(1)}, u32[]{:S(2)}, u32[]{:S(2)}) %collective-permute-start.27) | collective-permute-done | bytes 3104 | tf_op jit(solution)/shard_map/ppermute | solution.py:81
  205.3 2.6 %collective-permute-done.28 = f32[2,2,384]{2,0,1:T(2,128)S(1)} collective-permute-done((f32[2,2,384]{2,0,1:T(2,128)S(1)}, f32[2,2,384]{2,0,1:T(2,128)S(1)}, u32[]{:S(2)}, u32[]{:S(2)}) %collective-permute-start.28) | collective-permute-done | bytes 6176 | tf_op jit(solution)/shard_map/ppermute | solution.py:81
  209.8 3.4 %collective-permute-done.29 = f32[4,2,384]{2,0,1:T(4,128)S(1)} collective-permute-done((f32[4,2,384]{2,0,1:T(4,128)S(1)}, f32[4,2,384]{2,0,1:T(4,128)S(1)}, u32[]{:S(2)}, u32[]{:S(2)}) %collective-permute-start.29) | collective-permute-done | bytes 12320 | tf_op jit(solution)/shard_map/ppermute | solution.py:81
  (96 shorter events, 21.9 us)
Async XLA Ops:
  7.2 72.3 %all-gather.2.cloned.1.call-start = ((), (), s32[]{:S(2)}) async-start(), calls=%async_computation | async-start | bytes 14155776 | tf_op jit(solution)/shard_map/all_gather | solution.py:92
  7.9 3.6 %collective-permute-start = (s32[128]{0:T(128)S(1)}, s32[128]{0:T(128)S(1)}, u32[]{:S(2)}, u32[]{:S(2)}) collective-permute-start(s32[128]{0:T(128)S(1)} %copy-done.2), channel_id=1, source_target_pairs={{0,64},{64,0},{1,65},{65,1},{2,66},{66,2},{3,67},{67,3},{4,68},{68... | collective-permute-start | bytes 1544 | tf_op jit(solution)/shard_map/ppermute | solution.py:95
  10.0 3.6 %collective-permute-start.15 = (s32[192]{0:T(256)S(1)}, s32[192]{0:T(256)S(1)}, u32[]{:S(2)}, u32[]{:S(2)}) collective-permute-start(s32[192]{0:T(256)S(1)} %copy-done.1), channel_id=1, source_target_pairs={{0,64},{64,0},{1,65},{65,1},{2,66},{66,2},{3,67},{67,3},{4,68},{68... | collective-permute-start | bytes 2312 | tf_op jit(solution)/shard_map/ppermute | solution.py:96
  85.7 11.8 %collective-permute-start.3 = (f32[64,768]{1,0:T(8,128)S(1)}, f32[64,768]{1,0:T(8,128)S(1)}, u32[]{:S(2)}, u32[]{:S(2)}) collective-permute-start(f32[64,768]{1,0:T(8,128)S(1)} %get-tuple-element.8), channel_id=1, source_target_pairs={{0,6},{1,7},{2,0},{3,1},{4,2},{5,3},{6,4},{7,5},{8,14},{9,15},{10,... | collective-permute-start | bytes 589832 | tf_op jit(solution)/shard_map/ppermute | solution.py:33
  88.5 9.3 %collective-permute-start.2 = (f32[64,768]{1,0:T(8,128)S(1)}, f32[64,768]{1,0:T(8,128)S(1)}, u32[]{:S(2)}, u32[]{:S(2)}) collective-permute-start(f32[64,768]{1,0:T(8,128)S(1)} %get-tuple-element.9), channel_id=1, source_target_pairs={{0,4},{1,5},{2,6},{3,7},{4,0},{5,1},{6,2},{7,3},{8,12},{9,13},{10,... | collective-permute-start | bytes 589832 | tf_op jit(solution)/shard_map/ppermute | solution.py:33
  89.3 11.7 %collective-permute-start.1 = (f32[64,768]{1,0:T(8,128)S(1)}, f32[64,768]{1,0:T(8,128)S(1)}, u32[]{:S(2)}, u32[]{:S(2)}) collective-permute-start(f32[64,768]{1,0:T(8,128)S(1)} %get-tuple-element.7), channel_id=1, source_target_pairs={{0,2},{1,3},{2,4},{3,5},{4,6},{5,7},{6,0},{7,1},{8,10},{9,11},{10,... | collective-permute-start | bytes 589832 | tf_op jit(solution)/shard_map/ppermute | solution.py:33
  101.1 4.8 %collective-permute-start.4 = (f32[32,768]{1,0:T(8,128)S(1)}, f32[32,768]{1,0:T(8,128)S(1)}, u32[]{:S(2)}, u32[]{:S(2)}) collective-permute-start(f32[32,768]{1,0:T(8,128)S(1)} %slice_select_fusion.1), channel_id=1, source_target_pairs={{0,64},{64,0},{1,65},{65,1},{2,66},{66,2},{3,67},{67,3},{4,68},{68... | collective-permute-start | bytes 294920 | tf_op jit(solution)/shard_map/ppermute | solution.py:60
  102.8 10.0 %collective-permute-start.18 = (f32[96,768]{1,0:T(8,128)S(1)}, f32[96,768]{1,0:T(8,128)S(1)}, u32[]{:S(2)}, u32[]{:S(2)}) collective-permute-start(f32[96,768]{1,0:T(8,128)S(1)} %get-tuple-element.5), channel_id=1, source_target_pairs={{0,6},{1,7},{2,0},{3,1},{4,2},{5,3},{6,4},{7,5},{8,14},{9,15},{10,... | collective-permute-start | bytes 884744 | tf_op jit(solution)/shard_map/ppermute | solution.py:33
  103.5 11.5 %collective-permute-start.17 = (f32[96,768]{1,0:T(8,128)S(1)}, f32[96,768]{1,0:T(8,128)S(1)}, u32[]{:S(2)}, u32[]{:S(2)}) collective-permute-start(f32[96,768]{1,0:T(8,128)S(1)} %get-tuple-element.6), channel_id=1, source_target_pairs={{0,4},{1,5},{2,6},{3,7},{4,0},{5,1},{6,2},{7,3},{8,12},{9,13},{10,... | collective-permute-start | bytes 884744 | tf_op jit(solution)/shard_map/ppermute | solution.py:33
  104.3 15.1 %collective-permute-start.16 = (f32[96,768]{1,0:T(8,128)S(1)}, f32[96,768]{1,0:T(8,128)S(1)}, u32[]{:S(2)}, u32[]{:S(2)}) collective-permute-start(f32[96,768]{1,0:T(8,128)S(1)} %get-tuple-element.4), channel_id=1, source_target_pairs={{0,2},{1,3},{2,4},{3,5},{4,6},{5,7},{6,0},{7,1},{8,10},{9,11},{10,... | collective-permute-start | bytes 884744 | tf_op jit(solution)/shard_map/ppermute | solution.py:33
  105.9 13.6 %collective-permute-start.5 = (f32[16,768]{1,0:T(8,128)S(1)}, f32[16,768]{1,0:T(8,128)S(1)}, u32[]{:S(2)}, u32[]{:S(2)}) collective-permute-start(f32[16,768]{1,0:T(8,128)S(1)} %slice_select_fusion.3), channel_id=1, source_target_pairs={{0,1},{1,0},{2,3},{3,2},{4,5},{5,4},{6,7},{7,6},{8,9},{9,8},{10,11... | collective-permute-start | bytes 147464 | tf_op jit(solution)/shard_map/ppermute | solution.py:62
  119.5 6.2 %collective-permute-start.6 = (f32[16,768]{1,0:T(8,128)S(1)}, f32[16,768]{1,0:T(8,128)S(1)}, u32[]{:S(2)}, u32[]{:S(2)}) collective-permute-start(f32[16,768]{1,0:T(8,128)S(1)} %select_add_fusion.3), channel_id=1, source_target_pairs={{0,1},{1,0},{2,3},{3,2},{4,5},{5,4},{6,7},{7,6},{8,9},{9,8},{10,11... | collective-permute-start | bytes 147464 | tf_op jit(solution)/shard_map/ppermute | solution.py:63
  122.5 6.6 %collective-permute-start.19 = (f32[48,768]{1,0:T(8,128)S(1)}, f32[48,768]{1,0:T(8,128)S(1)}, u32[]{:S(2)}, u32[]{:S(2)}) collective-permute-start(f32[48,768]{1,0:T(8,128)S(1)} %slice_select_fusion), channel_id=1, source_target_pairs={{0,64},{64,0},{1,65},{65,1},{2,66},{66,2},{3,67},{67,3},{4,68},{68... | collective-permute-start | bytes 442376 | tf_op jit(solution)/shard_map/ppermute | solution.py:60
  125.8 5.4 %collective-permute-start.7 = (f32[32,768]{1,0:T(8,128)S(1)}, f32[32,768]{1,0:T(8,128)S(1)}, u32[]{:S(2)}, u32[]{:S(2)}) collective-permute-start(f32[32,768]{1,0:T(8,128)S(1)} %maximum_select_fusion.5), channel_id=1, source_target_pairs={{0,64},{64,0},{1,65},{65,1},{2,66},{66,2},{3,67},{67,3},{4,68},{68... | collective-permute-start | bytes 294920 | tf_op jit(solution)/shard_map/ppermute | solution.py:64
  129.2 5.9 %collective-permute-start.20 = (f32[24,768]{1,0:T(8,128)S(1)}, f32[24,768]{1,0:T(8,128)S(1)}, u32[]{:S(2)}, u32[]{:S(2)}) collective-permute-start(f32[24,768]{1,0:T(8,128)S(1)} %slice_select_fusion.2), channel_id=1, source_target_pairs={{0,1},{1,0},{2,3},{3,2},{4,5},{5,4},{6,7},{7,6},{8,9},{9,8},{10,11... | collective-permute-start | bytes 221192 | tf_op jit(solution)/shard_map/ppermute | solution.py:62
  131.2 12.0 %collective-permute-start.8 = (f32[64,768]{1,0:T(8,128)S(1)}, f32[64,768]{1,0:T(8,128)S(1)}, u32[]{:S(2)}, u32[]{:S(2)}) collective-permute-start(f32[64,768]{1,0:T(8,128)S(1)} %maximum_select_fusion.3), channel_id=1, source_target_pairs={{0,6},{1,7},{2,0},{3,1},{4,2},{5,3},{6,4},{7,5},{8,14},{9,15},{10,... | collective-permute-start | bytes 589832 | tf_op jit(solution)/shard_map/ppermute | solution.py:33
  131.5 11.7 %collective-permute-start.9 = (f32[64,768]{1,0:T(8,128)S(1)}, f32[64,768]{1,0:T(8,128)S(1)}, u32[]{:S(2)}, u32[]{:S(2)}) collective-permute-start(f32[64,768]{1,0:T(8,128)S(1)} %maximum_select_fusion.3), channel_id=1, source_target_pairs={{0,4},{1,5},{2,6},{3,7},{4,0},{5,1},{6,2},{7,3},{8,12},{9,13},{10,... | collective-permute-start | bytes 589832 | tf_op jit(solution)/shard_map/ppermute | solution.py:33
  132.2 11.1 %collective-permute-start.10 = (f32[64,768]{1,0:T(8,128)S(1)}, f32[64,768]{1,0:T(8,128)S(1)}, u32[]{:S(2)}, u32[]{:S(2)}) collective-permute-start(f32[64,768]{1,0:T(8,128)S(1)} %maximum_select_fusion.3), channel_id=1, source_target_pairs={{0,2},{1,3},{2,4},{3,5},{4,6},{5,7},{6,0},{7,1},{8,10},{9,11},{10,... | collective-permute-start | bytes 589832 | tf_op jit(solution)/shard_map/ppermute | solution.py:33
  135.1 6.2 %collective-permute-start.21 = (f32[24,768]{1,0:T(8,128)S(1)}, f32[24,768]{1,0:T(8,128)S(1)}, u32[]{:S(2)}, u32[]{:S(2)}) collective-permute-start(f32[24,768]{1,0:T(8,128)S(1)} %select_add_fusion.2), channel_id=1, source_target_pairs={{0,1},{1,0},{2,3},{3,2},{4,5},{5,4},{6,7},{7,6},{8,9},{9,8},{10,11... | collective-permute-start | bytes 221192 | tf_op jit(solution)/shard_map/ppermute | solution.py:63
  141.4 26.5 %collective-permute-start.22 = (f32[48,768]{1,0:T(8,128)S(1)}, f32[48,768]{1,0:T(8,128)S(1)}, u32[]{:S(2)}, u32[]{:S(2)}) collective-permute-start(f32[48,768]{1,0:T(8,128)S(1)} %maximum_select_fusion.4), channel_id=1, source_target_pairs={{0,64},{64,0},{1,65},{65,1},{2,66},{66,2},{3,67},{67,3},{4,68},{68... | collective-permute-start | bytes 442376 | tf_op jit(solution)/shard_map/ppermute | solution.py:64
  143.5 27.5 %copy-start = (f32[8192]{0:T(1024)S(1)}, f32[8192]{0:T(1024)}, u32[]{:S(2)}) copy-start(f32[8192]{0:T(1024)} %param.5) | copy-start | bytes 98308
  160.7 1.3 collective-permute-start.11
  162.0 3.7 %collective-permute-start.12 = (f32[4096]{0:T(1024)S(1)}, f32[4096]{0:T(1024)S(1)}, u32[]{:S(2)}, u32[]{:S(2)}) collective-permute-start(f32[4096]{0:T(1024)S(1)} %max.26), channel_id=1, source_target_pairs={{0,16},{8,24},{16,0},{24,8},{32,48},{40,56},{48,32},{56,40},{1,17}... | collective-permute-start | bytes 49160 | tf_op jit(solution)/shard_map/ppermute | solution.py:72
  165.7 5.2 %collective-permute-start.13 = (f32[4096]{0:T(1024)S(1)}, f32[4096]{0:T(1024)S(1)}, u32[]{:S(2)}, u32[]{:S(2)}) collective-permute-start(f32[4096]{0:T(1024)S(1)} %max.27), channel_id=1, source_target_pairs={{0,32},{8,40},{16,48},{24,56},{32,0},{40,8},{48,16},{56,24},{1,33}... | collective-permute-start | bytes 49160 | tf_op jit(solution)/shard_map/ppermute | solution.py:72
  167.9 10.0 %collective-permute-start.23 = (f32[96,768]{1,0:T(8,128)S(1)}, f32[96,768]{1,0:T(8,128)S(1)}, u32[]{:S(2)}, u32[]{:S(2)}) collective-permute-start(f32[96,768]{1,0:T(8,128)S(1)} %maximum_select_fusion.1), channel_id=1, source_target_pairs={{0,6},{1,7},{2,0},{3,1},{4,2},{5,3},{6,4},{7,5},{8,14},{9,15},{10,... | collective-permute-start | bytes 884744 | tf_op jit(solution)/shard_map/ppermute | solution.py:33
  168.0 11.6 %collective-permute-start.24 = (f32[96,768]{1,0:T(8,128)S(1)}, f32[96,768]{1,0:T(8,128)S(1)}, u32[]{:S(2)}, u32[]{:S(2)}) collective-permute-start(f32[96,768]{1,0:T(8,128)S(1)} %maximum_select_fusion.1), channel_id=1, source_target_pairs={{0,4},{1,5},{2,6},{3,7},{4,0},{5,1},{6,2},{7,3},{8,12},{9,13},{10,... | collective-permute-start | bytes 884744 | tf_op jit(solution)/shard_map/ppermute | solution.py:33
  169.5 14.0 %collective-permute-start.25 = (f32[96,768]{1,0:T(8,128)S(1)}, f32[96,768]{1,0:T(8,128)S(1)}, u32[]{:S(2)}, u32[]{:S(2)}) collective-permute-start(f32[96,768]{1,0:T(8,128)S(1)} %maximum_select_fusion.1), channel_id=1, source_target_pairs={{0,2},{1,3},{2,4},{3,5},{4,6},{5,7},{6,0},{7,1},{8,10},{9,11},{10,... | collective-permute-start | bytes 884744 | tf_op jit(solution)/shard_map/ppermute | solution.py:33
  195.4 3.7 %collective-permute-start.26 = (f32[1,384]{1,0:T(1,128)S(1)}, f32[1,384]{1,0:T(1,128)S(1)}, u32[]{:S(2)}, u32[]{:S(2)}) collective-permute-start(f32[1,384]{1,0:T(1,128)S(1)} %broadcast_in_dim.59), channel_id=1, source_target_pairs={{0,64},{64,0},{1,65},{65,1},{2,66},{66,2},{3,67},{67,3},{4,68},{68... | collective-permute-start | bytes 4616 | tf_op jit(solution)/shard_map/ppermute | solution.py:81
  199.0 5.1 %collective-permute-start.27 = (f32[1,2,384]{2,0,1:T(1,128)S(1)}, f32[1,2,384]{2,0,1:T(1,128)S(1)}, u32[]{:S(2)}, u32[]{:S(2)}) collective-permute-start(f32[1,2,384]{2,0,1:T(1,128)S(1)} %broadcast_select_fusion), channel_id=1, source_target_pairs={{0,1},{1,0},{2,3},{3,2},{4,5},{5,4},{6,7},{7,6},{8,9},{9,8},{10,11... | collective-permute-start | bytes 9224 | tf_op jit(solution)/shard_map/ppermute | solution.py:81
  204.2 3.7 %collective-permute-start.28 = (f32[2,2,384]{2,0,1:T(2,128)S(1)}, f32[2,2,384]{2,0,1:T(2,128)S(1)}, u32[]{:S(2)}, u32[]{:S(2)}) collective-permute-start(f32[2,2,384]{2,0,1:T(2,128)S(1)} %maximum_select_fusion.9), channel_id=1, source_target_pairs={{0,2},{1,3},{2,0},{3,1},{4,6},{5,7},{6,4},{7,5},{8,10},{9,11},{10,... | collective-permute-start | bytes 18440 | tf_op jit(solution)/shard_map/ppermute | solution.py:81
  204.3 4.9 %collective-permute-start.14 = (f32[4096]{0:T(1024)S(1)}, f32[4096]{0:T(1024)S(1)}, u32[]{:S(2)}, u32[]{:S(2)}) collective-permute-start(f32[4096]{0:T(1024)S(1)} %maximum_maximum_fusion), channel_id=1, source_target_pairs={{0,64},{64,0},{1,65},{65,1},{2,66},{66,2},{3,67},{67,3},{4,68},{68... | collective-permute-start | bytes 49160 | tf_op jit(solution)/shard_map/ppermute | solution.py:107
  207.9 5.3 %collective-permute-start.29 = (f32[4,2,384]{2,0,1:T(4,128)S(1)}, f32[4,2,384]{2,0,1:T(4,128)S(1)}, u32[]{:S(2)}, u32[]{:S(2)}) collective-permute-start(f32[4,2,384]{2,0,1:T(4,128)S(1)} %maximum_select_fusion.8), channel_id=1, source_target_pairs={{0,4},{1,5},{2,6},{3,7},{4,0},{5,1},{6,2},{7,3},{8,12},{9,13},{10,... | collective-permute-start | bytes 36872 | tf_op jit(solution)/shard_map/ppermute | solution.py:81
  (2 other events, 3.6 us)
Sparse Core Ops, SparseCore 0:
  9.7 69.7 all-gather.1

commit v9 on v8

--- a/solution.py
+++ b/solution.py
@@ -94,13 +94,13 @@
     zl_swap = [(0, 1), (1, 0)]
     both_sel = pair_join(sel_index, lax.ppermute(sel_index, "zl", zl_swap), zl == 0)
     both_cand = pair_join(cand_index, lax.ppermute(cand_index, "zl", zl_swap), zl == 0)
-    selected = group_masked_sum(lookup(half, both_sel, first_row))
-    chosen = group_masked_sum(lookup(half, both_cand, first_row))
-    reached = all_max(jnp.max(similar(selected, half), axis=0), "xc", n_xc)
+    n_sel = both_sel.shape[0]
+    picked = group_masked_sum(lookup(half, jnp.concatenate([both_sel, both_cand]), first_row))
+    scores = lax.optimization_barrier(similar(picked, half))
+    reached = all_max(jnp.max(scores[:n_sel], axis=0), "xc", n_xc)
     old = lax.dynamic_slice_in_dim(coverage_old, zl * half.shape[0], half.shape[0])
     coverage = jnp.maximum(old, reached)
-    scores = lax.optimization_barrier(similar(chosen, half))
-    gain_part = jnp.sum(jnp.maximum(scores - coverage[None, :], 0.0), axis=1)
+    gain_part = jnp.sum(jnp.maximum(scores[n_sel:] - coverage[None, :], 0.0), axis=1)
     parts = gather_in_order(gather_in_order(gain_part[None], "zl", 2)[None], "col", N_Y * N_Z)
     total = jnp.sum(parts.reshape(-1, gain_part.shape[0]), axis=0)
     total_gain = lax.dynamic_slice_in_dim(total, zl * cand_index.shape[0], cand_index.shape[0])

time: 221 us -> 229 us (1.036)
  waiting for transfers between devices: 128 us -> 144 us
  matrix products: 28.1 us -> 16 us
  other arithmetic: 2.41 us -> 9.33 us
  starting transfers between devices: 33.7 us -> 30.6 us
    ppermute x12 -> x6, waiting for transfers between devices: 26.3 us -> 40.2 us  [y_shift(): return lax.ppermute(value, 'col', pairs)]
    dot_general x2 -> x1, matrix products: 28.1 us -> 16 us  [similar(): lax.dot_general(left, right, (((1,), (1,)), ((), ())), precision=lax.Prec...]
    ppermute x2 -> x1, waiting for transfers between devices: 8.6 us -> 3.57 us  [group_masked_sum(): mine = pair_join(low, lax.ppermute(low, 'col', z_swap), z == 0)]
    gather x2 -> x1, local copies, waits for them, and re-layouts: 13 us -> 8.56 us  [lookup(): jnp.take(source, jnp.clip(position, 0, source.shape[0] - 1), axis=0)]
    unnamed x16 -> x9, local copies, waits for them, and re-layouts: 0.2 us -> 4.15 us
    ppermute x2 -> x1, waiting for transfers between devices: 1.78 us -> 4.92 us  [group_masked_sum(): own = pair_join(mine, lax.ppermute(mine, 'zl', zl_swap), zl == 0)]
    reduce_sum x1, other arithmetic: 0.76 us -> 3.49 us  [body(): jnp.sum(jnp.maximum(scores[n_sel:] - coverage[None, :], 0.0), axis=1)]
    ppermute x3, waiting for transfers between devices: 4.52 us -> 7.14 us  [all_max(): lax.ppermute(value, axis, [(i, i ^ bit) for i in range(n)])]
  transfers between devices with their start and end apart: 31 -> 21, of which waited for: 24 -> 17; matrix products, arithmetic and copies ran while one was open for 12% -> 1% of each run, Pallas kernels for 0% -> 0%
where the time goes in v9:
time: 229 us
  waiting for transfers between devices  144 us (63%)
  starting transfers between devices  30.6 us (13%)
  matrix products  16 us (7%)
  local copies, waits for them, and re-layouts  14.5 us (6%)
  between operations  14.2 us (6%)
  other arithmetic  9.33 us (4%)
    all_gather x1, waiting for transfers between devices, body(): half = lax.all_gather(slab_embed, 'xc', axis=0, tiled=True)  64.2 us
    ppermute x6, waiting for transfers between devices, y_shift(): return lax.ppermute(value, 'col', pairs)  40.2 us
    dot_general x1, matrix products, similar(): lax.dot_general(left, right, (((1,), (1,)), ((), ())), precision=lax.Prec...  16 us
    ppermute x4, waiting for transfers between devices, gather_in_order(): other = lax.ppermute(parts, axis, [(i, i ^ bit) for i in range(n)])  10.7 us
    ppermute x6, starting transfers between devices, y_shift(): return lax.ppermute(value, 'col', pairs)  9.44 us
    gather x1, local copies, waits for them, and re-layouts, lookup(): jnp.take(source, jnp.clip(position, 0, source.shape[0] - 1), axis=0)  8.56 us
    ppermute x3, waiting for transfers between devices, all_max(): lax.ppermute(value, axis, [(i, i ^ bit) for i in range(n)])  7.14 us
    ppermute x1, waiting for transfers between devices, group_masked_sum(): mine = mine + lax.ppermute(theirs, 'zl', zl_swap)  5.75 us
  transfers between devices with their start and end apart: 21, of which 17 were waited for; matrix products, arithmetic and copies ran while one was open for 1% of the time, Pallas kernels for 0%

profile of v9, /device:TPU:0, one launch (start us, length us, event | category | flops | bytes accessed | tf_op | source)
XLA Modules:
  0.0 228.7 jit_solution(4230364343696439103)
XLA Ops:
  7.9 2.1 collective-permute-start.1
  10.1 3.6 %collective-permute-done = s32[128]{0:T(128)S(1)} collective-permute-done((s32[128]{0:T(128)}, s32[128]{0:T(128)S(1)}, u32[]{:S(2)}, u32[]{:S(2)}) %collective-permute-start) | collective-permute-done | bytes 544 | tf_op jit(solution)/shard_map/ppermute | solution.py:95
  15.3 64.2 %all-gather.2.cloned.1.call-done = f32[4096,768]{1,0:T(8,128)} async-done(((f32[512,768]{1,0:T(8,128)}), f32[4096,768]{1,0:T(8,128)}) %all-gather.2.cloned.1.call-update) | async-done | bytes 12582928 | tf_op jit(solution)/shard_map/all_gather | solution.py:92
  79.5 8.6 %gather_fusion = f32[640,768]{1,0:T(8,128)} fusion(f32[4096,768]{1,0:T(8,128)} %all-gather.2.cloned.1.call-done, s32[1024]{0:T(1024)S(1)} %pad_clamp_fusion), kind=kCustom, calls=%fused_computation | custom fusion | bytes 3934720 | tf_op jit(solution)/shard_map/jit(_take)/gather | solution.py:23
  88.0 1.8 select_select_fusion
  90.8 1.5 collective-permute-start.2
  92.3 2.7 %collective-permute-start.3 = (f32[160,768]{1,0:T(8,128)S(1)}, f32[160,768]{1,0:T(8,128)}, u32[]{:S(2)}, u32[]{:S(2)}) collective-permute-start(f32[160,768]{1,0:T(8,128)S(1)} %get-tuple-element.4), channel_id=1, source_target_pairs={{0,4},{1,5},{2,6},{3,7},{4,0},{5,1},{6,2},{7,3},{8,12},{9,13},{10,... | collective-permute-start | bytes 1474568 | tf_op jit(solution)/shard_map/ppermute | solution.py:33
  96.5 9.2 %collective-permute-done.2 = f32[160,768]{1,0:T(8,128)S(1)} collective-permute-done((f32[160,768]{1,0:T(8,128)}, f32[160,768]{1,0:T(8,128)S(1)}, u32[]{:S(2)}, u32[]{:S(2)}) %collective-permute-start.2) | collective-permute-done | bytes 491552 | tf_op jit(solution)/shard_map/ppermute | solution.py:33
  105.6 11.6 %collective-permute-done.3 = f32[160,768]{1,0:T(8,128)} collective-permute-done((f32[160,768]{1,0:T(8,128)S(1)}, f32[160,768]{1,0:T(8,128)}, u32[]{:S(2)}, u32[]{:S(2)}) %collective-permute-start.3) | collective-permute-done | bytes 491552 | tf_op jit(solution)/shard_map/ppermute | solution.py:33
  118.6 1.6 collective-permute-start.5
  120.2 5.8 %collective-permute-done.5 = f32[80,768]{1,0:T(8,128)S(1)} collective-permute-done((f32[80,768]{1,0:T(8,128)S(1)}, f32[80,768]{1,0:T(8,128)S(1)}, u32[]{:S(2)}, u32[]{:S(2)}) %collective-permute-start.5) | collective-permute-done | bytes 245792 | tf_op jit(solution)/shard_map/ppermute | solution.py:60
  126.0 3.2 %collective-permute-start.6 = (f32[40,768]{1,0:T(8,128)S(1)}, f32[40,768]{1,0:T(8,128)S(1)}, u32[]{:S(2)}, u32[]{:S(2)}) collective-permute-start(f32[40,768]{1,0:T(8,128)S(1)} %slice_select_fusion.1), channel_id=1, source_target_pairs={{0,1},{1,0},{2,3},{3,2},{4,5},{5,4},{6,7},{7,6},{8,9},{9,8},{10,11... | collective-permute-start | bytes 368648 | tf_op jit(solution)/shard_map/ppermute | solution.py:62
  129.2 3.2 %collective-permute-done.6 = f32[40,768]{1,0:T(8,128)S(1)} collective-permute-done((f32[40,768]{1,0:T(8,128)S(1)}, f32[40,768]{1,0:T(8,128)S(1)}, u32[]{:S(2)}, u32[]{:S(2)}) %collective-permute-start.6) | collective-permute-done | bytes 122912 | tf_op jit(solution)/shard_map/ppermute | solution.py:62
  132.5 3.2 %collective-permute-start.7 = (f32[40,768]{1,0:T(8,128)S(1)}, f32[40,768]{1,0:T(8,128)S(1)}, u32[]{:S(2)}, u32[]{:S(2)}) collective-permute-start(f32[40,768]{1,0:T(8,128)S(1)} %select_add_fusion.1), channel_id=1, source_target_pairs={{0,1},{1,0},{2,3},{3,2},{4,5},{5,4},{6,7},{7,6},{8,9},{9,8},{10,11... | collective-permute-start | bytes 368648 | tf_op jit(solution)/shard_map/ppermute | solution.py:63
  135.7 3.6 %collective-permute-done.7 = f32[40,768]{1,0:T(8,128)S(1)} collective-permute-done((f32[40,768]{1,0:T(8,128)S(1)}, f32[40,768]{1,0:T(8,128)S(1)}, u32[]{:S(2)}, u32[]{:S(2)}) %collective-permute-start.7) | collective-permute-done | bytes 122912 | tf_op jit(solution)/shard_map/ppermute | solution.py:63
  140.7 4.9 %collective-permute-done.8 = f32[80,768]{1,0:T(8,128)S(1)} collective-permute-done((f32[80,768]{1,0:T(8,128)S(1)}, f32[80,768]{1,0:T(8,128)S(1)}, u32[]{:S(2)}, u32[]{:S(2)}) %collective-permute-start.8) | collective-permute-done | bytes 245792 | tf_op jit(solution)/shard_map/ppermute | solution.py:64
  145.6 2.4 %collective-permute-start.9 = (f32[160,768]{1,0:T(8,128)S(1)}, f32[160,768]{1,0:T(8,128)S(1)}, u32[]{:S(2)}, u32[]{:S(2)}) collective-permute-start(f32[160,768]{1,0:T(8,128)S(1)} %maximum_select_fusion.1), channel_id=1, source_target_pairs={{0,6},{1,7},{2,0},{3,1},{4,2},{5,3},{6,4},{7,5},{8,14},{9,15},{10,... | collective-permute-start | bytes 1474568 | tf_op jit(solution)/shard_map/ppermute | solution.py:33
  149.5 16.2 %collective-permute-done.9 = f32[160,768]{1,0:T(8,128)S(1)} collective-permute-done((f32[160,768]{1,0:T(8,128)S(1)}, f32[160,768]{1,0:T(8,128)S(1)}, u32[]{:S(2)}, u32[]{:S(2)}) %collective-permute-start.9) | collective-permute-done | bytes 491552 | tf_op jit(solution)/shard_map/ppermute | solution.py:33
  165.7 3.3 %collective-permute-done.11 = f32[160,768]{1,0:T(8,128)S(1)} collective-permute-done((f32[160,768]{1,0:T(8,128)S(1)}, f32[160,768]{1,0:T(8,128)S(1)}, u32[]{:S(2)}, u32[]{:S(2)}) %collective-permute-start.11) | collective-permute-done | bytes 491552 | tf_op jit(solution)/shard_map/ppermute | solution.py:33
  169.4 16.0 %fusion.7 = f32[640,4096]{1,0:T(8,128)S(1)} fusion(f32[640,768]{1,0:T(8,128)S(1)} %bitcast.16, f32[4096,768]{1,0:T(8,128)} %all-gather.2.cloned.1.call-done), kind=kOutput, calls=%fused_computation.44 | convolution fusion | flops 12079595520 | bytes 25034752 | tf_op jit(solution)/shard_map/dot_general | solution.py:11
  185.4 4.0 %copy-done = f32[640,4096]{1,0:T(8,128)} copy-done((f32[640,4096]{1,0:T(8,128)}, f32[640,4096]{1,0:T(8,128)S(1)}, u32[]{:S(2)}) %copy-start) | copy-done | bytes 10485784
  191.8 2.8 %collective-permute-done.13 = f32[4096]{0:T(1024)S(1)} collective-permute-done((f32[4096]{0:T(1024)S(1)}, f32[4096]{0:T(1024)S(1)}, u32[]{:S(2)}, u32[]{:S(2)}) %collective-permute-start.13) | collective-permute-done | bytes 16416 | tf_op jit(solution)/shard_map/ppermute | solution.py:72
  194.6 2.1 collective-permute-start.14
  196.7 3.1 %collective-permute-done.14 = f32[4096]{0:T(1024)S(1)} collective-permute-done((f32[4096]{0:T(1024)S(1)}, f32[4096]{0:T(1024)S(1)}, u32[]{:S(2)}, u32[]{:S(2)}) %collective-permute-start.14) | collective-permute-done | bytes 16416 | tf_op jit(solution)/shard_map/ppermute | solution.py:72
  199.9 3.5 %fusion.1 = f32[384]{0:T(512)S(1)} fusion(f32[640,4096]{1,0:T(8,128)} %copy-done, f32[4096]{0:T(1024)S(1)} %maximum_maximum_fusion), kind=kLoop, calls=%fused_computation.3 | loop fusion | flops 4718208 | bytes 6309376 | tf_op jit(solution)/shard_map/reduce_sum | solution.py:103
  203.4 1.6 collective-permute-start.16
  205.0 2.0 collective-permute-done.16
  207.0 2.4 %collective-permute-start.17 = (f32[1,2,384]{2,0,1:T(1,128)S(1)}, f32[1,2,384]{2,0,1:T(1,128)S(1)}, u32[]{:S(2)}, u32[]{:S(2)}) collective-permute-start(f32[1,2,384]{2,0,1:T(1,128)S(1)} %broadcast_select_fusion), channel_id=1, source_target_pairs={{0,1},{1,0},{2,3},{3,2},{4,5},{5,4},{6,7},{7,6},{8,9},{9,8},{10,11... | collective-permute-start | bytes 9224 | tf_op jit(solution)/shard_map/ppermute | solution.py:81
  209.5 2.7 %collective-permute-done.17 = f32[1,2,384]{2,0,1:T(1,128)S(1)} collective-permute-done((f32[1,2,384]{2,0,1:T(1,128)S(1)}, f32[1,2,384]{2,0,1:T(1,128)S(1)}, u32[]{:S(2)}, u32[]{:S(2)}) %collective-permute-start.17) | collective-permute-done | bytes 3104 | tf_op jit(solution)/shard_map/ppermute | solution.py:81
  212.3 1.6 collective-permute-start.15
  213.9 2.0 collective-permute-done.18
  217.2 4.0 %collective-permute-done.19 = f32[4,2,384]{2,0,1:T(4,128)S(1)} collective-permute-done((f32[4,2,384]{2,0,1:T(4,128)S(1)}, f32[4,2,384]{2,0,1:T(4,128)S(1)}, u32[]{:S(2)}, u32[]{:S(2)}) %collective-permute-start.19) | collective-permute-done | bytes 12320 | tf_op jit(solution)/shard_map/ppermute | solution.py:81
  (54 shorter events, 14.0 us)
Async XLA Ops:
  7.2 72.3 %all-gather.2.cloned.1.call-start = ((), (), s32[]{:S(2)}) async-start(), calls=%async_computation | async-start | bytes 14155776 | tf_op jit(solution)/shard_map/all_gather | solution.py:92
  7.9 6.5 %collective-permute-start.1 = (s32[192]{0:T(256)}, s32[192]{0:T(256)S(1)}, u32[]{:S(2)}, u32[]{:S(2)}) collective-permute-start(s32[192]{0:T(256)} %param.7), channel_id=1, source_target_pairs={{0,64},{64,0},{1,65},{65,1},{2,66},{66,2},{3,67},{67,3},{4,68},{68... | collective-permute-start | bytes 2312 | tf_op jit(solution)/shard_map/ppermute | solution.py:96
  10.0 3.7 %collective-permute-start = (s32[128]{0:T(128)}, s32[128]{0:T(128)S(1)}, u32[]{:S(2)}, u32[]{:S(2)}) collective-permute-start(s32[128]{0:T(128)} %param.6), channel_id=1, source_target_pairs={{0,64},{64,0},{1,65},{65,1},{2,66},{66,2},{3,67},{67,3},{4,68},{68... | collective-permute-start | bytes 1544 | tf_op jit(solution)/shard_map/ppermute | solution.py:95
  90.8 14.8 %collective-permute-start.2 = (f32[160,768]{1,0:T(8,128)}, f32[160,768]{1,0:T(8,128)S(1)}, u32[]{:S(2)}, u32[]{:S(2)}) collective-permute-start(f32[160,768]{1,0:T(8,128)} %get-tuple-element.2), channel_id=1, source_target_pairs={{0,2},{1,3},{2,4},{3,5},{4,6},{5,7},{6,0},{7,1},{8,10},{9,11},{10,... | collective-permute-start | bytes 1474568 | tf_op jit(solution)/shard_map/ppermute | solution.py:33
  92.3 24.9 %collective-permute-start.3 = (f32[160,768]{1,0:T(8,128)S(1)}, f32[160,768]{1,0:T(8,128)}, u32[]{:S(2)}, u32[]{:S(2)}) collective-permute-start(f32[160,768]{1,0:T(8,128)S(1)} %get-tuple-element.4), channel_id=1, source_target_pairs={{0,4},{1,5},{2,6},{3,7},{4,0},{5,1},{6,2},{7,3},{8,12},{9,13},{10,... | collective-permute-start | bytes 1474568 | tf_op jit(solution)/shard_map/ppermute | solution.py:33
  95.0 22.2 %collective-permute-start.4 = (f32[160,768]{1,0:T(8,128)S(1)}, f32[160,768]{1,0:T(8,128)}, u32[]{:S(2)}, u32[]{:S(2)}) collective-permute-start(f32[160,768]{1,0:T(8,128)S(1)} %get-tuple-element.3), channel_id=1, source_target_pairs={{0,6},{1,7},{2,0},{3,1},{4,2},{5,3},{6,4},{7,5},{8,14},{9,15},{10,... | collective-permute-start | bytes 1474568 | tf_op jit(solution)/shard_map/ppermute | solution.py:33
  118.6 7.4 %collective-permute-start.5 = (f32[80,768]{1,0:T(8,128)S(1)}, f32[80,768]{1,0:T(8,128)S(1)}, u32[]{:S(2)}, u32[]{:S(2)}) collective-permute-start(f32[80,768]{1,0:T(8,128)S(1)} %slice_select_fusion), channel_id=1, source_target_pairs={{0,64},{64,0},{1,65},{65,1},{2,66},{66,2},{3,67},{67,3},{4,68},{68... | collective-permute-start | bytes 737288 | tf_op jit(solution)/shard_map/ppermute | solution.py:60
  126.0 6.5 %collective-permute-start.6 = (f32[40,768]{1,0:T(8,128)S(1)}, f32[40,768]{1,0:T(8,128)S(1)}, u32[]{:S(2)}, u32[]{:S(2)}) collective-permute-start(f32[40,768]{1,0:T(8,128)S(1)} %slice_select_fusion.1), channel_id=1, source_target_pairs={{0,1},{1,0},{2,3},{3,2},{4,5},{5,4},{6,7},{7,6},{8,9},{9,8},{10,11... | collective-permute-start | bytes 368648 | tf_op jit(solution)/shard_map/ppermute | solution.py:62
  132.5 6.8 %collective-permute-start.7 = (f32[40,768]{1,0:T(8,128)S(1)}, f32[40,768]{1,0:T(8,128)S(1)}, u32[]{:S(2)}, u32[]{:S(2)}) collective-permute-start(f32[40,768]{1,0:T(8,128)S(1)} %select_add_fusion.1), channel_id=1, source_target_pairs={{0,1},{1,0},{2,3},{3,2},{4,5},{5,4},{6,7},{7,6},{8,9},{9,8},{10,11... | collective-permute-start | bytes 368648 | tf_op jit(solution)/shard_map/ppermute | solution.py:63
  139.3 6.3 %collective-permute-start.8 = (f32[80,768]{1,0:T(8,128)S(1)}, f32[80,768]{1,0:T(8,128)S(1)}, u32[]{:S(2)}, u32[]{:S(2)}) collective-permute-start(f32[80,768]{1,0:T(8,128)S(1)} %maximum_select_fusion.2), channel_id=1, source_target_pairs={{0,64},{64,0},{1,65},{65,1},{2,66},{66,2},{3,67},{67,3},{4,68},{68... | collective-permute-start | bytes 737288 | tf_op jit(solution)/shard_map/ppermute | solution.py:64
  145.6 20.0 %collective-permute-start.9 = (f32[160,768]{1,0:T(8,128)S(1)}, f32[160,768]{1,0:T(8,128)S(1)}, u32[]{:S(2)}, u32[]{:S(2)}) collective-permute-start(f32[160,768]{1,0:T(8,128)S(1)} %maximum_select_fusion.1), channel_id=1, source_target_pairs={{0,6},{1,7},{2,0},{3,1},{4,2},{5,3},{6,4},{7,5},{8,14},{9,15},{10,... | collective-permute-start | bytes 1474568 | tf_op jit(solution)/shard_map/ppermute | solution.py:33
  148.0 17.7 %collective-permute-start.10 = (f32[160,768]{1,0:T(8,128)S(1)}, f32[160,768]{1,0:T(8,128)S(1)}, u32[]{:S(2)}, u32[]{:S(2)}) collective-permute-start(f32[160,768]{1,0:T(8,128)S(1)} %maximum_select_fusion.1), channel_id=1, source_target_pairs={{0,4},{1,5},{2,6},{3,7},{4,0},{5,1},{6,2},{7,3},{8,12},{9,13},{10,... | collective-permute-start | bytes 1474568 | tf_op jit(solution)/shard_map/ppermute | solution.py:33
  148.9 20.1 %collective-permute-start.11 = (f32[160,768]{1,0:T(8,128)S(1)}, f32[160,768]{1,0:T(8,128)S(1)}, u32[]{:S(2)}, u32[]{:S(2)}) collective-permute-start(f32[160,768]{1,0:T(8,128)S(1)} %maximum_select_fusion.1), channel_id=1, source_target_pairs={{0,2},{1,3},{2,4},{3,5},{4,6},{5,7},{6,0},{7,1},{8,10},{9,11},{10,... | collective-permute-start | bytes 1474568 | tf_op jit(solution)/shard_map/ppermute | solution.py:33
  185.4 4.0 %copy-start = (f32[640,4096]{1,0:T(8,128)}, f32[640,4096]{1,0:T(8,128)S(1)}, u32[]{:S(2)}) copy-start(f32[640,4096]{1,0:T(8,128)S(1)} %fusion.7) | copy-start | bytes 31457284
  189.4 10.5 %copy-start.1 = (f32[8192]{0:T(1024)S(1)}, f32[8192]{0:T(1024)}, u32[]{:S(2)}) copy-start(f32[8192]{0:T(1024)} %param.5) | copy-start | bytes 98308
  189.6 1.3 collective-permute-start.12
  190.9 3.7 %collective-permute-start.13 = (f32[4096]{0:T(1024)S(1)}, f32[4096]{0:T(1024)S(1)}, u32[]{:S(2)}, u32[]{:S(2)}) collective-permute-start(f32[4096]{0:T(1024)S(1)} %max.22), channel_id=1, source_target_pairs={{0,16},{8,24},{16,0},{24,8},{32,48},{40,56},{48,32},{56,40},{1,17}... | collective-permute-start | bytes 49160 | tf_op jit(solution)/shard_map/ppermute | solution.py:72
  194.6 5.2 %collective-permute-start.14 = (f32[4096]{0:T(1024)S(1)}, f32[4096]{0:T(1024)S(1)}, u32[]{:S(2)}, u32[]{:S(2)}) collective-permute-start(f32[4096]{0:T(1024)S(1)} %max.23), channel_id=1, source_target_pairs={{0,32},{8,40},{16,48},{24,56},{32,0},{40,8},{48,16},{56,24},{1,33}... | collective-permute-start | bytes 49160 | tf_op jit(solution)/shard_map/ppermute | solution.py:72
  203.4 3.7 %collective-permute-start.16 = (f32[1,384]{1,0:T(1,128)S(1)}, f32[1,384]{1,0:T(1,128)S(1)}, u32[]{:S(2)}, u32[]{:S(2)}) collective-permute-start(f32[1,384]{1,0:T(1,128)S(1)} %broadcast_in_dim.32), channel_id=1, source_target_pairs={{0,64},{64,0},{1,65},{65,1},{2,66},{66,2},{3,67},{67,3},{4,68},{68... | collective-permute-start | bytes 4616 | tf_op jit(solution)/shard_map/ppermute | solution.py:81
  207.0 5.1 %collective-permute-start.17 = (f32[1,2,384]{2,0,1:T(1,128)S(1)}, f32[1,2,384]{2,0,1:T(1,128)S(1)}, u32[]{:S(2)}, u32[]{:S(2)}) collective-permute-start(f32[1,2,384]{2,0,1:T(1,128)S(1)} %broadcast_select_fusion), channel_id=1, source_target_pairs={{0,1},{1,0},{2,3},{3,2},{4,5},{5,4},{6,7},{7,6},{8,9},{9,8},{10,11... | collective-permute-start | bytes 9224 | tf_op jit(solution)/shard_map/ppermute | solution.py:81
  212.2 3.7 %collective-permute-start.18 = (f32[2,2,384]{2,0,1:T(2,128)S(1)}, f32[2,2,384]{2,0,1:T(2,128)S(1)}, u32[]{:S(2)}, u32[]{:S(2)}) collective-permute-start(f32[2,2,384]{2,0,1:T(2,128)S(1)} %maximum_select_fusion.6), channel_id=1, source_target_pairs={{0,2},{1,3},{2,0},{3,1},{4,6},{5,7},{6,4},{7,5},{8,10},{9,11},{10,... | collective-permute-start | bytes 18440 | tf_op jit(solution)/shard_map/ppermute | solution.py:81
  212.3 4.3 %collective-permute-start.15 = (f32[4096]{0:T(1024)S(1)}, f32[4096]{0:T(1024)S(1)}, u32[]{:S(2)}, u32[]{:S(2)}) collective-permute-start(f32[4096]{0:T(1024)S(1)} %maximum_maximum_fusion), channel_id=1, source_target_pairs={{0,64},{64,0},{1,65},{65,1},{2,66},{66,2},{3,67},{67,3},{4,68},{68... | collective-permute-start | bytes 49160 | tf_op jit(solution)/shard_map/ppermute | solution.py:107
  215.9 5.3 %collective-permute-start.19 = (f32[4,2,384]{2,0,1:T(4,128)S(1)}, f32[4,2,384]{2,0,1:T(4,128)S(1)}, u32[]{:S(2)}, u32[]{:S(2)}) collective-permute-start(f32[4,2,384]{2,0,1:T(4,128)S(1)} %maximum_select_fusion.5), channel_id=1, source_target_pairs={{0,4},{1,5},{2,6},{3,7},{4,0},{5,1},{6,2},{7,3},{8,12},{9,13},{10,... | collective-permute-start | bytes 36872 | tf_op jit(solution)/shard_map/ppermute | solution.py:81
Sparse Core Ops, SparseCore 0:
  9.7 69.7 all-gather.1

commit v10 on v9

--- a/solution.py
+++ b/solution.py
@@ -94,9 +94,10 @@
     zl_swap = [(0, 1), (1, 0)]
     both_sel = pair_join(sel_index, lax.ppermute(sel_index, "zl", zl_swap), zl == 0)
     both_cand = pair_join(cand_index, lax.ppermute(cand_index, "zl", zl_swap), zl == 0)
+    selected = group_masked_sum(lookup(half, both_sel, first_row))
+    chosen = group_masked_sum(lookup(half, both_cand, first_row))
     n_sel = both_sel.shape[0]
-    picked = group_masked_sum(lookup(half, jnp.concatenate([both_sel, both_cand]), first_row))
-    scores = lax.optimization_barrier(similar(picked, half))
+    scores = lax.optimization_barrier(similar(jnp.concatenate([selected, chosen]), half))
     reached = all_max(jnp.max(scores[:n_sel], axis=0), "xc", n_xc)
     old = lax.dynamic_slice_in_dim(coverage_old, zl * half.shape[0], half.shape[0])
     coverage = jnp.maximum(old, reached)

time: 229 us -> 219 us (0.956)
  waiting for transfers between devices: 144 us -> 121 us
  starting transfers between devices: 30.6 us -> 41.3 us
  local copies, waits for them, and re-layouts: 14.5 us -> 18.2 us
    ppermute x6 -> x12, waiting for transfers between devices: 40.2 us -> 20.9 us  [y_shift(): return lax.ppermute(value, 'col', pairs)]
    ppermute x6 -> x12, starting transfers between devices: 9.44 us -> 18.9 us  [y_shift(): return lax.ppermute(value, 'col', pairs)]
    gather x1 -> x2, local copies, waits for them, and re-layouts: 8.56 us -> 13 us  [lookup(): jnp.take(source, jnp.clip(position, 0, source.shape[0] - 1), axis=0)]
    ppermute x1 -> x2, waiting for transfers between devices: 3.57 us -> 7.57 us  [group_masked_sum(): mine = pair_join(low, lax.ppermute(low, 'col', z_swap), z == 0)]
    ppermute x1 -> x2, waiting for transfers between devices: 3.23 us -> 0.54 us  [group_masked_sum(): low = low + lax.ppermute(high, 'col', z_swap)]
    ppermute x1 -> x2, waiting for transfers between devices: 5.75 us -> 3.18 us  [group_masked_sum(): mine = mine + lax.ppermute(theirs, 'zl', zl_swap)]
    ppermute x1 -> x2, starting transfers between devices: 3.23 us -> 4.61 us  [group_masked_sum(): mine = pair_join(low, lax.ppermute(low, 'col', z_swap), z == 0)]
    ppermute x1 -> x2, waiting for transfers between devices: 4.92 us -> 4.07 us  [group_masked_sum(): own = pair_join(mine, lax.ppermute(mine, 'zl', zl_swap), zl == 0)]
  transfers between devices with their start and end apart: 21 -> 31, of which waited for: 17 -> 23; matrix products, arithmetic and copies ran while one was open for 1% -> 5% of each run, Pallas kernels for 0% -> 0%
where the time goes in v10:
time: 219 us
  waiting for transfers between devices  121 us (55%)
  starting transfers between devices  41.3 us (19%)
  local copies, waits for them, and re-layouts  18.2 us (8%)
  matrix products  16 us (7%)
  between operations  14.4 us (7%)
  other arithmetic  8.31 us (4%)
    all_gather x1, waiting for transfers between devices, body(): half = lax.all_gather(slab_embed, 'xc', axis=0, tiled=True)  64 us
    ppermute x12, waiting for transfers between devices, y_shift(): return lax.ppermute(value, 'col', pairs)  20.9 us
    ppermute x12, starting transfers between devices, y_shift(): return lax.ppermute(value, 'col', pairs)  18.9 us
    dot_general x1, matrix products, similar(): lax.dot_general(left, right, (((1,), (1,)), ((), ())), precision=lax.Prec...  16 us
    gather x2, local copies, waits for them, and re-layouts, lookup(): jnp.take(source, jnp.clip(position, 0, source.shape[0] - 1), axis=0)  13 us
    ppermute x4, waiting for transfers between devices, gather_in_order(): other = lax.ppermute(parts, axis, [(i, i ^ bit) for i in range(n)])  10.6 us
    ppermute x2, waiting for transfers between devices, group_masked_sum(): mine = pair_join(low, lax.ppermute(low, 'col', z_swap), z == 0)  7.57 us
    ppermute x3, waiting for transfers between devices, all_max(): lax.ppermute(value, axis, [(i, i ^ bit) for i in range(n)])  7.15 us
  transfers between devices with their start and end apart: 31, of which 23 were waited for; matrix products, arithmetic and copies ran while one was open for 5% of the time, Pallas kernels for 0%

profile of v10, /device:TPU:0, one launch (start us, length us, event | category | flops | bytes accessed | tf_op | source)
XLA Modules:
  0.0 219.0 jit_solution(11483035500036640329)
XLA Ops:
  7.9 2.1 collective-permute-start
  10.1 1.6 collective-permute-done
  15.5 64.0 %all-gather.2.cloned.1.call-done = f32[4096,768]{1,0:T(8,128)} async-done(((f32[512,768]{1,0:T(8,128)}), f32[4096,768]{1,0:T(8,128)}) %all-gather.2.cloned.1.call-update) | async-done | bytes 12582928 | tf_op jit(solution)/shard_map/all_gather | solution.py:92
  79.5 6.0 %gather_fusion = f32[256,768]{1,0:T(8,128)S(1)} fusion(f32[4096,768]{1,0:T(8,128)} %all-gather.2.cloned.1.call-done, s32[1024]{0:T(1024)S(1)} %pad_clamp_fusion.1), kind=kCustom, calls=%fused_computation | custom fusion | bytes 1573888 | tf_op jit(solution)/shard_map/jit(_take)/gather | solution.py:23
  87.2 2.7 %collective-permute-start.2 = (f32[64,768]{1,0:T(8,128)S(1)}, f32[64,768]{1,0:T(8,128)S(1)}, u32[]{:S(2)}, u32[]{:S(2)}) collective-permute-start(f32[64,768]{1,0:T(8,128)S(1)} %get-tuple-element.9), channel_id=1, source_target_pairs={{0,4},{1,5},{2,6},{3,7},{4,0},{5,1},{6,2},{7,3},{8,12},{9,13},{10,... | collective-permute-start | bytes 589832 | tf_op jit(solution)/shard_map/ppermute | solution.py:33
  91.4 7.1 %gather_fusion.1 = f32[384,768]{1,0:T(8,128)S(1)} fusion(f32[4096,768]{1,0:T(8,128)} %all-gather.2.cloned.1.call-done, s32[1024]{0:T(1024)S(1)} %pad_clamp_fusion), kind=kCustom, calls=%fused_computation.1 | custom fusion | bytes 2360832 | tf_op jit(solution)/shard_map/jit(_take)/gather | solution.py:23
  99.3 1.6 collective-permute-start.4
  102.4 2.4 %collective-permute-start.13 = (f32[96,768]{1,0:T(8,128)S(1)}, f32[96,768]{1,0:T(8,128)S(1)}, u32[]{:S(2)}, u32[]{:S(2)}) collective-permute-start(f32[96,768]{1,0:T(8,128)S(1)} %get-tuple-element.6), channel_id=1, source_target_pairs={{0,4},{1,5},{2,6},{3,7},{4,0},{5,1},{6,2},{7,3},{8,12},{9,13},{10,... | collective-permute-start | bytes 884744 | tf_op jit(solution)/shard_map/ppermute | solution.py:33
  104.8 1.6 collective-permute-start.14
  106.4 2.9 %collective-permute-start.5 = (f32[16,768]{1,0:T(8,128)S(1)}, f32[16,768]{1,0:T(8,128)S(1)}, u32[]{:S(2)}, u32[]{:S(2)}) collective-permute-start(f32[16,768]{1,0:T(8,128)S(1)} %slice_select_fusion.3), channel_id=1, source_target_pairs={{0,1},{1,0},{2,3},{3,2},{4,5},{5,4},{6,7},{7,6},{8,9},{9,8},{10,11... | collective-permute-start | bytes 147464 | tf_op jit(solution)/shard_map/ppermute | solution.py:62
  110.5 7.2 %collective-permute-done.13 = f32[96,768]{1,0:T(8,128)S(1)} collective-permute-done((f32[96,768]{1,0:T(8,128)S(1)}, f32[96,768]{1,0:T(8,128)S(1)}, u32[]{:S(2)}, u32[]{:S(2)}) %collective-permute-start.13) | collective-permute-done | bytes 294944 | tf_op jit(solution)/shard_map/ppermute | solution.py:33
  117.9 2.9 %collective-permute-start.6 = (f32[16,768]{1,0:T(8,128)S(1)}, f32[16,768]{1,0:T(8,128)S(1)}, u32[]{:S(2)}, u32[]{:S(2)}) collective-permute-start(f32[16,768]{1,0:T(8,128)S(1)} %select_add_fusion.3), channel_id=1, source_target_pairs={{0,1},{1,0},{2,3},{3,2},{4,5},{5,4},{6,7},{7,6},{8,9},{9,8},{10,11... | collective-permute-start | bytes 147464 | tf_op jit(solution)/shard_map/ppermute | solution.py:63
  121.1 2.8 %collective-permute-done.6 = f32[16,768]{1,0:T(8,128)S(1)} collective-permute-done((f32[16,768]{1,0:T(8,128)S(1)}, f32[16,768]{1,0:T(8,128)S(1)}, u32[]{:S(2)}, u32[]{:S(2)}) %collective-permute-start.6) | collective-permute-done | bytes 49184 | tf_op jit(solution)/shard_map/ppermute | solution.py:63
  124.3 3.2 %collective-permute-done.15 = f32[48,768]{1,0:T(8,128)S(1)} collective-permute-done((f32[48,768]{1,0:T(8,128)S(1)}, f32[48,768]{1,0:T(8,128)S(1)}, u32[]{:S(2)}, u32[]{:S(2)}) %collective-permute-start.15) | collective-permute-done | bytes 147488 | tf_op jit(solution)/shard_map/ppermute | solution.py:60
  128.7 3.1 %collective-permute-start.8 = (f32[64,768]{1,0:T(8,128)S(1)}, f32[64,768]{1,0:T(8,128)S(1)}, u32[]{:S(2)}, u32[]{:S(2)}) collective-permute-start(f32[64,768]{1,0:T(8,128)S(1)} %maximum_select_fusion.3), channel_id=1, source_target_pairs={{0,6},{1,7},{2,0},{3,1},{4,2},{5,3},{6,4},{7,5},{8,14},{9,15},{10,... | collective-permute-start | bytes 589832 | tf_op jit(solution)/shard_map/ppermute | solution.py:33
  133.5 1.7 collective-permute-start.17
  135.2 4.7 %collective-permute-done.17 = f32[24,768]{1,0:T(8,128)S(1)} collective-permute-done((f32[24,768]{1,0:T(8,128)S(1)}, f32[24,768]{1,0:T(8,128)S(1)}, u32[]{:S(2)}, u32[]{:S(2)}) %collective-permute-start.17) | collective-permute-done | bytes 73760 | tf_op jit(solution)/shard_map/ppermute | solution.py:63
  141.9 3.2 %collective-permute-done.18 = f32[48,768]{1,0:T(8,128)S(1)} collective-permute-done((f32[48,768]{1,0:T(8,128)S(1)}, f32[48,768]{1,0:T(8,128)S(1)}, u32[]{:S(2)}, u32[]{:S(2)}) %collective-permute-start.18) | collective-permute-done | bytes 147488 | tf_op jit(solution)/shard_map/ppermute | solution.py:64
  145.2 2.5 %collective-permute-start.19 = (f32[96,768]{1,0:T(8,128)S(1)}, f32[96,768]{1,0:T(8,128)S(1)}, u32[]{:S(2)}, u32[]{:S(2)}) collective-permute-start(f32[96,768]{1,0:T(8,128)S(1)} %maximum_select_fusion.1), channel_id=1, source_target_pairs={{0,6},{1,7},{2,0},{3,1},{4,2},{5,3},{6,4},{7,5},{8,14},{9,15},{10,... | collective-permute-start | bytes 884744 | tf_op jit(solution)/shard_map/ppermute | solution.py:33
  148.9 6.7 %collective-permute-done.19 = f32[96,768]{1,0:T(8,128)S(1)} collective-permute-done((f32[96,768]{1,0:T(8,128)S(1)}, f32[96,768]{1,0:T(8,128)S(1)}, u32[]{:S(2)}, u32[]{:S(2)}) %collective-permute-start.19) | collective-permute-done | bytes 294944 | tf_op jit(solution)/shard_map/ppermute | solution.py:33
  156.4 3.0 %collective-permute-done.21 = f32[96,768]{1,0:T(8,128)S(1)} collective-permute-done((f32[96,768]{1,0:T(8,128)S(1)}, f32[96,768]{1,0:T(8,128)S(1)}, u32[]{:S(2)}, u32[]{:S(2)}) %collective-permute-start.21) | collective-permute-done | bytes 294944 | tf_op jit(solution)/shard_map/ppermute | solution.py:33
  159.7 16.0 %fusion.2 = f32[640,4096]{1,0:T(8,128)S(1)} fusion(f32[4096,768]{1,0:T(8,128)} %all-gather.2.cloned.1.call-done, f32[384,768]{1,0:T(8,128)S(1)} %bitcast.31, f32[256,768]{1,0:T(8,128)S(1)} %bitcast.32), kind=kOutput, calls=%fused_computation.6 | convolution fusion | flops 12080087040 | bytes 25034752 | tf_op jit(solution)/shard_map/dot_general | solution.py:11
  175.7 4.0 %copy-done = f32[640,4096]{1,0:T(8,128)} copy-done((f32[640,4096]{1,0:T(8,128)}, f32[640,4096]{1,0:T(8,128)S(1)}, u32[]{:S(2)}) %copy-start) | copy-done | bytes 10485784
  182.1 2.8 %collective-permute-done.23 = f32[4096]{0:T(1024)S(1)} collective-permute-done((f32[4096]{0:T(1024)S(1)}, f32[4096]{0:T(1024)S(1)}, u32[]{:S(2)}, u32[]{:S(2)}) %collective-permute-start.23) | collective-permute-done | bytes 16416 | tf_op jit(solution)/shard_map/ppermute | solution.py:72
  184.9 2.1 collective-permute-start.24
  187.0 3.1 %collective-permute-done.24 = f32[4096]{0:T(1024)S(1)} collective-permute-done((f32[4096]{0:T(1024)S(1)}, f32[4096]{0:T(1024)S(1)}, u32[]{:S(2)}, u32[]{:S(2)}) %collective-permute-start.24) | collective-permute-done | bytes 16416 | tf_op jit(solution)/shard_map/ppermute | solution.py:72
  190.2 3.5 %fusion.1 = f32[384]{0:T(512)S(1)} fusion(f32[640,4096]{1,0:T(8,128)} %copy-done, f32[4096]{0:T(1024)S(1)} %maximum_maximum_fusion), kind=kLoop, calls=%fused_computation.4 | loop fusion | flops 4718208 | bytes 6309376 | tf_op jit(solution)/shard_map/reduce_sum | solution.py:104
  195.2 2.1 collective-permute-done.26
  197.3 2.1 collective-permute-start.27
  199.5 3.0 %collective-permute-done.27 = f32[1,2,384]{2,0,1:T(1,128)S(1)} collective-permute-done((f32[1,2,384]{2,0,1:T(1,128)S(1)}, f32[1,2,384]{2,0,1:T(1,128)S(1)}, u32[]{:S(2)}, u32[]{:S(2)}) %collective-permute-start.27) | collective-permute-done | bytes 3104 | tf_op jit(solution)/shard_map/ppermute | solution.py:81
  204.1 2.1 collective-permute-done.28
  208.1 3.4 %collective-permute-done.29 = f32[4,2,384]{2,0,1:T(4,128)S(1)} collective-permute-done((f32[4,2,384]{2,0,1:T(4,128)S(1)}, f32[4,2,384]{2,0,1:T(4,128)S(1)}, u32[]{:S(2)}, u32[]{:S(2)}) %collective-permute-start.29) | collective-permute-done | bytes 12320 | tf_op jit(solution)/shard_map/ppermute | solution.py:81
  (94 shorter events, 27.2 us)
Async XLA Ops:
  7.2 72.3 %all-gather.2.cloned.1.call-start = ((), (), s32[]{:S(2)}) async-start(), calls=%async_computation | async-start | bytes 14155776 | tf_op jit(solution)/shard_map/all_gather | solution.py:92
  7.9 3.8 %collective-permute-start = (s32[128]{0:T(128)}, s32[128]{0:T(128)S(1)}, u32[]{:S(2)}, u32[]{:S(2)}) collective-permute-start(s32[128]{0:T(128)} %param.6), channel_id=1, source_target_pairs={{0,64},{64,0},{1,65},{65,1},{2,66},{66,2},{3,67},{67,3},{4,68},{68... | collective-permute-start | bytes 1544 | tf_op jit(solution)/shard_map/ppermute | solution.py:95
  10.0 3.8 %collective-permute-start.11 = (s32[192]{0:T(256)}, s32[192]{0:T(256)S(1)}, u32[]{:S(2)}, u32[]{:S(2)}) collective-permute-start(s32[192]{0:T(256)} %param.7), channel_id=1, source_target_pairs={{0,64},{64,0},{1,65},{65,1},{2,66},{66,2},{3,67},{67,3},{4,68},{68... | collective-permute-start | bytes 2312 | tf_op jit(solution)/shard_map/ppermute | solution.py:96
  85.7 13.0 %collective-permute-start.1 = (f32[64,768]{1,0:T(8,128)S(1)}, f32[64,768]{1,0:T(8,128)S(1)}, u32[]{:S(2)}, u32[]{:S(2)}) collective-permute-start(f32[64,768]{1,0:T(8,128)S(1)} %get-tuple-element.7), channel_id=1, source_target_pairs={{0,2},{1,3},{2,4},{3,5},{4,6},{5,7},{6,0},{7,1},{8,10},{9,11},{10,... | collective-permute-start | bytes 589832 | tf_op jit(solution)/shard_map/ppermute | solution.py:33
  87.2 12.0 %collective-permute-start.2 = (f32[64,768]{1,0:T(8,128)S(1)}, f32[64,768]{1,0:T(8,128)S(1)}, u32[]{:S(2)}, u32[]{:S(2)}) collective-permute-start(f32[64,768]{1,0:T(8,128)S(1)} %get-tuple-element.9), channel_id=1, source_target_pairs={{0,4},{1,5},{2,6},{3,7},{4,0},{5,1},{6,2},{7,3},{8,12},{9,13},{10,... | collective-permute-start | bytes 589832 | tf_op jit(solution)/shard_map/ppermute | solution.py:33
  90.0 9.3 %collective-permute-start.3 = (f32[64,768]{1,0:T(8,128)S(1)}, f32[64,768]{1,0:T(8,128)S(1)}, u32[]{:S(2)}, u32[]{:S(2)}) collective-permute-start(f32[64,768]{1,0:T(8,128)S(1)} %get-tuple-element.8), channel_id=1, source_target_pairs={{0,6},{1,7},{2,0},{3,1},{4,2},{5,3},{6,4},{7,5},{8,14},{9,15},{10,... | collective-permute-start | bytes 589832 | tf_op jit(solution)/shard_map/ppermute | solution.py:33
  99.3 7.1 %collective-permute-start.4 = (f32[32,768]{1,0:T(8,128)S(1)}, f32[32,768]{1,0:T(8,128)S(1)}, u32[]{:S(2)}, u32[]{:S(2)}) collective-permute-start(f32[32,768]{1,0:T(8,128)S(1)} %slice_select_fusion.1), channel_id=1, source_target_pairs={{0,64},{64,0},{1,65},{65,1},{2,66},{66,2},{3,67},{67,3},{4,68},{68... | collective-permute-start | bytes 294920 | tf_op jit(solution)/shard_map/ppermute | solution.py:60
  101.0 9.5 %collective-permute-start.12 = (f32[96,768]{1,0:T(8,128)S(1)}, f32[96,768]{1,0:T(8,128)S(1)}, u32[]{:S(2)}, u32[]{:S(2)}) collective-permute-start(f32[96,768]{1,0:T(8,128)S(1)} %get-tuple-element.4), channel_id=1, source_target_pairs={{0,2},{1,3},{2,4},{3,5},{4,6},{5,7},{6,0},{7,1},{8,10},{9,11},{10,... | collective-permute-start | bytes 884744 | tf_op jit(solution)/shard_map/ppermute | solution.py:33
  102.4 15.3 %collective-permute-start.13 = (f32[96,768]{1,0:T(8,128)S(1)}, f32[96,768]{1,0:T(8,128)S(1)}, u32[]{:S(2)}, u32[]{:S(2)}) collective-permute-start(f32[96,768]{1,0:T(8,128)S(1)} %get-tuple-element.6), channel_id=1, source_target_pairs={{0,4},{1,5},{2,6},{3,7},{4,0},{5,1},{6,2},{7,3},{8,12},{9,13},{10,... | collective-permute-start | bytes 884744 | tf_op jit(solution)/shard_map/ppermute | solution.py:33
  104.8 12.9 %collective-permute-start.14 = (f32[96,768]{1,0:T(8,128)S(1)}, f32[96,768]{1,0:T(8,128)S(1)}, u32[]{:S(2)}, u32[]{:S(2)}) collective-permute-start(f32[96,768]{1,0:T(8,128)S(1)} %get-tuple-element.5), channel_id=1, source_target_pairs={{0,6},{1,7},{2,0},{3,1},{4,2},{5,3},{6,4},{7,5},{8,14},{9,15},{10,... | collective-permute-start | bytes 884744 | tf_op jit(solution)/shard_map/ppermute | solution.py:33
  106.4 11.4 %collective-permute-start.5 = (f32[16,768]{1,0:T(8,128)S(1)}, f32[16,768]{1,0:T(8,128)S(1)}, u32[]{:S(2)}, u32[]{:S(2)}) collective-permute-start(f32[16,768]{1,0:T(8,128)S(1)} %slice_select_fusion.3), channel_id=1, source_target_pairs={{0,1},{1,0},{2,3},{3,2},{4,5},{5,4},{6,7},{7,6},{8,9},{9,8},{10,11... | collective-permute-start | bytes 147464 | tf_op jit(solution)/shard_map/ppermute | solution.py:62
  117.9 6.0 %collective-permute-start.6 = (f32[16,768]{1,0:T(8,128)S(1)}, f32[16,768]{1,0:T(8,128)S(1)}, u32[]{:S(2)}, u32[]{:S(2)}) collective-permute-start(f32[16,768]{1,0:T(8,128)S(1)} %select_add_fusion.3), channel_id=1, source_target_pairs={{0,1},{1,0},{2,3},{3,2},{4,5},{5,4},{6,7},{7,6},{8,9},{9,8},{10,11... | collective-permute-start | bytes 147464 | tf_op jit(solution)/shard_map/ppermute | solution.py:63
  120.8 6.7 %collective-permute-start.15 = (f32[48,768]{1,0:T(8,128)S(1)}, f32[48,768]{1,0:T(8,128)S(1)}, u32[]{:S(2)}, u32[]{:S(2)}) collective-permute-start(f32[48,768]{1,0:T(8,128)S(1)} %slice_select_fusion), channel_id=1, source_target_pairs={{0,64},{64,0},{1,65},{65,1},{2,66},{66,2},{3,67},{67,3},{4,68},{68... | collective-permute-start | bytes 442376 | tf_op jit(solution)/shard_map/ppermute | solution.py:60
  123.9 4.7 %collective-permute-start.7 = (f32[32,768]{1,0:T(8,128)S(1)}, f32[32,768]{1,0:T(8,128)S(1)}, u32[]{:S(2)}, u32[]{:S(2)}) collective-permute-start(f32[32,768]{1,0:T(8,128)S(1)} %maximum_select_fusion.5), channel_id=1, source_target_pairs={{0,64},{64,0},{1,65},{65,1},{2,66},{66,2},{3,67},{67,3},{4,68},{68... | collective-permute-start | bytes 294920 | tf_op jit(solution)/shard_map/ppermute | solution.py:64
  127.6 5.9 %collective-permute-start.16 = (f32[24,768]{1,0:T(8,128)S(1)}, f32[24,768]{1,0:T(8,128)S(1)}, u32[]{:S(2)}, u32[]{:S(2)}) collective-permute-start(f32[24,768]{1,0:T(8,128)S(1)} %slice_select_fusion.2), channel_id=1, source_target_pairs={{0,1},{1,0},{2,3},{3,2},{4,5},{5,4},{6,7},{7,6},{8,9},{9,8},{10,11... | collective-permute-start | bytes 221192 | tf_op jit(solution)/shard_map/ppermute | solution.py:62
  128.7 11.7 %collective-permute-start.8 = (f32[64,768]{1,0:T(8,128)S(1)}, f32[64,768]{1,0:T(8,128)S(1)}, u32[]{:S(2)}, u32[]{:S(2)}) collective-permute-start(f32[64,768]{1,0:T(8,128)S(1)} %maximum_select_fusion.3), channel_id=1, source_target_pairs={{0,6},{1,7},{2,0},{3,1},{4,2},{5,3},{6,4},{7,5},{8,14},{9,15},{10,... | collective-permute-start | bytes 589832 | tf_op jit(solution)/shard_map/ppermute | solution.py:33
  131.8 8.7 %collective-permute-start.9 = (f32[64,768]{1,0:T(8,128)S(1)}, f32[64,768]{1,0:T(8,128)S(1)}, u32[]{:S(2)}, u32[]{:S(2)}) collective-permute-start(f32[64,768]{1,0:T(8,128)S(1)} %maximum_select_fusion.3), channel_id=1, source_target_pairs={{0,4},{1,5},{2,6},{3,7},{4,0},{5,1},{6,2},{7,3},{8,12},{9,13},{10,... | collective-permute-start | bytes 589832 | tf_op jit(solution)/shard_map/ppermute | solution.py:33
  133.0 8.9 %collective-permute-start.10 = (f32[64,768]{1,0:T(8,128)S(1)}, f32[64,768]{1,0:T(8,128)S(1)}, u32[]{:S(2)}, u32[]{:S(2)}) collective-permute-start(f32[64,768]{1,0:T(8,128)S(1)} %maximum_select_fusion.3), channel_id=1, source_target_pairs={{0,2},{1,3},{2,4},{3,5},{4,6},{5,7},{6,0},{7,1},{8,10},{9,11},{10,... | collective-permute-start | bytes 589832 | tf_op jit(solution)/shard_map/ppermute | solution.py:33
  133.5 6.4 %collective-permute-start.17 = (f32[24,768]{1,0:T(8,128)S(1)}, f32[24,768]{1,0:T(8,128)S(1)}, u32[]{:S(2)}, u32[]{:S(2)}) collective-permute-start(f32[24,768]{1,0:T(8,128)S(1)} %select_add_fusion.2), channel_id=1, source_target_pairs={{0,1},{1,0},{2,3},{3,2},{4,5},{5,4},{6,7},{7,6},{8,9},{9,8},{10,11... | collective-permute-start | bytes 221192 | tf_op jit(solution)/shard_map/ppermute | solution.py:63
  140.0 5.2 %collective-permute-start.18 = (f32[48,768]{1,0:T(8,128)S(1)}, f32[48,768]{1,0:T(8,128)S(1)}, u32[]{:S(2)}, u32[]{:S(2)}) collective-permute-start(f32[48,768]{1,0:T(8,128)S(1)} %maximum_select_fusion.4), channel_id=1, source_target_pairs={{0,64},{64,0},{1,65},{65,1},{2,66},{66,2},{3,67},{67,3},{4,68},{68... | collective-permute-start | bytes 442376 | tf_op jit(solution)/shard_map/ppermute | solution.py:64
  145.2 10.4 %collective-permute-start.19 = (f32[96,768]{1,0:T(8,128)S(1)}, f32[96,768]{1,0:T(8,128)S(1)}, u32[]{:S(2)}, u32[]{:S(2)}) collective-permute-start(f32[96,768]{1,0:T(8,128)S(1)} %maximum_select_fusion.1), channel_id=1, source_target_pairs={{0,6},{1,7},{2,0},{3,1},{4,2},{5,3},{6,4},{7,5},{8,14},{9,15},{10,... | collective-permute-start | bytes 884744 | tf_op jit(solution)/shard_map/ppermute | solution.py:33
  147.8 8.6 %collective-permute-start.20 = (f32[96,768]{1,0:T(8,128)S(1)}, f32[96,768]{1,0:T(8,128)S(1)}, u32[]{:S(2)}, u32[]{:S(2)}) collective-permute-start(f32[96,768]{1,0:T(8,128)S(1)} %maximum_select_fusion.1), channel_id=1, source_target_pairs={{0,4},{1,5},{2,6},{3,7},{4,0},{5,1},{6,2},{7,3},{8,12},{9,13},{10,... | collective-permute-start | bytes 884744 | tf_op jit(solution)/shard_map/ppermute | solution.py:33
  148.9 10.6 %collective-permute-start.21 = (f32[96,768]{1,0:T(8,128)S(1)}, f32[96,768]{1,0:T(8,128)S(1)}, u32[]{:S(2)}, u32[]{:S(2)}) collective-permute-start(f32[96,768]{1,0:T(8,128)S(1)} %maximum_select_fusion.1), channel_id=1, source_target_pairs={{0,2},{1,3},{2,4},{3,5},{4,6},{5,7},{6,0},{7,1},{8,10},{9,11},{10,... | collective-permute-start | bytes 884744 | tf_op jit(solution)/shard_map/ppermute | solution.py:33
  179.7 10.5 %copy-start.1 = (f32[8192]{0:T(1024)S(1)}, f32[8192]{0:T(1024)}, u32[]{:S(2)}) copy-start(f32[8192]{0:T(1024)} %param.5) | copy-start | bytes 98308
  179.9 1.3 collective-permute-start.22
  181.2 3.7 %collective-permute-start.23 = (f32[4096]{0:T(1024)S(1)}, f32[4096]{0:T(1024)S(1)}, u32[]{:S(2)}, u32[]{:S(2)}) collective-permute-start(f32[4096]{0:T(1024)S(1)} %max.26), channel_id=1, source_target_pairs={{0,16},{8,24},{16,0},{24,8},{32,48},{40,56},{48,32},{56,40},{1,17}... | collective-permute-start | bytes 49160 | tf_op jit(solution)/shard_map/ppermute | solution.py:72
  184.9 5.2 %collective-permute-start.24 = (f32[4096]{0:T(1024)S(1)}, f32[4096]{0:T(1024)S(1)}, u32[]{:S(2)}, u32[]{:S(2)}) collective-permute-start(f32[4096]{0:T(1024)S(1)} %max.27), channel_id=1, source_target_pairs={{0,32},{8,40},{16,48},{24,56},{32,0},{40,8},{48,16},{56,24},{1,33}... | collective-permute-start | bytes 49160 | tf_op jit(solution)/shard_map/ppermute | solution.py:72
  193.7 3.7 %collective-permute-start.26 = (f32[1,384]{1,0:T(1,128)S(1)}, f32[1,384]{1,0:T(1,128)S(1)}, u32[]{:S(2)}, u32[]{:S(2)}) collective-permute-start(f32[1,384]{1,0:T(1,128)S(1)} %broadcast_in_dim.59), channel_id=1, source_target_pairs={{0,64},{64,0},{1,65},{65,1},{2,66},{66,2},{3,67},{67,3},{4,68},{68... | collective-permute-start | bytes 4616 | tf_op jit(solution)/shard_map/ppermute | solution.py:81
  197.3 5.1 %collective-permute-start.27 = (f32[1,2,384]{2,0,1:T(1,128)S(1)}, f32[1,2,384]{2,0,1:T(1,128)S(1)}, u32[]{:S(2)}, u32[]{:S(2)}) collective-permute-start(f32[1,2,384]{2,0,1:T(1,128)S(1)} %broadcast_select_fusion), channel_id=1, source_target_pairs={{0,1},{1,0},{2,3},{3,2},{4,5},{5,4},{6,7},{7,6},{8,9},{9,8},{10,11... | collective-permute-start | bytes 9224 | tf_op jit(solution)/shard_map/ppermute | solution.py:81
  202.5 3.7 %collective-permute-start.28 = (f32[2,2,384]{2,0,1:T(2,128)S(1)}, f32[2,2,384]{2,0,1:T(2,128)S(1)}, u32[]{:S(2)}, u32[]{:S(2)}) collective-permute-start(f32[2,2,384]{2,0,1:T(2,128)S(1)} %maximum_select_fusion.9), channel_id=1, source_target_pairs={{0,2},{1,3},{2,0},{3,1},{4,6},{5,7},{6,4},{7,5},{8,10},{9,11},{10,... | collective-permute-start | bytes 18440 | tf_op jit(solution)/shard_map/ppermute | solution.py:81
  202.6 4.9 %collective-permute-start.25 = (f32[4096]{0:T(1024)S(1)}, f32[4096]{0:T(1024)S(1)}, u32[]{:S(2)}, u32[]{:S(2)}) collective-permute-start(f32[4096]{0:T(1024)S(1)} %maximum_maximum_fusion), channel_id=1, source_target_pairs={{0,64},{64,0},{1,65},{65,1},{2,66},{66,2},{3,67},{67,3},{4,68},{68... | collective-permute-start | bytes 49160 | tf_op jit(solution)/shard_map/ppermute | solution.py:108
  206.2 5.3 %collective-permute-start.29 = (f32[4,2,384]{2,0,1:T(4,128)S(1)}, f32[4,2,384]{2,0,1:T(4,128)S(1)}, u32[]{:S(2)}, u32[]{:S(2)}) collective-permute-start(f32[4,2,384]{2,0,1:T(4,128)S(1)} %maximum_select_fusion.8), channel_id=1, source_target_pairs={{0,4},{1,5},{2,6},{3,7},{4,0},{5,1},{6,2},{7,3},{8,12},{9,13},{10,... | collective-permute-start | bytes 36872 | tf_op jit(solution)/shard_map/ppermute | solution.py:81
  (1 other events, 4.0 us)
Sparse Core Ops, SparseCore 0:
  9.7 69.7 all-gather.1

commit v11 on v10

--- a/solution.py
+++ b/solution.py
@@ -85,23 +85,61 @@
     return parts
 
 
+def x_shift(value, step, n_x):
+    pairs = [(i, ((i // 2 + step) % n_x) * 2 + i % 2) for i in range(2 * n_x)]
+    return lax.ppermute(value, "xc", pairs)
+
+
+def xc_gather(shard, n_x):
+    here = lax.axis_index("xc")
+    core = here % 2
+    die = [(i, i ^ 1) for i in range(2 * n_x)]
+    rows = shard.shape[0] // 2
+    from_below = x_shift(shard, 1, n_x)
+    from_above = x_shift(shard, -1, n_x)
+    other = lax.ppermute(shard, "xc", die)
+    far = jnp.concatenate([x_shift(from_below[:rows], 1, n_x), x_shift(from_above[rows:], -1, n_x)])
+    near = lax.ppermute(jnp.stack([from_above, from_below]), "xc", die)
+    other_far = lax.ppermute(far, "xc", die)
+    mine = jnp.stack([shard, from_above, far, from_below])
+    theirs = jnp.stack([other, near[0], other_far, near[1]])
+    both = jnp.where(core == 0, jnp.stack([mine, theirs], axis=1), jnp.stack([theirs, mine], axis=1))
+    return both.reshape(-1, shard.shape[1])
+
+
 def body(slab_embed, coverage_old, sel_index, cand_index):
     n_xc = 8
     col_id = lax.axis_index("col")
     zl = lax.axis_index("zl")
-    half = lax.all_gather(slab_embed, "xc", axis=0, tiled=True)
+    n_x = n_xc // 2
+    x = lax.axis_index("xc") // 2
+    shard_rows = slab_embed.shape[0]
+    half = xc_gather(slab_embed, n_x)
     first_row = (col_id * 2 + zl) * half.shape[0]
+
+    def to_local(index):
+        canonical = index - first_row
+        source = (jnp.clip(canonical, 0, half.shape[0] - 1) // shard_rows) // 2
+        offset = (source - x) % n_x
+        return jnp.where(
+            (canonical >= 0) & (canonical < half.shape[0]),
+            offset * 2 * shard_rows + canonical % (2 * shard_rows),
+            -1,
+        )
+
     zl_swap = [(0, 1), (1, 0)]
     both_sel = pair_join(sel_index, lax.ppermute(sel_index, "zl", zl_swap), zl == 0)
     both_cand = pair_join(cand_index, lax.ppermute(cand_index, "zl", zl_swap), zl == 0)
-    selected = group_masked_sum(lookup(half, both_sel, first_row))
-    chosen = group_masked_sum(lookup(half, both_cand, first_row))
+    selected = group_masked_sum(lookup(half, to_local(both_sel), 0))
+    chosen = group_masked_sum(lookup(half, to_local(both_cand), 0))
     n_sel = both_sel.shape[0]
     scores = lax.optimization_barrier(similar(jnp.concatenate([selected, chosen]), half))
-    reached = all_max(jnp.max(scores[:n_sel], axis=0), "xc", n_xc)
+    partial = jnp.roll(jnp.max(scores[:n_sel], axis=0).reshape(n_x, -1), x, axis=0).reshape(-1)
+    reached = all_max(partial, "xc", n_xc)
     old = lax.dynamic_slice_in_dim(coverage_old, zl * half.shape[0], half.shape[0])
     coverage = jnp.maximum(old, reached)
-    gain_part = jnp.sum(jnp.maximum(scores[n_sel:] - coverage[None, :], 0.0), axis=1)
+    local_coverage = jnp.roll(coverage.reshape(n_x, -1), -x, axis=0).reshape(-1)
+    gain_part = jnp.sum(jnp.maximum(scores[n_sel:] - local_coverage[None, :], 0.0), axis=1)
     parts = gather_in_order(gather_in_order(gain_part[None], "zl", 2)[None], "col", N_Y * N_Z)
     total = jnp.sum(parts.reshape(-1, gain_part.shape[0]), axis=0)
     total_gain = lax.dynamic_slice_in_dim(total, zl * cand_index.shape[0], cand_index.shape[0])

time: 219 us -> 229 us (1.046)
  local copies, waits for them, and re-layouts: 18.2 us -> 34.6 us
  between operations: 14.4 us -> 1.12 us
  other arithmetic: 8.31 us -> 15.8 us
  waiting for transfers between devices: 121 us -> 118 us
    all_gather x1 -> x0, waiting for transfers between devices: 64 us -> none  [body(): half = lax.all_gather(slab_embed, 'xc', axis=0, tiled=True)]
    ppermute x0 -> x7, waiting for transfers between devices: none -> 49.8 us  [the longest x4 49.8 us: x_shift(): return lax.ppermute(value, 'xc', pairs)]
    select_n x0 -> x1, local copies, waits for them, and re-layouts: none -> 10 us  [xc_gather(): jnp.where(core == 0, jnp.stack([mine, theirs], axis=1), jnp.stack([theirs...]
    ppermute x12, waiting for transfers between devices: 20.9 us -> 29.7 us  [y_shift(): return lax.ppermute(value, 'col', pairs)]
    ppermute x12, starting transfers between devices: 18.9 us -> 11.9 us  [y_shift(): return lax.ppermute(value, 'col', pairs)]
    ppermute x0 -> x7, starting transfers between devices: none -> 6.63 us  [the longest x4 6.54 us: x_shift(): return lax.ppermute(value, 'xc', pairs)]
    another operation x0 -> x3, other arithmetic: none -> 5.24 us  [the longest x2 3.41 us: xc_gather(): jnp.stack([mine, theirs], axis=1)]
    select_n x0 -> x1, other arithmetic: none -> 5.03 us  [xc_gather(): jnp.where(core == 0, jnp.stack([mine, theirs], axis=1), jnp.stack([theirs...]
  transfers between devices with their start and end apart: 31 -> 37, of which waited for: 23 -> 26; matrix products, arithmetic and copies ran while one was open for 5% -> 4% of each run, Pallas kernels for 0% -> 0%
where the time goes in v11:
time: 229 us
  waiting for transfers between devices  118 us (52%)
  starting transfers between devices  43.3 us (19%)
  local copies, waits for them, and re-layouts  34.6 us (15%)
  matrix products  16 us (7%)
  other arithmetic  15.8 us (7%)
    ppermute x4, waiting for transfers between devices, x_shift(): return lax.ppermute(value, 'xc', pairs)  49.8 us
    ppermute x12, waiting for transfers between devices, y_shift(): return lax.ppermute(value, 'col', pairs)  29.7 us
    dot_general x1, matrix products, similar(): lax.dot_general(left, right, (((1,), (1,)), ((), ())), precision=lax.Prec...  16 us
    gather x2, local copies, waits for them, and re-layouts, lookup(): jnp.take(source, jnp.clip(position, 0, source.shape[0] - 1), axis=0)  13 us
    ppermute x4, waiting for transfers between devices, gather_in_order(): other = lax.ppermute(parts, axis, [(i, i ^ bit) for i in range(n)])  12 us
    ppermute x12, starting transfers between devices, y_shift(): return lax.ppermute(value, 'col', pairs)  11.9 us
    select_n x1, local copies, waits for them, and re-layouts, xc_gather(): jnp.where(core == 0, jnp.stack([mine, theirs], axis=1), jnp.stack([theirs...  10 us
    ppermute x3, waiting for transfers between devices, all_max(): lax.ppermute(value, axis, [(i, i ^ bit) for i in range(n)])  8.79 us
  transfers between devices with their start and end apart: 37, of which 26 were waited for; matrix products, arithmetic and copies ran while one was open for 4% of the time, Pallas kernels for 0%

profile of v11, /device:TPU:0, one launch (start us, length us, event | category | flops | bytes accessed | tf_op | source)
XLA Modules:
  0.0 229.1 jit_solution(16303725884115833781)
XLA Ops:
  3.9 34.2 %collective-permute-done.2 = f32[512,768]{1,0:T(8,128)S(1)} collective-permute-done((f32[512,768]{1,0:T(8,128)}, f32[512,768]{1,0:T(8,128)S(1)}, u32[]{:S(2)}, u32[]{:S(2)}) %collective-permute-start.2) | collective-permute-done | bytes 1572896 | tf_op jit(solution)/shard_map/ppermute | solution.py:90
  47.3 15.4 %collective-permute-done.3 = f32[256,768]{1,0:T(8,128)} collective-permute-done((f32[256,768]{1,0:T(8,128)}, f32[256,768]{1,0:T(8,128)}, u32[]{:S(2)}, u32[]{:S(2)}) %collective-permute-start.3) | collective-permute-done | bytes 786464 | tf_op jit(solution)/shard_map/ppermute | solution.py:90
  69.2 2.1 fusion.45
  73.0 5.0 %maximum_select_fusion = f32[4,2,512,768]{3,2,0,1:T(8,128)} fusion(f32[4,1,512,768]{3,2,0,1:T(8,128)S(1)} %maximum_bitcast_fusion.1, f32[4,1,512,768]{3,2,0,1:T(8,128)S(1)} %maximum_bitcast_fusion, pred[]{:T(512)S(6)} %eq.56), kind=kLoop, calls=%fused_computation.2 | loop fusion | flops 9437184 | bytes 25165824 | tf_op jit(solution)/shard_map/jit(_where)/select_n | solution.py:106
  78.0 10.0 %copy.8 = f32[4,2,512,768]{3,2,1,0:T(8,128)} copy(f32[4,2,512,768]{3,2,0,1:T(8,128)} %maximum_select_fusion) | data formatting | bytes 25165824 | tf_op jit(solution)/shard_map/jit(_where)/select_n | solution.py:106
  88.1 7.1 %gather_fusion.1 = f32[384,768]{1,0:T(8,128)S(1)} fusion(f32[4096,768]{1,0:T(8,128)} %bitcast.54, s32[1024]{0:T(1024)S(1)} %pad_clamp_fusion), kind=kCustom, calls=%fused_computation.1 | custom fusion | bytes 2360832 | tf_op jit(solution)/shard_map/jit(_take)/gather | solution.py:23
  95.1 6.0 %gather_fusion = f32[256,768]{1,0:T(8,128)S(1)} fusion(f32[4096,768]{1,0:T(8,128)} %bitcast.55, s32[1024]{0:T(1024)S(1)} %pad_clamp_fusion.1), kind=kCustom, calls=%fused_computation | custom fusion | bytes 1573888 | tf_op jit(solution)/shard_map/jit(_take)/gather | solution.py:23
  101.3 3.1 %collective-permute-start.10 = (f32[64,768]{1,0:T(8,128)S(1)}, f32[64,768]{1,0:T(8,128)S(1)}, u32[]{:S(2)}, u32[]{:S(2)}) collective-permute-start(f32[64,768]{1,0:T(8,128)S(1)} %get-tuple-element.13), channel_id=1, source_target_pairs={{0,6},{1,7},{2,0},{3,1},{4,2},{5,3},{6,4},{7,5},{8,14},{9,15},{10,... | collective-permute-start | bytes 589832 | tf_op jit(solution)/shard_map/ppermute | solution.py:33
  106.2 7.2 %collective-permute-done.10 = f32[64,768]{1,0:T(8,128)S(1)} collective-permute-done((f32[64,768]{1,0:T(8,128)S(1)}, f32[64,768]{1,0:T(8,128)S(1)}, u32[]{:S(2)}, u32[]{:S(2)}) %collective-permute-start.10) | collective-permute-done | bytes 196640 | tf_op jit(solution)/shard_map/ppermute | solution.py:33
  113.7 3.4 %collective-permute-done.8 = f32[64,768]{1,0:T(8,128)S(1)} collective-permute-done((f32[64,768]{1,0:T(8,128)S(1)}, f32[64,768]{1,0:T(8,128)S(1)}, u32[]{:S(2)}, u32[]{:S(2)}) %collective-permute-start.8) | collective-permute-done | bytes 196640 | tf_op jit(solution)/shard_map/ppermute | solution.py:33
  119.6 2.4 %collective-permute-done.11 = f32[32,768]{1,0:T(8,128)S(1)} collective-permute-done((f32[32,768]{1,0:T(8,128)S(1)}, f32[32,768]{1,0:T(8,128)S(1)}, u32[]{:S(2)}, u32[]{:S(2)}) %collective-permute-start.11) | collective-permute-done | bytes 98336 | tf_op jit(solution)/shard_map/ppermute | solution.py:60
  122.0 3.7 %collective-permute-start.12 = (f32[16,768]{1,0:T(8,128)S(1)}, f32[16,768]{1,0:T(8,128)S(1)}, u32[]{:S(2)}, u32[]{:S(2)}) collective-permute-start(f32[16,768]{1,0:T(8,128)S(1)} %slice_select_fusion.3), channel_id=1, source_target_pairs={{0,1},{1,0},{2,3},{3,2},{4,5},{5,4},{6,7},{7,6},{8,9},{9,8},{10,11... | collective-permute-start | bytes 147464 | tf_op jit(solution)/shard_map/ppermute | solution.py:62
  127.4 2.2 collective-permute-done.20
  129.6 4.7 %collective-permute-done.19 = f32[96,768]{1,0:T(8,128)S(1)} collective-permute-done((f32[96,768]{1,0:T(8,128)S(1)}, f32[96,768]{1,0:T(8,128)S(1)}, u32[]{:S(2)}, u32[]{:S(2)}) %collective-permute-start.19) | collective-permute-done | bytes 294944 | tf_op jit(solution)/shard_map/ppermute | solution.py:33
  134.4 3.8 %collective-permute-start.13 = (f32[16,768]{1,0:T(8,128)S(1)}, f32[16,768]{1,0:T(8,128)S(1)}, u32[]{:S(2)}, u32[]{:S(2)}) collective-permute-start(f32[16,768]{1,0:T(8,128)S(1)} %select_add_fusion.3), channel_id=1, source_target_pairs={{0,1},{1,0},{2,3},{3,2},{4,5},{5,4},{6,7},{7,6},{8,9},{9,8},{10,11... | collective-permute-start | bytes 147464 | tf_op jit(solution)/shard_map/ppermute | solution.py:63
  140.3 2.1 collective-permute-start.14
  142.4 2.6 %collective-permute-done.22 = f32[48,768]{1,0:T(8,128)S(1)} collective-permute-done((f32[48,768]{1,0:T(8,128)S(1)}, f32[48,768]{1,0:T(8,128)S(1)}, u32[]{:S(2)}, u32[]{:S(2)}) %collective-permute-start.22) | collective-permute-done | bytes 147488 | tf_op jit(solution)/shard_map/ppermute | solution.py:60
  149.0 2.2 collective-permute-done.23
  152.3 5.4 %collective-permute-done.24 = f32[24,768]{1,0:T(8,128)S(1)} collective-permute-done((f32[24,768]{1,0:T(8,128)S(1)}, f32[24,768]{1,0:T(8,128)S(1)}, u32[]{:S(2)}, u32[]{:S(2)}) %collective-permute-start.24) | collective-permute-done | bytes 73760 | tf_op jit(solution)/shard_map/ppermute | solution.py:63
  159.0 3.9 %collective-permute-done.25 = f32[48,768]{1,0:T(8,128)S(1)} collective-permute-done((f32[48,768]{1,0:T(8,128)S(1)}, f32[48,768]{1,0:T(8,128)S(1)}, u32[]{:S(2)}, u32[]{:S(2)}) %collective-permute-start.25) | collective-permute-done | bytes 147488 | tf_op jit(solution)/shard_map/ppermute | solution.py:64
  166.0 4.7 %collective-permute-done.26 = f32[96,768]{1,0:T(8,128)S(1)} collective-permute-done((f32[96,768]{1,0:T(8,128)S(1)}, f32[96,768]{1,0:T(8,128)S(1)}, u32[]{:S(2)}, u32[]{:S(2)}) %collective-permute-start.26) | collective-permute-done | bytes 294944 | tf_op jit(solution)/shard_map/ppermute | solution.py:33
  170.8 2.4 %collective-permute-done.27 = f32[96,768]{1,0:T(8,128)S(1)} collective-permute-done((f32[96,768]{1,0:T(8,128)S(1)}, f32[96,768]{1,0:T(8,128)S(1)}, u32[]{:S(2)}, u32[]{:S(2)}) %collective-permute-start.27) | collective-permute-done | bytes 294944 | tf_op jit(solution)/shard_map/ppermute | solution.py:33
  173.3 3.0 %collective-permute-done.28 = f32[96,768]{1,0:T(8,128)S(1)} collective-permute-done((f32[96,768]{1,0:T(8,128)S(1)}, f32[96,768]{1,0:T(8,128)S(1)}, u32[]{:S(2)}, u32[]{:S(2)}) %collective-permute-start.28) | collective-permute-done | bytes 294944 | tf_op jit(solution)/shard_map/ppermute | solution.py:33
  176.5 16.0 %fusion.2 = f32[640,4096]{1,0:T(8,128)S(1)} fusion(f32[4096,768]{1,0:T(8,128)} %bitcast.56, f32[384,768]{1,0:T(8,128)S(1)} %bitcast.61, f32[256,768]{1,0:T(8,128)S(1)} %bitcast.63), kind=kOutput, calls=%fused_computation.10 | convolution fusion | flops 12080087040 | bytes 25034752 | tf_op jit(solution)/shard_map/dot_general | solution.py:11
  192.5 4.0 %copy-done = f32[640,4096]{1,0:T(8,128)} copy-done((f32[640,4096]{1,0:T(8,128)}, f32[640,4096]{1,0:T(8,128)S(1)}, u32[]{:S(2)}) %copy-start) | copy-done | bytes 10485784
  198.0 3.7 %collective-permute-done.30 = f32[4096]{0:T(1024)S(1)} collective-permute-done((f32[4096]{0:T(1024)S(1)}, f32[4096]{0:T(1024)S(1)}, u32[]{:S(2)}, u32[]{:S(2)}) %collective-permute-start.30) | collective-permute-done | bytes 16416 | tf_op jit(solution)/shard_map/ppermute | solution.py:72
  203.1 3.9 %collective-permute-done.31 = f32[4096]{0:T(1024)S(1)} collective-permute-done((f32[4096]{0:T(1024)S(1)}, f32[4096]{0:T(1024)S(1)}, u32[]{:S(2)}, u32[]{:S(2)}) %collective-permute-start.31) | collective-permute-done | bytes 16416 | tf_op jit(solution)/shard_map/ppermute | solution.py:72
  207.1 3.5 %fusion.1 = f32[384]{0:T(512)S(1)} fusion(f32[640,4096]{1,0:T(8,128)} %copy-done, f32[4096]{0:T(1024)S(1)} %bitcast.73), kind=kLoop, calls=%fused_computation.5 | loop fusion | flops 4718208 | bytes 6309376 | tf_op jit(solution)/shard_map/reduce_sum | solution.py:142
  211.7 2.6 %collective-permute-done.33 = f32[1,384]{1,0:T(1,128)S(1)} collective-permute-done((f32[1,384]{1,0:T(1,128)S(1)}, f32[1,384]{1,0:T(1,128)S(1)}, u32[]{:S(2)}, u32[]{:S(2)}) %collective-permute-start.33) | collective-permute-done | bytes 1568 | tf_op jit(solution)/shard_map/ppermute | solution.py:81
  215.8 3.6 %collective-permute-done.34 = f32[1,2,384]{2,0,1:T(1,128)S(1)} collective-permute-done((f32[1,2,384]{2,0,1:T(1,128)S(1)}, f32[1,2,384]{2,0,1:T(1,128)S(1)}, u32[]{:S(2)}, u32[]{:S(2)}) %collective-permute-start.34) | collective-permute-done | bytes 3104 | tf_op jit(solution)/shard_map/ppermute | solution.py:81
  220.5 2.6 %collective-permute-done.35 = f32[2,2,384]{2,0,1:T(2,128)S(1)} collective-permute-done((f32[2,2,384]{2,0,1:T(2,128)S(1)}, f32[2,2,384]{2,0,1:T(2,128)S(1)}, u32[]{:S(2)}, u32[]{:S(2)}) %collective-permute-start.35) | collective-permute-done | bytes 6176 | tf_op jit(solution)/shard_map/ppermute | solution.py:81
  225.3 3.1 %collective-permute-done.36 = f32[4,2,384]{2,0,1:T(4,128)S(1)} collective-permute-done((f32[4,2,384]{2,0,1:T(4,128)S(1)}, f32[4,2,384]{2,0,1:T(4,128)S(1)}, u32[]{:S(2)}, u32[]{:S(2)}) %collective-permute-start.36) | collective-permute-done | bytes 12320 | tf_op jit(solution)/shard_map/ppermute | solution.py:81
  (126 shorter events, 48.4 us)
Async XLA Ops:
  0.6 37.5 %collective-permute-start.2 = (f32[512,768]{1,0:T(8,128)}, f32[512,768]{1,0:T(8,128)S(1)}, u32[]{:S(2)}, u32[]{:S(2)}) collective-permute-start(f32[512,768]{1,0:T(8,128)} %param.6), channel_id=1, source_target_pairs={{0,16},{8,24},{16,32},{24,40},{32,48},{40,56},{48,0},{56,8},{1,17}... | collective-permute-start | bytes 4718600 | tf_op jit(solution)/shard_map/ppermute | solution.py:90
  2.3 36.1 %collective-permute-start.1 = (f32[512,768]{1,0:T(8,128)}, f32[512,768]{1,0:T(8,128)S(1)}, u32[]{:S(2)}, u32[]{:S(2)}) collective-permute-start(f32[512,768]{1,0:T(8,128)} %param.6), channel_id=1, source_target_pairs={{0,48},{8,56},{16,0},{24,8},{32,16},{40,24},{48,32},{56,40},{1,49}... | collective-permute-start | bytes 4718600 | tf_op jit(solution)/shard_map/ppermute | solution.py:90
  40.2 29.0 %collective-permute-start.6 = (f32[2,512,768]{2,1,0:T(8,128)}, f32[2,512,768]{2,1,0:T(8,128)}, u32[]{:S(2)}, u32[]{:S(2)}) collective-permute-start(f32[2,512,768]{2,1,0:T(8,128)} %pad_maximum_fusion), channel_id=1, source_target_pairs={{0,8},{8,0},{16,24},{24,16},{32,40},{40,32},{48,56},{56,48},{1,9},... | collective-permute-start | bytes 9437192 | tf_op jit(solution)/shard_map/ppermute | solution.py:102
  41.2 21.5 %collective-permute-start.3 = (f32[256,768]{1,0:T(8,128)}, f32[256,768]{1,0:T(8,128)}, u32[]{:S(2)}, u32[]{:S(2)}) collective-permute-start(f32[256,768]{1,0:T(8,128)} %slice.76), channel_id=1, source_target_pairs={{0,16},{8,24},{16,32},{24,40},{32,48},{40,56},{48,0},{56,8},{1,17}... | collective-permute-start | bytes 2359304 | tf_op jit(solution)/shard_map/ppermute | solution.py:90
  43.6 22.2 %collective-permute-start.4 = (f32[256,768]{1,0:T(8,128)}, f32[256,768]{1,0:T(8,128)}, u32[]{:S(2)}, u32[]{:S(2)}) collective-permute-start(f32[256,768]{1,0:T(8,128)} %slice.77), channel_id=1, source_target_pairs={{0,48},{8,56},{16,0},{24,8},{32,16},{40,24},{48,32},{56,40},{1,49}... | collective-permute-start | bytes 2359304 | tf_op jit(solution)/shard_map/ppermute | solution.py:90
  45.3 25.9 %collective-permute-start.5 = (f32[512,768]{1,0:T(8,128)}, f32[512,768]{1,0:T(8,128)}, u32[]{:S(2)}, u32[]{:S(2)}) collective-permute-start(f32[512,768]{1,0:T(8,128)} %param.6), channel_id=1, source_target_pairs={{0,8},{8,0},{16,24},{24,16},{32,40},{40,32},{48,56},{56,48},{1,9},... | collective-permute-start | bytes 4718600 | tf_op jit(solution)/shard_map/ppermute | solution.py:100
  45.4 21.8 %collective-permute-start.18 = (s32[192]{0:T(256)S(1)}, s32[192]{0:T(256)S(1)}, u32[]{:S(2)}, u32[]{:S(2)}) collective-permute-start(s32[192]{0:T(256)S(1)} %copy-done.2), channel_id=1, source_target_pairs={{0,64},{64,0},{1,65},{65,1},{2,66},{66,2},{3,67},{67,3},{4,68},{68... | collective-permute-start | bytes 2312 | tf_op jit(solution)/shard_map/ppermute | solution.py:132
  62.6 4.4 %collective-permute-start = (s32[128]{0:T(128)S(1)}, s32[128]{0:T(128)S(1)}, u32[]{:S(2)}, u32[]{:S(2)}) collective-permute-start(s32[128]{0:T(128)S(1)} %copy-done.3), channel_id=1, source_target_pairs={{0,64},{64,0},{1,65},{65,1},{2,66},{66,2},{3,67},{67,3},{4,68},{68... | collective-permute-start | bytes 1544 | tf_op jit(solution)/shard_map/ppermute | solution.py:131
  101.3 12.1 %collective-permute-start.10 = (f32[64,768]{1,0:T(8,128)S(1)}, f32[64,768]{1,0:T(8,128)S(1)}, u32[]{:S(2)}, u32[]{:S(2)}) collective-permute-start(f32[64,768]{1,0:T(8,128)S(1)} %get-tuple-element.13), channel_id=1, source_target_pairs={{0,6},{1,7},{2,0},{3,1},{4,2},{5,3},{6,4},{7,5},{8,14},{9,15},{10,... | collective-permute-start | bytes 589832 | tf_op jit(solution)/shard_map/ppermute | solution.py:33
  104.4 9.3 %collective-permute-start.9 = (f32[64,768]{1,0:T(8,128)S(1)}, f32[64,768]{1,0:T(8,128)S(1)}, u32[]{:S(2)}, u32[]{:S(2)}) collective-permute-start(f32[64,768]{1,0:T(8,128)S(1)} %get-tuple-element.14), channel_id=1, source_target_pairs={{0,4},{1,5},{2,6},{3,7},{4,0},{5,1},{6,2},{7,3},{8,12},{9,13},{10,... | collective-permute-start | bytes 589832 | tf_op jit(solution)/shard_map/ppermute | solution.py:33
  105.0 12.1 %collective-permute-start.8 = (f32[64,768]{1,0:T(8,128)S(1)}, f32[64,768]{1,0:T(8,128)S(1)}, u32[]{:S(2)}, u32[]{:S(2)}) collective-permute-start(f32[64,768]{1,0:T(8,128)S(1)} %get-tuple-element.12), channel_id=1, source_target_pairs={{0,2},{1,3},{2,4},{3,5},{4,6},{5,7},{6,0},{7,1},{8,10},{9,11},{10,... | collective-permute-start | bytes 589832 | tf_op jit(solution)/shard_map/ppermute | solution.py:33
  117.2 4.8 %collective-permute-start.11 = (f32[32,768]{1,0:T(8,128)S(1)}, f32[32,768]{1,0:T(8,128)S(1)}, u32[]{:S(2)}, u32[]{:S(2)}) collective-permute-start(f32[32,768]{1,0:T(8,128)S(1)} %slice_select_fusion.1), channel_id=1, source_target_pairs={{0,64},{64,0},{1,65},{65,1},{2,66},{66,2},{3,67},{67,3},{4,68},{68... | collective-permute-start | bytes 294920 | tf_op jit(solution)/shard_map/ppermute | solution.py:60
  117.5 10.0 %collective-permute-start.21 = (f32[96,768]{1,0:T(8,128)S(1)}, f32[96,768]{1,0:T(8,128)S(1)}, u32[]{:S(2)}, u32[]{:S(2)}) collective-permute-start(f32[96,768]{1,0:T(8,128)S(1)} %get-tuple-element.10), channel_id=1, source_target_pairs={{0,6},{1,7},{2,0},{3,1},{4,2},{5,3},{6,4},{7,5},{8,14},{9,15},{10,... | collective-permute-start | bytes 884744 | tf_op jit(solution)/shard_map/ppermute | solution.py:33
  118.1 11.5 %collective-permute-start.20 = (f32[96,768]{1,0:T(8,128)S(1)}, f32[96,768]{1,0:T(8,128)S(1)}, u32[]{:S(2)}, u32[]{:S(2)}) collective-permute-start(f32[96,768]{1,0:T(8,128)S(1)} %get-tuple-element.11), channel_id=1, source_target_pairs={{0,4},{1,5},{2,6},{3,7},{4,0},{5,1},{6,2},{7,3},{8,12},{9,13},{10,... | collective-permute-start | bytes 884744 | tf_op jit(solution)/shard_map/ppermute | solution.py:33
  118.7 15.6 %collective-permute-start.19 = (f32[96,768]{1,0:T(8,128)S(1)}, f32[96,768]{1,0:T(8,128)S(1)}, u32[]{:S(2)}, u32[]{:S(2)}) collective-permute-start(f32[96,768]{1,0:T(8,128)S(1)} %get-tuple-element.9), channel_id=1, source_target_pairs={{0,2},{1,3},{2,4},{3,5},{4,6},{5,7},{6,0},{7,1},{8,10},{9,11},{10,... | collective-permute-start | bytes 884744 | tf_op jit(solution)/shard_map/ppermute | solution.py:33
  122.0 12.3 %collective-permute-start.12 = (f32[16,768]{1,0:T(8,128)S(1)}, f32[16,768]{1,0:T(8,128)S(1)}, u32[]{:S(2)}, u32[]{:S(2)}) collective-permute-start(f32[16,768]{1,0:T(8,128)S(1)} %slice_select_fusion.3), channel_id=1, source_target_pairs={{0,1},{1,0},{2,3},{3,2},{4,5},{5,4},{6,7},{7,6},{8,9},{9,8},{10,11... | collective-permute-start | bytes 147464 | tf_op jit(solution)/shard_map/ppermute | solution.py:62
  134.4 5.9 %collective-permute-start.13 = (f32[16,768]{1,0:T(8,128)S(1)}, f32[16,768]{1,0:T(8,128)S(1)}, u32[]{:S(2)}, u32[]{:S(2)}) collective-permute-start(f32[16,768]{1,0:T(8,128)S(1)} %select_add_fusion.3), channel_id=1, source_target_pairs={{0,1},{1,0},{2,3},{3,2},{4,5},{5,4},{6,7},{7,6},{8,9},{9,8},{10,11... | collective-permute-start | bytes 147464 | tf_op jit(solution)/shard_map/ppermute | solution.py:63
  138.2 6.8 %collective-permute-start.22 = (f32[48,768]{1,0:T(8,128)S(1)}, f32[48,768]{1,0:T(8,128)S(1)}, u32[]{:S(2)}, u32[]{:S(2)}) collective-permute-start(f32[48,768]{1,0:T(8,128)S(1)} %slice_select_fusion), channel_id=1, source_target_pairs={{0,64},{64,0},{1,65},{65,1},{2,66},{66,2},{3,67},{67,3},{4,68},{68... | collective-permute-start | bytes 442376 | tf_op jit(solution)/shard_map/ppermute | solution.py:60
  140.3 6.6 %collective-permute-start.14 = (f32[32,768]{1,0:T(8,128)S(1)}, f32[32,768]{1,0:T(8,128)S(1)}, u32[]{:S(2)}, u32[]{:S(2)}) collective-permute-start(f32[32,768]{1,0:T(8,128)S(1)} %maximum_select_fusion.6), channel_id=1, source_target_pairs={{0,64},{64,0},{1,65},{65,1},{2,66},{66,2},{3,67},{67,3},{4,68},{68... | collective-permute-start | bytes 294920 | tf_op jit(solution)/shard_map/ppermute | solution.py:64
  145.1 6.1 %collective-permute-start.23 = (f32[24,768]{1,0:T(8,128)S(1)}, f32[24,768]{1,0:T(8,128)S(1)}, u32[]{:S(2)}, u32[]{:S(2)}) collective-permute-start(f32[24,768]{1,0:T(8,128)S(1)} %slice_select_fusion.2), channel_id=1, source_target_pairs={{0,1},{1,0},{2,3},{3,2},{4,5},{5,4},{6,7},{7,6},{8,9},{9,8},{10,11... | collective-permute-start | bytes 221192 | tf_op jit(solution)/shard_map/ppermute | solution.py:62
  146.9 12.0 %collective-permute-start.15 = (f32[64,768]{1,0:T(8,128)S(1)}, f32[64,768]{1,0:T(8,128)S(1)}, u32[]{:S(2)}, u32[]{:S(2)}) collective-permute-start(f32[64,768]{1,0:T(8,128)S(1)} %maximum_select_fusion.4), channel_id=1, source_target_pairs={{0,6},{1,7},{2,0},{3,1},{4,2},{5,3},{6,4},{7,5},{8,14},{9,15},{10,... | collective-permute-start | bytes 589832 | tf_op jit(solution)/shard_map/ppermute | solution.py:33
  147.5 11.4 %collective-permute-start.16 = (f32[64,768]{1,0:T(8,128)S(1)}, f32[64,768]{1,0:T(8,128)S(1)}, u32[]{:S(2)}, u32[]{:S(2)}) collective-permute-start(f32[64,768]{1,0:T(8,128)S(1)} %maximum_select_fusion.4), channel_id=1, source_target_pairs={{0,4},{1,5},{2,6},{3,7},{4,0},{5,1},{6,2},{7,3},{8,12},{9,13},{10,... | collective-permute-start | bytes 589832 | tf_op jit(solution)/shard_map/ppermute | solution.py:33
  147.7 11.3 %collective-permute-start.17 = (f32[64,768]{1,0:T(8,128)S(1)}, f32[64,768]{1,0:T(8,128)S(1)}, u32[]{:S(2)}, u32[]{:S(2)}) collective-permute-start(f32[64,768]{1,0:T(8,128)S(1)} %maximum_select_fusion.4), channel_id=1, source_target_pairs={{0,2},{1,3},{2,4},{3,5},{4,6},{5,7},{6,0},{7,1},{8,10},{9,11},{10,... | collective-permute-start | bytes 589832 | tf_op jit(solution)/shard_map/ppermute | solution.py:33
  151.2 6.5 %collective-permute-start.24 = (f32[24,768]{1,0:T(8,128)S(1)}, f32[24,768]{1,0:T(8,128)S(1)}, u32[]{:S(2)}, u32[]{:S(2)}) collective-permute-start(f32[24,768]{1,0:T(8,128)S(1)} %select_add_fusion.2), channel_id=1, source_target_pairs={{0,1},{1,0},{2,3},{3,2},{4,5},{5,4},{6,7},{7,6},{8,9},{9,8},{10,11... | collective-permute-start | bytes 221192 | tf_op jit(solution)/shard_map/ppermute | solution.py:63
  157.7 5.2 %collective-permute-start.25 = (f32[48,768]{1,0:T(8,128)S(1)}, f32[48,768]{1,0:T(8,128)S(1)}, u32[]{:S(2)}, u32[]{:S(2)}) collective-permute-start(f32[48,768]{1,0:T(8,128)S(1)} %maximum_select_fusion.5), channel_id=1, source_target_pairs={{0,64},{64,0},{1,65},{65,1},{2,66},{66,2},{3,67},{67,3},{4,68},{68... | collective-permute-start | bytes 442376 | tf_op jit(solution)/shard_map/ppermute | solution.py:64
  162.9 7.8 %collective-permute-start.26 = (f32[96,768]{1,0:T(8,128)S(1)}, f32[96,768]{1,0:T(8,128)S(1)}, u32[]{:S(2)}, u32[]{:S(2)}) collective-permute-start(f32[96,768]{1,0:T(8,128)S(1)} %maximum_select_fusion.2), channel_id=1, source_target_pairs={{0,6},{1,7},{2,0},{3,1},{4,2},{5,3},{6,4},{7,5},{8,14},{9,15},{10,... | collective-permute-start | bytes 884744 | tf_op jit(solution)/shard_map/ppermute | solution.py:33
  163.1 10.1 %collective-permute-start.27 = (f32[96,768]{1,0:T(8,128)S(1)}, f32[96,768]{1,0:T(8,128)S(1)}, u32[]{:S(2)}, u32[]{:S(2)}) collective-permute-start(f32[96,768]{1,0:T(8,128)S(1)} %maximum_select_fusion.2), channel_id=1, source_target_pairs={{0,4},{1,5},{2,6},{3,7},{4,0},{5,1},{6,2},{7,3},{8,12},{9,13},{10,... | collective-permute-start | bytes 884744 | tf_op jit(solution)/shard_map/ppermute | solution.py:33
  164.6 11.6 %collective-permute-start.28 = (f32[96,768]{1,0:T(8,128)S(1)}, f32[96,768]{1,0:T(8,128)S(1)}, u32[]{:S(2)}, u32[]{:S(2)}) collective-permute-start(f32[96,768]{1,0:T(8,128)S(1)} %maximum_select_fusion.2), channel_id=1, source_target_pairs={{0,2},{1,3},{2,4},{3,5},{4,6},{5,7},{6,0},{7,1},{8,10},{9,11},{10,... | collective-permute-start | bytes 884744 | tf_op jit(solution)/shard_map/ppermute | solution.py:33
  201.8 5.2 %collective-permute-start.31 = (f32[4096]{0:T(1024)S(1)}, f32[4096]{0:T(1024)S(1)}, u32[]{:S(2)}, u32[]{:S(2)}) collective-permute-start(f32[4096]{0:T(1024)S(1)} %max.31), channel_id=1, source_target_pairs={{0,32},{8,40},{16,48},{24,56},{32,0},{40,8},{48,16},{56,24},{1,33}... | collective-permute-start | bytes 49160 | tf_op jit(solution)/shard_map/ppermute | solution.py:72
  214.3 5.1 %collective-permute-start.34 = (f32[1,2,384]{2,0,1:T(1,128)S(1)}, f32[1,2,384]{2,0,1:T(1,128)S(1)}, u32[]{:S(2)}, u32[]{:S(2)}) collective-permute-start(f32[1,2,384]{2,0,1:T(1,128)S(1)} %broadcast_select_fusion), channel_id=1, source_target_pairs={{0,1},{1,0},{2,3},{3,2},{4,5},{5,4},{6,7},{7,6},{8,9},{9,8},{10,11... | collective-permute-start | bytes 9224 | tf_op jit(solution)/shard_map/ppermute | solution.py:81
  219.5 5.2 %collective-permute-start.32 = (f32[4096]{0:T(1024)S(1)}, f32[4096]{0:T(1024)S(1)}, u32[]{:S(2)}, u32[]{:S(2)}) collective-permute-start(f32[4096]{0:T(1024)S(1)} %maximum_maximum_fusion), channel_id=1, source_target_pairs={{0,64},{64,0},{1,65},{65,1},{2,66},{66,2},{3,67},{67,3},{4,68},{68... | collective-permute-start | bytes 49160 | tf_op jit(solution)/shard_map/ppermute | solution.py:146
  223.1 5.3 %collective-permute-start.36 = (f32[4,2,384]{2,0,1:T(4,128)S(1)}, f32[4,2,384]{2,0,1:T(4,128)S(1)}, u32[]{:S(2)}, u32[]{:S(2)}) collective-permute-start(f32[4,2,384]{2,0,1:T(4,128)S(1)} %maximum_select_fusion.9), channel_id=1, source_target_pairs={{0,4},{1,5},{2,6},{3,7},{4,0},{5,1},{6,2},{7,3},{8,12},{9,13},{10,... | collective-permute-start | bytes 36872 | tf_op jit(solution)/shard_map/ppermute | solution.py:81
  (9 other events, 58.9 us)

commit v12 on v11

--- a/solution.py
+++ b/solution.py
@@ -91,20 +91,19 @@
 
 
 def xc_gather(shard, n_x):
-    here = lax.axis_index("xc")
-    core = here % 2
     die = [(i, i ^ 1) for i in range(2 * n_x)]
     rows = shard.shape[0] // 2
     from_below = x_shift(shard, 1, n_x)
     from_above = x_shift(shard, -1, n_x)
     other = lax.ppermute(shard, "xc", die)
-    far = jnp.concatenate([x_shift(from_below[:rows], 1, n_x), x_shift(from_above[rows:], -1, n_x)])
+    far_low = x_shift(from_below[:rows], 1, n_x)
+    far_high = x_shift(from_above[rows:], -1, n_x)
     near = lax.ppermute(jnp.stack([from_above, from_below]), "xc", die)
-    other_far = lax.ppermute(far, "xc", die)
-    mine = jnp.stack([shard, from_above, far, from_below])
-    theirs = jnp.stack([other, near[0], other_far, near[1]])
-    both = jnp.where(core == 0, jnp.stack([mine, theirs], axis=1), jnp.stack([theirs, mine], axis=1))
-    return both.reshape(-1, shard.shape[1])
+    other_far_low = lax.ppermute(far_low, "xc", die)
+    other_far_high = lax.ppermute(far_high, "xc", die)
+    return jnp.concatenate(
+        [shard, other, from_above, near[0], far_low, far_high, other_far_low, other_far_high, from_below, near[1]]
+    )
 
 
 def body(slab_embed, coverage_old, sel_index, cand_index):
@@ -113,19 +112,29 @@
     zl = lax.axis_index("zl")
     n_x = n_xc // 2
     x = lax.axis_index("xc") // 2
+    core = lax.axis_index("xc") % 2
     shard_rows = slab_embed.shape[0]
     half = xc_gather(slab_embed, n_x)
     first_row = (col_id * 2 + zl) * half.shape[0]
 
     def to_local(index):
         canonical = index - first_row
-        source = (jnp.clip(canonical, 0, half.shape[0] - 1) // shard_rows) // 2
-        offset = (source - x) % n_x
+        source = jnp.clip(canonical, 0, half.shape[0] - 1) // shard_rows
+        offset = (source // 2 - x) % n_x
         return jnp.where(
             (canonical >= 0) & (canonical < half.shape[0]),
-            offset * 2 * shard_rows + canonical % (2 * shard_rows),
+            (offset * 2 + (source % 2 ^ core)) * shard_rows + canonical % shard_rows,
             -1,
         )
+
+    def to_canonical(value):
+        parts = value.reshape(n_x, 2, -1)
+        parts = jnp.where(core == 0, parts, parts[:, ::-1])
+        return jnp.roll(parts, x, axis=0).reshape(-1)
+
+    def to_relative(value):
+        parts = jnp.roll(value.reshape(n_x, 2, -1), -x, axis=0)
+        return jnp.where(core == 0, parts, parts[:, ::-1]).reshape(-1)
 
     zl_swap = [(0, 1), (1, 0)]
     both_sel = pair_join(sel_index, lax.ppermute(sel_index, "zl", zl_swap), zl == 0)
@@ -134,11 +143,11 @@
     chosen = group_masked_sum(lookup(half, to_local(both_cand), 0))
     n_sel = both_sel.shape[0]
     scores = lax.optimization_barrier(similar(jnp.concatenate([selected, chosen]), half))
-    partial = jnp.roll(jnp.max(scores[:n_sel], axis=0).reshape(n_x, -1), x, axis=0).reshape(-1)
+    partial = to_canonical(jnp.max(scores[:n_sel], axis=0))
     reached = all_max(partial, "xc", n_xc)
     old = lax.dynamic_slice_in_dim(coverage_old, zl * half.shape[0], half.shape[0])
     coverage = jnp.maximum(old, reached)
-    local_coverage = jnp.roll(coverage.reshape(n_x, -1), -x, axis=0).reshape(-1)
+    local_coverage = to_relative(coverage)
     gain_part = jnp.sum(jnp.maximum(scores[n_sel:] - local_coverage[None, :], 0.0), axis=1)
     parts = gather_in_order(gather_in_order(gain_part[None], "zl", 2)[None], "col", N_Y * N_Z)
     total = jnp.sum(parts.reshape(-1, gain_part.shape[0]), axis=0)

time: 229 us -> 225 us (0.983)
  other arithmetic: 15.8 us -> 7.47 us
  waiting for transfers between devices: 118 us -> 125 us
  starting transfers between devices: 43.3 us -> 39 us
    unnamed x21 -> x29, local copies, waits for them, and re-layouts: 5.39 us -> 18.6 us
    select_n x1 -> x0, local copies, waits for them, and re-layouts: 10 us -> none  [xc_gather(): jnp.where(core == 0, jnp.stack([mine, theirs], axis=1), jnp.stack([theirs...]
    select_n x1, other arithmetic: 5.03 us -> 0.01 us  [to_canonical(): parts = jnp.where(core == 0, parts, parts[:, ::-1])]
    slice x3 -> x2, local copies, waits for them, and re-layouts: 4.01 us -> 0.1 us  [the longest x1 0.05 us: xc_gather(): far_high = x_shift(from_above[rows:], -1, n_x)]
    ppermute x4, waiting for transfers between devices: 49.8 us -> 53.2 us  [x_shift(): return lax.ppermute(value, 'xc', pairs)]
    another operation x2 -> x0, other arithmetic: 3.41 us -> none  [xc_gather(): jnp.stack([mine, theirs], axis=1)]
  transfers between devices with their start and end apart: 37 -> 38, of which waited for: 26 -> 27; matrix products, arithmetic and copies ran while one was open for 4% -> 6% of each run, Pallas kernels for 0% -> 0%
where the time goes in v12:
time: 225 us
  waiting for transfers between devices  125 us (56%)
  starting transfers between devices  39 us (17%)
  local copies, waits for them, and re-layouts  35.8 us (16%)
  matrix products  16 us (7%)
  other arithmetic  7.47 us (3%)
    ppermute x4, waiting for transfers between devices, x_shift(): return lax.ppermute(value, 'xc', pairs)  53.2 us
    ppermute x12, waiting for transfers between devices, y_shift(): return lax.ppermute(value, 'col', pairs)  29.9 us
    unnamed x29, local copies, waits for them, and re-layouts  18.6 us
    dot_general x1, matrix products, similar(): lax.dot_general(left, right, (((1,), (1,)), ((), ())), precision=lax.Prec...  16 us
    gather x2, local copies, waits for them, and re-layouts, lookup(): jnp.take(source, jnp.clip(position, 0, source.shape[0] - 1), axis=0)  13 us
    ppermute x12, starting transfers between devices, y_shift(): return lax.ppermute(value, 'col', pairs)  11.8 us
    ppermute x4, waiting for transfers between devices, gather_in_order(): other = lax.ppermute(parts, axis, [(i, i ^ bit) for i in range(n)])  10.4 us
    ppermute x3, waiting for transfers between devices, all_max(): lax.ppermute(value, axis, [(i, i ^ bit) for i in range(n)])  10.1 us
  transfers between devices with their start and end apart: 38, of which 27 were waited for; matrix products, arithmetic and copies ran while one was open for 6% of the time, Pallas kernels for 0%

profile of v12, /device:TPU:0, one launch (start us, length us, event | category | flops | bytes accessed | tf_op | source)
XLA Modules:
  0.0 224.6 jit_solution(9824495737571445186)
XLA Ops:
  0.6 2.9 %collective-permute-start.2 = (f32[512,768]{1,0:T(8,128)}, f32[512,768]{1,0:T(8,128)S(1)}, u32[]{:S(2)}, u32[]{:S(2)}) collective-permute-start(f32[512,768]{1,0:T(8,128)} %param.6), channel_id=1, source_target_pairs={{0,48},{8,56},{16,0},{24,8},{32,16},{40,24},{48,32},{56,40},{1,49}... | collective-permute-start | bytes 4718600 | tf_op jit(solution)/shard_map/ppermute | solution.py:90
  3.5 34.0 %collective-permute-done.2 = f32[512,768]{1,0:T(8,128)S(1)} collective-permute-done((f32[512,768]{1,0:T(8,128)}, f32[512,768]{1,0:T(8,128)S(1)}, u32[]{:S(2)}, u32[]{:S(2)}) %collective-permute-start.2) | collective-permute-done | bytes 1572896 | tf_op jit(solution)/shard_map/ppermute | solution.py:90
  37.5 3.3 %collective-permute-done.3 = f32[512,768]{1,0:T(8,128)S(1)} collective-permute-done((f32[512,768]{1,0:T(8,128)}, f32[512,768]{1,0:T(8,128)S(1)}, u32[]{:S(2)}, u32[]{:S(2)}) %collective-permute-start.3) | collective-permute-done | bytes 1572896 | tf_op jit(solution)/shard_map/ppermute | solution.py:90
  45.2 2.7 %constant_dynamic-update-slice_fusion.7 = f32[4096,768]{1,0:T(8,128)} fusion(f32[512,768]{1,0:T(8,128)} %param.6), kind=kLoop, calls=%fused_computation.54 | loop fusion | bytes 3145728
  48.9 3.3 %collective-permute-start.6 = (f32[256,768]{1,0:T(8,128)S(1)}, f32[256,768]{1,0:T(8,128)S(1)}, u32[]{:S(2)}, u32[]{:S(2)}) collective-permute-start(f32[256,768]{1,0:T(8,128)S(1)} %slice.78), channel_id=1, source_target_pairs={{0,48},{8,56},{16,0},{24,8},{32,16},{40,24},{48,32},{56,40},{1,49}... | collective-permute-start | bytes 2359304 | tf_op jit(solution)/shard_map/ppermute | solution.py:90
  52.5 15.9 %collective-permute-done.5 = f32[256,768]{1,0:T(8,128)S(1)} collective-permute-done((f32[256,768]{1,0:T(8,128)S(1)}, f32[256,768]{1,0:T(8,128)S(1)}, u32[]{:S(2)}, u32[]{:S(2)}) %collective-permute-start.5) | collective-permute-done | bytes 786464 | tf_op jit(solution)/shard_map/ppermute | solution.py:90
  68.5 2.7 %constant_dynamic-update-slice_fusion.6 = f32[4096,768]{1,0:T(8,128)} fusion(f32[4096,768]{1,0:T(8,128)} %constant_dynamic-update-slice_fusion.7, f32[512,768]{1,0:T(8,128)} %collective-permute-done.1), kind=kLoop, calls=%fused_computation.53 | loop fusion | bytes 3145728
  72.9 2.7 %fusion.7 = f32[4096,768]{1,0:T(8,128)} fusion(f32[4096,768]{1,0:T(8,128)} %constant_dynamic-update-slice_fusion.5, f32[2,512,768]{2,1,0:T(8,128)} %collective-permute-done.4), kind=kLoop, calls=%fused_computation.14 | loop fusion | bytes 3145728
  80.7 2.7 %fusion.6 = f32[4096,768]{1,0:T(8,128)} fusion(f32[4096,768]{1,0:T(8,128)} %constant_dynamic-update-slice_fusion, f32[2,512,768]{2,1,0:T(8,128)} %collective-permute-done.4), kind=kLoop, calls=%fused_computation.12 | loop fusion | bytes 3145728 | tf_op jit(solution)/shard_map/concatenate | solution.py:104
  83.4 7.1 %gather_fusion.1 = f32[384,768]{1,0:T(8,128)S(1)} fusion(f32[4096,768]{1,0:T(8,128)} %fusion.6, s32[1024]{0:T(1024)S(1)} %pad_clamp_fusion), kind=kCustom, calls=%fused_computation.1 | custom fusion | bytes 2360832 | tf_op jit(solution)/shard_map/jit(_take)/gather | solution.py:23
  90.5 6.0 %gather_fusion = f32[256,768]{1,0:T(8,128)S(1)} fusion(f32[4096,768]{1,0:T(8,128)} %fusion.6, s32[1024]{0:T(1024)S(1)} %pad_clamp_fusion.1), kind=kCustom, calls=%fused_computation | custom fusion | bytes 1573888 | tf_op jit(solution)/shard_map/jit(_take)/gather | solution.py:23
  96.7 3.1 %collective-permute-start.11 = (f32[64,768]{1,0:T(8,128)S(1)}, f32[64,768]{1,0:T(8,128)S(1)}, u32[]{:S(2)}, u32[]{:S(2)}) collective-permute-start(f32[64,768]{1,0:T(8,128)S(1)} %get-tuple-element.11), channel_id=1, source_target_pairs={{0,6},{1,7},{2,0},{3,1},{4,2},{5,3},{6,4},{7,5},{8,14},{9,15},{10,... | collective-permute-start | bytes 589832 | tf_op jit(solution)/shard_map/ppermute | solution.py:33
  101.6 6.7 %collective-permute-done.11 = f32[64,768]{1,0:T(8,128)S(1)} collective-permute-done((f32[64,768]{1,0:T(8,128)S(1)}, f32[64,768]{1,0:T(8,128)S(1)}, u32[]{:S(2)}, u32[]{:S(2)}) %collective-permute-start.11) | collective-permute-done | bytes 196640 | tf_op jit(solution)/shard_map/ppermute | solution.py:33
  109.1 2.9 %collective-permute-done.9 = f32[64,768]{1,0:T(8,128)S(1)} collective-permute-done((f32[64,768]{1,0:T(8,128)S(1)}, f32[64,768]{1,0:T(8,128)S(1)}, u32[]{:S(2)}, u32[]{:S(2)}) %collective-permute-start.9) | collective-permute-done | bytes 196640 | tf_op jit(solution)/shard_map/ppermute | solution.py:33
  116.9 3.7 %collective-permute-start.13 = (f32[16,768]{1,0:T(8,128)S(1)}, f32[16,768]{1,0:T(8,128)S(1)}, u32[]{:S(2)}, u32[]{:S(2)}) collective-permute-start(f32[16,768]{1,0:T(8,128)S(1)} %slice_select_fusion.3), channel_id=1, source_target_pairs={{0,1},{1,0},{2,3},{3,2},{4,5},{5,4},{6,7},{7,6},{8,9},{9,8},{10,11... | collective-permute-start | bytes 147464 | tf_op jit(solution)/shard_map/ppermute | solution.py:62
  120.6 3.3 %collective-permute-done.22 = f32[96,768]{1,0:T(8,128)S(1)} collective-permute-done((f32[96,768]{1,0:T(8,128)S(1)}, f32[96,768]{1,0:T(8,128)S(1)}, u32[]{:S(2)}, u32[]{:S(2)}) %collective-permute-start.22) | collective-permute-done | bytes 294944 | tf_op jit(solution)/shard_map/ppermute | solution.py:33
  126.1 4.5 %collective-permute-done.20 = f32[96,768]{1,0:T(8,128)S(1)} collective-permute-done((f32[96,768]{1,0:T(8,128)S(1)}, f32[96,768]{1,0:T(8,128)S(1)}, u32[]{:S(2)}, u32[]{:S(2)}) %collective-permute-start.20) | collective-permute-done | bytes 294944 | tf_op jit(solution)/shard_map/ppermute | solution.py:33
  130.6 3.7 %collective-permute-start.14 = (f32[16,768]{1,0:T(8,128)S(1)}, f32[16,768]{1,0:T(8,128)S(1)}, u32[]{:S(2)}, u32[]{:S(2)}) collective-permute-start(f32[16,768]{1,0:T(8,128)S(1)} %select_add_fusion.3), channel_id=1, source_target_pairs={{0,1},{1,0},{2,3},{3,2},{4,5},{5,4},{6,7},{7,6},{8,9},{9,8},{10,11... | collective-permute-start | bytes 147464 | tf_op jit(solution)/shard_map/ppermute | solution.py:63
  134.5 2.4 %collective-permute-done.14 = f32[16,768]{1,0:T(8,128)S(1)} collective-permute-done((f32[16,768]{1,0:T(8,128)S(1)}, f32[16,768]{1,0:T(8,128)S(1)}, u32[]{:S(2)}, u32[]{:S(2)}) %collective-permute-start.14) | collective-permute-done | bytes 49184 | tf_op jit(solution)/shard_map/ppermute | solution.py:63
  137.0 3.9 %collective-permute-done.23 = f32[48,768]{1,0:T(8,128)S(1)} collective-permute-done((f32[48,768]{1,0:T(8,128)S(1)}, f32[48,768]{1,0:T(8,128)S(1)}, u32[]{:S(2)}, u32[]{:S(2)}) %collective-permute-start.23) | collective-permute-done | bytes 147488 | tf_op jit(solution)/shard_map/ppermute | solution.py:60
  147.4 6.1 %collective-permute-done.25 = f32[24,768]{1,0:T(8,128)S(1)} collective-permute-done((f32[24,768]{1,0:T(8,128)S(1)}, f32[24,768]{1,0:T(8,128)S(1)}, u32[]{:S(2)}, u32[]{:S(2)}) %collective-permute-start.25) | collective-permute-done | bytes 73760 | tf_op jit(solution)/shard_map/ppermute | solution.py:63
  154.9 3.9 %collective-permute-done.26 = f32[48,768]{1,0:T(8,128)S(1)} collective-permute-done((f32[48,768]{1,0:T(8,128)S(1)}, f32[48,768]{1,0:T(8,128)S(1)}, u32[]{:S(2)}, u32[]{:S(2)}) %collective-permute-start.26) | collective-permute-done | bytes 147488 | tf_op jit(solution)/shard_map/ppermute | solution.py:64
  161.8 3.8 %collective-permute-done.27 = f32[96,768]{1,0:T(8,128)S(1)} collective-permute-done((f32[96,768]{1,0:T(8,128)S(1)}, f32[96,768]{1,0:T(8,128)S(1)}, u32[]{:S(2)}, u32[]{:S(2)}) %collective-permute-start.27) | collective-permute-done | bytes 294944 | tf_op jit(solution)/shard_map/ppermute | solution.py:33
  165.6 2.7 %collective-permute-done.28 = f32[96,768]{1,0:T(8,128)S(1)} collective-permute-done((f32[96,768]{1,0:T(8,128)S(1)}, f32[96,768]{1,0:T(8,128)S(1)}, u32[]{:S(2)}, u32[]{:S(2)}) %collective-permute-start.28) | collective-permute-done | bytes 294944 | tf_op jit(solution)/shard_map/ppermute | solution.py:33
  168.4 3.0 %collective-permute-done.29 = f32[96,768]{1,0:T(8,128)S(1)} collective-permute-done((f32[96,768]{1,0:T(8,128)S(1)}, f32[96,768]{1,0:T(8,128)S(1)}, u32[]{:S(2)}, u32[]{:S(2)}) %collective-permute-start.29) | collective-permute-done | bytes 294944 | tf_op jit(solution)/shard_map/ppermute | solution.py:33
  171.6 16.0 %fusion.2 = f32[640,4096]{1,0:T(8,128)S(1)} fusion(f32[4096,768]{1,0:T(8,128)} %fusion.6, f32[384,768]{1,0:T(8,128)S(1)} %bitcast.52, f32[256,768]{1,0:T(8,128)S(1)} %bitcast.53), kind=kOutput, calls=%fused_computation.7 | convolution fusion | flops 12080087040 | bytes 25034752 | tf_op jit(solution)/shard_map/dot_general | solution.py:11
  187.6 4.0 %copy-done = f32[640,4096]{1,0:T(8,128)} copy-done((f32[640,4096]{1,0:T(8,128)}, f32[640,4096]{1,0:T(8,128)S(1)}, u32[]{:S(2)}) %copy-start) | copy-done | bytes 10485784
  193.3 3.7 %collective-permute-done.31 = f32[4096]{0:T(1024)S(1)} collective-permute-done((f32[4096]{0:T(1024)S(1)}, f32[4096]{0:T(1024)S(1)}, u32[]{:S(2)}, u32[]{:S(2)}) %collective-permute-start.31) | collective-permute-done | bytes 16416 | tf_op jit(solution)/shard_map/ppermute | solution.py:72
  197.1 5.2 %collective-permute-done.32 = f32[4096]{0:T(1024)S(1)} collective-permute-done((f32[4096]{0:T(1024)S(1)}, f32[4096]{0:T(1024)S(1)}, u32[]{:S(2)}, u32[]{:S(2)}) %collective-permute-start.32) | collective-permute-done | bytes 16416 | tf_op jit(solution)/shard_map/ppermute | solution.py:72
  202.6 3.5 %fusion.1 = f32[384]{0:T(512)S(1)} fusion(f32[640,4096]{1,0:T(8,128)} %copy-done, f32[4096]{0:T(1024)S(1)} %bitcast.63), kind=kLoop, calls=%fused_computation.4 | loop fusion | flops 4718208 | bytes 6309376 | tf_op jit(solution)/shard_map/reduce_sum | solution.py:151
  211.8 3.2 %collective-permute-done.35 = f32[1,2,384]{2,0,1:T(1,128)S(1)} collective-permute-done((f32[1,2,384]{2,0,1:T(1,128)S(1)}, f32[1,2,384]{2,0,1:T(1,128)S(1)}, u32[]{:S(2)}, u32[]{:S(2)}) %collective-permute-start.35) | collective-permute-done | bytes 3104 | tf_op jit(solution)/shard_map/ppermute | solution.py:81
  220.8 3.1 %collective-permute-done.37 = f32[4,2,384]{2,0,1:T(4,128)S(1)} collective-permute-done((f32[4,2,384]{2,0,1:T(4,128)S(1)}, f32[4,2,384]{2,0,1:T(4,128)S(1)}, u32[]{:S(2)}, u32[]{:S(2)}) %collective-permute-start.37) | collective-permute-done | bytes 12320 | tf_op jit(solution)/shard_map/ppermute | solution.py:81
  (135 shorter events, 47.9 us)
Async XLA Ops:
  0.6 36.9 %collective-permute-start.2 = (f32[512,768]{1,0:T(8,128)}, f32[512,768]{1,0:T(8,128)S(1)}, u32[]{:S(2)}, u32[]{:S(2)}) collective-permute-start(f32[512,768]{1,0:T(8,128)} %param.6), channel_id=1, source_target_pairs={{0,48},{8,56},{16,0},{24,8},{32,16},{40,24},{48,32},{56,40},{1,49}... | collective-permute-start | bytes 4718600 | tf_op jit(solution)/shard_map/ppermute | solution.py:90
  3.5 37.3 %collective-permute-start.3 = (f32[512,768]{1,0:T(8,128)}, f32[512,768]{1,0:T(8,128)S(1)}, u32[]{:S(2)}, u32[]{:S(2)}) collective-permute-start(f32[512,768]{1,0:T(8,128)} %param.6), channel_id=1, source_target_pairs={{0,16},{8,24},{16,32},{24,40},{32,48},{40,56},{48,0},{56,8},{1,17}... | collective-permute-start | bytes 4718600 | tf_op jit(solution)/shard_map/ppermute | solution.py:90
  42.7 30.2 %collective-permute-start.4 = (f32[2,512,768]{2,1,0:T(8,128)}, f32[2,512,768]{2,1,0:T(8,128)}, u32[]{:S(2)}, u32[]{:S(2)}) collective-permute-start(f32[2,512,768]{2,1,0:T(8,128)} %pad_maximum_fusion), channel_id=1, source_target_pairs={{0,8},{8,0},{16,24},{24,16},{32,40},{40,32},{48,56},{56,48},{1,9},... | collective-permute-start | bytes 9437192 | tf_op jit(solution)/shard_map/ppermute | solution.py:101
  42.7 25.8 %collective-permute-start.1 = (f32[512,768]{1,0:T(8,128)}, f32[512,768]{1,0:T(8,128)}, u32[]{:S(2)}, u32[]{:S(2)}) collective-permute-start(f32[512,768]{1,0:T(8,128)} %param.6), channel_id=1, source_target_pairs={{0,8},{8,0},{16,24},{24,16},{32,40},{40,32},{48,56},{56,48},{1,9},... | collective-permute-start | bytes 4718600 | tf_op jit(solution)/shard_map/ppermute | solution.py:98
  43.2 9.1 %collective-permute-start.19 = (s32[192]{0:T(256)S(1)}, s32[192]{0:T(256)S(1)}, u32[]{:S(2)}, u32[]{:S(2)}) collective-permute-start(s32[192]{0:T(256)S(1)} %copy-done.2), channel_id=1, source_target_pairs={{0,64},{64,0},{1,65},{65,1},{2,66},{66,2},{3,67},{67,3},{4,68},{68... | collective-permute-start | bytes 2312 | tf_op jit(solution)/shard_map/ppermute | solution.py:141
  48.8 19.7 %collective-permute-start.5 = (f32[256,768]{1,0:T(8,128)S(1)}, f32[256,768]{1,0:T(8,128)S(1)}, u32[]{:S(2)}, u32[]{:S(2)}) collective-permute-start(f32[256,768]{1,0:T(8,128)S(1)} %slice.77), channel_id=1, source_target_pairs={{0,16},{8,24},{16,32},{24,40},{32,48},{40,56},{48,0},{56,8},{1,17}... | collective-permute-start | bytes 2359304 | tf_op jit(solution)/shard_map/ppermute | solution.py:90
  48.9 22.2 %collective-permute-start.6 = (f32[256,768]{1,0:T(8,128)S(1)}, f32[256,768]{1,0:T(8,128)S(1)}, u32[]{:S(2)}, u32[]{:S(2)}) collective-permute-start(f32[256,768]{1,0:T(8,128)S(1)} %slice.78), channel_id=1, source_target_pairs={{0,48},{8,56},{16,0},{24,8},{32,16},{40,24},{48,32},{56,40},{1,49}... | collective-permute-start | bytes 2359304 | tf_op jit(solution)/shard_map/ppermute | solution.py:90
  68.5 9.1 %collective-permute-start.7 = (f32[256,768]{1,0:T(8,128)S(1)}, f32[256,768]{1,0:T(8,128)S(1)}, u32[]{:S(2)}, u32[]{:S(2)}) collective-permute-start(f32[256,768]{1,0:T(8,128)S(1)} %collective-permute-done.5), channel_id=1, source_target_pairs={{0,8},{8,0},{16,24},{24,16},{32,40},{40,32},{48,56},{56,48},{1,9},... | collective-permute-start | bytes 2359304 | tf_op jit(solution)/shard_map/ppermute | solution.py:102
  71.1 7.4 %collective-permute-start.8 = (f32[256,768]{1,0:T(8,128)S(1)}, f32[256,768]{1,0:T(8,128)S(1)}, u32[]{:S(2)}, u32[]{:S(2)}) collective-permute-start(f32[256,768]{1,0:T(8,128)S(1)} %collective-permute-done.6), channel_id=1, source_target_pairs={{0,8},{8,0},{16,24},{24,16},{32,40},{40,32},{48,56},{56,48},{1,9},... | collective-permute-start | bytes 2359304 | tf_op jit(solution)/shard_map/ppermute | solution.py:103
  96.7 11.6 %collective-permute-start.11 = (f32[64,768]{1,0:T(8,128)S(1)}, f32[64,768]{1,0:T(8,128)S(1)}, u32[]{:S(2)}, u32[]{:S(2)}) collective-permute-start(f32[64,768]{1,0:T(8,128)S(1)} %get-tuple-element.11), channel_id=1, source_target_pairs={{0,6},{1,7},{2,0},{3,1},{4,2},{5,3},{6,4},{7,5},{8,14},{9,15},{10,... | collective-permute-start | bytes 589832 | tf_op jit(solution)/shard_map/ppermute | solution.py:33
  99.8 9.4 %collective-permute-start.10 = (f32[64,768]{1,0:T(8,128)S(1)}, f32[64,768]{1,0:T(8,128)S(1)}, u32[]{:S(2)}, u32[]{:S(2)}) collective-permute-start(f32[64,768]{1,0:T(8,128)S(1)} %get-tuple-element.12), channel_id=1, source_target_pairs={{0,4},{1,5},{2,6},{3,7},{4,0},{5,1},{6,2},{7,3},{8,12},{9,13},{10,... | collective-permute-start | bytes 589832 | tf_op jit(solution)/shard_map/ppermute | solution.py:33
  100.4 11.6 %collective-permute-start.9 = (f32[64,768]{1,0:T(8,128)S(1)}, f32[64,768]{1,0:T(8,128)S(1)}, u32[]{:S(2)}, u32[]{:S(2)}) collective-permute-start(f32[64,768]{1,0:T(8,128)S(1)} %get-tuple-element.10), channel_id=1, source_target_pairs={{0,2},{1,3},{2,4},{3,5},{4,6},{5,7},{6,0},{7,1},{8,10},{9,11},{10,... | collective-permute-start | bytes 589832 | tf_op jit(solution)/shard_map/ppermute | solution.py:33
  113.9 10.0 %collective-permute-start.22 = (f32[96,768]{1,0:T(8,128)S(1)}, f32[96,768]{1,0:T(8,128)S(1)}, u32[]{:S(2)}, u32[]{:S(2)}) collective-permute-start(f32[96,768]{1,0:T(8,128)S(1)} %get-tuple-element.8), channel_id=1, source_target_pairs={{0,6},{1,7},{2,0},{3,1},{4,2},{5,3},{6,4},{7,5},{8,14},{9,15},{10,... | collective-permute-start | bytes 884744 | tf_op jit(solution)/shard_map/ppermute | solution.py:33
  114.6 11.5 %collective-permute-start.21 = (f32[96,768]{1,0:T(8,128)S(1)}, f32[96,768]{1,0:T(8,128)S(1)}, u32[]{:S(2)}, u32[]{:S(2)}) collective-permute-start(f32[96,768]{1,0:T(8,128)S(1)} %get-tuple-element.9), channel_id=1, source_target_pairs={{0,4},{1,5},{2,6},{3,7},{4,0},{5,1},{6,2},{7,3},{8,12},{9,13},{10,... | collective-permute-start | bytes 884744 | tf_op jit(solution)/shard_map/ppermute | solution.py:33
  115.2 15.3 %collective-permute-start.20 = (f32[96,768]{1,0:T(8,128)S(1)}, f32[96,768]{1,0:T(8,128)S(1)}, u32[]{:S(2)}, u32[]{:S(2)}) collective-permute-start(f32[96,768]{1,0:T(8,128)S(1)} %get-tuple-element.7), channel_id=1, source_target_pairs={{0,2},{1,3},{2,4},{3,5},{4,6},{5,7},{6,0},{7,1},{8,10},{9,11},{10,... | collective-permute-start | bytes 884744 | tf_op jit(solution)/shard_map/ppermute | solution.py:33
  116.9 13.7 %collective-permute-start.13 = (f32[16,768]{1,0:T(8,128)S(1)}, f32[16,768]{1,0:T(8,128)S(1)}, u32[]{:S(2)}, u32[]{:S(2)}) collective-permute-start(f32[16,768]{1,0:T(8,128)S(1)} %slice_select_fusion.3), channel_id=1, source_target_pairs={{0,1},{1,0},{2,3},{3,2},{4,5},{5,4},{6,7},{7,6},{8,9},{9,8},{10,11... | collective-permute-start | bytes 147464 | tf_op jit(solution)/shard_map/ppermute | solution.py:62
  130.6 6.2 %collective-permute-start.14 = (f32[16,768]{1,0:T(8,128)S(1)}, f32[16,768]{1,0:T(8,128)S(1)}, u32[]{:S(2)}, u32[]{:S(2)}) collective-permute-start(f32[16,768]{1,0:T(8,128)S(1)} %select_add_fusion.3), channel_id=1, source_target_pairs={{0,1},{1,0},{2,3},{3,2},{4,5},{5,4},{6,7},{7,6},{8,9},{9,8},{10,11... | collective-permute-start | bytes 147464 | tf_op jit(solution)/shard_map/ppermute | solution.py:63
  134.3 6.6 %collective-permute-start.23 = (f32[48,768]{1,0:T(8,128)S(1)}, f32[48,768]{1,0:T(8,128)S(1)}, u32[]{:S(2)}, u32[]{:S(2)}) collective-permute-start(f32[48,768]{1,0:T(8,128)S(1)} %slice_select_fusion), channel_id=1, source_target_pairs={{0,64},{64,0},{1,65},{65,1},{2,66},{66,2},{3,67},{67,3},{4,68},{68... | collective-permute-start | bytes 442376 | tf_op jit(solution)/shard_map/ppermute | solution.py:60
  136.9 5.8 %collective-permute-start.15 = (f32[32,768]{1,0:T(8,128)S(1)}, f32[32,768]{1,0:T(8,128)S(1)}, u32[]{:S(2)}, u32[]{:S(2)}) collective-permute-start(f32[32,768]{1,0:T(8,128)S(1)} %maximum_select_fusion.5), channel_id=1, source_target_pairs={{0,64},{64,0},{1,65},{65,1},{2,66},{66,2},{3,67},{67,3},{4,68},{68... | collective-permute-start | bytes 294920 | tf_op jit(solution)/shard_map/ppermute | solution.py:64
  141.0 5.9 %collective-permute-start.24 = (f32[24,768]{1,0:T(8,128)S(1)}, f32[24,768]{1,0:T(8,128)S(1)}, u32[]{:S(2)}, u32[]{:S(2)}) collective-permute-start(f32[24,768]{1,0:T(8,128)S(1)} %slice_select_fusion.2), channel_id=1, source_target_pairs={{0,1},{1,0},{2,3},{3,2},{4,5},{5,4},{6,7},{7,6},{8,9},{9,8},{10,11... | collective-permute-start | bytes 221192 | tf_op jit(solution)/shard_map/ppermute | solution.py:62
  142.7 12.0 %collective-permute-start.16 = (f32[64,768]{1,0:T(8,128)S(1)}, f32[64,768]{1,0:T(8,128)S(1)}, u32[]{:S(2)}, u32[]{:S(2)}) collective-permute-start(f32[64,768]{1,0:T(8,128)S(1)} %maximum_select_fusion.3), channel_id=1, source_target_pairs={{0,6},{1,7},{2,0},{3,1},{4,2},{5,3},{6,4},{7,5},{8,14},{9,15},{10,... | collective-permute-start | bytes 589832 | tf_op jit(solution)/shard_map/ppermute | solution.py:33
  143.3 11.4 %collective-permute-start.17 = (f32[64,768]{1,0:T(8,128)S(1)}, f32[64,768]{1,0:T(8,128)S(1)}, u32[]{:S(2)}, u32[]{:S(2)}) collective-permute-start(f32[64,768]{1,0:T(8,128)S(1)} %maximum_select_fusion.3), channel_id=1, source_target_pairs={{0,4},{1,5},{2,6},{3,7},{4,0},{5,1},{6,2},{7,3},{8,12},{9,13},{10,... | collective-permute-start | bytes 589832 | tf_op jit(solution)/shard_map/ppermute | solution.py:33
  143.5 11.2 %collective-permute-start.18 = (f32[64,768]{1,0:T(8,128)S(1)}, f32[64,768]{1,0:T(8,128)S(1)}, u32[]{:S(2)}, u32[]{:S(2)}) collective-permute-start(f32[64,768]{1,0:T(8,128)S(1)} %maximum_select_fusion.3), channel_id=1, source_target_pairs={{0,2},{1,3},{2,4},{3,5},{4,6},{5,7},{6,0},{7,1},{8,10},{9,11},{10,... | collective-permute-start | bytes 589832 | tf_op jit(solution)/shard_map/ppermute | solution.py:33
  146.9 6.6 %collective-permute-start.25 = (f32[24,768]{1,0:T(8,128)S(1)}, f32[24,768]{1,0:T(8,128)S(1)}, u32[]{:S(2)}, u32[]{:S(2)}) collective-permute-start(f32[24,768]{1,0:T(8,128)S(1)} %select_add_fusion.2), channel_id=1, source_target_pairs={{0,1},{1,0},{2,3},{3,2},{4,5},{5,4},{6,7},{7,6},{8,9},{9,8},{10,11... | collective-permute-start | bytes 221192 | tf_op jit(solution)/shard_map/ppermute | solution.py:63
  153.6 5.2 %collective-permute-start.26 = (f32[48,768]{1,0:T(8,128)S(1)}, f32[48,768]{1,0:T(8,128)S(1)}, u32[]{:S(2)}, u32[]{:S(2)}) collective-permute-start(f32[48,768]{1,0:T(8,128)S(1)} %maximum_select_fusion.4), channel_id=1, source_target_pairs={{0,64},{64,0},{1,65},{65,1},{2,66},{66,2},{3,67},{67,3},{4,68},{68... | collective-permute-start | bytes 442376 | tf_op jit(solution)/shard_map/ppermute | solution.py:64
  158.8 6.8 %collective-permute-start.27 = (f32[96,768]{1,0:T(8,128)S(1)}, f32[96,768]{1,0:T(8,128)S(1)}, u32[]{:S(2)}, u32[]{:S(2)}) collective-permute-start(f32[96,768]{1,0:T(8,128)S(1)} %maximum_select_fusion.1), channel_id=1, source_target_pairs={{0,6},{1,7},{2,0},{3,1},{4,2},{5,3},{6,4},{7,5},{8,14},{9,15},{10,... | collective-permute-start | bytes 884744 | tf_op jit(solution)/shard_map/ppermute | solution.py:33
  159.5 8.8 %collective-permute-start.28 = (f32[96,768]{1,0:T(8,128)S(1)}, f32[96,768]{1,0:T(8,128)S(1)}, u32[]{:S(2)}, u32[]{:S(2)}) collective-permute-start(f32[96,768]{1,0:T(8,128)S(1)} %maximum_select_fusion.1), channel_id=1, source_target_pairs={{0,4},{1,5},{2,6},{3,7},{4,0},{5,1},{6,2},{7,3},{8,12},{9,13},{10,... | collective-permute-start | bytes 884744 | tf_op jit(solution)/shard_map/ppermute | solution.py:33
  160.4 11.0 %collective-permute-start.29 = (f32[96,768]{1,0:T(8,128)S(1)}, f32[96,768]{1,0:T(8,128)S(1)}, u32[]{:S(2)}, u32[]{:S(2)}) collective-permute-start(f32[96,768]{1,0:T(8,128)S(1)} %maximum_select_fusion.1), channel_id=1, source_target_pairs={{0,2},{1,3},{2,4},{3,5},{4,6},{5,7},{6,0},{7,1},{8,10},{9,11},{10,... | collective-permute-start | bytes 884744 | tf_op jit(solution)/shard_map/ppermute | solution.py:33
  197.1 5.2 %collective-permute-start.32 = (f32[4096]{0:T(1024)S(1)}, f32[4096]{0:T(1024)S(1)}, u32[]{:S(2)}, u32[]{:S(2)}) collective-permute-start(f32[4096]{0:T(1024)S(1)} %max.31), channel_id=1, source_target_pairs={{0,32},{8,40},{16,48},{24,56},{32,0},{40,8},{48,16},{56,24},{1,33}... | collective-permute-start | bytes 49160 | tf_op jit(solution)/shard_map/ppermute | solution.py:72
  209.8 5.1 %collective-permute-start.35 = (f32[1,2,384]{2,0,1:T(1,128)S(1)}, f32[1,2,384]{2,0,1:T(1,128)S(1)}, u32[]{:S(2)}, u32[]{:S(2)}) collective-permute-start(f32[1,2,384]{2,0,1:T(1,128)S(1)} %broadcast_select_fusion.1), channel_id=1, source_target_pairs={{0,1},{1,0},{2,3},{3,2},{4,5},{5,4},{6,7},{7,6},{8,9},{9,8},{10,11... | collective-permute-start | bytes 9224 | tf_op jit(solution)/shard_map/ppermute | solution.py:81
  215.1 5.1 %collective-permute-start.33 = (f32[4096]{0:T(1024)S(1)}, f32[4096]{0:T(1024)S(1)}, u32[]{:S(2)}, u32[]{:S(2)}) collective-permute-start(f32[4096]{0:T(1024)S(1)} %maximum_maximum_fusion), channel_id=1, source_target_pairs={{0,64},{64,0},{1,65},{65,1},{2,66},{66,2},{3,67},{67,3},{4,68},{68... | collective-permute-start | bytes 49160 | tf_op jit(solution)/shard_map/ppermute | solution.py:155
  218.7 5.3 %collective-permute-start.37 = (f32[4,2,384]{2,0,1:T(4,128)S(1)}, f32[4,2,384]{2,0,1:T(4,128)S(1)}, u32[]{:S(2)}, u32[]{:S(2)}) collective-permute-start(f32[4,2,384]{2,0,1:T(4,128)S(1)} %maximum_select_fusion.8), channel_id=1, source_target_pairs={{0,4},{1,5},{2,6},{3,7},{4,0},{5,1},{6,2},{7,3},{8,12},{9,13},{10,... | collective-permute-start | bytes 36872 | tf_op jit(solution)/shard_map/ppermute | solution.py:81
  (10 other events, 42.1 us)

commit v13 on v10

--- a/solution.py
+++ b/solution.py
@@ -66,6 +66,30 @@
     return jnp.roll(jnp.stack(pieces), y, axis=0).reshape(value.shape)
 
 
+def group_masked_sum_z_first(value):
+    here = lax.axis_index("col")
+    y, z = here // N_Z, here % N_Z
+    zl = lax.axis_index("zl")
+    zl_swap = [(0, 1), (1, 0)]
+    z_swap = [(c, c ^ 1) for c in range(N_Y * N_Z)]
+    mine, theirs = pair_split(value, zl == 0)
+    mine = mine + lax.ppermute(theirs, "zl", zl_swap)
+    low, high = pair_split(mine, z == 0)
+    low = low + lax.ppermute(high, "col", z_swap)
+    quarter = low.shape[0] // N_Y
+
+    def part(k):
+        return lax.dynamic_slice_in_dim(low, ((y + k) % N_Y) * quarter, quarter)
+
+    own = part(0)
+    for k in range(1, N_Y):
+        own = own + y_shift(part(k), k)
+    pieces = [own] + [y_shift(own, -k) for k in range(1, N_Y)]
+    low = jnp.roll(jnp.stack(pieces), y, axis=0).reshape(low.shape)
+    mine = pair_join(low, lax.ppermute(low, "col", z_swap), z == 0)
+    return pair_join(mine, lax.ppermute(mine, "zl", zl_swap), zl == 0)
+
+
 def all_max(value, axis, n):
     bit = 1
     while bit < n:
@@ -95,7 +119,7 @@
     both_sel = pair_join(sel_index, lax.ppermute(sel_index, "zl", zl_swap), zl == 0)
     both_cand = pair_join(cand_index, lax.ppermute(cand_index, "zl", zl_swap), zl == 0)
     selected = group_masked_sum(lookup(half, both_sel, first_row))
-    chosen = group_masked_sum(lookup(half, both_cand, first_row))
+    chosen = group_masked_sum_z_first(lookup(half, both_cand, first_row))
     n_sel = both_sel.shape[0]
     scores = lax.optimization_barrier(similar(jnp.concatenate([selected, chosen]), half))
     reached = all_max(jnp.max(scores[:n_sel], axis=0), "xc", n_xc)

time: 219 us -> 240 us (1.096)
  waiting for transfers between devices: 121 us -> 143 us
  other arithmetic: 8.31 us -> 5.51 us
    ppermute x0 -> x4, waiting for transfers between devices: none -> 22.5 us  [the longest x1 9.34 us: group_masked_sum_z_first(): return pair_join(mine, lax.ppermute(mine, 'zl', zl_swap), zl == 0)]
    ppermute x12, waiting for transfers between devices: 20.9 us -> 11.9 us  [y_shift(): return lax.ppermute(value, 'col', pairs)]
    ppermute x0 -> x4, starting transfers between devices: none -> 5.75 us  [the longest x1 2.36 us: group_masked_sum_z_first(): mine = pair_join(low, lax.ppermute(low, 'col', z_swap), z == 0)]
    ppermute x2 -> x1, waiting for transfers between devices: 7.57 us -> 9.21 us  [group_masked_sum(): mine = pair_join(low, lax.ppermute(low, 'col', z_swap), z == 0)]
  transfers between devices with their start and end apart: 31 -> 31, of which waited for: 23 -> 24; matrix products, arithmetic and copies ran while one was open for 5% -> 4% of each run, Pallas kernels for 0% -> 0%
where the time goes in v13:
time: 240 us
  waiting for transfers between devices  143 us (60%)
  starting transfers between devices  42.7 us (18%)
  local copies, waits for them, and re-layouts  18 us (8%)
  matrix products  16 us (7%)
  between operations  14.4 us (6%)
  other arithmetic  5.51 us (2%)
    all_gather x1, waiting for transfers between devices, body(): half = lax.all_gather(slab_embed, 'xc', axis=0, tiled=True)  65.8 us
    ppermute x12, starting transfers between devices, y_shift(): return lax.ppermute(value, 'col', pairs)  18.9 us
    dot_general x1, matrix products, similar(): lax.dot_general(left, right, (((1,), (1,)), ((), ())), precision=lax.Prec...  16 us
    gather x2, local copies, waits for them, and re-layouts, lookup(): jnp.take(source, jnp.clip(position, 0, source.shape[0] - 1), axis=0)  13 us
    ppermute x4, waiting for transfers between devices, gather_in_order(): other = lax.ppermute(parts, axis, [(i, i ^ bit) for i in range(n)])  12.7 us
    ppermute x12, waiting for transfers between devices, y_shift(): return lax.ppermute(value, 'col', pairs)  11.9 us
    ppermute x1, waiting for transfers between devices, group_masked_sum_z_first(): return pair_join(mine, lax.ppermute(mine, 'zl', zl_swap), zl == 0)  9.34 us
    ppermute x1, waiting for transfers between devices, group_masked_sum(): mine = pair_join(low, lax.ppermute(low, 'col', z_swap), z == 0)  9.21 us
  transfers between devices with their start and end apart: 31, of which 24 were waited for; matrix products, arithmetic and copies ran while one was open for 4% of the time, Pallas kernels for 0%

profile of v13, /device:TPU:0, one launch (start us, length us, event | category | flops | bytes accessed | tf_op | source)
XLA Modules:
  0.0 239.5 jit_solution(4221239560405799511)
XLA Ops:
  7.9 2.1 collective-permute-start
  13.7 65.8 %all-gather.2.cloned.1.call-done = f32[4096,768]{1,0:T(8,128)} async-done(((f32[512,768]{1,0:T(8,128)}), f32[4096,768]{1,0:T(8,128)}) %all-gather.2.cloned.1.call-update) | async-done | bytes 12582928 | tf_op jit(solution)/shard_map/all_gather | solution.py:116
  79.5 6.0 %gather_fusion = f32[256,768]{1,0:T(8,128)S(1)} fusion(f32[4096,768]{1,0:T(8,128)} %all-gather.2.cloned.1.call-done, s32[1024]{0:T(1024)S(1)} %pad_clamp_fusion.1), kind=kCustom, calls=%fused_computation | custom fusion | bytes 1573888 | tf_op jit(solution)/shard_map/jit(_take)/gather | solution.py:23
  87.3 2.7 %collective-permute-start.2 = (f32[64,768]{1,0:T(8,128)S(1)}, f32[64,768]{1,0:T(8,128)S(1)}, u32[]{:S(2)}, u32[]{:S(2)}) collective-permute-start(f32[64,768]{1,0:T(8,128)S(1)} %get-tuple-element.8), channel_id=1, source_target_pairs={{0,4},{1,5},{2,6},{3,7},{4,0},{5,1},{6,2},{7,3},{8,12},{9,13},{10,... | collective-permute-start | bytes 589832 | tf_op jit(solution)/shard_map/ppermute | solution.py:33
  91.5 7.1 %gather_fusion.1 = f32[384,768]{1,0:T(8,128)S(1)} fusion(f32[4096,768]{1,0:T(8,128)} %all-gather.2.cloned.1.call-done, s32[1024]{0:T(1024)S(1)} %pad_clamp_fusion), kind=kCustom, calls=%fused_computation.1 | custom fusion | bytes 2360832 | tf_op jit(solution)/shard_map/jit(_take)/gather | solution.py:23
  101.1 2.9 %collective-permute-done.4 = f32[32,768]{1,0:T(8,128)S(1)} collective-permute-done((f32[32,768]{1,0:T(8,128)S(1)}, f32[32,768]{1,0:T(8,128)S(1)}, u32[]{:S(2)}, u32[]{:S(2)}) %collective-permute-start.4) | collective-permute-done | bytes 98336 | tf_op jit(solution)/shard_map/ppermute | solution.py:60
  104.0 3.2 %collective-permute-start.5 = (f32[16,768]{1,0:T(8,128)S(1)}, f32[16,768]{1,0:T(8,128)S(1)}, u32[]{:S(2)}, u32[]{:S(2)}) collective-permute-start(f32[16,768]{1,0:T(8,128)S(1)} %slice_select_fusion.3), channel_id=1, source_target_pairs={{0,1},{1,0},{2,3},{3,2},{4,5},{5,4},{6,7},{7,6},{8,9},{9,8},{10,11... | collective-permute-start | bytes 147464 | tf_op jit(solution)/shard_map/ppermute | solution.py:62
  108.1 2.1 collective-permute-done.5
  110.2 3.3 %collective-permute-start.6 = (f32[16,768]{1,0:T(8,128)S(1)}, f32[16,768]{1,0:T(8,128)S(1)}, u32[]{:S(2)}, u32[]{:S(2)}) collective-permute-start(f32[16,768]{1,0:T(8,128)S(1)} %select_add_fusion.3), channel_id=1, source_target_pairs={{0,1},{1,0},{2,3},{3,2},{4,5},{5,4},{6,7},{7,6},{8,9},{9,8},{10,11... | collective-permute-start | bytes 147464 | tf_op jit(solution)/shard_map/ppermute | solution.py:63
  113.5 9.2 %collective-permute-done.6 = f32[16,768]{1,0:T(8,128)S(1)} collective-permute-done((f32[16,768]{1,0:T(8,128)S(1)}, f32[16,768]{1,0:T(8,128)S(1)}, u32[]{:S(2)}, u32[]{:S(2)}) %collective-permute-start.6) | collective-permute-done | bytes 49184 | tf_op jit(solution)/shard_map/ppermute | solution.py:63
  122.9 4.6 %collective-permute-done.7 = f32[32,768]{1,0:T(8,128)S(1)} collective-permute-done((f32[32,768]{1,0:T(8,128)S(1)}, f32[32,768]{1,0:T(8,128)S(1)}, u32[]{:S(2)}, u32[]{:S(2)}) %collective-permute-start.7) | collective-permute-done | bytes 98336 | tf_op jit(solution)/shard_map/ppermute | solution.py:64
  127.5 3.1 %collective-permute-start.8 = (f32[64,768]{1,0:T(8,128)S(1)}, f32[64,768]{1,0:T(8,128)S(1)}, u32[]{:S(2)}, u32[]{:S(2)}) collective-permute-start(f32[64,768]{1,0:T(8,128)S(1)} %maximum_select_fusion.3), channel_id=1, source_target_pairs={{0,6},{1,7},{2,0},{3,1},{4,2},{5,3},{6,4},{7,5},{8,14},{9,15},{10,... | collective-permute-start | bytes 589832 | tf_op jit(solution)/shard_map/ppermute | solution.py:33
  133.7 2.3 collective-permute-done.8
  136.0 4.0 %collective-permute-done.13 = f32[96,768]{1,0:T(8,128)S(1)} collective-permute-done((f32[96,768]{1,0:T(8,128)S(1)}, f32[96,768]{1,0:T(8,128)S(1)}, u32[]{:S(2)}, u32[]{:S(2)}) %collective-permute-start.13) | collective-permute-done | bytes 294944 | tf_op jit(solution)/shard_map/ppermute | solution.py:78
  140.1 2.6 %collective-permute-start.14 = (f32[24,768]{1,0:T(8,128)S(1)}, f32[24,768]{1,0:T(8,128)S(1)}, u32[]{:S(2)}, u32[]{:S(2)}) collective-permute-start(f32[24,768]{1,0:T(8,128)S(1)} %get-tuple-element.9), channel_id=1, source_target_pairs={{0,2},{1,3},{2,4},{3,5},{4,6},{5,7},{6,0},{7,1},{8,10},{9,11},{10,... | collective-permute-start | bytes 221192 | tf_op jit(solution)/shard_map/ppermute | solution.py:33
  145.7 3.0 %collective-permute-done.15 = f32[24,768]{1,0:T(8,128)S(1)} collective-permute-done((f32[24,768]{1,0:T(8,128)S(1)}, f32[24,768]{1,0:T(8,128)S(1)}, u32[]{:S(2)}, u32[]{:S(2)}) %collective-permute-start.15) | collective-permute-done | bytes 73760 | tf_op jit(solution)/shard_map/ppermute | solution.py:33
  148.8 2.8 %collective-permute-start.17 = (f32[24,768]{1,0:T(8,128)S(1)}, f32[24,768]{1,0:T(8,128)S(1)}, u32[]{:S(2)}, u32[]{:S(2)}) collective-permute-start(f32[24,768]{1,0:T(8,128)S(1)} %get-tuple-element.5), channel_id=1, source_target_pairs={{0,6},{1,7},{2,0},{3,1},{4,2},{5,3},{6,4},{7,5},{8,14},{9,15},{10,... | collective-permute-start | bytes 221192 | tf_op jit(solution)/shard_map/ppermute | solution.py:33
  154.3 3.3 %collective-permute-done.18 = f32[24,768]{1,0:T(8,128)S(1)} collective-permute-done((f32[24,768]{1,0:T(8,128)S(1)}, f32[24,768]{1,0:T(8,128)S(1)}, u32[]{:S(2)}, u32[]{:S(2)}) %collective-permute-start.18) | collective-permute-done | bytes 73760 | tf_op jit(solution)/shard_map/ppermute | solution.py:33
  158.4 2.4 collective-permute-start.20
  160.8 9.1 %collective-permute-done.20 = f32[96,768]{1,0:T(8,128)S(1)} collective-permute-done((f32[96,768]{1,0:T(8,128)S(1)}, f32[96,768]{1,0:T(8,128)S(1)}, u32[]{:S(2)}, u32[]{:S(2)}) %collective-permute-start.20) | collective-permute-done | bytes 294944 | tf_op jit(solution)/shard_map/ppermute | solution.py:89
  170.8 9.3 %collective-permute-done.21 = f32[192,768]{1,0:T(8,128)S(1)} collective-permute-done((f32[192,768]{1,0:T(8,128)S(1)}, f32[192,768]{1,0:T(8,128)S(1)}, u32[]{:S(2)}, u32[]{:S(2)}) %collective-permute-start.21) | collective-permute-done | bytes 589856 | tf_op jit(solution)/shard_map/ppermute | solution.py:90
  180.2 16.0 %fusion.2 = f32[640,4096]{1,0:T(8,128)S(1)} fusion(f32[4096,768]{1,0:T(8,128)} %all-gather.2.cloned.1.call-done, f32[384,768]{1,0:T(8,128)S(1)} %maximum_select_fusion, f32[256,768]{1,0:T(8,128)S(1)} %bitcast.32), kind=kOutput, calls=%fused_computation.6 | convolution fusion | flops 12080087040 | bytes 25034752 | tf_op jit(solution)/shard_map/dot_general | solution.py:11
  196.2 4.0 %copy-done = f32[640,4096]{1,0:T(8,128)} copy-done((f32[640,4096]{1,0:T(8,128)}, f32[640,4096]{1,0:T(8,128)S(1)}, u32[]{:S(2)}) %copy-start) | copy-done | bytes 10485784
  202.6 2.8 %collective-permute-done.23 = f32[4096]{0:T(1024)S(1)} collective-permute-done((f32[4096]{0:T(1024)S(1)}, f32[4096]{0:T(1024)S(1)}, u32[]{:S(2)}, u32[]{:S(2)}) %collective-permute-start.23) | collective-permute-done | bytes 16416 | tf_op jit(solution)/shard_map/ppermute | solution.py:96
  205.5 2.1 collective-permute-start.24
  207.6 3.1 %collective-permute-done.24 = f32[4096]{0:T(1024)S(1)} collective-permute-done((f32[4096]{0:T(1024)S(1)}, f32[4096]{0:T(1024)S(1)}, u32[]{:S(2)}, u32[]{:S(2)}) %collective-permute-start.24) | collective-permute-done | bytes 16416 | tf_op jit(solution)/shard_map/ppermute | solution.py:96
  210.7 3.5 %fusion.1 = f32[384]{0:T(512)S(1)} fusion(f32[640,4096]{1,0:T(8,128)} %copy-done, f32[4096]{0:T(1024)S(1)} %maximum_maximum_fusion), kind=kLoop, calls=%fused_computation.4 | loop fusion | flops 4718208 | bytes 6309376 | tf_op jit(solution)/shard_map/reduce_sum | solution.py:128
  214.7 3.1 %collective-permute-done.26 = f32[1,384]{1,0:T(1,128)S(1)} collective-permute-done((f32[1,384]{1,0:T(1,128)S(1)}, f32[1,384]{1,0:T(1,128)S(1)}, u32[]{:S(2)}, u32[]{:S(2)}) %collective-permute-start.26) | collective-permute-done | bytes 1568 | tf_op jit(solution)/shard_map/ppermute | solution.py:105
  217.9 2.0 collective-permute-start.27
  219.9 3.1 %collective-permute-done.27 = f32[1,2,384]{2,0,1:T(1,128)S(1)} collective-permute-done((f32[1,2,384]{2,0,1:T(1,128)S(1)}, f32[1,2,384]{2,0,1:T(1,128)S(1)}, u32[]{:S(2)}, u32[]{:S(2)}) %collective-permute-start.27) | collective-permute-done | bytes 3104 | tf_op jit(solution)/shard_map/ppermute | solution.py:105
  223.6 3.1 %collective-permute-done.28 = f32[2,2,384]{2,0,1:T(2,128)S(1)} collective-permute-done((f32[2,2,384]{2,0,1:T(2,128)S(1)}, f32[2,2,384]{2,0,1:T(2,128)S(1)}, u32[]{:S(2)}, u32[]{:S(2)}) %collective-permute-start.28) | collective-permute-done | bytes 6176 | tf_op jit(solution)/shard_map/ppermute | solution.py:105
  228.7 3.3 %collective-permute-done.29 = f32[4,2,384]{2,0,1:T(4,128)S(1)} collective-permute-done((f32[4,2,384]{2,0,1:T(4,128)S(1)}, f32[4,2,384]{2,0,1:T(4,128)S(1)}, u32[]{:S(2)}, u32[]{:S(2)}) %collective-permute-start.29) | collective-permute-done | bytes 12320 | tf_op jit(solution)/shard_map/ppermute | solution.py:105
  (97 shorter events, 28.0 us)
Async XLA Ops:
  7.2 72.3 %all-gather.2.cloned.1.call-start = ((), (), s32[]{:S(2)}) async-start(), calls=%async_computation | async-start | bytes 14155776 | tf_op jit(solution)/shard_map/all_gather | solution.py:116
  7.9 3.6 %collective-permute-start = (s32[128]{0:T(128)S(1)}, s32[128]{0:T(128)S(1)}, u32[]{:S(2)}, u32[]{:S(2)}) collective-permute-start(s32[128]{0:T(128)S(1)} %copy-done.3), channel_id=1, source_target_pairs={{0,64},{64,0},{1,65},{65,1},{2,66},{66,2},{3,67},{67,3},{4,68},{68... | collective-permute-start | bytes 1544 | tf_op jit(solution)/shard_map/ppermute | solution.py:119
  10.0 3.6 %collective-permute-start.11 = (s32[192]{0:T(256)S(1)}, s32[192]{0:T(256)S(1)}, u32[]{:S(2)}, u32[]{:S(2)}) collective-permute-start(s32[192]{0:T(256)S(1)} %copy-done.2), channel_id=1, source_target_pairs={{0,64},{64,0},{1,65},{65,1},{2,66},{66,2},{3,67},{67,3},{4,68},{68... | collective-permute-start | bytes 2312 | tf_op jit(solution)/shard_map/ppermute | solution.py:120
  85.7 12.9 %collective-permute-start.1 = (f32[64,768]{1,0:T(8,128)S(1)}, f32[64,768]{1,0:T(8,128)S(1)}, u32[]{:S(2)}, u32[]{:S(2)}) collective-permute-start(f32[64,768]{1,0:T(8,128)S(1)} %get-tuple-element.6), channel_id=1, source_target_pairs={{0,2},{1,3},{2,4},{3,5},{4,6},{5,7},{6,0},{7,1},{8,10},{9,11},{10,... | collective-permute-start | bytes 589832 | tf_op jit(solution)/shard_map/ppermute | solution.py:33
  87.3 12.0 %collective-permute-start.2 = (f32[64,768]{1,0:T(8,128)S(1)}, f32[64,768]{1,0:T(8,128)S(1)}, u32[]{:S(2)}, u32[]{:S(2)}) collective-permute-start(f32[64,768]{1,0:T(8,128)S(1)} %get-tuple-element.8), channel_id=1, source_target_pairs={{0,4},{1,5},{2,6},{3,7},{4,0},{5,1},{6,2},{7,3},{8,12},{9,13},{10,... | collective-permute-start | bytes 589832 | tf_op jit(solution)/shard_map/ppermute | solution.py:33
  90.0 9.3 %collective-permute-start.3 = (f32[64,768]{1,0:T(8,128)S(1)}, f32[64,768]{1,0:T(8,128)S(1)}, u32[]{:S(2)}, u32[]{:S(2)}) collective-permute-start(f32[64,768]{1,0:T(8,128)S(1)} %get-tuple-element.7), channel_id=1, source_target_pairs={{0,6},{1,7},{2,0},{3,1},{4,2},{5,3},{6,4},{7,5},{8,14},{9,15},{10,... | collective-permute-start | bytes 589832 | tf_op jit(solution)/shard_map/ppermute | solution.py:33
  99.3 4.7 %collective-permute-start.4 = (f32[32,768]{1,0:T(8,128)S(1)}, f32[32,768]{1,0:T(8,128)S(1)}, u32[]{:S(2)}, u32[]{:S(2)}) collective-permute-start(f32[32,768]{1,0:T(8,128)S(1)} %slice_select_fusion.2), channel_id=1, source_target_pairs={{0,64},{64,0},{1,65},{65,1},{2,66},{66,2},{3,67},{67,3},{4,68},{68... | collective-permute-start | bytes 294920 | tf_op jit(solution)/shard_map/ppermute | solution.py:60
  104.0 6.2 %collective-permute-start.5 = (f32[16,768]{1,0:T(8,128)S(1)}, f32[16,768]{1,0:T(8,128)S(1)}, u32[]{:S(2)}, u32[]{:S(2)}) collective-permute-start(f32[16,768]{1,0:T(8,128)S(1)} %slice_select_fusion.3), channel_id=1, source_target_pairs={{0,1},{1,0},{2,3},{3,2},{4,5},{5,4},{6,7},{7,6},{8,9},{9,8},{10,11... | collective-permute-start | bytes 147464 | tf_op jit(solution)/shard_map/ppermute | solution.py:62
  107.3 24.2 %collective-permute-start.12 = (f32[192,768]{1,0:T(8,128)S(1)}, f32[192,768]{1,0:T(8,128)S(1)}, u32[]{:S(2)}, u32[]{:S(2)}) collective-permute-start(f32[192,768]{1,0:T(8,128)S(1)} %slice_select_fusion), channel_id=1, source_target_pairs={{0,64},{64,0},{1,65},{65,1},{2,66},{66,2},{3,67},{67,3},{4,68},{68... | collective-permute-start | bytes 1769480 | tf_op jit(solution)/shard_map/ppermute | solution.py:76
  110.2 12.6 %collective-permute-start.6 = (f32[16,768]{1,0:T(8,128)S(1)}, f32[16,768]{1,0:T(8,128)S(1)}, u32[]{:S(2)}, u32[]{:S(2)}) collective-permute-start(f32[16,768]{1,0:T(8,128)S(1)} %select_add_fusion.3), channel_id=1, source_target_pairs={{0,1},{1,0},{2,3},{3,2},{4,5},{5,4},{6,7},{7,6},{8,9},{9,8},{10,11... | collective-permute-start | bytes 147464 | tf_op jit(solution)/shard_map/ppermute | solution.py:63
  122.8 4.7 %collective-permute-start.7 = (f32[32,768]{1,0:T(8,128)S(1)}, f32[32,768]{1,0:T(8,128)S(1)}, u32[]{:S(2)}, u32[]{:S(2)}) collective-permute-start(f32[32,768]{1,0:T(8,128)S(1)} %maximum_select_fusion.4), channel_id=1, source_target_pairs={{0,64},{64,0},{1,65},{65,1},{2,66},{66,2},{3,67},{67,3},{4,68},{68... | collective-permute-start | bytes 294920 | tf_op jit(solution)/shard_map/ppermute | solution.py:64
  127.5 8.5 %collective-permute-start.8 = (f32[64,768]{1,0:T(8,128)S(1)}, f32[64,768]{1,0:T(8,128)S(1)}, u32[]{:S(2)}, u32[]{:S(2)}) collective-permute-start(f32[64,768]{1,0:T(8,128)S(1)} %maximum_select_fusion.3), channel_id=1, source_target_pairs={{0,6},{1,7},{2,0},{3,1},{4,2},{5,3},{6,4},{7,5},{8,14},{9,15},{10,... | collective-permute-start | bytes 589832 | tf_op jit(solution)/shard_map/ppermute | solution.py:33
  130.6 14.9 %collective-permute-start.9 = (f32[64,768]{1,0:T(8,128)S(1)}, f32[64,768]{1,0:T(8,128)S(1)}, u32[]{:S(2)}, u32[]{:S(2)}) collective-permute-start(f32[64,768]{1,0:T(8,128)S(1)} %maximum_select_fusion.3), channel_id=1, source_target_pairs={{0,4},{1,5},{2,6},{3,7},{4,0},{5,1},{6,2},{7,3},{8,12},{9,13},{10,... | collective-permute-start | bytes 589832 | tf_op jit(solution)/shard_map/ppermute | solution.py:33
  130.9 20.7 %collective-permute-start.10 = (f32[64,768]{1,0:T(8,128)S(1)}, f32[64,768]{1,0:T(8,128)S(1)}, u32[]{:S(2)}, u32[]{:S(2)}) collective-permute-start(f32[64,768]{1,0:T(8,128)S(1)} %maximum_select_fusion.3), channel_id=1, source_target_pairs={{0,2},{1,3},{2,4},{3,5},{4,6},{5,7},{6,0},{7,1},{8,10},{9,11},{10,... | collective-permute-start | bytes 589832 | tf_op jit(solution)/shard_map/ppermute | solution.py:33
  131.7 8.3 %collective-permute-start.13 = (f32[96,768]{1,0:T(8,128)S(1)}, f32[96,768]{1,0:T(8,128)S(1)}, u32[]{:S(2)}, u32[]{:S(2)}) collective-permute-start(f32[96,768]{1,0:T(8,128)S(1)} %slice_select_fusion.1), channel_id=1, source_target_pairs={{0,1},{1,0},{2,3},{3,2},{4,5},{5,4},{6,7},{7,6},{8,9},{9,8},{10,11... | collective-permute-start | bytes 884744 | tf_op jit(solution)/shard_map/ppermute | solution.py:78
  140.1 5.6 %collective-permute-start.14 = (f32[24,768]{1,0:T(8,128)S(1)}, f32[24,768]{1,0:T(8,128)S(1)}, u32[]{:S(2)}, u32[]{:S(2)}) collective-permute-start(f32[24,768]{1,0:T(8,128)S(1)} %get-tuple-element.9), channel_id=1, source_target_pairs={{0,2},{1,3},{2,4},{3,5},{4,6},{5,7},{6,0},{7,1},{8,10},{9,11},{10,... | collective-permute-start | bytes 221192 | tf_op jit(solution)/shard_map/ppermute | solution.py:33
  142.7 6.1 %collective-permute-start.15 = (f32[24,768]{1,0:T(8,128)S(1)}, f32[24,768]{1,0:T(8,128)S(1)}, u32[]{:S(2)}, u32[]{:S(2)}) collective-permute-start(f32[24,768]{1,0:T(8,128)S(1)} %get-tuple-element.11), channel_id=1, source_target_pairs={{0,4},{1,5},{2,6},{3,7},{4,0},{5,1},{6,2},{7,3},{8,12},{9,13},{10,... | collective-permute-start | bytes 221192 | tf_op jit(solution)/shard_map/ppermute | solution.py:33
  144.2 4.6 %collective-permute-start.16 = (f32[24,768]{1,0:T(8,128)S(1)}, f32[24,768]{1,0:T(8,128)S(1)}, u32[]{:S(2)}, u32[]{:S(2)}) collective-permute-start(f32[24,768]{1,0:T(8,128)S(1)} %get-tuple-element.10), channel_id=1, source_target_pairs={{0,6},{1,7},{2,0},{3,1},{4,2},{5,3},{6,4},{7,5},{8,14},{9,15},{10,... | collective-permute-start | bytes 221192 | tf_op jit(solution)/shard_map/ppermute | solution.py:33
  148.8 5.5 %collective-permute-start.17 = (f32[24,768]{1,0:T(8,128)S(1)}, f32[24,768]{1,0:T(8,128)S(1)}, u32[]{:S(2)}, u32[]{:S(2)}) collective-permute-start(f32[24,768]{1,0:T(8,128)S(1)} %get-tuple-element.5), channel_id=1, source_target_pairs={{0,6},{1,7},{2,0},{3,1},{4,2},{5,3},{6,4},{7,5},{8,14},{9,15},{10,... | collective-permute-start | bytes 221192 | tf_op jit(solution)/shard_map/ppermute | solution.py:33
  151.6 6.0 %collective-permute-start.18 = (f32[24,768]{1,0:T(8,128)S(1)}, f32[24,768]{1,0:T(8,128)S(1)}, u32[]{:S(2)}, u32[]{:S(2)}) collective-permute-start(f32[24,768]{1,0:T(8,128)S(1)} %get-tuple-element.5), channel_id=1, source_target_pairs={{0,4},{1,5},{2,6},{3,7},{4,0},{5,1},{6,2},{7,3},{8,12},{9,13},{10,... | collective-permute-start | bytes 221192 | tf_op jit(solution)/shard_map/ppermute | solution.py:33
  152.4 5.9 %collective-permute-start.19 = (f32[24,768]{1,0:T(8,128)S(1)}, f32[24,768]{1,0:T(8,128)S(1)}, u32[]{:S(2)}, u32[]{:S(2)}) collective-permute-start(f32[24,768]{1,0:T(8,128)S(1)} %get-tuple-element.5), channel_id=1, source_target_pairs={{0,2},{1,3},{2,4},{3,5},{4,6},{5,7},{6,0},{7,1},{8,10},{9,11},{10,... | collective-permute-start | bytes 221192 | tf_op jit(solution)/shard_map/ppermute | solution.py:33
  158.4 11.5 %collective-permute-start.20 = (f32[96,768]{1,0:T(8,128)S(1)}, f32[96,768]{1,0:T(8,128)S(1)}, u32[]{:S(2)}, u32[]{:S(2)}) collective-permute-start(f32[96,768]{1,0:T(8,128)S(1)} %bitcast.35), channel_id=1, source_target_pairs={{0,1},{1,0},{2,3},{3,2},{4,5},{5,4},{6,7},{7,6},{8,9},{9,8},{10,11... | collective-permute-start | bytes 884744 | tf_op jit(solution)/shard_map/ppermute | solution.py:89
  170.0 10.1 %collective-permute-start.21 = (f32[192,768]{1,0:T(8,128)S(1)}, f32[192,768]{1,0:T(8,128)S(1)}, u32[]{:S(2)}, u32[]{:S(2)}) collective-permute-start(f32[192,768]{1,0:T(8,128)S(1)} %maximum_select_fusion.1), channel_id=1, source_target_pairs={{0,64},{64,0},{1,65},{65,1},{2,66},{66,2},{3,67},{67,3},{4,68},{68... | collective-permute-start | bytes 1769480 | tf_op jit(solution)/shard_map/ppermute | solution.py:90
  200.2 10.5 %copy-start.1 = (f32[8192]{0:T(1024)S(1)}, f32[8192]{0:T(1024)}, u32[]{:S(2)}) copy-start(f32[8192]{0:T(1024)} %param.5) | copy-start | bytes 98308
  200.4 1.3 collective-permute-start.22
  201.7 3.7 %collective-permute-start.23 = (f32[4096]{0:T(1024)S(1)}, f32[4096]{0:T(1024)S(1)}, u32[]{:S(2)}, u32[]{:S(2)}) collective-permute-start(f32[4096]{0:T(1024)S(1)} %max.26), channel_id=1, source_target_pairs={{0,16},{8,24},{16,0},{24,8},{32,48},{40,56},{48,32},{56,40},{1,17}... | collective-permute-start | bytes 49160 | tf_op jit(solution)/shard_map/ppermute | solution.py:96
  205.5 5.2 %collective-permute-start.24 = (f32[4096]{0:T(1024)S(1)}, f32[4096]{0:T(1024)S(1)}, u32[]{:S(2)}, u32[]{:S(2)}) collective-permute-start(f32[4096]{0:T(1024)S(1)} %max.27), channel_id=1, source_target_pairs={{0,32},{8,40},{16,48},{24,56},{32,0},{40,8},{48,16},{56,24},{1,33}... | collective-permute-start | bytes 49160 | tf_op jit(solution)/shard_map/ppermute | solution.py:96
  214.2 3.7 %collective-permute-start.26 = (f32[1,384]{1,0:T(1,128)S(1)}, f32[1,384]{1,0:T(1,128)S(1)}, u32[]{:S(2)}, u32[]{:S(2)}) collective-permute-start(f32[1,384]{1,0:T(1,128)S(1)} %broadcast_in_dim.59), channel_id=1, source_target_pairs={{0,64},{64,0},{1,65},{65,1},{2,66},{66,2},{3,67},{67,3},{4,68},{68... | collective-permute-start | bytes 4616 | tf_op jit(solution)/shard_map/ppermute | solution.py:105
  217.9 5.1 %collective-permute-start.27 = (f32[1,2,384]{2,0,1:T(1,128)S(1)}, f32[1,2,384]{2,0,1:T(1,128)S(1)}, u32[]{:S(2)}, u32[]{:S(2)}) collective-permute-start(f32[1,2,384]{2,0,1:T(1,128)S(1)} %broadcast_select_fusion), channel_id=1, source_target_pairs={{0,1},{1,0},{2,3},{3,2},{4,5},{5,4},{6,7},{7,6},{8,9},{9,8},{10,11... | collective-permute-start | bytes 9224 | tf_op jit(solution)/shard_map/ppermute | solution.py:105
  223.0 3.7 %collective-permute-start.28 = (f32[2,2,384]{2,0,1:T(2,128)S(1)}, f32[2,2,384]{2,0,1:T(2,128)S(1)}, u32[]{:S(2)}, u32[]{:S(2)}) collective-permute-start(f32[2,2,384]{2,0,1:T(2,128)S(1)} %maximum_select_fusion.8), channel_id=1, source_target_pairs={{0,2},{1,3},{2,0},{3,1},{4,6},{5,7},{6,4},{7,5},{8,10},{9,11},{10,... | collective-permute-start | bytes 18440 | tf_op jit(solution)/shard_map/ppermute | solution.py:105
  223.1 5.0 %collective-permute-start.25 = (f32[4096]{0:T(1024)S(1)}, f32[4096]{0:T(1024)S(1)}, u32[]{:S(2)}, u32[]{:S(2)}) collective-permute-start(f32[4096]{0:T(1024)S(1)} %maximum_maximum_fusion), channel_id=1, source_target_pairs={{0,64},{64,0},{1,65},{65,1},{2,66},{66,2},{3,67},{67,3},{4,68},{68... | collective-permute-start | bytes 49160 | tf_op jit(solution)/shard_map/ppermute | solution.py:132
  226.7 5.3 %collective-permute-start.29 = (f32[4,2,384]{2,0,1:T(4,128)S(1)}, f32[4,2,384]{2,0,1:T(4,128)S(1)}, u32[]{:S(2)}, u32[]{:S(2)}) collective-permute-start(f32[4,2,384]{2,0,1:T(4,128)S(1)} %maximum_select_fusion.7), channel_id=1, source_target_pairs={{0,4},{1,5},{2,6},{3,7},{4,0},{5,1},{6,2},{7,3},{8,12},{9,13},{10,... | collective-permute-start | bytes 36872 | tf_op jit(solution)/shard_map/ppermute | solution.py:105
  (3 other events, 7.6 us)
Sparse Core Ops, SparseCore 0:
  9.7 69.7 all-gather.1

commit v14 on v10

--- a/solution.py
+++ b/solution.py
@@ -94,9 +94,10 @@
     zl_swap = [(0, 1), (1, 0)]
     both_sel = pair_join(sel_index, lax.ppermute(sel_index, "zl", zl_swap), zl == 0)
     both_cand = pair_join(cand_index, lax.ppermute(cand_index, "zl", zl_swap), zl == 0)
-    selected = group_masked_sum(lookup(half, both_sel, first_row))
-    chosen = group_masked_sum(lookup(half, both_cand, first_row))
     n_sel = both_sel.shape[0]
+    picked = lookup(half, jnp.concatenate([both_sel, both_cand]), first_row)
+    selected = group_masked_sum(picked[:n_sel])
+    chosen = group_masked_sum(picked[n_sel:])
     scores = lax.optimization_barrier(similar(jnp.concatenate([selected, chosen]), half))
     reached = all_max(jnp.max(scores[:n_sel], axis=0), "xc", n_xc)
     old = lax.dynamic_slice_in_dim(coverage_old, zl * half.shape[0], half.shape[0])

time: 219 us -> 225 us (1.027)
  waiting for transfers between devices: 121 us -> 130 us
  local copies, waits for them, and re-layouts: 18.2 us -> 14.6 us
    ppermute x12, waiting for transfers between devices: 20.9 us -> 28.4 us  [y_shift(): return lax.ppermute(value, 'col', pairs)]
    gather x2 -> x1, local copies, waits for them, and re-layouts: 13 us -> 8.6 us  [lookup(): jnp.take(source, jnp.clip(position, 0, source.shape[0] - 1), axis=0)]
  transfers between devices with their start and end apart: 31 -> 31, of which waited for: 23 -> 23; matrix products, arithmetic and copies ran while one was open for 5% -> 1% of each run, Pallas kernels for 0% -> 0%
where the time goes in v14:
time: 225 us
  waiting for transfers between devices  130 us (58%)
  starting transfers between devices  41.2 us (18%)
  matrix products  16 us (7%)
  local copies, waits for them, and re-layouts  14.6 us (6%)
  between operations  14.3 us (6%)
  other arithmetic  9.12 us (4%)
    all_gather x1, waiting for transfers between devices, body(): half = lax.all_gather(slab_embed, 'xc', axis=0, tiled=True)  64.2 us
    ppermute x12, waiting for transfers between devices, y_shift(): return lax.ppermute(value, 'col', pairs)  28.4 us
    ppermute x12, starting transfers between devices, y_shift(): return lax.ppermute(value, 'col', pairs)  18.9 us
    dot_general x1, matrix products, similar(): lax.dot_general(left, right, (((1,), (1,)), ((), ())), precision=lax.Prec...  16 us
    ppermute x4, waiting for transfers between devices, gather_in_order(): other = lax.ppermute(parts, axis, [(i, i ^ bit) for i in range(n)])  10.7 us
    gather x1, local copies, waits for them, and re-layouts, lookup(): jnp.take(source, jnp.clip(position, 0, source.shape[0] - 1), axis=0)  8.6 us
    ppermute x2, waiting for transfers between devices, group_masked_sum(): mine = pair_join(low, lax.ppermute(low, 'col', z_swap), z == 0)  7.46 us
    ppermute x3, waiting for transfers between devices, all_max(): lax.ppermute(value, axis, [(i, i ^ bit) for i in range(n)])  7.15 us
  transfers between devices with their start and end apart: 31, of which 23 were waited for; matrix products, arithmetic and copies ran while one was open for 1% of the time, Pallas kernels for 0%

profile of v14, /device:TPU:0, one launch (start us, length us, event | category | flops | bytes accessed | tf_op | source)
XLA Modules:
  0.0 225.0 jit_solution(7007153397095610677)
XLA Ops:
  7.9 2.1 collective-permute-start.1
  10.1 3.6 %collective-permute-done = s32[128]{0:T(128)S(1)} collective-permute-done((s32[128]{0:T(128)}, s32[128]{0:T(128)S(1)}, u32[]{:S(2)}, u32[]{:S(2)}) %collective-permute-start) | collective-permute-done | bytes 544 | tf_op jit(solution)/shard_map/ppermute | solution.py:95
  15.3 64.2 %all-gather.2.cloned.1.call-done = f32[4096,768]{1,0:T(8,128)} async-done(((f32[512,768]{1,0:T(8,128)}), f32[4096,768]{1,0:T(8,128)}) %all-gather.2.cloned.1.call-update) | async-done | bytes 12582928 | tf_op jit(solution)/shard_map/all_gather | solution.py:92
  79.5 8.6 %gather_fusion = f32[640,768]{1,0:T(8,128)} fusion(f32[4096,768]{1,0:T(8,128)} %all-gather.2.cloned.1.call-done, s32[1024]{0:T(1024)S(1)} %pad_clamp_fusion), kind=kCustom, calls=%fused_computation | custom fusion | bytes 3934720 | tf_op jit(solution)/shard_map/jit(_take)/gather | solution.py:23
  88.1 1.8 select_select_fusion
  92.2 2.7 %collective-permute-start.3 = (f32[64,768]{1,0:T(8,128)S(1)}, f32[64,768]{1,0:T(8,128)S(1)}, u32[]{:S(2)}, u32[]{:S(2)}) collective-permute-start(f32[64,768]{1,0:T(8,128)S(1)} %get-tuple-element.7), channel_id=1, source_target_pairs={{0,4},{1,5},{2,6},{3,7},{4,0},{5,1},{6,2},{7,3},{8,12},{9,13},{10,... | collective-permute-start | bytes 589832 | tf_op jit(solution)/shard_map/ppermute | solution.py:33
  96.5 2.8 %collective-permute-done.2 = f32[64,768]{1,0:T(8,128)S(1)} collective-permute-done((f32[64,768]{1,0:T(8,128)}, f32[64,768]{1,0:T(8,128)S(1)}, u32[]{:S(2)}, u32[]{:S(2)}) %collective-permute-start.2) | collective-permute-done | bytes 196640 | tf_op jit(solution)/shard_map/ppermute | solution.py:33
  99.2 5.2 %collective-permute-done.3 = f32[64,768]{1,0:T(8,128)S(1)} collective-permute-done((f32[64,768]{1,0:T(8,128)S(1)}, f32[64,768]{1,0:T(8,128)S(1)}, u32[]{:S(2)}, u32[]{:S(2)}) %collective-permute-start.3) | collective-permute-done | bytes 196640 | tf_op jit(solution)/shard_map/ppermute | solution.py:33
  108.4 2.4 %collective-permute-start.13 = (f32[96,768]{1,0:T(8,128)S(1)}, f32[96,768]{1,0:T(8,128)S(1)}, u32[]{:S(2)}, u32[]{:S(2)}) collective-permute-start(f32[96,768]{1,0:T(8,128)S(1)} %get-tuple-element.4), channel_id=1, source_target_pairs={{0,4},{1,5},{2,6},{3,7},{4,0},{5,1},{6,2},{7,3},{8,12},{9,13},{10,... | collective-permute-start | bytes 884744 | tf_op jit(solution)/shard_map/ppermute | solution.py:33
  112.4 2.9 %collective-permute-start.6 = (f32[16,768]{1,0:T(8,128)S(1)}, f32[16,768]{1,0:T(8,128)S(1)}, u32[]{:S(2)}, u32[]{:S(2)}) collective-permute-start(f32[16,768]{1,0:T(8,128)S(1)} %slice_select_fusion.3), channel_id=1, source_target_pairs={{0,1},{1,0},{2,3},{3,2},{4,5},{5,4},{6,7},{7,6},{8,9},{9,8},{10,11... | collective-permute-start | bytes 147464 | tf_op jit(solution)/shard_map/ppermute | solution.py:62
  116.7 7.0 %collective-permute-done.13 = f32[96,768]{1,0:T(8,128)S(1)} collective-permute-done((f32[96,768]{1,0:T(8,128)S(1)}, f32[96,768]{1,0:T(8,128)S(1)}, u32[]{:S(2)}, u32[]{:S(2)}) %collective-permute-start.13) | collective-permute-done | bytes 294944 | tf_op jit(solution)/shard_map/ppermute | solution.py:33
  123.9 2.9 %collective-permute-start.7 = (f32[16,768]{1,0:T(8,128)S(1)}, f32[16,768]{1,0:T(8,128)S(1)}, u32[]{:S(2)}, u32[]{:S(2)}) collective-permute-start(f32[16,768]{1,0:T(8,128)S(1)} %select_add_fusion.3), channel_id=1, source_target_pairs={{0,1},{1,0},{2,3},{3,2},{4,5},{5,4},{6,7},{7,6},{8,9},{9,8},{10,11... | collective-permute-start | bytes 147464 | tf_op jit(solution)/shard_map/ppermute | solution.py:63
  127.1 2.8 %collective-permute-done.7 = f32[16,768]{1,0:T(8,128)S(1)} collective-permute-done((f32[16,768]{1,0:T(8,128)S(1)}, f32[16,768]{1,0:T(8,128)S(1)}, u32[]{:S(2)}, u32[]{:S(2)}) %collective-permute-start.7) | collective-permute-done | bytes 49184 | tf_op jit(solution)/shard_map/ppermute | solution.py:63
  130.3 3.2 %collective-permute-done.15 = f32[48,768]{1,0:T(8,128)S(1)} collective-permute-done((f32[48,768]{1,0:T(8,128)S(1)}, f32[48,768]{1,0:T(8,128)S(1)}, u32[]{:S(2)}, u32[]{:S(2)}) %collective-permute-start.15) | collective-permute-done | bytes 147488 | tf_op jit(solution)/shard_map/ppermute | solution.py:60
  134.7 3.2 %collective-permute-start.9 = (f32[64,768]{1,0:T(8,128)S(1)}, f32[64,768]{1,0:T(8,128)S(1)}, u32[]{:S(2)}, u32[]{:S(2)}) collective-permute-start(f32[64,768]{1,0:T(8,128)S(1)} %maximum_select_fusion.3), channel_id=1, source_target_pairs={{0,6},{1,7},{2,0},{3,1},{4,2},{5,3},{6,4},{7,5},{8,14},{9,15},{10,... | collective-permute-start | bytes 589832 | tf_op jit(solution)/shard_map/ppermute | solution.py:33
  139.5 1.7 collective-permute-start.17
  141.2 4.6 %collective-permute-done.17 = f32[24,768]{1,0:T(8,128)S(1)} collective-permute-done((f32[24,768]{1,0:T(8,128)S(1)}, f32[24,768]{1,0:T(8,128)S(1)}, u32[]{:S(2)}, u32[]{:S(2)}) %collective-permute-start.17) | collective-permute-done | bytes 73760 | tf_op jit(solution)/shard_map/ppermute | solution.py:63
  148.0 3.0 %collective-permute-done.18 = f32[48,768]{1,0:T(8,128)S(1)} collective-permute-done((f32[48,768]{1,0:T(8,128)S(1)}, f32[48,768]{1,0:T(8,128)S(1)}, u32[]{:S(2)}, u32[]{:S(2)}) %collective-permute-start.18) | collective-permute-done | bytes 147488 | tf_op jit(solution)/shard_map/ppermute | solution.py:64
  151.1 2.4 %collective-permute-start.19 = (f32[96,768]{1,0:T(8,128)S(1)}, f32[96,768]{1,0:T(8,128)S(1)}, u32[]{:S(2)}, u32[]{:S(2)}) collective-permute-start(f32[96,768]{1,0:T(8,128)S(1)} %maximum_select_fusion.1), channel_id=1, source_target_pairs={{0,6},{1,7},{2,0},{3,1},{4,2},{5,3},{6,4},{7,5},{8,14},{9,15},{10,... | collective-permute-start | bytes 884744 | tf_op jit(solution)/shard_map/ppermute | solution.py:33
  155.0 6.6 %collective-permute-done.19 = f32[96,768]{1,0:T(8,128)S(1)} collective-permute-done((f32[96,768]{1,0:T(8,128)S(1)}, f32[96,768]{1,0:T(8,128)S(1)}, u32[]{:S(2)}, u32[]{:S(2)}) %collective-permute-start.19) | collective-permute-done | bytes 294944 | tf_op jit(solution)/shard_map/ppermute | solution.py:33
  162.4 3.0 %collective-permute-done.21 = f32[96,768]{1,0:T(8,128)S(1)} collective-permute-done((f32[96,768]{1,0:T(8,128)S(1)}, f32[96,768]{1,0:T(8,128)S(1)}, u32[]{:S(2)}, u32[]{:S(2)}) %collective-permute-start.21) | collective-permute-done | bytes 294944 | tf_op jit(solution)/shard_map/ppermute | solution.py:33
  165.7 16.0 %fusion.2 = f32[640,4096]{1,0:T(8,128)S(1)} fusion(f32[4096,768]{1,0:T(8,128)} %all-gather.2.cloned.1.call-done, f32[384,768]{1,0:T(8,128)S(1)} %bitcast.27, f32[256,768]{1,0:T(8,128)S(1)} %bitcast.28), kind=kOutput, calls=%fused_computation.5 | convolution fusion | flops 12080087040 | bytes 25034752 | tf_op jit(solution)/shard_map/dot_general | solution.py:11
  181.7 4.0 %copy-done = f32[640,4096]{1,0:T(8,128)} copy-done((f32[640,4096]{1,0:T(8,128)}, f32[640,4096]{1,0:T(8,128)S(1)}, u32[]{:S(2)}) %copy-start) | copy-done | bytes 10485784
  188.1 2.8 %collective-permute-done.23 = f32[4096]{0:T(1024)S(1)} collective-permute-done((f32[4096]{0:T(1024)S(1)}, f32[4096]{0:T(1024)S(1)}, u32[]{:S(2)}, u32[]{:S(2)}) %collective-permute-start.23) | collective-permute-done | bytes 16416 | tf_op jit(solution)/shard_map/ppermute | solution.py:72
  190.9 2.1 collective-permute-start.24
  193.0 3.1 %collective-permute-done.24 = f32[4096]{0:T(1024)S(1)} collective-permute-done((f32[4096]{0:T(1024)S(1)}, f32[4096]{0:T(1024)S(1)}, u32[]{:S(2)}, u32[]{:S(2)}) %collective-permute-start.24) | collective-permute-done | bytes 16416 | tf_op jit(solution)/shard_map/ppermute | solution.py:72
  196.2 3.5 %fusion.1 = f32[384]{0:T(512)S(1)} fusion(f32[640,4096]{1,0:T(8,128)} %copy-done, f32[4096]{0:T(1024)S(1)} %maximum_maximum_fusion), kind=kLoop, calls=%fused_computation.3 | loop fusion | flops 4718208 | bytes 6309376 | tf_op jit(solution)/shard_map/reduce_sum | solution.py:105
  201.2 2.1 collective-permute-done.26
  203.3 1.9 collective-permute-start.27
  205.3 3.2 %collective-permute-done.27 = f32[1,2,384]{2,0,1:T(1,128)S(1)} collective-permute-done((f32[1,2,384]{2,0,1:T(1,128)S(1)}, f32[1,2,384]{2,0,1:T(1,128)S(1)}, u32[]{:S(2)}, u32[]{:S(2)}) %collective-permute-start.27) | collective-permute-done | bytes 3104 | tf_op jit(solution)/shard_map/ppermute | solution.py:81
  210.1 2.1 collective-permute-done.28
  214.2 3.3 %collective-permute-done.29 = f32[4,2,384]{2,0,1:T(4,128)S(1)} collective-permute-done((f32[4,2,384]{2,0,1:T(4,128)S(1)}, f32[4,2,384]{2,0,1:T(4,128)S(1)}, u32[]{:S(2)}, u32[]{:S(2)}) %collective-permute-start.29) | collective-permute-done | bytes 12320 | tf_op jit(solution)/shard_map/ppermute | solution.py:81
  (93 shorter events, 29.7 us)
Async XLA Ops:
  7.2 72.3 %all-gather.2.cloned.1.call-start = ((), (), s32[]{:S(2)}) async-start(), calls=%async_computation | async-start | bytes 14155776 | tf_op jit(solution)/shard_map/all_gather | solution.py:92
  7.9 6.5 %collective-permute-start.1 = (s32[192]{0:T(256)}, s32[192]{0:T(256)S(1)}, u32[]{:S(2)}, u32[]{:S(2)}) collective-permute-start(s32[192]{0:T(256)} %param.7), channel_id=1, source_target_pairs={{0,64},{64,0},{1,65},{65,1},{2,66},{66,2},{3,67},{67,3},{4,68},{68... | collective-permute-start | bytes 2312 | tf_op jit(solution)/shard_map/ppermute | solution.py:96
  10.0 3.7 %collective-permute-start = (s32[128]{0:T(128)}, s32[128]{0:T(128)S(1)}, u32[]{:S(2)}, u32[]{:S(2)}) collective-permute-start(s32[128]{0:T(128)} %param.6), channel_id=1, source_target_pairs={{0,64},{64,0},{1,65},{65,1},{2,66},{66,2},{3,67},{67,3},{4,68},{68... | collective-permute-start | bytes 1544 | tf_op jit(solution)/shard_map/ppermute | solution.py:95
  90.7 8.5 %collective-permute-start.2 = (f32[64,768]{1,0:T(8,128)}, f32[64,768]{1,0:T(8,128)S(1)}, u32[]{:S(2)}, u32[]{:S(2)}) collective-permute-start(f32[64,768]{1,0:T(8,128)} %get-tuple-element.5), channel_id=1, source_target_pairs={{0,2},{1,3},{2,4},{3,5},{4,6},{5,7},{6,0},{7,1},{8,10},{9,11},{10,... | collective-permute-start | bytes 589832 | tf_op jit(solution)/shard_map/ppermute | solution.py:33
  92.2 12.2 %collective-permute-start.3 = (f32[64,768]{1,0:T(8,128)S(1)}, f32[64,768]{1,0:T(8,128)S(1)}, u32[]{:S(2)}, u32[]{:S(2)}) collective-permute-start(f32[64,768]{1,0:T(8,128)S(1)} %get-tuple-element.7), channel_id=1, source_target_pairs={{0,4},{1,5},{2,6},{3,7},{4,0},{5,1},{6,2},{7,3},{8,12},{9,13},{10,... | collective-permute-start | bytes 589832 | tf_op jit(solution)/shard_map/ppermute | solution.py:33
  94.9 9.5 %collective-permute-start.4 = (f32[64,768]{1,0:T(8,128)S(1)}, f32[64,768]{1,0:T(8,128)}, u32[]{:S(2)}, u32[]{:S(2)}) collective-permute-start(f32[64,768]{1,0:T(8,128)S(1)} %get-tuple-element.6), channel_id=1, source_target_pairs={{0,6},{1,7},{2,0},{3,1},{4,2},{5,3},{6,4},{7,5},{8,14},{9,15},{10,... | collective-permute-start | bytes 589832 | tf_op jit(solution)/shard_map/ppermute | solution.py:33
  105.4 7.0 %collective-permute-start.5 = (f32[32,768]{1,0:T(8,128)S(1)}, f32[32,768]{1,0:T(8,128)S(1)}, u32[]{:S(2)}, u32[]{:S(2)}) collective-permute-start(f32[32,768]{1,0:T(8,128)S(1)} %slice_select_fusion.1), channel_id=1, source_target_pairs={{0,64},{64,0},{1,65},{65,1},{2,66},{66,2},{3,67},{67,3},{4,68},{68... | collective-permute-start | bytes 294920 | tf_op jit(solution)/shard_map/ppermute | solution.py:60
  107.1 9.6 %collective-permute-start.12 = (f32[96,768]{1,0:T(8,128)S(1)}, f32[96,768]{1,0:T(8,128)S(1)}, u32[]{:S(2)}, u32[]{:S(2)}) collective-permute-start(f32[96,768]{1,0:T(8,128)S(1)} %get-tuple-element.2), channel_id=1, source_target_pairs={{0,2},{1,3},{2,4},{3,5},{4,6},{5,7},{6,0},{7,1},{8,10},{9,11},{10,... | collective-permute-start | bytes 884744 | tf_op jit(solution)/shard_map/ppermute | solution.py:33
  108.4 15.3 %collective-permute-start.13 = (f32[96,768]{1,0:T(8,128)S(1)}, f32[96,768]{1,0:T(8,128)S(1)}, u32[]{:S(2)}, u32[]{:S(2)}) collective-permute-start(f32[96,768]{1,0:T(8,128)S(1)} %get-tuple-element.4), channel_id=1, source_target_pairs={{0,4},{1,5},{2,6},{3,7},{4,0},{5,1},{6,2},{7,3},{8,12},{9,13},{10,... | collective-permute-start | bytes 884744 | tf_op jit(solution)/shard_map/ppermute | solution.py:33
  110.8 12.9 %collective-permute-start.14 = (f32[96,768]{1,0:T(8,128)S(1)}, f32[96,768]{1,0:T(8,128)S(1)}, u32[]{:S(2)}, u32[]{:S(2)}) collective-permute-start(f32[96,768]{1,0:T(8,128)S(1)} %get-tuple-element.3), channel_id=1, source_target_pairs={{0,6},{1,7},{2,0},{3,1},{4,2},{5,3},{6,4},{7,5},{8,14},{9,15},{10,... | collective-permute-start | bytes 884744 | tf_op jit(solution)/shard_map/ppermute | solution.py:33
  112.4 11.4 %collective-permute-start.6 = (f32[16,768]{1,0:T(8,128)S(1)}, f32[16,768]{1,0:T(8,128)S(1)}, u32[]{:S(2)}, u32[]{:S(2)}) collective-permute-start(f32[16,768]{1,0:T(8,128)S(1)} %slice_select_fusion.3), channel_id=1, source_target_pairs={{0,1},{1,0},{2,3},{3,2},{4,5},{5,4},{6,7},{7,6},{8,9},{9,8},{10,11... | collective-permute-start | bytes 147464 | tf_op jit(solution)/shard_map/ppermute | solution.py:62
  123.9 6.0 %collective-permute-start.7 = (f32[16,768]{1,0:T(8,128)S(1)}, f32[16,768]{1,0:T(8,128)S(1)}, u32[]{:S(2)}, u32[]{:S(2)}) collective-permute-start(f32[16,768]{1,0:T(8,128)S(1)} %select_add_fusion.3), channel_id=1, source_target_pairs={{0,1},{1,0},{2,3},{3,2},{4,5},{5,4},{6,7},{7,6},{8,9},{9,8},{10,11... | collective-permute-start | bytes 147464 | tf_op jit(solution)/shard_map/ppermute | solution.py:63
  126.8 6.7 %collective-permute-start.15 = (f32[48,768]{1,0:T(8,128)S(1)}, f32[48,768]{1,0:T(8,128)S(1)}, u32[]{:S(2)}, u32[]{:S(2)}) collective-permute-start(f32[48,768]{1,0:T(8,128)S(1)} %slice_select_fusion), channel_id=1, source_target_pairs={{0,64},{64,0},{1,65},{65,1},{2,66},{66,2},{3,67},{67,3},{4,68},{68... | collective-permute-start | bytes 442376 | tf_op jit(solution)/shard_map/ppermute | solution.py:60
  129.9 4.7 %collective-permute-start.8 = (f32[32,768]{1,0:T(8,128)S(1)}, f32[32,768]{1,0:T(8,128)S(1)}, u32[]{:S(2)}, u32[]{:S(2)}) collective-permute-start(f32[32,768]{1,0:T(8,128)S(1)} %maximum_select_fusion.5), channel_id=1, source_target_pairs={{0,64},{64,0},{1,65},{65,1},{2,66},{66,2},{3,67},{67,3},{4,68},{68... | collective-permute-start | bytes 294920 | tf_op jit(solution)/shard_map/ppermute | solution.py:64
  133.6 5.9 %collective-permute-start.16 = (f32[24,768]{1,0:T(8,128)S(1)}, f32[24,768]{1,0:T(8,128)S(1)}, u32[]{:S(2)}, u32[]{:S(2)}) collective-permute-start(f32[24,768]{1,0:T(8,128)S(1)} %slice_select_fusion.2), channel_id=1, source_target_pairs={{0,1},{1,0},{2,3},{3,2},{4,5},{5,4},{6,7},{7,6},{8,9},{9,8},{10,11... | collective-permute-start | bytes 221192 | tf_op jit(solution)/shard_map/ppermute | solution.py:62
  134.7 11.7 %collective-permute-start.9 = (f32[64,768]{1,0:T(8,128)S(1)}, f32[64,768]{1,0:T(8,128)S(1)}, u32[]{:S(2)}, u32[]{:S(2)}) collective-permute-start(f32[64,768]{1,0:T(8,128)S(1)} %maximum_select_fusion.3), channel_id=1, source_target_pairs={{0,6},{1,7},{2,0},{3,1},{4,2},{5,3},{6,4},{7,5},{8,14},{9,15},{10,... | collective-permute-start | bytes 589832 | tf_op jit(solution)/shard_map/ppermute | solution.py:33
  137.9 8.5 %collective-permute-start.10 = (f32[64,768]{1,0:T(8,128)S(1)}, f32[64,768]{1,0:T(8,128)S(1)}, u32[]{:S(2)}, u32[]{:S(2)}) collective-permute-start(f32[64,768]{1,0:T(8,128)S(1)} %maximum_select_fusion.3), channel_id=1, source_target_pairs={{0,4},{1,5},{2,6},{3,7},{4,0},{5,1},{6,2},{7,3},{8,12},{9,13},{10,... | collective-permute-start | bytes 589832 | tf_op jit(solution)/shard_map/ppermute | solution.py:33
  138.9 9.0 %collective-permute-start.11 = (f32[64,768]{1,0:T(8,128)S(1)}, f32[64,768]{1,0:T(8,128)S(1)}, u32[]{:S(2)}, u32[]{:S(2)}) collective-permute-start(f32[64,768]{1,0:T(8,128)S(1)} %maximum_select_fusion.3), channel_id=1, source_target_pairs={{0,2},{1,3},{2,4},{3,5},{4,6},{5,7},{6,0},{7,1},{8,10},{9,11},{10,... | collective-permute-start | bytes 589832 | tf_op jit(solution)/shard_map/ppermute | solution.py:33
  139.5 6.3 %collective-permute-start.17 = (f32[24,768]{1,0:T(8,128)S(1)}, f32[24,768]{1,0:T(8,128)S(1)}, u32[]{:S(2)}, u32[]{:S(2)}) collective-permute-start(f32[24,768]{1,0:T(8,128)S(1)} %select_add_fusion.2), channel_id=1, source_target_pairs={{0,1},{1,0},{2,3},{3,2},{4,5},{5,4},{6,7},{7,6},{8,9},{9,8},{10,11... | collective-permute-start | bytes 221192 | tf_op jit(solution)/shard_map/ppermute | solution.py:63
  145.9 5.2 %collective-permute-start.18 = (f32[48,768]{1,0:T(8,128)S(1)}, f32[48,768]{1,0:T(8,128)S(1)}, u32[]{:S(2)}, u32[]{:S(2)}) collective-permute-start(f32[48,768]{1,0:T(8,128)S(1)} %maximum_select_fusion.4), channel_id=1, source_target_pairs={{0,64},{64,0},{1,65},{65,1},{2,66},{66,2},{3,67},{67,3},{4,68},{68... | collective-permute-start | bytes 442376 | tf_op jit(solution)/shard_map/ppermute | solution.py:64
  151.1 10.5 %collective-permute-start.19 = (f32[96,768]{1,0:T(8,128)S(1)}, f32[96,768]{1,0:T(8,128)S(1)}, u32[]{:S(2)}, u32[]{:S(2)}) collective-permute-start(f32[96,768]{1,0:T(8,128)S(1)} %maximum_select_fusion.1), channel_id=1, source_target_pairs={{0,6},{1,7},{2,0},{3,1},{4,2},{5,3},{6,4},{7,5},{8,14},{9,15},{10,... | collective-permute-start | bytes 884744 | tf_op jit(solution)/shard_map/ppermute | solution.py:33
  153.6 8.8 %collective-permute-start.20 = (f32[96,768]{1,0:T(8,128)S(1)}, f32[96,768]{1,0:T(8,128)S(1)}, u32[]{:S(2)}, u32[]{:S(2)}) collective-permute-start(f32[96,768]{1,0:T(8,128)S(1)} %maximum_select_fusion.1), channel_id=1, source_target_pairs={{0,4},{1,5},{2,6},{3,7},{4,0},{5,1},{6,2},{7,3},{8,12},{9,13},{10,... | collective-permute-start | bytes 884744 | tf_op jit(solution)/shard_map/ppermute | solution.py:33
  155.0 10.5 %collective-permute-start.21 = (f32[96,768]{1,0:T(8,128)S(1)}, f32[96,768]{1,0:T(8,128)S(1)}, u32[]{:S(2)}, u32[]{:S(2)}) collective-permute-start(f32[96,768]{1,0:T(8,128)S(1)} %maximum_select_fusion.1), channel_id=1, source_target_pairs={{0,2},{1,3},{2,4},{3,5},{4,6},{5,7},{6,0},{7,1},{8,10},{9,11},{10,... | collective-permute-start | bytes 884744 | tf_op jit(solution)/shard_map/ppermute | solution.py:33
  185.7 10.5 %copy-start.1 = (f32[8192]{0:T(1024)S(1)}, f32[8192]{0:T(1024)}, u32[]{:S(2)}) copy-start(f32[8192]{0:T(1024)} %param.5) | copy-start | bytes 98308
  185.9 1.3 collective-permute-start.22
  187.2 3.7 %collective-permute-start.23 = (f32[4096]{0:T(1024)S(1)}, f32[4096]{0:T(1024)S(1)}, u32[]{:S(2)}, u32[]{:S(2)}) collective-permute-start(f32[4096]{0:T(1024)S(1)} %max.22), channel_id=1, source_target_pairs={{0,16},{8,24},{16,0},{24,8},{32,48},{40,56},{48,32},{56,40},{1,17}... | collective-permute-start | bytes 49160 | tf_op jit(solution)/shard_map/ppermute | solution.py:72
  190.9 5.2 %collective-permute-start.24 = (f32[4096]{0:T(1024)S(1)}, f32[4096]{0:T(1024)S(1)}, u32[]{:S(2)}, u32[]{:S(2)}) collective-permute-start(f32[4096]{0:T(1024)S(1)} %max.23), channel_id=1, source_target_pairs={{0,32},{8,40},{16,48},{24,56},{32,0},{40,8},{48,16},{56,24},{1,33}... | collective-permute-start | bytes 49160 | tf_op jit(solution)/shard_map/ppermute | solution.py:72
  199.7 3.7 %collective-permute-start.26 = (f32[1,384]{1,0:T(1,128)S(1)}, f32[1,384]{1,0:T(1,128)S(1)}, u32[]{:S(2)}, u32[]{:S(2)}) collective-permute-start(f32[1,384]{1,0:T(1,128)S(1)} %broadcast_in_dim.32), channel_id=1, source_target_pairs={{0,64},{64,0},{1,65},{65,1},{2,66},{66,2},{3,67},{67,3},{4,68},{68... | collective-permute-start | bytes 4616 | tf_op jit(solution)/shard_map/ppermute | solution.py:81
  203.3 5.1 %collective-permute-start.27 = (f32[1,2,384]{2,0,1:T(1,128)S(1)}, f32[1,2,384]{2,0,1:T(1,128)S(1)}, u32[]{:S(2)}, u32[]{:S(2)}) collective-permute-start(f32[1,2,384]{2,0,1:T(1,128)S(1)} %broadcast_select_fusion), channel_id=1, source_target_pairs={{0,1},{1,0},{2,3},{3,2},{4,5},{5,4},{6,7},{7,6},{8,9},{9,8},{10,11... | collective-permute-start | bytes 9224 | tf_op jit(solution)/shard_map/ppermute | solution.py:81
  208.5 3.7 %collective-permute-start.28 = (f32[2,2,384]{2,0,1:T(2,128)S(1)}, f32[2,2,384]{2,0,1:T(2,128)S(1)}, u32[]{:S(2)}, u32[]{:S(2)}) collective-permute-start(f32[2,2,384]{2,0,1:T(2,128)S(1)} %maximum_select_fusion.9), channel_id=1, source_target_pairs={{0,2},{1,3},{2,0},{3,1},{4,6},{5,7},{6,4},{7,5},{8,10},{9,11},{10,... | collective-permute-start | bytes 18440 | tf_op jit(solution)/shard_map/ppermute | solution.py:81
  208.6 5.0 %collective-permute-start.25 = (f32[4096]{0:T(1024)S(1)}, f32[4096]{0:T(1024)S(1)}, u32[]{:S(2)}, u32[]{:S(2)}) collective-permute-start(f32[4096]{0:T(1024)S(1)} %maximum_maximum_fusion), channel_id=1, source_target_pairs={{0,64},{64,0},{1,65},{65,1},{2,66},{66,2},{3,67},{67,3},{4,68},{68... | collective-permute-start | bytes 49160 | tf_op jit(solution)/shard_map/ppermute | solution.py:109
  212.2 5.3 %collective-permute-start.29 = (f32[4,2,384]{2,0,1:T(4,128)S(1)}, f32[4,2,384]{2,0,1:T(4,128)S(1)}, u32[]{:S(2)}, u32[]{:S(2)}) collective-permute-start(f32[4,2,384]{2,0,1:T(4,128)S(1)} %maximum_select_fusion.8), channel_id=1, source_target_pairs={{0,4},{1,5},{2,6},{3,7},{4,0},{5,1},{6,2},{7,3},{8,12},{9,13},{10,... | collective-permute-start | bytes 36872 | tf_op jit(solution)/shard_map/ppermute | solution.py:81
  (1 other events, 4.0 us)
Sparse Core Ops, SparseCore 0:
  9.7 69.7 all-gather.1

commit v15 on v8

--- a/solution.py
+++ b/solution.py
@@ -95,7 +95,8 @@
     both_sel = pair_join(sel_index, lax.ppermute(sel_index, "zl", zl_swap), zl == 0)
     both_cand = pair_join(cand_index, lax.ppermute(cand_index, "zl", zl_swap), zl == 0)
     selected = group_masked_sum(lookup(half, both_sel, first_row))
-    chosen = group_masked_sum(lookup(half, both_cand, first_row))
+    selected, cand_rows = lax.optimization_barrier((selected, lookup(half, both_cand, first_row)))
+    chosen = group_masked_sum(cand_rows)
     reached = all_max(jnp.max(similar(selected, half), axis=0), "xc", n_xc)
     old = lax.dynamic_slice_in_dim(coverage_old, zl * half.shape[0], half.shape[0])
     coverage = jnp.maximum(old, reached)

time: 221 us -> 249 us (1.13)
  waiting for transfers between devices: 128 us -> 151 us
  starting transfers between devices: 33.7 us -> 38.3 us
    ppermute x12, waiting for transfers between devices: 26.3 us -> 42.7 us  [y_shift(): return lax.ppermute(value, 'col', pairs)]
    ppermute x2, waiting for transfers between devices: 3.6 us -> 7.29 us  [group_masked_sum(): mine = mine + lax.ppermute(theirs, 'zl', zl_swap)]
  transfers between devices with their start and end apart: 31 -> 31, of which waited for: 24 -> 27; matrix products, arithmetic and copies ran while one was open for 12% -> 10% of each run, Pallas kernels for 0% -> 0%
where the time goes in v15:
time: 249 us
  waiting for transfers between devices  151 us (61%)
  starting transfers between devices  38.3 us (15%)
  matrix products  28.1 us (11%)
  between operations  14.4 us (6%)
  local copies, waits for them, and re-layouts  14.2 us (6%)
  other arithmetic  3.34 us (1%)
    all_gather x1, waiting for transfers between devices, body(): half = lax.all_gather(slab_embed, 'xc', axis=0, tiled=True)  67.9 us
    ppermute x12, waiting for transfers between devices, y_shift(): return lax.ppermute(value, 'col', pairs)  42.7 us
    dot_general x2, matrix products, similar(): lax.dot_general(left, right, (((1,), (1,)), ((), ())), precision=lax.Prec...  28.1 us
    gather x2, local copies, waits for them, and re-layouts, lookup(): jnp.take(source, jnp.clip(position, 0, source.shape[0] - 1), axis=0)  13 us
    ppermute x4, waiting for transfers between devices, gather_in_order(): other = lax.ppermute(parts, axis, [(i, i ^ bit) for i in range(n)])  11.5 us
    ppermute x12, starting transfers between devices, y_shift(): return lax.ppermute(value, 'col', pairs)  11 us
    ppermute x2, waiting for transfers between devices, group_masked_sum(): mine = mine + lax.ppermute(theirs, 'zl', zl_swap)  7.29 us
    ppermute x3, waiting for transfers between devices, all_max(): lax.ppermute(value, axis, [(i, i ^ bit) for i in range(n)])  6.54 us
  transfers between devices with their start and end apart: 31, of which 27 were waited for; matrix products, arithmetic and copies ran while one was open for 10% of the time, Pallas kernels for 0%

profile of v15, /device:TPU:0, one launch (start us, length us, event | category | flops | bytes accessed | tf_op | source)
XLA Modules:
  0.0 249.2 jit_solution(17644925483087499134)
XLA Ops:
  11.6 67.9 %all-gather.2.cloned.1.call-done = f32[4096,768]{1,0:T(8,128)} async-done(((f32[512,768]{1,0:T(8,128)}), f32[4096,768]{1,0:T(8,128)}) %all-gather.2.cloned.1.call-update) | async-done | bytes 12582928 | tf_op jit(solution)/shard_map/all_gather | solution.py:92
  79.5 6.0 %gather_fusion = f32[256,768]{1,0:T(8,128)S(1)} fusion(f32[4096,768]{1,0:T(8,128)} %all-gather.2.cloned.1.call-done, s32[1024]{0:T(1024)S(1)} %pad_clamp_fusion.1), kind=kCustom, calls=%fused_computation | custom fusion | bytes 1573888 | tf_op jit(solution)/shard_map/jit(_take)/gather | solution.py:23
  85.7 2.8 %collective-permute-start.3 = (f32[64,768]{1,0:T(8,128)S(1)}, f32[64,768]{1,0:T(8,128)S(1)}, u32[]{:S(2)}, u32[]{:S(2)}) collective-permute-start(f32[64,768]{1,0:T(8,128)S(1)} %get-tuple-element.12), channel_id=1, source_target_pairs={{0,6},{1,7},{2,0},{3,1},{4,2},{5,3},{6,4},{7,5},{8,14},{9,15},{10,... | collective-permute-start | bytes 589832 | tf_op jit(solution)/shard_map/ppermute | solution.py:33
  90.2 7.1 %collective-permute-done.3 = f32[64,768]{1,0:T(8,128)S(1)} collective-permute-done((f32[64,768]{1,0:T(8,128)S(1)}, f32[64,768]{1,0:T(8,128)S(1)}, u32[]{:S(2)}, u32[]{:S(2)}) %collective-permute-start.3) | collective-permute-done | bytes 196640 | tf_op jit(solution)/shard_map/ppermute | solution.py:33
  97.8 3.2 %collective-permute-done.1 = f32[64,768]{1,0:T(8,128)S(1)} collective-permute-done((f32[64,768]{1,0:T(8,128)S(1)}, f32[64,768]{1,0:T(8,128)S(1)}, u32[]{:S(2)}, u32[]{:S(2)}) %collective-permute-start.1) | collective-permute-done | bytes 196640 | tf_op jit(solution)/shard_map/ppermute | solution.py:33
  102.7 3.2 %collective-permute-done.4 = f32[32,768]{1,0:T(8,128)S(1)} collective-permute-done((f32[32,768]{1,0:T(8,128)S(1)}, f32[32,768]{1,0:T(8,128)S(1)}, u32[]{:S(2)}, u32[]{:S(2)}) %collective-permute-start.4) | collective-permute-done | bytes 98336 | tf_op jit(solution)/shard_map/ppermute | solution.py:60
  105.9 3.2 %collective-permute-start.5 = (f32[16,768]{1,0:T(8,128)S(1)}, f32[16,768]{1,0:T(8,128)S(1)}, u32[]{:S(2)}, u32[]{:S(2)}) collective-permute-start(f32[16,768]{1,0:T(8,128)S(1)} %slice_select_fusion.3), channel_id=1, source_target_pairs={{0,1},{1,0},{2,3},{3,2},{4,5},{5,4},{6,7},{7,6},{8,9},{9,8},{10,11... | collective-permute-start | bytes 147464 | tf_op jit(solution)/shard_map/ppermute | solution.py:62
  109.8 2.9 %collective-permute-done.11 = s32[192]{0:T(256)S(1)} collective-permute-done((s32[192]{0:T(256)S(1)}, s32[192]{0:T(256)S(1)}, u32[]{:S(2)}, u32[]{:S(2)}) %collective-permute-start.11) | collective-permute-done | bytes 800 | tf_op jit(solution)/shard_map/ppermute | solution.py:96
  114.8 3.7 %collective-permute-done.6 = f32[16,768]{1,0:T(8,128)S(1)} collective-permute-done((f32[16,768]{1,0:T(8,128)S(1)}, f32[16,768]{1,0:T(8,128)S(1)}, u32[]{:S(2)}, u32[]{:S(2)}) %collective-permute-start.6) | collective-permute-done | bytes 49184 | tf_op jit(solution)/shard_map/ppermute | solution.py:63
  119.4 7.1 %gather_fusion.1 = f32[384,768]{1,0:T(8,128)S(1)} fusion(f32[4096,768]{1,0:T(8,128)} %all-gather.2.cloned.1.call-done, s32[1024]{0:T(1024)S(1)} %pad_clamp_fusion), kind=kCustom, calls=%fused_computation.1 | custom fusion | bytes 2360832 | tf_op jit(solution)/shard_map/jit(_take)/gather | solution.py:23
  129.1 3.1 %collective-permute-done.8 = f32[64,768]{1,0:T(8,128)S(1)} collective-permute-done((f32[64,768]{1,0:T(8,128)S(1)}, f32[64,768]{1,0:T(8,128)S(1)}, u32[]{:S(2)}, u32[]{:S(2)}) %collective-permute-start.8) | collective-permute-done | bytes 196640 | tf_op jit(solution)/shard_map/ppermute | solution.py:33
  132.2 3.0 %collective-permute-done.9 = f32[64,768]{1,0:T(8,128)S(1)} collective-permute-done((f32[64,768]{1,0:T(8,128)S(1)}, f32[64,768]{1,0:T(8,128)S(1)}, u32[]{:S(2)}, u32[]{:S(2)}) %collective-permute-start.9) | collective-permute-done | bytes 196640 | tf_op jit(solution)/shard_map/ppermute | solution.py:33
  135.2 2.7 %collective-permute-done.10 = f32[64,768]{1,0:T(8,128)S(1)} collective-permute-done((f32[64,768]{1,0:T(8,128)S(1)}, f32[64,768]{1,0:T(8,128)S(1)}, u32[]{:S(2)}, u32[]{:S(2)}) %collective-permute-start.10) | collective-permute-done | bytes 196640 | tf_op jit(solution)/shard_map/ppermute | solution.py:33
  140.3 4.7 %collective-permute-done.18 = f32[96,768]{1,0:T(8,128)S(1)} collective-permute-done((f32[96,768]{1,0:T(8,128)S(1)}, f32[96,768]{1,0:T(8,128)S(1)}, u32[]{:S(2)}, u32[]{:S(2)}) %collective-permute-start.18) | collective-permute-done | bytes 294944 | tf_op jit(solution)/shard_map/ppermute | solution.py:33
  145.0 2.1 collective-permute-done.17
  147.1 3.2 %collective-permute-done.16 = f32[96,768]{1,0:T(8,128)} collective-permute-done((f32[96,768]{1,0:T(8,128)S(1)}, f32[96,768]{1,0:T(8,128)}, u32[]{:S(2)}, u32[]{:S(2)}) %collective-permute-start.16) | collective-permute-done | bytes 294944 | tf_op jit(solution)/shard_map/ppermute | solution.py:33
  152.4 4.1 %collective-permute-done.19 = f32[48,768]{1,0:T(8,128)S(1)} collective-permute-done((f32[48,768]{1,0:T(8,128)S(1)}, f32[48,768]{1,0:T(8,128)S(1)}, u32[]{:S(2)}, u32[]{:S(2)}) %collective-permute-start.19) | collective-permute-done | bytes 147488 | tf_op jit(solution)/shard_map/ppermute | solution.py:60
  156.6 2.5 %collective-permute-start.20 = (f32[24,768]{1,0:T(8,128)S(1)}, f32[24,768]{1,0:T(8,128)S(1)}, u32[]{:S(2)}, u32[]{:S(2)}) collective-permute-start(f32[24,768]{1,0:T(8,128)S(1)} %slice_select_fusion.2), channel_id=1, source_target_pairs={{0,1},{1,0},{2,3},{3,2},{4,5},{5,4},{6,7},{7,6},{8,9},{9,8},{10,11... | collective-permute-start | bytes 221192 | tf_op jit(solution)/shard_map/ppermute | solution.py:62
  159.1 3.4 %collective-permute-done.20 = f32[24,768]{1,0:T(8,128)S(1)} collective-permute-done((f32[24,768]{1,0:T(8,128)S(1)}, f32[24,768]{1,0:T(8,128)S(1)}, u32[]{:S(2)}, u32[]{:S(2)}) %collective-permute-start.20) | collective-permute-done | bytes 73760 | tf_op jit(solution)/shard_map/ppermute | solution.py:62
  162.5 3.2 %collective-permute-start.21 = (f32[24,768]{1,0:T(8,128)S(1)}, f32[24,768]{1,0:T(8,128)S(1)}, u32[]{:S(2)}, u32[]{:S(2)}) collective-permute-start(f32[24,768]{1,0:T(8,128)S(1)} %select_add_fusion.2), channel_id=1, source_target_pairs={{0,1},{1,0},{2,3},{3,2},{4,5},{5,4},{6,7},{7,6},{8,9},{9,8},{10,11... | collective-permute-start | bytes 221192 | tf_op jit(solution)/shard_map/ppermute | solution.py:63
  165.7 2.7 %collective-permute-done.21 = f32[24,768]{1,0:T(8,128)S(1)} collective-permute-done((f32[24,768]{1,0:T(8,128)S(1)}, f32[24,768]{1,0:T(8,128)S(1)}, u32[]{:S(2)}, u32[]{:S(2)}) %collective-permute-start.21) | collective-permute-done | bytes 73760 | tf_op jit(solution)/shard_map/ppermute | solution.py:63
  169.9 17.2 %convolution_reduce_fusion = f32[4096]{0:T(1024)S(1)} fusion(f32[256,768]{1,0:T(8,128)S(1)} %bitcast.35, f32[4096,768]{1,0:T(8,128)} %all-gather.2.cloned.1.call-done), kind=kOutput, calls=%fused_computation.3 | convolution fusion | flops 4832882688 | bytes 13385728 | tf_op jit(solution)/shard_map/dot_general | solution.py:11
  189.3 2.8 %collective-permute-done.13 = f32[4096]{0:T(1024)S(1)} collective-permute-done((f32[4096]{0:T(1024)S(1)}, f32[4096]{0:T(1024)S(1)}, u32[]{:S(2)}, u32[]{:S(2)}) %collective-permute-start.13) | collective-permute-done | bytes 16416 | tf_op jit(solution)/shard_map/ppermute | solution.py:72
  194.8 2.5 %collective-permute-done.14 = f32[4096]{0:T(1024)S(1)} collective-permute-done((f32[4096]{0:T(1024)S(1)}, f32[4096]{0:T(1024)S(1)}, u32[]{:S(2)}, u32[]{:S(2)}) %collective-permute-start.14) | collective-permute-done | bytes 16416 | tf_op jit(solution)/shard_map/ppermute | solution.py:72
  198.9 5.4 %collective-permute-done.23 = f32[96,768]{1,0:T(8,128)S(1)} collective-permute-done((f32[96,768]{1,0:T(8,128)S(1)}, f32[96,768]{1,0:T(8,128)S(1)}, u32[]{:S(2)}, u32[]{:S(2)}) %collective-permute-start.23) | collective-permute-done | bytes 294944 | tf_op jit(solution)/shard_map/ppermute | solution.py:33
  204.3 4.6 %collective-permute-done.24 = f32[96,768]{1,0:T(8,128)S(1)} collective-permute-done((f32[96,768]{1,0:T(8,128)S(1)}, f32[96,768]{1,0:T(8,128)S(1)}, u32[]{:S(2)}, u32[]{:S(2)}) %collective-permute-start.24) | collective-permute-done | bytes 294944 | tf_op jit(solution)/shard_map/ppermute | solution.py:33
  208.9 3.1 %collective-permute-done.25 = f32[96,768]{1,0:T(8,128)S(1)} collective-permute-done((f32[96,768]{1,0:T(8,128)S(1)}, f32[96,768]{1,0:T(8,128)S(1)}, u32[]{:S(2)}, u32[]{:S(2)}) %collective-permute-start.25) | collective-permute-done | bytes 294944 | tf_op jit(solution)/shard_map/ppermute | solution.py:33
  212.3 10.8 %fusion.13 = f32[384,4096]{1,0:T(8,128)S(1)} fusion(f32[384,768]{1,0:T(8,128)S(1)} %bitcast.34, f32[4096,768]{1,0:T(8,128)} %all-gather.2.cloned.1.call-done), kind=kOutput, calls=%fused_computation.74 | convolution fusion | flops 7247757312 | bytes 20054016 | tf_op jit(solution)/shard_map/dot_general | solution.py:11
  224.9 2.7 %collective-permute-done.26 = f32[1,384]{1,0:T(1,128)S(1)} collective-permute-done((f32[1,384]{1,0:T(1,128)S(1)}, f32[1,384]{1,0:T(1,128)S(1)}, u32[]{:S(2)}, u32[]{:S(2)}) %collective-permute-start.26) | collective-permute-done | bytes 1568 | tf_op jit(solution)/shard_map/ppermute | solution.py:81
  229.6 3.1 %collective-permute-done.27 = f32[1,2,384]{2,0,1:T(1,128)S(1)} collective-permute-done((f32[1,2,384]{2,0,1:T(1,128)S(1)}, f32[1,2,384]{2,0,1:T(1,128)S(1)}, u32[]{:S(2)}, u32[]{:S(2)}) %collective-permute-start.27) | collective-permute-done | bytes 3104 | tf_op jit(solution)/shard_map/ppermute | solution.py:81
  233.8 2.6 %collective-permute-done.28 = f32[2,2,384]{2,0,1:T(2,128)S(1)} collective-permute-done((f32[2,2,384]{2,0,1:T(2,128)S(1)}, f32[2,2,384]{2,0,1:T(2,128)S(1)}, u32[]{:S(2)}, u32[]{:S(2)}) %collective-permute-start.28) | collective-permute-done | bytes 6176 | tf_op jit(solution)/shard_map/ppermute | solution.py:81
  238.5 3.2 %collective-permute-done.29 = f32[4,2,384]{2,0,1:T(4,128)S(1)} collective-permute-done((f32[4,2,384]{2,0,1:T(4,128)S(1)}, f32[4,2,384]{2,0,1:T(4,128)S(1)}, u32[]{:S(2)}, u32[]{:S(2)}) %collective-permute-start.29) | collective-permute-done | bytes 12320 | tf_op jit(solution)/shard_map/ppermute | solution.py:81
  (96 shorter events, 34.9 us)
Async XLA Ops:
  7.2 72.3 %all-gather.2.cloned.1.call-start = ((), (), s32[]{:S(2)}) async-start(), calls=%async_computation | async-start | bytes 14155776 | tf_op jit(solution)/shard_map/all_gather | solution.py:92
  7.9 3.6 %collective-permute-start = (s32[128]{0:T(128)S(1)}, s32[128]{0:T(128)S(1)}, u32[]{:S(2)}, u32[]{:S(2)}) collective-permute-start(s32[128]{0:T(128)S(1)} %copy-done.2), channel_id=1, source_target_pairs={{0,64},{64,0},{1,65},{65,1},{2,66},{66,2},{3,67},{67,3},{4,68},{68... | collective-permute-start | bytes 1544 | tf_op jit(solution)/shard_map/ppermute | solution.py:95
  85.7 11.6 %collective-permute-start.3 = (f32[64,768]{1,0:T(8,128)S(1)}, f32[64,768]{1,0:T(8,128)S(1)}, u32[]{:S(2)}, u32[]{:S(2)}) collective-permute-start(f32[64,768]{1,0:T(8,128)S(1)} %get-tuple-element.12), channel_id=1, source_target_pairs={{0,6},{1,7},{2,0},{3,1},{4,2},{5,3},{6,4},{7,5},{8,14},{9,15},{10,... | collective-permute-start | bytes 589832 | tf_op jit(solution)/shard_map/ppermute | solution.py:33
  88.5 9.3 %collective-permute-start.2 = (f32[64,768]{1,0:T(8,128)S(1)}, f32[64,768]{1,0:T(8,128)S(1)}, u32[]{:S(2)}, u32[]{:S(2)}) collective-permute-start(f32[64,768]{1,0:T(8,128)S(1)} %get-tuple-element.13), channel_id=1, source_target_pairs={{0,4},{1,5},{2,6},{3,7},{4,0},{5,1},{6,2},{7,3},{8,12},{9,13},{10,... | collective-permute-start | bytes 589832 | tf_op jit(solution)/shard_map/ppermute | solution.py:33
  89.3 11.7 %collective-permute-start.1 = (f32[64,768]{1,0:T(8,128)S(1)}, f32[64,768]{1,0:T(8,128)S(1)}, u32[]{:S(2)}, u32[]{:S(2)}) collective-permute-start(f32[64,768]{1,0:T(8,128)S(1)} %get-tuple-element.11), channel_id=1, source_target_pairs={{0,2},{1,3},{2,4},{3,5},{4,6},{5,7},{6,0},{7,1},{8,10},{9,11},{10,... | collective-permute-start | bytes 589832 | tf_op jit(solution)/shard_map/ppermute | solution.py:33
  101.1 4.8 %collective-permute-start.4 = (f32[32,768]{1,0:T(8,128)S(1)}, f32[32,768]{1,0:T(8,128)S(1)}, u32[]{:S(2)}, u32[]{:S(2)}) collective-permute-start(f32[32,768]{1,0:T(8,128)S(1)} %slice_select_fusion.1), channel_id=1, source_target_pairs={{0,64},{64,0},{1,65},{65,1},{2,66},{66,2},{3,67},{67,3},{4,68},{68... | collective-permute-start | bytes 294920 | tf_op jit(solution)/shard_map/ppermute | solution.py:60
  105.9 6.9 %collective-permute-start.5 = (f32[16,768]{1,0:T(8,128)S(1)}, f32[16,768]{1,0:T(8,128)S(1)}, u32[]{:S(2)}, u32[]{:S(2)}) collective-permute-start(f32[16,768]{1,0:T(8,128)S(1)} %slice_select_fusion.3), channel_id=1, source_target_pairs={{0,1},{1,0},{2,3},{3,2},{4,5},{5,4},{6,7},{7,6},{8,9},{9,8},{10,11... | collective-permute-start | bytes 147464 | tf_op jit(solution)/shard_map/ppermute | solution.py:62
  109.2 3.6 %collective-permute-start.11 = (s32[192]{0:T(256)S(1)}, s32[192]{0:T(256)S(1)}, u32[]{:S(2)}, u32[]{:S(2)}) collective-permute-start(s32[192]{0:T(256)S(1)} %copy-done.1), channel_id=1, source_target_pairs={{0,64},{64,0},{1,65},{65,1},{2,66},{66,2},{3,67},{67,3},{4,68},{68... | collective-permute-start | bytes 2312 | tf_op jit(solution)/shard_map/ppermute | solution.py:96
  112.9 5.7 %collective-permute-start.6 = (f32[16,768]{1,0:T(8,128)S(1)}, f32[16,768]{1,0:T(8,128)S(1)}, u32[]{:S(2)}, u32[]{:S(2)}) collective-permute-start(f32[16,768]{1,0:T(8,128)S(1)} %select_add_fusion.3), channel_id=1, source_target_pairs={{0,1},{1,0},{2,3},{3,2},{4,5},{5,4},{6,7},{7,6},{8,9},{9,8},{10,11... | collective-permute-start | bytes 147464 | tf_op jit(solution)/shard_map/ppermute | solution.py:63
  118.5 7.9 %collective-permute-start.7 = (f32[32,768]{1,0:T(8,128)S(1)}, f32[32,768]{1,0:T(8,128)S(1)}, u32[]{:S(2)}, u32[]{:S(2)}) collective-permute-start(f32[32,768]{1,0:T(8,128)S(1)} %maximum_select_fusion.5), channel_id=1, source_target_pairs={{0,64},{64,0},{1,65},{65,1},{2,66},{66,2},{3,67},{67,3},{4,68},{68... | collective-permute-start | bytes 294920 | tf_op jit(solution)/shard_map/ppermute | solution.py:64
  126.5 5.7 %collective-permute-start.8 = (f32[64,768]{1,0:T(8,128)S(1)}, f32[64,768]{1,0:T(8,128)S(1)}, u32[]{:S(2)}, u32[]{:S(2)}) collective-permute-start(f32[64,768]{1,0:T(8,128)S(1)} %maximum_select_fusion.3), channel_id=1, source_target_pairs={{0,6},{1,7},{2,0},{3,1},{4,2},{5,3},{6,4},{7,5},{8,14},{9,15},{10,... | collective-permute-start | bytes 589832 | tf_op jit(solution)/shard_map/ppermute | solution.py:33
  127.8 7.4 %collective-permute-start.9 = (f32[64,768]{1,0:T(8,128)S(1)}, f32[64,768]{1,0:T(8,128)S(1)}, u32[]{:S(2)}, u32[]{:S(2)}) collective-permute-start(f32[64,768]{1,0:T(8,128)S(1)} %maximum_select_fusion.3), channel_id=1, source_target_pairs={{0,4},{1,5},{2,6},{3,7},{4,0},{5,1},{6,2},{7,3},{8,12},{9,13},{10,... | collective-permute-start | bytes 589832 | tf_op jit(solution)/shard_map/ppermute | solution.py:33
  128.7 9.2 %collective-permute-start.10 = (f32[64,768]{1,0:T(8,128)S(1)}, f32[64,768]{1,0:T(8,128)S(1)}, u32[]{:S(2)}, u32[]{:S(2)}) collective-permute-start(f32[64,768]{1,0:T(8,128)S(1)} %maximum_select_fusion.3), channel_id=1, source_target_pairs={{0,2},{1,3},{2,4},{3,5},{4,6},{5,7},{6,0},{7,1},{8,10},{9,11},{10,... | collective-permute-start | bytes 589832 | tf_op jit(solution)/shard_map/ppermute | solution.py:33
  138.2 6.8 %collective-permute-start.18 = (f32[96,768]{1,0:T(8,128)S(1)}, f32[96,768]{1,0:T(8,128)S(1)}, u32[]{:S(2)}, u32[]{:S(2)}) collective-permute-start(f32[96,768]{1,0:T(8,128)S(1)} %get-tuple-element.9), channel_id=1, source_target_pairs={{0,6},{1,7},{2,0},{3,1},{4,2},{5,3},{6,4},{7,5},{8,14},{9,15},{10,... | collective-permute-start | bytes 884744 | tf_op jit(solution)/shard_map/ppermute | solution.py:33
  138.8 8.3 %collective-permute-start.17 = (f32[96,768]{1,0:T(8,128)S(1)}, f32[96,768]{1,0:T(8,128)S(1)}, u32[]{:S(2)}, u32[]{:S(2)}) collective-permute-start(f32[96,768]{1,0:T(8,128)S(1)} %get-tuple-element.10), channel_id=1, source_target_pairs={{0,4},{1,5},{2,6},{3,7},{4,0},{5,1},{6,2},{7,3},{8,12},{9,13},{10,... | collective-permute-start | bytes 884744 | tf_op jit(solution)/shard_map/ppermute | solution.py:33
  139.6 10.6 %collective-permute-start.16 = (f32[96,768]{1,0:T(8,128)S(1)}, f32[96,768]{1,0:T(8,128)}, u32[]{:S(2)}, u32[]{:S(2)}) collective-permute-start(f32[96,768]{1,0:T(8,128)S(1)} %get-tuple-element.8), channel_id=1, source_target_pairs={{0,2},{1,3},{2,4},{3,5},{4,6},{5,7},{6,0},{7,1},{8,10},{9,11},{10,... | collective-permute-start | bytes 884744 | tf_op jit(solution)/shard_map/ppermute | solution.py:33
  151.3 5.2 %collective-permute-start.19 = (f32[48,768]{1,0:T(8,128)S(1)}, f32[48,768]{1,0:T(8,128)S(1)}, u32[]{:S(2)}, u32[]{:S(2)}) collective-permute-start(f32[48,768]{1,0:T(8,128)S(1)} %slice_select_fusion), channel_id=1, source_target_pairs={{0,64},{64,0},{1,65},{65,1},{2,66},{66,2},{3,67},{67,3},{4,68},{68... | collective-permute-start | bytes 442376 | tf_op jit(solution)/shard_map/ppermute | solution.py:60
  156.6 5.9 %collective-permute-start.20 = (f32[24,768]{1,0:T(8,128)S(1)}, f32[24,768]{1,0:T(8,128)S(1)}, u32[]{:S(2)}, u32[]{:S(2)}) collective-permute-start(f32[24,768]{1,0:T(8,128)S(1)} %slice_select_fusion.2), channel_id=1, source_target_pairs={{0,1},{1,0},{2,3},{3,2},{4,5},{5,4},{6,7},{7,6},{8,9},{9,8},{10,11... | collective-permute-start | bytes 221192 | tf_op jit(solution)/shard_map/ppermute | solution.py:62
  162.5 5.9 %collective-permute-start.21 = (f32[24,768]{1,0:T(8,128)S(1)}, f32[24,768]{1,0:T(8,128)S(1)}, u32[]{:S(2)}, u32[]{:S(2)}) collective-permute-start(f32[24,768]{1,0:T(8,128)S(1)} %select_add_fusion.2), channel_id=1, source_target_pairs={{0,1},{1,0},{2,3},{3,2},{4,5},{5,4},{6,7},{7,6},{8,9},{9,8},{10,11... | collective-permute-start | bytes 221192 | tf_op jit(solution)/shard_map/ppermute | solution.py:63
  168.5 28.9 %copy-start = (f32[8192]{0:T(1024)S(1)}, f32[8192]{0:T(1024)}, u32[]{:S(2)}) copy-start(f32[8192]{0:T(1024)} %param.5) | copy-start | bytes 98308
  168.5 25.7 %collective-permute-start.22 = (f32[48,768]{1,0:T(8,128)S(1)}, f32[48,768]{1,0:T(8,128)S(1)}, u32[]{:S(2)}, u32[]{:S(2)}) collective-permute-start(f32[48,768]{1,0:T(8,128)S(1)} %maximum_select_fusion.4), channel_id=1, source_target_pairs={{0,64},{64,0},{1,65},{65,1},{2,66},{66,2},{3,67},{67,3},{4,68},{68... | collective-permute-start | bytes 442376 | tf_op jit(solution)/shard_map/ppermute | solution.py:64
  187.1 1.3 collective-permute-start.12
  188.4 3.7 %collective-permute-start.13 = (f32[4096]{0:T(1024)S(1)}, f32[4096]{0:T(1024)S(1)}, u32[]{:S(2)}, u32[]{:S(2)}) collective-permute-start(f32[4096]{0:T(1024)S(1)} %max.26), channel_id=1, source_target_pairs={{0,16},{8,24},{16,0},{24,8},{32,48},{40,56},{48,32},{56,40},{1,17}... | collective-permute-start | bytes 49160 | tf_op jit(solution)/shard_map/ppermute | solution.py:72
  192.1 5.2 %collective-permute-start.14 = (f32[4096]{0:T(1024)S(1)}, f32[4096]{0:T(1024)S(1)}, u32[]{:S(2)}, u32[]{:S(2)}) collective-permute-start(f32[4096]{0:T(1024)S(1)} %max.27), channel_id=1, source_target_pairs={{0,32},{8,40},{16,48},{24,56},{32,0},{40,8},{48,16},{56,24},{1,33}... | collective-permute-start | bytes 49160 | tf_op jit(solution)/shard_map/ppermute | solution.py:72
  194.3 10.0 %collective-permute-start.23 = (f32[96,768]{1,0:T(8,128)S(1)}, f32[96,768]{1,0:T(8,128)S(1)}, u32[]{:S(2)}, u32[]{:S(2)}) collective-permute-start(f32[96,768]{1,0:T(8,128)S(1)} %maximum_select_fusion.1), channel_id=1, source_target_pairs={{0,6},{1,7},{2,0},{3,1},{4,2},{5,3},{6,4},{7,5},{8,14},{9,15},{10,... | collective-permute-start | bytes 884744 | tf_op jit(solution)/shard_map/ppermute | solution.py:33
  197.4 11.5 %collective-permute-start.24 = (f32[96,768]{1,0:T(8,128)S(1)}, f32[96,768]{1,0:T(8,128)S(1)}, u32[]{:S(2)}, u32[]{:S(2)}) collective-permute-start(f32[96,768]{1,0:T(8,128)S(1)} %maximum_select_fusion.1), channel_id=1, source_target_pairs={{0,4},{1,5},{2,6},{3,7},{4,0},{5,1},{6,2},{7,3},{8,12},{9,13},{10,... | collective-permute-start | bytes 884744 | tf_op jit(solution)/shard_map/ppermute | solution.py:33
  198.8 13.2 %collective-permute-start.25 = (f32[96,768]{1,0:T(8,128)S(1)}, f32[96,768]{1,0:T(8,128)S(1)}, u32[]{:S(2)}, u32[]{:S(2)}) collective-permute-start(f32[96,768]{1,0:T(8,128)S(1)} %maximum_select_fusion.1), channel_id=1, source_target_pairs={{0,2},{1,3},{2,4},{3,5},{4,6},{5,7},{6,0},{7,1},{8,10},{9,11},{10,... | collective-permute-start | bytes 884744 | tf_op jit(solution)/shard_map/ppermute | solution.py:33
  223.9 3.7 %collective-permute-start.26 = (f32[1,384]{1,0:T(1,128)S(1)}, f32[1,384]{1,0:T(1,128)S(1)}, u32[]{:S(2)}, u32[]{:S(2)}) collective-permute-start(f32[1,384]{1,0:T(1,128)S(1)} %broadcast_in_dim.59), channel_id=1, source_target_pairs={{0,64},{64,0},{1,65},{65,1},{2,66},{66,2},{3,67},{67,3},{4,68},{68... | collective-permute-start | bytes 4616 | tf_op jit(solution)/shard_map/ppermute | solution.py:81
  227.6 5.1 %collective-permute-start.27 = (f32[1,2,384]{2,0,1:T(1,128)S(1)}, f32[1,2,384]{2,0,1:T(1,128)S(1)}, u32[]{:S(2)}, u32[]{:S(2)}) collective-permute-start(f32[1,2,384]{2,0,1:T(1,128)S(1)} %broadcast_select_fusion), channel_id=1, source_target_pairs={{0,1},{1,0},{2,3},{3,2},{4,5},{5,4},{6,7},{7,6},{8,9},{9,8},{10,11... | collective-permute-start | bytes 9224 | tf_op jit(solution)/shard_map/ppermute | solution.py:81
  232.7 3.7 %collective-permute-start.28 = (f32[2,2,384]{2,0,1:T(2,128)S(1)}, f32[2,2,384]{2,0,1:T(2,128)S(1)}, u32[]{:S(2)}, u32[]{:S(2)}) collective-permute-start(f32[2,2,384]{2,0,1:T(2,128)S(1)} %maximum_select_fusion.9), channel_id=1, source_target_pairs={{0,2},{1,3},{2,0},{3,1},{4,6},{5,7},{6,4},{7,5},{8,10},{9,11},{10,... | collective-permute-start | bytes 18440 | tf_op jit(solution)/shard_map/ppermute | solution.py:81
  232.8 5.1 %collective-permute-start.15 = (f32[4096]{0:T(1024)S(1)}, f32[4096]{0:T(1024)S(1)}, u32[]{:S(2)}, u32[]{:S(2)}) collective-permute-start(f32[4096]{0:T(1024)S(1)} %maximum_maximum_fusion), channel_id=1, source_target_pairs={{0,64},{64,0},{1,65},{65,1},{2,66},{66,2},{3,67},{67,3},{4,68},{68... | collective-permute-start | bytes 49160 | tf_op jit(solution)/shard_map/ppermute | solution.py:108
  236.4 5.3 %collective-permute-start.29 = (f32[4,2,384]{2,0,1:T(4,128)S(1)}, f32[4,2,384]{2,0,1:T(4,128)S(1)}, u32[]{:S(2)}, u32[]{:S(2)}) collective-permute-start(f32[4,2,384]{2,0,1:T(4,128)S(1)} %maximum_select_fusion.8), channel_id=1, source_target_pairs={{0,4},{1,5},{2,6},{3,7},{4,0},{5,1},{6,2},{7,3},{8,12},{9,13},{10,... | collective-permute-start | bytes 36872 | tf_op jit(solution)/shard_map/ppermute | solution.py:81
  (2 other events, 24.3 us)
Sparse Core Ops, SparseCore 0:
  9.7 69.7 all-gather.1

commit v16 on v10

--- a/solution.py
+++ b/solution.py
@@ -42,10 +42,19 @@
     return jnp.where(low, jnp.concatenate([mine, other]), jnp.concatenate([other, mine]))
 
 
+def z_group_shift(value, k):
+    if k == 1:
+        return lax.ppermute(value, "col", [(c, c ^ 1) for c in range(N_Y * N_Z)])
+    if k == 2:
+        return lax.ppermute(value, "zl", [(0, 1), (1, 0)])
+    n = 2 * N_Y * N_Z
+    return lax.ppermute(value, ("zl", "col"), [(i, i ^ (N_Y * N_Z) ^ 1) for i in range(n)])
+
+
 def group_masked_sum(value):
     here = lax.axis_index("col")
     y, z = here // N_Z, here % N_Z
-    zl = lax.axis_index("zl")
+    g = lax.axis_index("zl") * 2 + z
     quarter = value.shape[0] // N_Y
 
     def part(k):
@@ -54,14 +63,16 @@
     own = part(0)
     for k in range(1, N_Y):
         own = own + y_shift(part(k), k)
-    zl_swap = [(0, 1), (1, 0)]
-    z_swap = [(c, c ^ 1) for c in range(N_Y * N_Z)]
-    mine, theirs = pair_split(own, zl == 0)
-    mine = mine + lax.ppermute(theirs, "zl", zl_swap)
-    low, high = pair_split(mine, z == 0)
-    low = low + lax.ppermute(high, "col", z_swap)
-    mine = pair_join(low, lax.ppermute(low, "col", z_swap), z == 0)
-    own = pair_join(mine, lax.ppermute(mine, "zl", zl_swap), zl == 0)
+    piece = quarter // 4
+
+    def z_part(k):
+        return lax.dynamic_slice_in_dim(own, (g ^ k) * piece, piece)
+
+    mine = z_part(0)
+    for k in range(1, 4):
+        mine = mine + z_group_shift(z_part(k), k)
+    received = jnp.stack([mine] + [z_group_shift(mine, k) for k in range(1, 4)])
+    own = jnp.take(received, jnp.arange(4) ^ g, axis=0).reshape(own.shape)
     pieces = [own] + [y_shift(own, -k) for k in range(1, N_Y)]
     return jnp.roll(jnp.stack(pieces), y, axis=0).reshape(value.shape)
 

time: 219 us -> 215 us (0.982)
  waiting for transfers between devices: 121 us -> 109 us
  starting transfers between devices: 41.3 us -> 45.3 us
  local copies, waits for them, and re-layouts: 18.2 us -> 20.5 us
    ppermute x8 -> x12, waiting for transfers between devices: 15.4 us -> 7.48 us  [the longest x4 3.12 us: z_group_shift(): lax.ppermute(value, ('zl', 'col'), [(i, i ^ N_Y * N_Z ^ 1) for i in range...]
    ppermute x8 -> x12, starting transfers between devices: 10.6 us -> 16.8 us  [the longest x4 7.16 us: z_group_shift(): lax.ppermute(value, ('zl', 'col'), [(i, i ^ N_Y * N_Z ^ 1) for i in range...]
    ppermute x12, waiting for transfers between devices: 20.9 us -> 14.7 us  [y_shift(): return lax.ppermute(value, 'col', pairs)]
    ppermute x4, waiting for transfers between devices: 10.6 us -> 12.8 us  [gather_in_order(): other = lax.ppermute(parts, axis, [(i, i ^ bit) for i in range(n)])]
  transfers between devices with their start and end apart: 31 -> 35, of which waited for: 23 -> 20; matrix products, arithmetic and copies ran while one was open for 5% -> 6% of each run, Pallas kernels for 0% -> 0%
where the time goes in v16:
time: 215 us
  waiting for transfers between devices  109 us (51%)
  starting transfers between devices  45.3 us (21%)
  local copies, waits for them, and re-layouts  20.5 us (10%)
  matrix products  16 us (7%)
  between operations  14.4 us (7%)
  other arithmetic  9.66 us (4%)
    all_gather x1, waiting for transfers between devices, body(): half = lax.all_gather(slab_embed, 'xc', axis=0, tiled=True)  64 us
    ppermute x12, starting transfers between devices, y_shift(): return lax.ppermute(value, 'col', pairs)  18.9 us
    dot_general x1, matrix products, similar(): lax.dot_general(left, right, (((1,), (1,)), ((), ())), precision=lax.Prec...  16 us
    ppermute x12, waiting for transfers between devices, y_shift(): return lax.ppermute(value, 'col', pairs)  14.7 us
    gather x2, local copies, waits for them, and re-layouts, lookup(): jnp.take(source, jnp.clip(position, 0, source.shape[0] - 1), axis=0)  13 us
    ppermute x4, waiting for transfers between devices, gather_in_order(): other = lax.ppermute(parts, axis, [(i, i ^ bit) for i in range(n)])  12.8 us
    ppermute x4, starting transfers between devices, z_group_shift(): lax.ppermute(value, ('zl', 'col'), [(i, i ^ N_Y * N_Z ^ 1) for i in range...  7.16 us
    ppermute x3, waiting for transfers between devices, all_max(): lax.ppermute(value, axis, [(i, i ^ bit) for i in range(n)])  7.15 us
  transfers between devices with their start and end apart: 35, of which 20 were waited for; matrix products, arithmetic and copies ran while one was open for 6% of the time, Pallas kernels for 0%

profile of v16, /device:TPU:0, one launch (start us, length us, event | category | flops | bytes accessed | tf_op | source)
XLA Modules:
  0.0 214.8 jit_solution(2128265026001209177)
XLA Ops:
  7.9 2.1 collective-permute-start
  10.1 1.5 collective-permute-done
  15.5 64.0 %all-gather.2.cloned.1.call-done = f32[4096,768]{1,0:T(8,128)} async-done(((f32[512,768]{1,0:T(8,128)}), f32[4096,768]{1,0:T(8,128)}) %all-gather.2.cloned.1.call-update) | async-done | bytes 12582928 | tf_op jit(solution)/shard_map/all_gather | solution.py:103
  79.5 6.0 %gather_fusion = f32[256,768]{1,0:T(8,128)S(1)} fusion(f32[4096,768]{1,0:T(8,128)} %all-gather.2.cloned.1.call-done, s32[1024]{0:T(1024)S(1)} %pad_clamp_fusion.2), kind=kCustom, calls=%fused_computation | custom fusion | bytes 1573888 | tf_op jit(solution)/shard_map/jit(_take)/gather | solution.py:23
  86.5 1.5 collective-permute-start.1
  88.0 2.7 %collective-permute-start.2 = (f32[64,768]{1,0:T(8,128)}, f32[64,768]{1,0:T(8,128)}, u32[]{:S(2)}, u32[]{:S(2)}) collective-permute-start(f32[64,768]{1,0:T(8,128)} %get-tuple-element.9), channel_id=1, source_target_pairs={{0,4},{1,5},{2,6},{3,7},{4,0},{5,1},{6,2},{7,3},{8,12},{9,13},{10,... | collective-permute-start | bytes 589832 | tf_op jit(solution)/shard_map/ppermute | solution.py:33
  92.1 7.1 %gather_fusion.2 = f32[384,768]{1,0:T(8,128)S(1)} fusion(f32[4096,768]{1,0:T(8,128)} %all-gather.2.cloned.1.call-done, s32[1024]{0:T(1024)S(1)} %pad_clamp_fusion), kind=kCustom, calls=%fused_computation.2 | custom fusion | bytes 2360832 | tf_op jit(solution)/shard_map/jit(_take)/gather | solution.py:23
  101.4 3.2 %collective-permute-start.4 = (f32[16,768]{1,0:T(8,128)S(1)}, f32[16,768]{1,0:T(8,128)S(1)}, u32[]{:S(2)}, u32[]{:S(2)}) collective-permute-start(f32[16,768]{1,0:T(8,128)S(1)} %get-tuple-element.13), channel_id=1, source_target_pairs={{0,1},{1,0},{2,3},{3,2},{4,5},{5,4},{6,7},{7,6},{8,9},{9,8},{10,11... | collective-permute-start | bytes 147464 | tf_op jit(solution)/shard_map/ppermute | solution.py:47
  105.9 2.6 %collective-permute-start.15 = (f32[96,768]{1,0:T(8,128)S(1)}, f32[96,768]{1,0:T(8,128)S(1)}, u32[]{:S(2)}, u32[]{:S(2)}) collective-permute-start(f32[96,768]{1,0:T(8,128)S(1)} %get-tuple-element.6), channel_id=1, source_target_pairs={{0,4},{1,5},{2,6},{3,7},{4,0},{5,1},{6,2},{7,3},{8,12},{9,13},{10,... | collective-permute-start | bytes 884744 | tf_op jit(solution)/shard_map/ppermute | solution.py:33
  108.5 1.6 collective-permute-start.16
  111.4 2.7 %collective-permute-done.5 = f32[16,768]{1,0:T(8,128)S(1)} collective-permute-done((f32[16,768]{1,0:T(8,128)S(1)}, f32[16,768]{1,0:T(8,128)S(1)}, u32[]{:S(2)}, u32[]{:S(2)}) %collective-permute-start.5) | collective-permute-done | bytes 49184 | tf_op jit(solution)/shard_map/ppermute | solution.py:49
  114.1 1.9 collective-permute-done.6
  117.4 2.8 %collective-permute-start.9 = (f32[16,768]{1,0:T(8,128)S(1)}, f32[16,768]{1,0:T(8,128)S(1)}, u32[]{:S(2)}, u32[]{:S(2)}) collective-permute-start(f32[16,768]{1,0:T(8,128)S(1)} %add_add_fusion.3), channel_id=1, source_target_pairs={{0,65},{1,64},{2,67},{3,66},{4,69},{5,68},{6,71},{7,70},{64,1},{65... | collective-permute-start | bytes 147464 | tf_op jit(solution)/shard_map/ppermute | solution.py:51
  122.0 1.6 collective-permute-start.18
  123.5 2.2 %collective-permute-start.19 = (f32[24,768]{1,0:T(8,128)S(1)}, f32[24,768]{1,0:T(8,128)S(1)}, u32[]{:S(2)}, u32[]{:S(2)}) collective-permute-start(f32[24,768]{1,0:T(8,128)S(1)} %get-tuple-element.11), channel_id=1, source_target_pairs={{0,65},{1,64},{2,67},{3,66},{4,69},{5,68},{6,71},{7,70},{64,1},{65... | collective-permute-start | bytes 221192 | tf_op jit(solution)/shard_map/ppermute | solution.py:51
  126.4 2.2 %collective-permute-start.10 = (f32[64,768]{1,0:T(8,128)S(1)}, f32[64,768]{1,0:T(8,128)S(1)}, u32[]{:S(2)}, u32[]{:S(2)}) collective-permute-start(f32[64,768]{1,0:T(8,128)S(1)} %bitcast_select_fusion.2), channel_id=1, source_target_pairs={{0,6},{1,7},{2,0},{3,1},{4,2},{5,3},{6,4},{7,5},{8,14},{9,15},{10,... | collective-permute-start | bytes 589832 | tf_op jit(solution)/shard_map/ppermute | solution.py:33
  132.2 1.8 collective-permute-start.22
  134.1 1.7 collective-permute-done.20
  138.5 2.2 %collective-permute-start.23 = (f32[96,768]{1,0:T(8,128)S(1)}, f32[96,768]{1,0:T(8,128)S(1)}, u32[]{:S(2)}, u32[]{:S(2)}) collective-permute-start(f32[96,768]{1,0:T(8,128)S(1)} %bitcast_select_fusion), channel_id=1, source_target_pairs={{0,6},{1,7},{2,0},{3,1},{4,2},{5,3},{6,4},{7,5},{8,14},{9,15},{10,... | collective-permute-start | bytes 884744 | tf_op jit(solution)/shard_map/ppermute | solution.py:33
  143.0 8.3 %collective-permute-done.23 = f32[96,768]{1,0:T(8,128)S(1)} collective-permute-done((f32[96,768]{1,0:T(8,128)S(1)}, f32[96,768]{1,0:T(8,128)S(1)}, u32[]{:S(2)}, u32[]{:S(2)}) %collective-permute-start.23) | collective-permute-done | bytes 294944 | tf_op jit(solution)/shard_map/ppermute | solution.py:33
  152.2 3.1 %collective-permute-done.25 = f32[96,768]{1,0:T(8,128)S(1)} collective-permute-done((f32[96,768]{1,0:T(8,128)S(1)}, f32[96,768]{1,0:T(8,128)S(1)}, u32[]{:S(2)}, u32[]{:S(2)}) %collective-permute-start.25) | collective-permute-done | bytes 294944 | tf_op jit(solution)/shard_map/ppermute | solution.py:33
  155.6 16.0 %fusion.2 = f32[640,4096]{1,0:T(8,128)S(1)} fusion(f32[4096,768]{1,0:T(8,128)} %all-gather.2.cloned.1.call-done, f32[384,768]{1,0:T(8,128)S(1)} %bitcast.57, f32[256,768]{1,0:T(8,128)S(1)} %bitcast.60), kind=kOutput, calls=%fused_computation.8 | convolution fusion | flops 12080087040 | bytes 25034752 | tf_op jit(solution)/shard_map/dot_general | solution.py:11
  171.6 4.0 %copy-done = f32[640,4096]{1,0:T(8,128)} copy-done((f32[640,4096]{1,0:T(8,128)}, f32[640,4096]{1,0:T(8,128)S(1)}, u32[]{:S(2)}) %copy-start) | copy-done | bytes 10485784
  177.9 2.8 %collective-permute-done.27 = f32[4096]{0:T(1024)S(1)} collective-permute-done((f32[4096]{0:T(1024)S(1)}, f32[4096]{0:T(1024)S(1)}, u32[]{:S(2)}, u32[]{:S(2)}) %collective-permute-start.27) | collective-permute-done | bytes 16416 | tf_op jit(solution)/shard_map/ppermute | solution.py:83
  180.8 2.1 collective-permute-start.28
  182.9 3.1 %collective-permute-done.28 = f32[4096]{0:T(1024)S(1)} collective-permute-done((f32[4096]{0:T(1024)S(1)}, f32[4096]{0:T(1024)S(1)}, u32[]{:S(2)}, u32[]{:S(2)}) %collective-permute-start.28) | collective-permute-done | bytes 16416 | tf_op jit(solution)/shard_map/ppermute | solution.py:83
  186.0 3.5 %fusion.1 = f32[384]{0:T(512)S(1)} fusion(f32[640,4096]{1,0:T(8,128)} %copy-done, f32[4096]{0:T(1024)S(1)} %maximum_maximum_fusion), kind=kLoop, calls=%fused_computation.6 | loop fusion | flops 4718208 | bytes 6309376 | tf_op jit(solution)/shard_map/reduce_sum | solution.py:115
  190.3 2.9 %collective-permute-done.30 = f32[1,384]{1,0:T(1,128)S(1)} collective-permute-done((f32[1,384]{1,0:T(1,128)S(1)}, f32[1,384]{1,0:T(1,128)S(1)}, u32[]{:S(2)}, u32[]{:S(2)}) %collective-permute-start.30) | collective-permute-done | bytes 1568 | tf_op jit(solution)/shard_map/ppermute | solution.py:92
  193.2 1.5 collective-permute-start.31
  194.7 3.6 %collective-permute-done.31 = f32[1,2,384]{2,0,1:T(1,128)S(1)} collective-permute-done((f32[1,2,384]{2,0,1:T(1,128)S(1)}, f32[1,2,384]{2,0,1:T(1,128)S(1)}, u32[]{:S(2)}, u32[]{:S(2)}) %collective-permute-start.31) | collective-permute-done | bytes 3104 | tf_op jit(solution)/shard_map/ppermute | solution.py:92
  199.1 2.9 %collective-permute-done.32 = f32[2,2,384]{2,0,1:T(2,128)S(1)} collective-permute-done((f32[2,2,384]{2,0,1:T(2,128)S(1)}, f32[2,2,384]{2,0,1:T(2,128)S(1)}, u32[]{:S(2)}, u32[]{:S(2)}) %collective-permute-start.32) | collective-permute-done | bytes 6176 | tf_op jit(solution)/shard_map/ppermute | solution.py:92
  203.9 3.4 %collective-permute-done.33 = f32[4,2,384]{2,0,1:T(4,128)S(1)} collective-permute-done((f32[4,2,384]{2,0,1:T(4,128)S(1)}, f32[4,2,384]{2,0,1:T(4,128)S(1)}, u32[]{:S(2)}, u32[]{:S(2)}) %collective-permute-start.33) | collective-permute-done | bytes 12320 | tf_op jit(solution)/shard_map/ppermute | solution.py:92
  (107 shorter events, 31.9 us)
Async XLA Ops:
  7.2 72.3 %all-gather.2.cloned.1.call-start = ((), (), s32[]{:S(2)}) async-start(), calls=%async_computation | async-start | bytes 14155776 | tf_op jit(solution)/shard_map/all_gather | solution.py:103
  7.9 3.8 %collective-permute-start = (s32[128]{0:T(128)}, s32[128]{0:T(128)S(1)}, u32[]{:S(2)}, u32[]{:S(2)}) collective-permute-start(s32[128]{0:T(128)} %param.6), channel_id=1, source_target_pairs={{0,64},{64,0},{1,65},{65,1},{2,66},{66,2},{3,67},{67,3},{4,68},{68... | collective-permute-start | bytes 1544 | tf_op jit(solution)/shard_map/ppermute | solution.py:106
  10.0 3.8 %collective-permute-start.13 = (s32[192]{0:T(256)}, s32[192]{0:T(256)S(1)}, u32[]{:S(2)}, u32[]{:S(2)}) collective-permute-start(s32[192]{0:T(256)} %param.7), channel_id=1, source_target_pairs={{0,64},{64,0},{1,65},{65,1},{2,66},{66,2},{3,67},{67,3},{4,68},{68... | collective-permute-start | bytes 2312 | tf_op jit(solution)/shard_map/ppermute | solution.py:107
  86.5 12.9 %collective-permute-start.1 = (f32[64,768]{1,0:T(8,128)}, f32[64,768]{1,0:T(8,128)S(1)}, u32[]{:S(2)}, u32[]{:S(2)}) collective-permute-start(f32[64,768]{1,0:T(8,128)} %get-tuple-element.7), channel_id=1, source_target_pairs={{0,2},{1,3},{2,4},{3,5},{4,6},{5,7},{6,0},{7,1},{8,10},{9,11},{10,... | collective-permute-start | bytes 589832 | tf_op jit(solution)/shard_map/ppermute | solution.py:33
  88.0 12.3 %collective-permute-start.2 = (f32[64,768]{1,0:T(8,128)}, f32[64,768]{1,0:T(8,128)}, u32[]{:S(2)}, u32[]{:S(2)}) collective-permute-start(f32[64,768]{1,0:T(8,128)} %get-tuple-element.9), channel_id=1, source_target_pairs={{0,4},{1,5},{2,6},{3,7},{4,0},{5,1},{6,2},{7,3},{8,12},{9,13},{10,... | collective-permute-start | bytes 589832 | tf_op jit(solution)/shard_map/ppermute | solution.py:33
  90.7 9.6 %collective-permute-start.3 = (f32[64,768]{1,0:T(8,128)S(1)}, f32[64,768]{1,0:T(8,128)}, u32[]{:S(2)}, u32[]{:S(2)}) collective-permute-start(f32[64,768]{1,0:T(8,128)S(1)} %get-tuple-element.8), channel_id=1, source_target_pairs={{0,6},{1,7},{2,0},{3,1},{4,2},{5,3},{6,4},{7,5},{8,14},{9,15},{10,... | collective-permute-start | bytes 589832 | tf_op jit(solution)/shard_map/ppermute | solution.py:33
  101.4 9.3 %collective-permute-start.4 = (f32[16,768]{1,0:T(8,128)S(1)}, f32[16,768]{1,0:T(8,128)S(1)}, u32[]{:S(2)}, u32[]{:S(2)}) collective-permute-start(f32[16,768]{1,0:T(8,128)S(1)} %get-tuple-element.13), channel_id=1, source_target_pairs={{0,1},{1,0},{2,3},{3,2},{4,5},{5,4},{6,7},{7,6},{8,9},{9,8},{10,11... | collective-permute-start | bytes 147464 | tf_op jit(solution)/shard_map/ppermute | solution.py:47
  104.7 12.7 %collective-permute-start.14 = (f32[96,768]{1,0:T(8,128)S(1)}, f32[96,768]{1,0:T(8,128)S(1)}, u32[]{:S(2)}, u32[]{:S(2)}) collective-permute-start(f32[96,768]{1,0:T(8,128)S(1)} %get-tuple-element.4), channel_id=1, source_target_pairs={{0,2},{1,3},{2,4},{3,5},{4,6},{5,7},{6,0},{7,1},{8,10},{9,11},{10,... | collective-permute-start | bytes 884744 | tf_op jit(solution)/shard_map/ppermute | solution.py:33
  105.9 15.5 %collective-permute-start.15 = (f32[96,768]{1,0:T(8,128)S(1)}, f32[96,768]{1,0:T(8,128)S(1)}, u32[]{:S(2)}, u32[]{:S(2)}) collective-permute-start(f32[96,768]{1,0:T(8,128)S(1)} %get-tuple-element.6), channel_id=1, source_target_pairs={{0,4},{1,5},{2,6},{3,7},{4,0},{5,1},{6,2},{7,3},{8,12},{9,13},{10,... | collective-permute-start | bytes 884744 | tf_op jit(solution)/shard_map/ppermute | solution.py:33
  108.5 12.9 %collective-permute-start.16 = (f32[96,768]{1,0:T(8,128)S(1)}, f32[96,768]{1,0:T(8,128)S(1)}, u32[]{:S(2)}, u32[]{:S(2)}) collective-permute-start(f32[96,768]{1,0:T(8,128)S(1)} %get-tuple-element.5), channel_id=1, source_target_pairs={{0,6},{1,7},{2,0},{3,1},{4,2},{5,3},{6,4},{7,5},{8,14},{9,15},{10,... | collective-permute-start | bytes 884744 | tf_op jit(solution)/shard_map/ppermute | solution.py:33
  110.0 4.1 %collective-permute-start.5 = (f32[16,768]{1,0:T(8,128)S(1)}, f32[16,768]{1,0:T(8,128)S(1)}, u32[]{:S(2)}, u32[]{:S(2)}) collective-permute-start(f32[16,768]{1,0:T(8,128)S(1)} %get-tuple-element.15), channel_id=1, source_target_pairs={{0,64},{64,0},{1,65},{65,1},{2,66},{66,2},{3,67},{67,3},{4,68},{68... | collective-permute-start | bytes 147464 | tf_op jit(solution)/shard_map/ppermute | solution.py:49
  110.7 5.3 %collective-permute-start.6 = (f32[16,768]{1,0:T(8,128)S(1)}, f32[16,768]{1,0:T(8,128)S(1)}, u32[]{:S(2)}, u32[]{:S(2)}) collective-permute-start(f32[16,768]{1,0:T(8,128)S(1)} %get-tuple-element.14), channel_id=1, source_target_pairs={{0,65},{1,64},{2,67},{3,66},{4,69},{5,68},{6,71},{7,70},{64,1},{65... | collective-permute-start | bytes 147464 | tf_op jit(solution)/shard_map/ppermute | solution.py:51
  116.0 7.5 %collective-permute-start.7 = (f32[16,768]{1,0:T(8,128)S(1)}, f32[16,768]{1,0:T(8,128)S(1)}, u32[]{:S(2)}, u32[]{:S(2)}) collective-permute-start(f32[16,768]{1,0:T(8,128)S(1)} %add_add_fusion.3), channel_id=1, source_target_pairs={{0,1},{1,0},{2,3},{3,2},{4,5},{5,4},{6,7},{7,6},{8,9},{9,8},{10,11... | collective-permute-start | bytes 147464 | tf_op jit(solution)/shard_map/ppermute | solution.py:47
  116.8 8.9 %collective-permute-start.8 = (f32[16,768]{1,0:T(8,128)S(1)}, f32[16,768]{1,0:T(8,128)S(1)}, u32[]{:S(2)}, u32[]{:S(2)}) collective-permute-start(f32[16,768]{1,0:T(8,128)S(1)} %add_add_fusion.3), channel_id=1, source_target_pairs={{0,64},{64,0},{1,65},{65,1},{2,66},{66,2},{3,67},{67,3},{4,68},{68... | collective-permute-start | bytes 147464 | tf_op jit(solution)/shard_map/ppermute | solution.py:49
  117.4 8.3 %collective-permute-start.9 = (f32[16,768]{1,0:T(8,128)S(1)}, f32[16,768]{1,0:T(8,128)S(1)}, u32[]{:S(2)}, u32[]{:S(2)}) collective-permute-start(f32[16,768]{1,0:T(8,128)S(1)} %add_add_fusion.3), channel_id=1, source_target_pairs={{0,65},{1,64},{2,67},{3,66},{4,69},{5,68},{6,71},{7,70},{64,1},{65... | collective-permute-start | bytes 147464 | tf_op jit(solution)/shard_map/ppermute | solution.py:51
  121.5 8.2 %collective-permute-start.17 = (f32[24,768]{1,0:T(8,128)S(1)}, f32[24,768]{1,0:T(8,128)S(1)}, u32[]{:S(2)}, u32[]{:S(2)}) collective-permute-start(f32[24,768]{1,0:T(8,128)S(1)} %get-tuple-element.10), channel_id=1, source_target_pairs={{0,1},{1,0},{2,3},{3,2},{4,5},{5,4},{6,7},{7,6},{8,9},{9,8},{10,11... | collective-permute-start | bytes 221192 | tf_op jit(solution)/shard_map/ppermute | solution.py:47
  122.0 7.8 %collective-permute-start.18 = (f32[24,768]{1,0:T(8,128)S(1)}, f32[24,768]{1,0:T(8,128)S(1)}, u32[]{:S(2)}, u32[]{:S(2)}) collective-permute-start(f32[24,768]{1,0:T(8,128)S(1)} %get-tuple-element.12), channel_id=1, source_target_pairs={{0,64},{64,0},{1,65},{65,1},{2,66},{66,2},{3,67},{67,3},{4,68},{68... | collective-permute-start | bytes 221192 | tf_op jit(solution)/shard_map/ppermute | solution.py:49
  123.5 6.2 %collective-permute-start.19 = (f32[24,768]{1,0:T(8,128)S(1)}, f32[24,768]{1,0:T(8,128)S(1)}, u32[]{:S(2)}, u32[]{:S(2)}) collective-permute-start(f32[24,768]{1,0:T(8,128)S(1)} %get-tuple-element.11), channel_id=1, source_target_pairs={{0,65},{1,64},{2,67},{3,66},{4,69},{5,68},{6,71},{7,70},{64,1},{65... | collective-permute-start | bytes 221192 | tf_op jit(solution)/shard_map/ppermute | solution.py:51
  126.4 15.6 %collective-permute-start.10 = (f32[64,768]{1,0:T(8,128)S(1)}, f32[64,768]{1,0:T(8,128)S(1)}, u32[]{:S(2)}, u32[]{:S(2)}) collective-permute-start(f32[64,768]{1,0:T(8,128)S(1)} %bitcast_select_fusion.2), channel_id=1, source_target_pairs={{0,6},{1,7},{2,0},{3,1},{4,2},{5,3},{6,4},{7,5},{8,14},{9,15},{10,... | collective-permute-start | bytes 589832 | tf_op jit(solution)/shard_map/ppermute | solution.py:33
  128.6 13.7 %collective-permute-start.11 = (f32[64,768]{1,0:T(8,128)S(1)}, f32[64,768]{1,0:T(8,128)S(1)}, u32[]{:S(2)}, u32[]{:S(2)}) collective-permute-start(f32[64,768]{1,0:T(8,128)S(1)} %bitcast_select_fusion.2), channel_id=1, source_target_pairs={{0,4},{1,5},{2,6},{3,7},{4,0},{5,1},{6,2},{7,3},{8,12},{9,13},{10,... | collective-permute-start | bytes 589832 | tf_op jit(solution)/shard_map/ppermute | solution.py:33
  129.8 5.9 %collective-permute-start.20 = (f32[24,768]{1,0:T(8,128)S(1)}, f32[24,768]{1,0:T(8,128)S(1)}, u32[]{:S(2)}, u32[]{:S(2)}) collective-permute-start(f32[24,768]{1,0:T(8,128)S(1)} %add_add_fusion.2), channel_id=1, source_target_pairs={{0,1},{1,0},{2,3},{3,2},{4,5},{5,4},{6,7},{7,6},{8,9},{9,8},{10,11... | collective-permute-start | bytes 221192 | tf_op jit(solution)/shard_map/ppermute | solution.py:47
  130.8 5.7 %collective-permute-start.21 = (f32[24,768]{1,0:T(8,128)S(1)}, f32[24,768]{1,0:T(8,128)S(1)}, u32[]{:S(2)}, u32[]{:S(2)}) collective-permute-start(f32[24,768]{1,0:T(8,128)S(1)} %add_add_fusion.2), channel_id=1, source_target_pairs={{0,64},{64,0},{1,65},{65,1},{2,66},{66,2},{3,67},{67,3},{4,68},{68... | collective-permute-start | bytes 221192 | tf_op jit(solution)/shard_map/ppermute | solution.py:49
  132.2 5.6 %collective-permute-start.22 = (f32[24,768]{1,0:T(8,128)S(1)}, f32[24,768]{1,0:T(8,128)S(1)}, u32[]{:S(2)}, u32[]{:S(2)}) collective-permute-start(f32[24,768]{1,0:T(8,128)S(1)} %add_add_fusion.2), channel_id=1, source_target_pairs={{0,65},{1,64},{2,67},{3,66},{4,69},{5,68},{6,71},{7,70},{64,1},{65... | collective-permute-start | bytes 221192 | tf_op jit(solution)/shard_map/ppermute | solution.py:51
  135.7 7.0 %collective-permute-start.12 = (f32[64,768]{1,0:T(8,128)S(1)}, f32[64,768]{1,0:T(8,128)S(1)}, u32[]{:S(2)}, u32[]{:S(2)}) collective-permute-start(f32[64,768]{1,0:T(8,128)S(1)} %bitcast_select_fusion.2), channel_id=1, source_target_pairs={{0,2},{1,3},{2,4},{3,5},{4,6},{5,7},{6,0},{7,1},{8,10},{9,11},{10,... | collective-permute-start | bytes 589832 | tf_op jit(solution)/shard_map/ppermute | solution.py:33
  138.5 12.9 %collective-permute-start.23 = (f32[96,768]{1,0:T(8,128)S(1)}, f32[96,768]{1,0:T(8,128)S(1)}, u32[]{:S(2)}, u32[]{:S(2)}) collective-permute-start(f32[96,768]{1,0:T(8,128)S(1)} %bitcast_select_fusion), channel_id=1, source_target_pairs={{0,6},{1,7},{2,0},{3,1},{4,2},{5,3},{6,4},{7,5},{8,14},{9,15},{10,... | collective-permute-start | bytes 884744 | tf_op jit(solution)/shard_map/ppermute | solution.py:33
  140.7 11.4 %collective-permute-start.24 = (f32[96,768]{1,0:T(8,128)S(1)}, f32[96,768]{1,0:T(8,128)S(1)}, u32[]{:S(2)}, u32[]{:S(2)}) collective-permute-start(f32[96,768]{1,0:T(8,128)S(1)} %bitcast_select_fusion), channel_id=1, source_target_pairs={{0,4},{1,5},{2,6},{3,7},{4,0},{5,1},{6,2},{7,3},{8,12},{9,13},{10,... | collective-permute-start | bytes 884744 | tf_op jit(solution)/shard_map/ppermute | solution.py:33
  142.0 13.3 %collective-permute-start.25 = (f32[96,768]{1,0:T(8,128)S(1)}, f32[96,768]{1,0:T(8,128)S(1)}, u32[]{:S(2)}, u32[]{:S(2)}) collective-permute-start(f32[96,768]{1,0:T(8,128)S(1)} %bitcast_select_fusion), channel_id=1, source_target_pairs={{0,2},{1,3},{2,4},{3,5},{4,6},{5,7},{6,0},{7,1},{8,10},{9,11},{10,... | collective-permute-start | bytes 884744 | tf_op jit(solution)/shard_map/ppermute | solution.py:33
  177.0 3.7 %collective-permute-start.27 = (f32[4096]{0:T(1024)S(1)}, f32[4096]{0:T(1024)S(1)}, u32[]{:S(2)}, u32[]{:S(2)}) collective-permute-start(f32[4096]{0:T(1024)S(1)} %max.26), channel_id=1, source_target_pairs={{0,16},{8,24},{16,0},{24,8},{32,48},{40,56},{48,32},{56,40},{1,17}... | collective-permute-start | bytes 49160 | tf_op jit(solution)/shard_map/ppermute | solution.py:83
  180.8 5.2 %collective-permute-start.28 = (f32[4096]{0:T(1024)S(1)}, f32[4096]{0:T(1024)S(1)}, u32[]{:S(2)}, u32[]{:S(2)}) collective-permute-start(f32[4096]{0:T(1024)S(1)} %max.27), channel_id=1, source_target_pairs={{0,32},{8,40},{16,48},{24,56},{32,0},{40,8},{48,16},{56,24},{1,33}... | collective-permute-start | bytes 49160 | tf_op jit(solution)/shard_map/ppermute | solution.py:83
  193.2 5.1 %collective-permute-start.31 = (f32[1,2,384]{2,0,1:T(1,128)S(1)}, f32[1,2,384]{2,0,1:T(1,128)S(1)}, u32[]{:S(2)}, u32[]{:S(2)}) collective-permute-start(f32[1,2,384]{2,0,1:T(1,128)S(1)} %broadcast_select_fusion), channel_id=1, source_target_pairs={{0,1},{1,0},{2,3},{3,2},{4,5},{5,4},{6,7},{7,6},{8,9},{9,8},{10,11... | collective-permute-start | bytes 9224 | tf_op jit(solution)/shard_map/ppermute | solution.py:92
  198.4 4.9 %collective-permute-start.29 = (f32[4096]{0:T(1024)S(1)}, f32[4096]{0:T(1024)S(1)}, u32[]{:S(2)}, u32[]{:S(2)}) collective-permute-start(f32[4096]{0:T(1024)S(1)} %maximum_maximum_fusion), channel_id=1, source_target_pairs={{0,64},{64,0},{1,65},{65,1},{2,66},{66,2},{3,67},{67,3},{4,68},{68... | collective-permute-start | bytes 49160 | tf_op jit(solution)/shard_map/ppermute | solution.py:119
  202.0 5.3 %collective-permute-start.33 = (f32[4,2,384]{2,0,1:T(4,128)S(1)}, f32[4,2,384]{2,0,1:T(4,128)S(1)}, u32[]{:S(2)}, u32[]{:S(2)}) collective-permute-start(f32[4,2,384]{2,0,1:T(4,128)S(1)} %maximum_select_fusion.2), channel_id=1, source_target_pairs={{0,4},{1,5},{2,6},{3,7},{4,0},{5,1},{6,2},{7,3},{8,12},{9,13},{10,... | collective-permute-start | bytes 36872 | tf_op jit(solution)/shard_map/ppermute | solution.py:92
  (5 other events, 23.1 us)
Sparse Core Ops, SparseCore 0:
  9.7 69.7 all-gather.1

commit v17 on v16

--- a/solution.py
+++ b/solution.py
@@ -77,6 +77,25 @@
     return jnp.roll(jnp.stack(pieces), y, axis=0).reshape(value.shape)
 
 
+def all_max_two_rounds(value, axis, n):
+    for bits in ((1, 2, 3), (4,)):
+        received = [lax.ppermute(value, axis, [(i, i ^ k) for i in range(n)]) for k in bits]
+        for other in received:
+            value = jnp.maximum(value, other)
+    return value
+
+
+def group_gather_in_order(value):
+    here = lax.axis_index("col")
+    y, z = here // N_Z, here % N_Z
+    g = lax.axis_index("zl") * 2 + z
+    received = jnp.stack([value] + [z_group_shift(value, k) for k in range(1, 4)])
+    z_ordered = jnp.take(received, jnp.arange(4) ^ g, axis=0)
+    col_pairs = [[(c, c ^ (2 * k)) for c in range(N_Y * N_Z)] for k in range(1, N_Y)]
+    received = jnp.stack([z_ordered] + [lax.ppermute(z_ordered, "col", pairs) for pairs in col_pairs])
+    return jnp.take(received, jnp.arange(N_Y) ^ y, axis=0)
+
+
 def all_max(value, axis, n):
     bit = 1
     while bit < n:
@@ -109,11 +128,11 @@
     chosen = group_masked_sum(lookup(half, both_cand, first_row))
     n_sel = both_sel.shape[0]
     scores = lax.optimization_barrier(similar(jnp.concatenate([selected, chosen]), half))
-    reached = all_max(jnp.max(scores[:n_sel], axis=0), "xc", n_xc)
+    reached = all_max_two_rounds(jnp.max(scores[:n_sel], axis=0), "xc", n_xc)
     old = lax.dynamic_slice_in_dim(coverage_old, zl * half.shape[0], half.shape[0])
     coverage = jnp.maximum(old, reached)
     gain_part = jnp.sum(jnp.maximum(scores[n_sel:] - coverage[None, :], 0.0), axis=1)
-    parts = gather_in_order(gather_in_order(gain_part[None], "zl", 2)[None], "col", N_Y * N_Z)
+    parts = group_gather_in_order(gain_part)
     total = jnp.sum(parts.reshape(-1, gain_part.shape[0]), axis=0)
     total_gain = lax.dynamic_slice_in_dim(total, zl * cand_index.shape[0], cand_index.shape[0])
     full_coverage = pair_join(coverage, lax.ppermute(coverage, "zl", zl_swap), zl == 0)

time: 215 us -> 213 us (level)
  waiting for transfers between devices: 109 us -> 99.4 us
  starting transfers between devices: 45.3 us -> 51.5 us
    ppermute x7, waiting for transfers between devices: 20 us -> 7.63 us  [the longest x4 5.5 us: all_max_two_rounds(): lax.ppermute(value, axis, [(i, i ^ k) for i in range(n)])]
    ppermute x4 -> x5, waiting for transfers between devices: 3.12 us -> 5.66 us  [z_group_shift(): lax.ppermute(value, ('zl', 'col'), [(i, i ^ N_Y * N_Z ^ 1) for i in range...]
    ppermute x4 -> x5, starting transfers between devices: 5.49 us -> 7.03 us  [z_group_shift(): return lax.ppermute(value, 'col', [(c, c ^ 1) for c in range(N_Y * N_Z)])]
    ppermute x4 -> x5, starting transfers between devices: 4.19 us -> 5.56 us  [z_group_shift(): return lax.ppermute(value, 'zl', [(0, 1), (1, 0)])]
    ppermute x4 -> x5, starting transfers between devices: 7.16 us -> 8.41 us  [z_group_shift(): lax.ppermute(value, ('zl', 'col'), [(i, i ^ N_Y * N_Z ^ 1) for i in range...]
  transfers between devices with their start and end apart: 35 -> 38, of which waited for: 20 -> 20; matrix products, arithmetic and copies ran while one was open for 6% -> 7% of each run, Pallas kernels for 0% -> 0%
where the time goes in v17:
time: 213 us
  waiting for transfers between devices  99.4 us (47%)
  starting transfers between devices  51.5 us (24%)
  local copies, waits for them, and re-layouts  21.6 us (10%)
  matrix products  16 us (8%)
  between operations  14.4 us (7%)
  other arithmetic  9.93 us (5%)
    all_gather x1, waiting for transfers between devices, body(): half = lax.all_gather(slab_embed, 'xc', axis=0, tiled=True)  64 us
    ppermute x12, starting transfers between devices, y_shift(): return lax.ppermute(value, 'col', pairs)  18.9 us
    dot_general x1, matrix products, similar(): lax.dot_general(left, right, (((1,), (1,)), ((), ())), precision=lax.Prec...  16 us
    ppermute x12, waiting for transfers between devices, y_shift(): return lax.ppermute(value, 'col', pairs)  14.7 us
    gather x2, local copies, waits for them, and re-layouts, lookup(): jnp.take(source, jnp.clip(position, 0, source.shape[0] - 1), axis=0)  13 us
    ppermute x5, starting transfers between devices, z_group_shift(): lax.ppermute(value, ('zl', 'col'), [(i, i ^ N_Y * N_Z ^ 1) for i in range...  8.41 us
    ppermute x5, starting transfers between devices, z_group_shift(): return lax.ppermute(value, 'col', [(c, c ^ 1) for c in range(N_Y * N_Z)])  7.03 us
    ppermute x5, waiting for transfers between devices, z_group_shift(): lax.ppermute(value, ('zl', 'col'), [(i, i ^ N_Y * N_Z ^ 1) for i in range...  5.66 us
  transfers between devices with their start and end apart: 38, of which 20 were waited for; matrix products, arithmetic and copies ran while one was open for 7% of the time, Pallas kernels for 0%

profile of v17, /device:TPU:0, one launch (start us, length us, event | category | flops | bytes accessed | tf_op | source)
XLA Modules:
  0.0 212.9 jit_solution(14506142108492523135)
XLA Ops:
  7.9 2.1 collective-permute-start
  10.1 1.5 collective-permute-done
  15.5 64.0 %all-gather.2.cloned.1.call-done = f32[4096,768]{1,0:T(8,128)} async-done(((f32[512,768]{1,0:T(8,128)}), f32[4096,768]{1,0:T(8,128)}) %all-gather.2.cloned.1.call-update) | async-done | bytes 12582928 | tf_op jit(solution)/shard_map/all_gather | solution.py:122
  79.5 6.0 %gather_fusion = f32[256,768]{1,0:T(8,128)S(1)} fusion(f32[4096,768]{1,0:T(8,128)} %all-gather.2.cloned.1.call-done, s32[1024]{0:T(1024)S(1)} %pad_clamp_fusion.3), kind=kCustom, calls=%fused_computation | custom fusion | bytes 1573888 | tf_op jit(solution)/shard_map/jit(_take)/gather | solution.py:23
  86.5 1.5 collective-permute-start.1
  88.0 2.7 %collective-permute-start.2 = (f32[64,768]{1,0:T(8,128)}, f32[64,768]{1,0:T(8,128)}, u32[]{:S(2)}, u32[]{:S(2)}) collective-permute-start(f32[64,768]{1,0:T(8,128)} %get-tuple-element.9), channel_id=1, source_target_pairs={{0,4},{1,5},{2,6},{3,7},{4,0},{5,1},{6,2},{7,3},{8,12},{9,13},{10,... | collective-permute-start | bytes 589832 | tf_op jit(solution)/shard_map/ppermute | solution.py:33
  92.1 7.1 %gather_fusion.2 = f32[384,768]{1,0:T(8,128)S(1)} fusion(f32[4096,768]{1,0:T(8,128)} %all-gather.2.cloned.1.call-done, s32[1024]{0:T(1024)S(1)} %pad_clamp_fusion.1), kind=kCustom, calls=%fused_computation.2 | custom fusion | bytes 2360832 | tf_op jit(solution)/shard_map/jit(_take)/gather | solution.py:23
  101.3 3.2 %collective-permute-start.4 = (f32[16,768]{1,0:T(8,128)S(1)}, f32[16,768]{1,0:T(8,128)S(1)}, u32[]{:S(2)}, u32[]{:S(2)}) collective-permute-start(f32[16,768]{1,0:T(8,128)S(1)} %get-tuple-element.13), channel_id=1, source_target_pairs={{0,1},{1,0},{2,3},{3,2},{4,5},{5,4},{6,7},{7,6},{8,9},{9,8},{10,11... | collective-permute-start | bytes 147464 | tf_op jit(solution)/shard_map/ppermute | solution.py:47
  105.9 2.6 %collective-permute-start.15 = (f32[96,768]{1,0:T(8,128)S(1)}, f32[96,768]{1,0:T(8,128)S(1)}, u32[]{:S(2)}, u32[]{:S(2)}) collective-permute-start(f32[96,768]{1,0:T(8,128)S(1)} %get-tuple-element.6), channel_id=1, source_target_pairs={{0,4},{1,5},{2,6},{3,7},{4,0},{5,1},{6,2},{7,3},{8,12},{9,13},{10,... | collective-permute-start | bytes 884744 | tf_op jit(solution)/shard_map/ppermute | solution.py:33
  108.5 1.6 collective-permute-start.16
  111.4 2.7 %collective-permute-done.5 = f32[16,768]{1,0:T(8,128)S(1)} collective-permute-done((f32[16,768]{1,0:T(8,128)S(1)}, f32[16,768]{1,0:T(8,128)S(1)}, u32[]{:S(2)}, u32[]{:S(2)}) %collective-permute-start.5) | collective-permute-done | bytes 49184 | tf_op jit(solution)/shard_map/ppermute | solution.py:49
  114.1 1.9 collective-permute-done.6
  117.3 2.8 %collective-permute-start.9 = (f32[16,768]{1,0:T(8,128)S(1)}, f32[16,768]{1,0:T(8,128)S(1)}, u32[]{:S(2)}, u32[]{:S(2)}) collective-permute-start(f32[16,768]{1,0:T(8,128)S(1)} %add_add_fusion.3), channel_id=1, source_target_pairs={{0,65},{1,64},{2,67},{3,66},{4,69},{5,68},{6,71},{7,70},{64,1},{65... | collective-permute-start | bytes 147464 | tf_op jit(solution)/shard_map/ppermute | solution.py:51
  122.0 1.6 collective-permute-start.18
  123.5 2.2 %collective-permute-start.19 = (f32[24,768]{1,0:T(8,128)S(1)}, f32[24,768]{1,0:T(8,128)S(1)}, u32[]{:S(2)}, u32[]{:S(2)}) collective-permute-start(f32[24,768]{1,0:T(8,128)S(1)} %get-tuple-element.11), channel_id=1, source_target_pairs={{0,65},{1,64},{2,67},{3,66},{4,69},{5,68},{6,71},{7,70},{64,1},{65... | collective-permute-start | bytes 221192 | tf_op jit(solution)/shard_map/ppermute | solution.py:51
  126.4 2.2 %collective-permute-start.10 = (f32[64,768]{1,0:T(8,128)S(1)}, f32[64,768]{1,0:T(8,128)S(1)}, u32[]{:S(2)}, u32[]{:S(2)}) collective-permute-start(f32[64,768]{1,0:T(8,128)S(1)} %bitcast_select_fusion.2), channel_id=1, source_target_pairs={{0,6},{1,7},{2,0},{3,1},{4,2},{5,3},{6,4},{7,5},{8,14},{9,15},{10,... | collective-permute-start | bytes 589832 | tf_op jit(solution)/shard_map/ppermute | solution.py:33
  132.2 1.8 collective-permute-start.22
  134.0 1.7 collective-permute-done.20
  138.5 2.2 %collective-permute-start.23 = (f32[96,768]{1,0:T(8,128)S(1)}, f32[96,768]{1,0:T(8,128)S(1)}, u32[]{:S(2)}, u32[]{:S(2)}) collective-permute-start(f32[96,768]{1,0:T(8,128)S(1)} %bitcast_select_fusion), channel_id=1, source_target_pairs={{0,6},{1,7},{2,0},{3,1},{4,2},{5,3},{6,4},{7,5},{8,14},{9,15},{10,... | collective-permute-start | bytes 884744 | tf_op jit(solution)/shard_map/ppermute | solution.py:33
  143.0 8.3 %collective-permute-done.23 = f32[96,768]{1,0:T(8,128)S(1)} collective-permute-done((f32[96,768]{1,0:T(8,128)S(1)}, f32[96,768]{1,0:T(8,128)S(1)}, u32[]{:S(2)}, u32[]{:S(2)}) %collective-permute-start.23) | collective-permute-done | bytes 294944 | tf_op jit(solution)/shard_map/ppermute | solution.py:33
  152.1 3.1 %collective-permute-done.25 = f32[96,768]{1,0:T(8,128)S(1)} collective-permute-done((f32[96,768]{1,0:T(8,128)S(1)}, f32[96,768]{1,0:T(8,128)S(1)}, u32[]{:S(2)}, u32[]{:S(2)}) %collective-permute-start.25) | collective-permute-done | bytes 294944 | tf_op jit(solution)/shard_map/ppermute | solution.py:33
  155.6 16.0 %fusion.2 = f32[640,4096]{1,0:T(8,128)S(1)} fusion(f32[4096,768]{1,0:T(8,128)} %all-gather.2.cloned.1.call-done, f32[384,768]{1,0:T(8,128)S(1)} %bitcast.63, f32[256,768]{1,0:T(8,128)S(1)} %bitcast.66), kind=kOutput, calls=%fused_computation.10 | convolution fusion | flops 12080087040 | bytes 25034752 | tf_op jit(solution)/shard_map/dot_general | solution.py:11
  171.5 4.0 %copy-done = f32[640,4096]{1,0:T(8,128)} copy-done((f32[640,4096]{1,0:T(8,128)}, f32[640,4096]{1,0:T(8,128)S(1)}, u32[]{:S(2)}) %copy-start) | copy-done | bytes 10485784
  177.7 2.0 collective-permute-done.27
  180.0 2.0 collective-permute-start.29
  182.0 3.2 %collective-permute-done.29 = f32[4096]{0:T(1024)S(1)} collective-permute-done((f32[4096]{0:T(1024)S(1)}, f32[4096]{0:T(1024)S(1)}, u32[]{:S(2)}, u32[]{:S(2)}) %collective-permute-start.29) | collective-permute-done | bytes 16416 | tf_op jit(solution)/shard_map/ppermute | solution.py:82
  185.3 3.6 %fusion.1 = f32[384]{0:T(512)S(1)} fusion(f32[640,4096]{1,0:T(8,128)} %copy-done, f32[4096]{0:T(1024)S(1)} %maximum_maximum_fusion), kind=kLoop, calls=%fused_computation.8 | loop fusion | flops 4718208 | bytes 6309376 | tf_op jit(solution)/shard_map/reduce_sum | solution.py:134
  188.8 1.5 collective-permute-start.31
  194.0 2.5 %collective-permute-done.33 = f32[384]{0:T(512)S(1)} collective-permute-done((f32[384]{0:T(512)S(1)}, f32[384]{0:T(512)S(1)}, u32[]{:S(2)}, u32[]{:S(2)}) %collective-permute-start.33) | collective-permute-done | bytes 1568 | tf_op jit(solution)/shard_map/ppermute | solution.py:51
  197.2 2.1 collective-permute-start.35
  199.3 2.6 %collective-permute-start.36 = (f32[4,384]{1,0:T(4,128)S(1)}, f32[4,384]{1,0:T(4,128)S(1)}, u32[]{:S(2)}, u32[]{:S(2)}) collective-permute-start(f32[4,384]{1,0:T(4,128)S(1)} %broadcast_select_fusion), channel_id=1, source_target_pairs={{0,6},{1,7},{2,4},{3,5},{4,2},{5,3},{6,0},{7,1},{8,14},{9,15},{10,... | collective-permute-start | bytes 18440 | tf_op jit(solution)/shard_map/ppermute | solution.py:95
  202.4 1.7 collective-permute-done.36
  (119 shorter events, 34.7 us)
Async XLA Ops:
  7.2 72.3 %all-gather.2.cloned.1.call-start = ((), (), s32[]{:S(2)}) async-start(), calls=%async_computation | async-start | bytes 14155776 | tf_op jit(solution)/shard_map/all_gather | solution.py:122
  86.5 12.9 %collective-permute-start.1 = (f32[64,768]{1,0:T(8,128)}, f32[64,768]{1,0:T(8,128)S(1)}, u32[]{:S(2)}, u32[]{:S(2)}) collective-permute-start(f32[64,768]{1,0:T(8,128)} %get-tuple-element.7), channel_id=1, source_target_pairs={{0,2},{1,3},{2,4},{3,5},{4,6},{5,7},{6,0},{7,1},{8,10},{9,11},{10,... | collective-permute-start | bytes 589832 | tf_op jit(solution)/shard_map/ppermute | solution.py:33
  88.0 12.3 %collective-permute-start.2 = (f32[64,768]{1,0:T(8,128)}, f32[64,768]{1,0:T(8,128)}, u32[]{:S(2)}, u32[]{:S(2)}) collective-permute-start(f32[64,768]{1,0:T(8,128)} %get-tuple-element.9), channel_id=1, source_target_pairs={{0,4},{1,5},{2,6},{3,7},{4,0},{5,1},{6,2},{7,3},{8,12},{9,13},{10,... | collective-permute-start | bytes 589832 | tf_op jit(solution)/shard_map/ppermute | solution.py:33
  90.7 9.6 %collective-permute-start.3 = (f32[64,768]{1,0:T(8,128)S(1)}, f32[64,768]{1,0:T(8,128)}, u32[]{:S(2)}, u32[]{:S(2)}) collective-permute-start(f32[64,768]{1,0:T(8,128)S(1)} %get-tuple-element.8), channel_id=1, source_target_pairs={{0,6},{1,7},{2,0},{3,1},{4,2},{5,3},{6,4},{7,5},{8,14},{9,15},{10,... | collective-permute-start | bytes 589832 | tf_op jit(solution)/shard_map/ppermute | solution.py:33
  101.3 9.3 %collective-permute-start.4 = (f32[16,768]{1,0:T(8,128)S(1)}, f32[16,768]{1,0:T(8,128)S(1)}, u32[]{:S(2)}, u32[]{:S(2)}) collective-permute-start(f32[16,768]{1,0:T(8,128)S(1)} %get-tuple-element.13), channel_id=1, source_target_pairs={{0,1},{1,0},{2,3},{3,2},{4,5},{5,4},{6,7},{7,6},{8,9},{9,8},{10,11... | collective-permute-start | bytes 147464 | tf_op jit(solution)/shard_map/ppermute | solution.py:47
  104.6 12.7 %collective-permute-start.14 = (f32[96,768]{1,0:T(8,128)S(1)}, f32[96,768]{1,0:T(8,128)S(1)}, u32[]{:S(2)}, u32[]{:S(2)}) collective-permute-start(f32[96,768]{1,0:T(8,128)S(1)} %get-tuple-element.4), channel_id=1, source_target_pairs={{0,2},{1,3},{2,4},{3,5},{4,6},{5,7},{6,0},{7,1},{8,10},{9,11},{10,... | collective-permute-start | bytes 884744 | tf_op jit(solution)/shard_map/ppermute | solution.py:33
  105.9 15.5 %collective-permute-start.15 = (f32[96,768]{1,0:T(8,128)S(1)}, f32[96,768]{1,0:T(8,128)S(1)}, u32[]{:S(2)}, u32[]{:S(2)}) collective-permute-start(f32[96,768]{1,0:T(8,128)S(1)} %get-tuple-element.6), channel_id=1, source_target_pairs={{0,4},{1,5},{2,6},{3,7},{4,0},{5,1},{6,2},{7,3},{8,12},{9,13},{10,... | collective-permute-start | bytes 884744 | tf_op jit(solution)/shard_map/ppermute | solution.py:33
  108.5 12.9 %collective-permute-start.16 = (f32[96,768]{1,0:T(8,128)S(1)}, f32[96,768]{1,0:T(8,128)S(1)}, u32[]{:S(2)}, u32[]{:S(2)}) collective-permute-start(f32[96,768]{1,0:T(8,128)S(1)} %get-tuple-element.5), channel_id=1, source_target_pairs={{0,6},{1,7},{2,0},{3,1},{4,2},{5,3},{6,4},{7,5},{8,14},{9,15},{10,... | collective-permute-start | bytes 884744 | tf_op jit(solution)/shard_map/ppermute | solution.py:33
  110.0 4.1 %collective-permute-start.5 = (f32[16,768]{1,0:T(8,128)S(1)}, f32[16,768]{1,0:T(8,128)S(1)}, u32[]{:S(2)}, u32[]{:S(2)}) collective-permute-start(f32[16,768]{1,0:T(8,128)S(1)} %get-tuple-element.15), channel_id=1, source_target_pairs={{0,64},{64,0},{1,65},{65,1},{2,66},{66,2},{3,67},{67,3},{4,68},{68... | collective-permute-start | bytes 147464 | tf_op jit(solution)/shard_map/ppermute | solution.py:49
  110.7 5.3 %collective-permute-start.6 = (f32[16,768]{1,0:T(8,128)S(1)}, f32[16,768]{1,0:T(8,128)S(1)}, u32[]{:S(2)}, u32[]{:S(2)}) collective-permute-start(f32[16,768]{1,0:T(8,128)S(1)} %get-tuple-element.14), channel_id=1, source_target_pairs={{0,65},{1,64},{2,67},{3,66},{4,69},{5,68},{6,71},{7,70},{64,1},{65... | collective-permute-start | bytes 147464 | tf_op jit(solution)/shard_map/ppermute | solution.py:51
  116.0 7.5 %collective-permute-start.7 = (f32[16,768]{1,0:T(8,128)S(1)}, f32[16,768]{1,0:T(8,128)S(1)}, u32[]{:S(2)}, u32[]{:S(2)}) collective-permute-start(f32[16,768]{1,0:T(8,128)S(1)} %add_add_fusion.3), channel_id=1, source_target_pairs={{0,1},{1,0},{2,3},{3,2},{4,5},{5,4},{6,7},{7,6},{8,9},{9,8},{10,11... | collective-permute-start | bytes 147464 | tf_op jit(solution)/shard_map/ppermute | solution.py:47
  116.7 8.9 %collective-permute-start.8 = (f32[16,768]{1,0:T(8,128)S(1)}, f32[16,768]{1,0:T(8,128)S(1)}, u32[]{:S(2)}, u32[]{:S(2)}) collective-permute-start(f32[16,768]{1,0:T(8,128)S(1)} %add_add_fusion.3), channel_id=1, source_target_pairs={{0,64},{64,0},{1,65},{65,1},{2,66},{66,2},{3,67},{67,3},{4,68},{68... | collective-permute-start | bytes 147464 | tf_op jit(solution)/shard_map/ppermute | solution.py:49
  117.3 8.3 %collective-permute-start.9 = (f32[16,768]{1,0:T(8,128)S(1)}, f32[16,768]{1,0:T(8,128)S(1)}, u32[]{:S(2)}, u32[]{:S(2)}) collective-permute-start(f32[16,768]{1,0:T(8,128)S(1)} %add_add_fusion.3), channel_id=1, source_target_pairs={{0,65},{1,64},{2,67},{3,66},{4,69},{5,68},{6,71},{7,70},{64,1},{65... | collective-permute-start | bytes 147464 | tf_op jit(solution)/shard_map/ppermute | solution.py:51
  121.5 8.2 %collective-permute-start.17 = (f32[24,768]{1,0:T(8,128)S(1)}, f32[24,768]{1,0:T(8,128)S(1)}, u32[]{:S(2)}, u32[]{:S(2)}) collective-permute-start(f32[24,768]{1,0:T(8,128)S(1)} %get-tuple-element.10), channel_id=1, source_target_pairs={{0,1},{1,0},{2,3},{3,2},{4,5},{5,4},{6,7},{7,6},{8,9},{9,8},{10,11... | collective-permute-start | bytes 221192 | tf_op jit(solution)/shard_map/ppermute | solution.py:47
  122.0 7.8 %collective-permute-start.18 = (f32[24,768]{1,0:T(8,128)S(1)}, f32[24,768]{1,0:T(8,128)S(1)}, u32[]{:S(2)}, u32[]{:S(2)}) collective-permute-start(f32[24,768]{1,0:T(8,128)S(1)} %get-tuple-element.12), channel_id=1, source_target_pairs={{0,64},{64,0},{1,65},{65,1},{2,66},{66,2},{3,67},{67,3},{4,68},{68... | collective-permute-start | bytes 221192 | tf_op jit(solution)/shard_map/ppermute | solution.py:49
  123.5 6.2 %collective-permute-start.19 = (f32[24,768]{1,0:T(8,128)S(1)}, f32[24,768]{1,0:T(8,128)S(1)}, u32[]{:S(2)}, u32[]{:S(2)}) collective-permute-start(f32[24,768]{1,0:T(8,128)S(1)} %get-tuple-element.11), channel_id=1, source_target_pairs={{0,65},{1,64},{2,67},{3,66},{4,69},{5,68},{6,71},{7,70},{64,1},{65... | collective-permute-start | bytes 221192 | tf_op jit(solution)/shard_map/ppermute | solution.py:51
  126.4 15.6 %collective-permute-start.10 = (f32[64,768]{1,0:T(8,128)S(1)}, f32[64,768]{1,0:T(8,128)S(1)}, u32[]{:S(2)}, u32[]{:S(2)}) collective-permute-start(f32[64,768]{1,0:T(8,128)S(1)} %bitcast_select_fusion.2), channel_id=1, source_target_pairs={{0,6},{1,7},{2,0},{3,1},{4,2},{5,3},{6,4},{7,5},{8,14},{9,15},{10,... | collective-permute-start | bytes 589832 | tf_op jit(solution)/shard_map/ppermute | solution.py:33
  128.6 13.7 %collective-permute-start.11 = (f32[64,768]{1,0:T(8,128)S(1)}, f32[64,768]{1,0:T(8,128)S(1)}, u32[]{:S(2)}, u32[]{:S(2)}) collective-permute-start(f32[64,768]{1,0:T(8,128)S(1)} %bitcast_select_fusion.2), channel_id=1, source_target_pairs={{0,4},{1,5},{2,6},{3,7},{4,0},{5,1},{6,2},{7,3},{8,12},{9,13},{10,... | collective-permute-start | bytes 589832 | tf_op jit(solution)/shard_map/ppermute | solution.py:33
  129.8 5.9 %collective-permute-start.20 = (f32[24,768]{1,0:T(8,128)S(1)}, f32[24,768]{1,0:T(8,128)S(1)}, u32[]{:S(2)}, u32[]{:S(2)}) collective-permute-start(f32[24,768]{1,0:T(8,128)S(1)} %add_add_fusion.2), channel_id=1, source_target_pairs={{0,1},{1,0},{2,3},{3,2},{4,5},{5,4},{6,7},{7,6},{8,9},{9,8},{10,11... | collective-permute-start | bytes 221192 | tf_op jit(solution)/shard_map/ppermute | solution.py:47
  130.8 5.7 %collective-permute-start.21 = (f32[24,768]{1,0:T(8,128)S(1)}, f32[24,768]{1,0:T(8,128)S(1)}, u32[]{:S(2)}, u32[]{:S(2)}) collective-permute-start(f32[24,768]{1,0:T(8,128)S(1)} %add_add_fusion.2), channel_id=1, source_target_pairs={{0,64},{64,0},{1,65},{65,1},{2,66},{66,2},{3,67},{67,3},{4,68},{68... | collective-permute-start | bytes 221192 | tf_op jit(solution)/shard_map/ppermute | solution.py:49
  132.2 5.6 %collective-permute-start.22 = (f32[24,768]{1,0:T(8,128)S(1)}, f32[24,768]{1,0:T(8,128)S(1)}, u32[]{:S(2)}, u32[]{:S(2)}) collective-permute-start(f32[24,768]{1,0:T(8,128)S(1)} %add_add_fusion.2), channel_id=1, source_target_pairs={{0,65},{1,64},{2,67},{3,66},{4,69},{5,68},{6,71},{7,70},{64,1},{65... | collective-permute-start | bytes 221192 | tf_op jit(solution)/shard_map/ppermute | solution.py:51
  135.7 7.0 %collective-permute-start.12 = (f32[64,768]{1,0:T(8,128)S(1)}, f32[64,768]{1,0:T(8,128)S(1)}, u32[]{:S(2)}, u32[]{:S(2)}) collective-permute-start(f32[64,768]{1,0:T(8,128)S(1)} %bitcast_select_fusion.2), channel_id=1, source_target_pairs={{0,2},{1,3},{2,4},{3,5},{4,6},{5,7},{6,0},{7,1},{8,10},{9,11},{10,... | collective-permute-start | bytes 589832 | tf_op jit(solution)/shard_map/ppermute | solution.py:33
  138.5 12.9 %collective-permute-start.23 = (f32[96,768]{1,0:T(8,128)S(1)}, f32[96,768]{1,0:T(8,128)S(1)}, u32[]{:S(2)}, u32[]{:S(2)}) collective-permute-start(f32[96,768]{1,0:T(8,128)S(1)} %bitcast_select_fusion), channel_id=1, source_target_pairs={{0,6},{1,7},{2,0},{3,1},{4,2},{5,3},{6,4},{7,5},{8,14},{9,15},{10,... | collective-permute-start | bytes 884744 | tf_op jit(solution)/shard_map/ppermute | solution.py:33
  140.7 11.4 %collective-permute-start.24 = (f32[96,768]{1,0:T(8,128)S(1)}, f32[96,768]{1,0:T(8,128)S(1)}, u32[]{:S(2)}, u32[]{:S(2)}) collective-permute-start(f32[96,768]{1,0:T(8,128)S(1)} %bitcast_select_fusion), channel_id=1, source_target_pairs={{0,4},{1,5},{2,6},{3,7},{4,0},{5,1},{6,2},{7,3},{8,12},{9,13},{10,... | collective-permute-start | bytes 884744 | tf_op jit(solution)/shard_map/ppermute | solution.py:33
  141.9 13.3 %collective-permute-start.25 = (f32[96,768]{1,0:T(8,128)S(1)}, f32[96,768]{1,0:T(8,128)S(1)}, u32[]{:S(2)}, u32[]{:S(2)}) collective-permute-start(f32[96,768]{1,0:T(8,128)S(1)} %bitcast_select_fusion), channel_id=1, source_target_pairs={{0,2},{1,3},{2,4},{3,5},{4,6},{5,7},{6,0},{7,1},{8,10},{9,11},{10,... | collective-permute-start | bytes 884744 | tf_op jit(solution)/shard_map/ppermute | solution.py:33
  180.0 5.2 %collective-permute-start.29 = (f32[4096]{0:T(1024)S(1)}, f32[4096]{0:T(1024)S(1)}, u32[]{:S(2)}, u32[]{:S(2)}) collective-permute-start(f32[4096]{0:T(1024)S(1)} %maximum_maximum_fusion.1), channel_id=1, source_target_pairs={{0,32},{8,40},{16,48},{24,56},{32,0},{40,8},{48,16},{56,24},{1,33}... | collective-permute-start | bytes 49160 | tf_op jit(solution)/shard_map/ppermute | solution.py:82
  188.8 5.2 %collective-permute-start.31 = (f32[384]{0:T(512)S(1)}, f32[384]{0:T(512)S(1)}, u32[]{:S(2)}, u32[]{:S(2)}) collective-permute-start(f32[384]{0:T(512)S(1)} %fusion.1), channel_id=1, source_target_pairs={{0,1},{1,0},{2,3},{3,2},{4,5},{5,4},{6,7},{7,6},{8,9},{9,8},{10,11... | collective-permute-start | bytes 4616 | tf_op jit(solution)/shard_map/ppermute | solution.py:47
  191.7 4.8 %collective-permute-start.33 = (f32[384]{0:T(512)S(1)}, f32[384]{0:T(512)S(1)}, u32[]{:S(2)}, u32[]{:S(2)}) collective-permute-start(f32[384]{0:T(512)S(1)} %fusion.1), channel_id=1, source_target_pairs={{0,65},{1,64},{2,67},{3,66},{4,69},{5,68},{6,71},{7,70},{64,1},{65... | collective-permute-start | bytes 4616 | tf_op jit(solution)/shard_map/ppermute | solution.py:51
  193.0 12.4 %collective-permute-start.30 = (f32[4096]{0:T(1024)S(1)}, f32[4096]{0:T(1024)S(1)}, u32[]{:S(2)}, u32[]{:S(2)}) collective-permute-start(f32[4096]{0:T(1024)S(1)} %maximum_maximum_fusion), channel_id=1, source_target_pairs={{0,64},{64,0},{1,65},{65,1},{2,66},{66,2},{3,67},{67,3},{4,68},{68... | collective-permute-start | bytes 49160 | tf_op jit(solution)/shard_map/ppermute | solution.py:138
  197.2 4.8 %collective-permute-start.34 = (f32[4,384]{1,0:T(4,128)S(1)}, f32[4,384]{1,0:T(4,128)S(1)}, u32[]{:S(2)}, u32[]{:S(2)}) collective-permute-start(f32[4,384]{1,0:T(4,128)S(1)} %broadcast_select_fusion), channel_id=1, source_target_pairs={{0,2},{1,3},{2,0},{3,1},{4,6},{5,7},{6,4},{7,5},{8,10},{9,11},{10,... | collective-permute-start | bytes 18440 | tf_op jit(solution)/shard_map/ppermute | solution.py:95
  197.2 5.2 %collective-permute-start.35 = (f32[4,384]{1,0:T(4,128)S(1)}, f32[4,384]{1,0:T(4,128)S(1)}, u32[]{:S(2)}, u32[]{:S(2)}) collective-permute-start(f32[4,384]{1,0:T(4,128)S(1)} %broadcast_select_fusion), channel_id=1, source_target_pairs={{0,4},{1,5},{2,6},{3,7},{4,0},{5,1},{6,2},{7,3},{8,12},{9,13},{10,... | collective-permute-start | bytes 18440 | tf_op jit(solution)/shard_map/ppermute | solution.py:95
  199.3 4.8 %collective-permute-start.36 = (f32[4,384]{1,0:T(4,128)S(1)}, f32[4,384]{1,0:T(4,128)S(1)}, u32[]{:S(2)}, u32[]{:S(2)}) collective-permute-start(f32[4,384]{1,0:T(4,128)S(1)} %broadcast_select_fusion), channel_id=1, source_target_pairs={{0,6},{1,7},{2,4},{3,5},{4,2},{5,3},{6,0},{7,1},{8,14},{9,15},{10,... | collective-permute-start | bytes 18440 | tf_op jit(solution)/shard_map/ppermute | solution.py:95
  (8 other events, 33.8 us)
Sparse Core Ops, SparseCore 0:
  9.7 69.7 all-gather.1

commit v18 on v17

--- a/solution.py
+++ b/solution.py
@@ -127,11 +127,11 @@
     selected = group_masked_sum(lookup(half, both_sel, first_row))
     chosen = group_masked_sum(lookup(half, both_cand, first_row))
     n_sel = both_sel.shape[0]
-    scores = lax.optimization_barrier(similar(jnp.concatenate([selected, chosen]), half))
-    reached = all_max_two_rounds(jnp.max(scores[:n_sel], axis=0), "xc", n_xc)
+    sel_scores = lax.optimization_barrier(similar(selected, half))
+    reached = all_max_two_rounds(jnp.max(sel_scores, axis=0), "xc", n_xc)
     old = lax.dynamic_slice_in_dim(coverage_old, zl * half.shape[0], half.shape[0])
     coverage = jnp.maximum(old, reached)
-    gain_part = jnp.sum(jnp.maximum(scores[n_sel:] - coverage[None, :], 0.0), axis=1)
+    gain_part = jnp.sum(jnp.maximum(similar(chosen, half) - coverage[None, :], 0.0), axis=1)
     parts = group_gather_in_order(gain_part)
     total = jnp.sum(parts.reshape(-1, gain_part.shape[0]), axis=0)
     total_gain = lax.dynamic_slice_in_dim(total, zl * cand_index.shape[0], cand_index.shape[0])

time: 213 us -> 209 us (0.981)
  starting transfers between devices: 51.5 us -> 44.7 us
  waiting for transfers between devices: 99.4 us -> 105 us
  matrix products: 16 us -> 21.1 us
  other arithmetic: 9.93 us -> 5.59 us
  local copies, waits for them, and re-layouts: 21.6 us -> 17.6 us
    ppermute x12, starting transfers between devices: 18.9 us -> 10.1 us  [y_shift(): return lax.ppermute(value, 'col', pairs)]
    ppermute x5, starting transfers between devices: 7.03 us -> 14 us  [z_group_shift(): return lax.ppermute(value, 'col', [(c, c ^ 1) for c in range(N_Y * N_Z)])]
    ppermute x12, waiting for transfers between devices: 14.7 us -> 21.3 us  [y_shift(): return lax.ppermute(value, 'col', pairs)]
    dot_general x1 -> x2, matrix products: 16 us -> 21.1 us  [similar(): lax.dot_general(left, right, (((1,), (1,)), ((), ())), precision=lax.Prec...]
    ppermute x5, waiting for transfers between devices: 5.66 us -> 1.13 us  [z_group_shift(): lax.ppermute(value, ('zl', 'col'), [(i, i ^ N_Y * N_Z ^ 1) for i in range...]
    ppermute x5, waiting for transfers between devices: 1.94 us -> 5.99 us  [z_group_shift(): return lax.ppermute(value, 'col', [(c, c ^ 1) for c in range(N_Y * N_Z)])]
    unnamed x14 -> x16, local copies, waits for them, and re-layouts: 4.2 us -> 0.2 us
    ppermute x5, starting transfers between devices: 5.56 us -> 1.91 us  [z_group_shift(): return lax.ppermute(value, 'zl', [(0, 1), (1, 0)])]
  transfers between devices with their start and end apart: 38 -> 38, of which waited for: 20 -> 21; matrix products, arithmetic and copies ran while one was open for 7% -> 10% of each run, Pallas kernels for 0% -> 0%
where the time goes in v18:
time: 209 us
  waiting for transfers between devices  105 us (50%)
  starting transfers between devices  44.7 us (21%)
  matrix products  21.1 us (10%)
  local copies, waits for them, and re-layouts  17.6 us (8%)
  between operations  14.5 us (7%)
  other arithmetic  5.59 us (3%)
    all_gather x1, waiting for transfers between devices, body(): half = lax.all_gather(slab_embed, 'xc', axis=0, tiled=True)  65.7 us
    ppermute x12, waiting for transfers between devices, y_shift(): return lax.ppermute(value, 'col', pairs)  21.3 us
    dot_general x2, matrix products, similar(): lax.dot_general(left, right, (((1,), (1,)), ((), ())), precision=lax.Prec...  21.1 us
    ppermute x5, starting transfers between devices, z_group_shift(): return lax.ppermute(value, 'col', [(c, c ^ 1) for c in range(N_Y * N_Z)])  14 us
    gather x2, local copies, waits for them, and re-layouts, lookup(): jnp.take(source, jnp.clip(position, 0, source.shape[0] - 1), axis=0)  13 us
    ppermute x12, starting transfers between devices, y_shift(): return lax.ppermute(value, 'col', pairs)  10.1 us
    ppermute x5, starting transfers between devices, z_group_shift(): lax.ppermute(value, ('zl', 'col'), [(i, i ^ N_Y * N_Z ^ 1) for i in range...  8.14 us
    ppermute x5, waiting for transfers between devices, z_group_shift(): return lax.ppermute(value, 'col', [(c, c ^ 1) for c in range(N_Y * N_Z)])  5.99 us
  transfers between devices with their start and end apart: 38, of which 21 were waited for; matrix products, arithmetic and copies ran while one was open for 10% of the time, Pallas kernels for 0%

profile of v18, /device:TPU:0, one launch (start us, length us, event | category | flops | bytes accessed | tf_op | source)
XLA Modules:
  0.0 208.7 jit_solution(4479311752094828596)
XLA Ops:
  7.9 2.1 collective-permute-start
  10.2 1.3 collective-permute-done
  11.6 2.0 collective-permute-done.18
  13.8 65.7 %all-gather.2.cloned.1.call-done = f32[4096,768]{1,0:T(8,128)} async-done(((f32[512,768]{1,0:T(8,128)}), f32[4096,768]{1,0:T(8,128)}) %all-gather.2.cloned.1.call-update) | async-done | bytes 12582928 | tf_op jit(solution)/shard_map/all_gather | solution.py:122
  79.5 6.0 %gather_fusion = f32[256,768]{1,0:T(8,128)S(1)} fusion(f32[4096,768]{1,0:T(8,128)} %all-gather.2.cloned.1.call-done, s32[1024]{0:T(1024)S(1)} %pad_clamp_fusion.3), kind=kCustom, calls=%fused_computation | custom fusion | bytes 1573888 | tf_op jit(solution)/shard_map/jit(_take)/gather | solution.py:23
  86.5 2.7 %collective-permute-start.3 = (f32[64,768]{1,0:T(8,128)}, f32[64,768]{1,0:T(8,128)S(1)}, u32[]{:S(2)}, u32[]{:S(2)}) collective-permute-start(f32[64,768]{1,0:T(8,128)} %get-tuple-element.8), channel_id=1, source_target_pairs={{0,6},{1,7},{2,0},{3,1},{4,2},{5,3},{6,4},{7,5},{8,14},{9,15},{10,... | collective-permute-start | bytes 589832 | tf_op jit(solution)/shard_map/ppermute | solution.py:33
  90.9 7.1 %gather_fusion.2 = f32[384,768]{1,0:T(8,128)S(1)} fusion(f32[4096,768]{1,0:T(8,128)} %all-gather.2.cloned.1.call-done, s32[1024]{0:T(1024)S(1)} %pad_clamp_fusion.1), kind=kCustom, calls=%fused_computation.2 | custom fusion | bytes 2360832 | tf_op jit(solution)/shard_map/jit(_take)/gather | solution.py:23
  98.9 3.2 %collective-permute-done.1 = f32[64,768]{1,0:T(8,128)} collective-permute-done((f32[64,768]{1,0:T(8,128)S(1)}, f32[64,768]{1,0:T(8,128)}, u32[]{:S(2)}, u32[]{:S(2)}) %collective-permute-start.1) | collective-permute-done | bytes 196640 | tf_op jit(solution)/shard_map/ppermute | solution.py:33
  103.1 3.0 %collective-permute-start.6 = (f32[16,768]{1,0:T(8,128)S(1)}, f32[16,768]{1,0:T(8,128)S(1)}, u32[]{:S(2)}, u32[]{:S(2)}) collective-permute-start(f32[16,768]{1,0:T(8,128)S(1)} %get-tuple-element.14), channel_id=1, source_target_pairs={{0,65},{1,64},{2,67},{3,66},{4,69},{5,68},{6,71},{7,70},{64,1},{65... | collective-permute-start | bytes 147464 | tf_op jit(solution)/shard_map/ppermute | solution.py:51
  108.7 1.8 collective-permute-start.4
  110.8 2.0 collective-permute-done.5
  112.8 1.5 collective-permute-done.4
  114.3 2.8 %collective-permute-start.9 = (f32[16,768]{1,0:T(8,128)S(1)}, f32[16,768]{1,0:T(8,128)S(1)}, u32[]{:S(2)}, u32[]{:S(2)}) collective-permute-start(f32[16,768]{1,0:T(8,128)S(1)} %add_add_fusion.3), channel_id=1, source_target_pairs={{0,65},{1,64},{2,67},{3,66},{4,69},{5,68},{6,71},{7,70},{64,1},{65... | collective-permute-start | bytes 147464 | tf_op jit(solution)/shard_map/ppermute | solution.py:51
  117.2 1.9 collective-permute-start.7
  119.1 3.8 %collective-permute-done.19 = f32[96,768]{1,0:T(8,128)S(1)} collective-permute-done((f32[96,768]{1,0:T(8,128)S(1)}, f32[96,768]{1,0:T(8,128)S(1)}, u32[]{:S(2)}, u32[]{:S(2)}) %collective-permute-start.19) | collective-permute-done | bytes 294944 | tf_op jit(solution)/shard_map/ppermute | solution.py:33
  123.7 4.1 %collective-permute-start.22 = (f32[24,768]{1,0:T(8,128)S(1)}, f32[24,768]{1,0:T(8,128)S(1)}, u32[]{:S(2)}, u32[]{:S(2)}) collective-permute-start(f32[24,768]{1,0:T(8,128)S(1)} %get-tuple-element.10), channel_id=1, source_target_pairs={{0,1},{1,0},{2,3},{3,2},{4,5},{5,4},{6,7},{7,6},{8,9},{9,8},{10,11... | collective-permute-start | bytes 221192 | tf_op jit(solution)/shard_map/ppermute | solution.py:47
  128.4 1.1 collective-permute-start.10
  129.9 1.3 collective-permute-done.22
  132.3 1.4 collective-permute-start.26
  133.7 2.3 %collective-permute-start.25 = (f32[24,768]{1,0:T(8,128)S(1)}, f32[24,768]{1,0:T(8,128)S(1)}, u32[]{:S(2)}, u32[]{:S(2)}) collective-permute-start(f32[24,768]{1,0:T(8,128)S(1)} %add_add_fusion.2), channel_id=1, source_target_pairs={{0,1},{1,0},{2,3},{3,2},{4,5},{5,4},{6,7},{7,6},{8,9},{9,8},{10,11... | collective-permute-start | bytes 221192 | tf_op jit(solution)/shard_map/ppermute | solution.py:47
  137.2 2.3 %collective-permute-done.25 = f32[24,768]{1,0:T(8,128)S(1)} collective-permute-done((f32[24,768]{1,0:T(8,128)S(1)}, f32[24,768]{1,0:T(8,128)S(1)}, u32[]{:S(2)}, u32[]{:S(2)}) %collective-permute-start.25) | collective-permute-done | bytes 73760 | tf_op jit(solution)/shard_map/ppermute | solution.py:47
  140.2 3.9 %collective-permute-done.12 = f32[64,768]{1,0:T(8,128)S(1)} collective-permute-done((f32[64,768]{1,0:T(8,128)S(1)}, f32[64,768]{1,0:T(8,128)S(1)}, u32[]{:S(2)}, u32[]{:S(2)}) %collective-permute-start.12) | collective-permute-done | bytes 196640 | tf_op jit(solution)/shard_map/ppermute | solution.py:33
  144.4 10.2 %fusion.14 = f32[256,4096]{1,0:T(8,128)} fusion(f32[256,768]{1,0:T(8,128)S(1)} %bitcast.68, f32[4096,768]{1,0:T(8,128)} %all-gather.2.cloned.1.call-done), kind=kOutput, calls=%fused_computation.88 | convolution fusion | flops 4831838208 | bytes 17563648 | tf_op jit(solution)/shard_map/dot_general | solution.py:11
  154.6 2.4 %reduce_max.9 = f32[4096]{0:T(1024)S(1)} reduce(f32[256,4096]{1,0:T(8,128)} %fusion.14, f32[]{:T(128)} %constant.196.clone.1), dimensions={0}, to_apply=%region_0.1 | reduce | flops 1044480 | bytes 4210692 | tf_op jit(solution)/shard_map/reduce_max | solution.py:131
  161.2 2.2 %collective-permute-start.16 = (f32[4096]{0:T(1024)S(1)}, f32[4096]{0:T(1024)S(1)}, u32[]{:S(2)}, u32[]{:S(2)}) collective-permute-start(f32[4096]{0:T(1024)S(1)} %maximum_maximum_fusion.1), channel_id=1, source_target_pairs={{0,32},{8,40},{16,48},{24,56},{32,0},{40,8},{48,16},{56,24},{1,33}... | collective-permute-start | bytes 49160 | tf_op jit(solution)/shard_map/ppermute | solution.py:82
  163.5 3.0 %collective-permute-done.16 = f32[4096]{0:T(1024)S(1)} collective-permute-done((f32[4096]{0:T(1024)S(1)}, f32[4096]{0:T(1024)S(1)}, u32[]{:S(2)}, u32[]{:S(2)}) %collective-permute-start.16) | collective-permute-done | bytes 16416 | tf_op jit(solution)/shard_map/ppermute | solution.py:82
  166.6 2.4 %collective-permute-done.28 = f32[96,768]{1,0:T(8,128)S(1)} collective-permute-done((f32[96,768]{1,0:T(8,128)S(1)}, f32[96,768]{1,0:T(8,128)S(1)}, u32[]{:S(2)}, u32[]{:S(2)}) %collective-permute-start.28) | collective-permute-done | bytes 294944 | tf_op jit(solution)/shard_map/ppermute | solution.py:33
  169.0 2.4 %collective-permute-done.29 = f32[96,768]{1,0:T(8,128)S(1)} collective-permute-done((f32[96,768]{1,0:T(8,128)S(1)}, f32[96,768]{1,0:T(8,128)S(1)}, u32[]{:S(2)}, u32[]{:S(2)}) %collective-permute-start.29) | collective-permute-done | bytes 294944 | tf_op jit(solution)/shard_map/ppermute | solution.py:33
  171.5 5.0 %collective-permute-done.30 = f32[96,768]{1,0:T(8,128)S(1)} collective-permute-done((f32[96,768]{1,0:T(8,128)S(1)}, f32[96,768]{1,0:T(8,128)S(1)}, u32[]{:S(2)}, u32[]{:S(2)}) %collective-permute-start.30) | collective-permute-done | bytes 294944 | tf_op jit(solution)/shard_map/ppermute | solution.py:33
  176.8 10.8 %maximum_reduce_fusion = f32[384]{0:T(512)S(1)} fusion(f32[384,768]{1,0:T(8,128)S(1)} %bitcast.71, f32[4096,768]{1,0:T(8,128)} %all-gather.2.cloned.1.call-done, f32[4096]{0:T(1024)S(1)} %maximum_maximum_fusion), kind=kOutput, calls=%fused_computation.6 | convolution fusion | flops 7252475392 | bytes 13780480 | tf_op jit(solution)/shard_map/dot_general | solution.py:11
  188.5 3.9 %collective-permute-start.31 = (f32[384]{0:T(512)S(1)}, f32[384]{0:T(512)S(1)}, u32[]{:S(2)}, u32[]{:S(2)}) collective-permute-start(f32[384]{0:T(512)S(1)} %maximum_reduce_fusion), channel_id=1, source_target_pairs={{0,1},{1,0},{2,3},{3,2},{4,5},{5,4},{6,7},{7,6},{8,9},{9,8},{10,11... | collective-permute-start | bytes 4616 | tf_op jit(solution)/shard_map/ppermute | solution.py:47
  195.5 3.2 %collective-permute-start.34 = (f32[4,384]{1,0:T(4,128)S(1)}, f32[4,384]{1,0:T(4,128)S(1)}, u32[]{:S(2)}, u32[]{:S(2)}) collective-permute-start(f32[4,384]{1,0:T(4,128)S(1)} %broadcast_select_fusion), channel_id=1, source_target_pairs={{0,2},{1,3},{2,0},{3,1},{4,6},{5,7},{6,4},{7,5},{8,10},{9,11},{10,... | collective-permute-start | bytes 18440 | tf_op jit(solution)/shard_map/ppermute | solution.py:95
  (121 shorter events, 25.2 us)
Async XLA Ops:
  7.2 72.3 %all-gather.2.cloned.1.call-start = ((), (), s32[]{:S(2)}) async-start(), calls=%async_computation | async-start | bytes 14155776 | tf_op jit(solution)/shard_map/all_gather | solution.py:122
  86.5 11.9 %collective-permute-start.3 = (f32[64,768]{1,0:T(8,128)}, f32[64,768]{1,0:T(8,128)S(1)}, u32[]{:S(2)}, u32[]{:S(2)}) collective-permute-start(f32[64,768]{1,0:T(8,128)} %get-tuple-element.8), channel_id=1, source_target_pairs={{0,6},{1,7},{2,0},{3,1},{4,2},{5,3},{6,4},{7,5},{8,14},{9,15},{10,... | collective-permute-start | bytes 589832 | tf_op jit(solution)/shard_map/ppermute | solution.py:33
  89.2 9.6 %collective-permute-start.2 = (f32[64,768]{1,0:T(8,128)}, f32[64,768]{1,0:T(8,128)}, u32[]{:S(2)}, u32[]{:S(2)}) collective-permute-start(f32[64,768]{1,0:T(8,128)} %get-tuple-element.9), channel_id=1, source_target_pairs={{0,4},{1,5},{2,6},{3,7},{4,0},{5,1},{6,2},{7,3},{8,12},{9,13},{10,... | collective-permute-start | bytes 589832 | tf_op jit(solution)/shard_map/ppermute | solution.py:33
  90.0 12.0 %collective-permute-start.1 = (f32[64,768]{1,0:T(8,128)S(1)}, f32[64,768]{1,0:T(8,128)}, u32[]{:S(2)}, u32[]{:S(2)}) collective-permute-start(f32[64,768]{1,0:T(8,128)S(1)} %get-tuple-element.7), channel_id=1, source_target_pairs={{0,2},{1,3},{2,4},{3,5},{4,6},{5,7},{6,0},{7,1},{8,10},{9,11},{10,... | collective-permute-start | bytes 589832 | tf_op jit(solution)/shard_map/ppermute | solution.py:33
  103.1 5.6 %collective-permute-start.6 = (f32[16,768]{1,0:T(8,128)S(1)}, f32[16,768]{1,0:T(8,128)S(1)}, u32[]{:S(2)}, u32[]{:S(2)}) collective-permute-start(f32[16,768]{1,0:T(8,128)S(1)} %get-tuple-element.14), channel_id=1, source_target_pairs={{0,65},{1,64},{2,67},{3,66},{4,69},{5,68},{6,71},{7,70},{64,1},{65... | collective-permute-start | bytes 147464 | tf_op jit(solution)/shard_map/ppermute | solution.py:51
  106.2 10.9 %collective-permute-start.21 = (f32[96,768]{1,0:T(8,128)S(1)}, f32[96,768]{1,0:T(8,128)S(1)}, u32[]{:S(2)}, u32[]{:S(2)}) collective-permute-start(f32[96,768]{1,0:T(8,128)S(1)} %get-tuple-element.5), channel_id=1, source_target_pairs={{0,6},{1,7},{2,0},{3,1},{4,2},{5,3},{6,4},{7,5},{8,14},{9,15},{10,... | collective-permute-start | bytes 884744 | tf_op jit(solution)/shard_map/ppermute | solution.py:33
  106.9 12.2 %collective-permute-start.20 = (f32[96,768]{1,0:T(8,128)S(1)}, f32[96,768]{1,0:T(8,128)S(1)}, u32[]{:S(2)}, u32[]{:S(2)}) collective-permute-start(f32[96,768]{1,0:T(8,128)S(1)} %get-tuple-element.6), channel_id=1, source_target_pairs={{0,4},{1,5},{2,6},{3,7},{4,0},{5,1},{6,2},{7,3},{8,12},{9,13},{10,... | collective-permute-start | bytes 884744 | tf_op jit(solution)/shard_map/ppermute | solution.py:33
  107.7 15.1 %collective-permute-start.19 = (f32[96,768]{1,0:T(8,128)S(1)}, f32[96,768]{1,0:T(8,128)S(1)}, u32[]{:S(2)}, u32[]{:S(2)}) collective-permute-start(f32[96,768]{1,0:T(8,128)S(1)} %get-tuple-element.4), channel_id=1, source_target_pairs={{0,2},{1,3},{2,4},{3,5},{4,6},{5,7},{6,0},{7,1},{8,10},{9,11},{10,... | collective-permute-start | bytes 884744 | tf_op jit(solution)/shard_map/ppermute | solution.py:33
  108.7 5.6 %collective-permute-start.4 = (f32[16,768]{1,0:T(8,128)S(1)}, f32[16,768]{1,0:T(8,128)S(1)}, u32[]{:S(2)}, u32[]{:S(2)}) collective-permute-start(f32[16,768]{1,0:T(8,128)S(1)} %get-tuple-element.13), channel_id=1, source_target_pairs={{0,1},{1,0},{2,3},{3,2},{4,5},{5,4},{6,7},{7,6},{8,9},{9,8},{10,11... | collective-permute-start | bytes 147464 | tf_op jit(solution)/shard_map/ppermute | solution.py:47
  114.3 9.4 %collective-permute-start.9 = (f32[16,768]{1,0:T(8,128)S(1)}, f32[16,768]{1,0:T(8,128)S(1)}, u32[]{:S(2)}, u32[]{:S(2)}) collective-permute-start(f32[16,768]{1,0:T(8,128)S(1)} %add_add_fusion.3), channel_id=1, source_target_pairs={{0,65},{1,64},{2,67},{3,66},{4,69},{5,68},{6,71},{7,70},{64,1},{65... | collective-permute-start | bytes 147464 | tf_op jit(solution)/shard_map/ppermute | solution.py:51
  117.2 10.6 %collective-permute-start.8 = (f32[16,768]{1,0:T(8,128)S(1)}, f32[16,768]{1,0:T(8,128)S(1)}, u32[]{:S(2)}, u32[]{:S(2)}) collective-permute-start(f32[16,768]{1,0:T(8,128)S(1)} %add_add_fusion.3), channel_id=1, source_target_pairs={{0,64},{64,0},{1,65},{65,1},{2,66},{66,2},{3,67},{67,3},{4,68},{68... | collective-permute-start | bytes 147464 | tf_op jit(solution)/shard_map/ppermute | solution.py:49
  117.2 10.6 %collective-permute-start.7 = (f32[16,768]{1,0:T(8,128)S(1)}, f32[16,768]{1,0:T(8,128)S(1)}, u32[]{:S(2)}, u32[]{:S(2)}) collective-permute-start(f32[16,768]{1,0:T(8,128)S(1)} %add_add_fusion.3), channel_id=1, source_target_pairs={{0,1},{1,0},{2,3},{3,2},{4,5},{5,4},{6,7},{7,6},{8,9},{9,8},{10,11... | collective-permute-start | bytes 147464 | tf_op jit(solution)/shard_map/ppermute | solution.py:47
  123.0 7.0 %collective-permute-start.24 = (f32[24,768]{1,0:T(8,128)S(1)}, f32[24,768]{1,0:T(8,128)S(1)}, u32[]{:S(2)}, u32[]{:S(2)}) collective-permute-start(f32[24,768]{1,0:T(8,128)S(1)} %get-tuple-element.11), channel_id=1, source_target_pairs={{0,65},{1,64},{2,67},{3,66},{4,69},{5,68},{6,71},{7,70},{64,1},{65... | collective-permute-start | bytes 221192 | tf_op jit(solution)/shard_map/ppermute | solution.py:51
  123.4 6.6 %collective-permute-start.23 = (f32[24,768]{1,0:T(8,128)S(1)}, f32[24,768]{1,0:T(8,128)S(1)}, u32[]{:S(2)}, u32[]{:S(2)}) collective-permute-start(f32[24,768]{1,0:T(8,128)S(1)} %get-tuple-element.12), channel_id=1, source_target_pairs={{0,64},{64,0},{1,65},{65,1},{2,66},{66,2},{3,67},{67,3},{4,68},{68... | collective-permute-start | bytes 221192 | tf_op jit(solution)/shard_map/ppermute | solution.py:49
  123.7 7.5 %collective-permute-start.22 = (f32[24,768]{1,0:T(8,128)S(1)}, f32[24,768]{1,0:T(8,128)S(1)}, u32[]{:S(2)}, u32[]{:S(2)}) collective-permute-start(f32[24,768]{1,0:T(8,128)S(1)} %get-tuple-element.10), channel_id=1, source_target_pairs={{0,1},{1,0},{2,3},{3,2},{4,5},{5,4},{6,7},{7,6},{8,9},{9,8},{10,11... | collective-permute-start | bytes 221192 | tf_op jit(solution)/shard_map/ppermute | solution.py:47
  128.4 11.7 %collective-permute-start.10 = (f32[64,768]{1,0:T(8,128)S(1)}, f32[64,768]{1,0:T(8,128)S(1)}, u32[]{:S(2)}, u32[]{:S(2)}) collective-permute-start(f32[64,768]{1,0:T(8,128)S(1)} %bitcast_select_fusion.2), channel_id=1, source_target_pairs={{0,6},{1,7},{2,0},{3,1},{4,2},{5,3},{6,4},{7,5},{8,14},{9,15},{10,... | collective-permute-start | bytes 589832 | tf_op jit(solution)/shard_map/ppermute | solution.py:33
  129.6 10.6 %collective-permute-start.11 = (f32[64,768]{1,0:T(8,128)S(1)}, f32[64,768]{1,0:T(8,128)S(1)}, u32[]{:S(2)}, u32[]{:S(2)}) collective-permute-start(f32[64,768]{1,0:T(8,128)S(1)} %bitcast_select_fusion.2), channel_id=1, source_target_pairs={{0,4},{1,5},{2,6},{3,7},{4,0},{5,1},{6,2},{7,3},{8,12},{9,13},{10,... | collective-permute-start | bytes 589832 | tf_op jit(solution)/shard_map/ppermute | solution.py:33
  131.2 6.0 %collective-permute-start.27 = (f32[24,768]{1,0:T(8,128)S(1)}, f32[24,768]{1,0:T(8,128)S(1)}, u32[]{:S(2)}, u32[]{:S(2)}) collective-permute-start(f32[24,768]{1,0:T(8,128)S(1)} %add_add_fusion.2), channel_id=1, source_target_pairs={{0,65},{1,64},{2,67},{3,66},{4,69},{5,68},{6,71},{7,70},{64,1},{65... | collective-permute-start | bytes 221192 | tf_op jit(solution)/shard_map/ppermute | solution.py:51
  132.3 5.0 %collective-permute-start.26 = (f32[24,768]{1,0:T(8,128)S(1)}, f32[24,768]{1,0:T(8,128)S(1)}, u32[]{:S(2)}, u32[]{:S(2)}) collective-permute-start(f32[24,768]{1,0:T(8,128)S(1)} %add_add_fusion.2), channel_id=1, source_target_pairs={{0,64},{64,0},{1,65},{65,1},{2,66},{66,2},{3,67},{67,3},{4,68},{68... | collective-permute-start | bytes 221192 | tf_op jit(solution)/shard_map/ppermute | solution.py:49
  133.7 5.9 %collective-permute-start.25 = (f32[24,768]{1,0:T(8,128)S(1)}, f32[24,768]{1,0:T(8,128)S(1)}, u32[]{:S(2)}, u32[]{:S(2)}) collective-permute-start(f32[24,768]{1,0:T(8,128)S(1)} %add_add_fusion.2), channel_id=1, source_target_pairs={{0,1},{1,0},{2,3},{3,2},{4,5},{5,4},{6,7},{7,6},{8,9},{9,8},{10,11... | collective-permute-start | bytes 221192 | tf_op jit(solution)/shard_map/ppermute | solution.py:47
  137.2 6.9 %collective-permute-start.12 = (f32[64,768]{1,0:T(8,128)S(1)}, f32[64,768]{1,0:T(8,128)S(1)}, u32[]{:S(2)}, u32[]{:S(2)}) collective-permute-start(f32[64,768]{1,0:T(8,128)S(1)} %bitcast_select_fusion.2), channel_id=1, source_target_pairs={{0,2},{1,3},{2,4},{3,5},{4,6},{5,7},{6,0},{7,1},{8,10},{9,11},{10,... | collective-permute-start | bytes 589832 | tf_op jit(solution)/shard_map/ppermute | solution.py:33
  159.1 9.9 %collective-permute-start.28 = (f32[96,768]{1,0:T(8,128)S(1)}, f32[96,768]{1,0:T(8,128)S(1)}, u32[]{:S(2)}, u32[]{:S(2)}) collective-permute-start(f32[96,768]{1,0:T(8,128)S(1)} %bitcast_select_fusion), channel_id=1, source_target_pairs={{0,6},{1,7},{2,0},{3,1},{4,2},{5,3},{6,4},{7,5},{8,14},{9,15},{10,... | collective-permute-start | bytes 884744 | tf_op jit(solution)/shard_map/ppermute | solution.py:33
  160.0 11.5 %collective-permute-start.29 = (f32[96,768]{1,0:T(8,128)S(1)}, f32[96,768]{1,0:T(8,128)S(1)}, u32[]{:S(2)}, u32[]{:S(2)}) collective-permute-start(f32[96,768]{1,0:T(8,128)S(1)} %bitcast_select_fusion), channel_id=1, source_target_pairs={{0,4},{1,5},{2,6},{3,7},{4,0},{5,1},{6,2},{7,3},{8,12},{9,13},{10,... | collective-permute-start | bytes 884744 | tf_op jit(solution)/shard_map/ppermute | solution.py:33
  160.3 16.2 %collective-permute-start.30 = (f32[96,768]{1,0:T(8,128)S(1)}, f32[96,768]{1,0:T(8,128)S(1)}, u32[]{:S(2)}, u32[]{:S(2)}) collective-permute-start(f32[96,768]{1,0:T(8,128)S(1)} %bitcast_select_fusion), channel_id=1, source_target_pairs={{0,2},{1,3},{2,4},{3,5},{4,6},{5,7},{6,0},{7,1},{8,10},{9,11},{10,... | collective-permute-start | bytes 884744 | tf_op jit(solution)/shard_map/ppermute | solution.py:33
  161.2 5.3 %collective-permute-start.16 = (f32[4096]{0:T(1024)S(1)}, f32[4096]{0:T(1024)S(1)}, u32[]{:S(2)}, u32[]{:S(2)}) collective-permute-start(f32[4096]{0:T(1024)S(1)} %maximum_maximum_fusion.1), channel_id=1, source_target_pairs={{0,32},{8,40},{16,48},{24,56},{32,0},{40,8},{48,16},{56,24},{1,33}... | collective-permute-start | bytes 49160 | tf_op jit(solution)/shard_map/ppermute | solution.py:82
  166.5 25.9 %collective-permute-start.17 = (f32[4096]{0:T(1024)S(1)}, f32[4096]{0:T(1024)S(1)}, u32[]{:S(2)}, u32[]{:S(2)}) collective-permute-start(f32[4096]{0:T(1024)S(1)} %maximum_maximum_fusion), channel_id=1, source_target_pairs={{0,64},{64,0},{1,65},{65,1},{2,66},{66,2},{3,67},{67,3},{4,68},{68... | collective-permute-start | bytes 49160 | tf_op jit(solution)/shard_map/ppermute | solution.py:138
  187.6 5.4 %collective-permute-start.33 = (f32[384]{0:T(512)S(1)}, f32[384]{0:T(512)S(1)}, u32[]{:S(2)}, u32[]{:S(2)}) collective-permute-start(f32[384]{0:T(512)S(1)} %maximum_reduce_fusion), channel_id=1, source_target_pairs={{0,65},{1,64},{2,67},{3,66},{4,69},{5,68},{6,71},{7,70},{64,1},{65... | collective-permute-start | bytes 4616 | tf_op jit(solution)/shard_map/ppermute | solution.py:51
  188.5 4.5 %collective-permute-start.32 = (f32[384]{0:T(512)S(1)}, f32[384]{0:T(512)S(1)}, u32[]{:S(2)}, u32[]{:S(2)}) collective-permute-start(f32[384]{0:T(512)S(1)} %maximum_reduce_fusion), channel_id=1, source_target_pairs={{0,64},{64,0},{1,65},{65,1},{2,66},{66,2},{3,67},{67,3},{4,68},{68... | collective-permute-start | bytes 4616 | tf_op jit(solution)/shard_map/ppermute | solution.py:49
  188.5 5.5 %collective-permute-start.31 = (f32[384]{0:T(512)S(1)}, f32[384]{0:T(512)S(1)}, u32[]{:S(2)}, u32[]{:S(2)}) collective-permute-start(f32[384]{0:T(512)S(1)} %maximum_reduce_fusion), channel_id=1, source_target_pairs={{0,1},{1,0},{2,3},{3,2},{4,5},{5,4},{6,7},{7,6},{8,9},{9,8},{10,11... | collective-permute-start | bytes 4616 | tf_op jit(solution)/shard_map/ppermute | solution.py:47
  194.6 4.9 %collective-permute-start.36 = (f32[4,384]{1,0:T(4,128)S(1)}, f32[4,384]{1,0:T(4,128)S(1)}, u32[]{:S(2)}, u32[]{:S(2)}) collective-permute-start(f32[4,384]{1,0:T(4,128)S(1)} %broadcast_select_fusion), channel_id=1, source_target_pairs={{0,6},{1,7},{2,4},{3,5},{4,2},{5,3},{6,0},{7,1},{8,14},{9,15},{10,... | collective-permute-start | bytes 18440 | tf_op jit(solution)/shard_map/ppermute | solution.py:95
  195.3 5.1 %collective-permute-start.35 = (f32[4,384]{1,0:T(4,128)S(1)}, f32[4,384]{1,0:T(4,128)S(1)}, u32[]{:S(2)}, u32[]{:S(2)}) collective-permute-start(f32[4,384]{1,0:T(4,128)S(1)} %broadcast_select_fusion), channel_id=1, source_target_pairs={{0,4},{1,5},{2,6},{3,7},{4,0},{5,1},{6,2},{7,3},{8,12},{9,13},{10,... | collective-permute-start | bytes 18440 | tf_op jit(solution)/shard_map/ppermute | solution.py:95
  195.5 5.0 %collective-permute-start.34 = (f32[4,384]{1,0:T(4,128)S(1)}, f32[4,384]{1,0:T(4,128)S(1)}, u32[]{:S(2)}, u32[]{:S(2)}) collective-permute-start(f32[4,384]{1,0:T(4,128)S(1)} %broadcast_select_fusion), channel_id=1, source_target_pairs={{0,2},{1,3},{2,0},{3,1},{4,6},{5,7},{6,4},{7,5},{8,10},{9,11},{10,... | collective-permute-start | bytes 18440 | tf_op jit(solution)/shard_map/ppermute | solution.py:95
  (9 other events, 37.3 us)
Sparse Core Ops, SparseCore 0:
  9.7 69.7 all-gather.1

commit v19 on v18

--- a/solution.py
+++ b/solution.py
@@ -124,8 +124,9 @@
     zl_swap = [(0, 1), (1, 0)]
     both_sel = pair_join(sel_index, lax.ppermute(sel_index, "zl", zl_swap), zl == 0)
     both_cand = pair_join(cand_index, lax.ppermute(cand_index, "zl", zl_swap), zl == 0)
-    selected = group_masked_sum(lookup(half, both_sel, first_row))
-    chosen = group_masked_sum(lookup(half, both_cand, first_row))
+    cand_rows, sel_source = lax.optimization_barrier((lookup(half, both_cand, first_row), half))
+    chosen = group_masked_sum(cand_rows)
+    selected = group_masked_sum(lookup(sel_source, both_sel, first_row))
     n_sel = both_sel.shape[0]
     sel_scores = lax.optimization_barrier(similar(selected, half))
     reached = all_max_two_rounds(jnp.max(sel_scores, axis=0), "xc", n_xc)

time: 209 us -> 215 us (1.029)
  starting transfers between devices: 44.7 us -> 50.7 us
    ppermute x12, starting transfers between devices: 10.1 us -> 17.9 us  [y_shift(): return lax.ppermute(value, 'col', pairs)]
    ppermute x5, starting transfers between devices: 14 us -> 7.05 us  [z_group_shift(): return lax.ppermute(value, 'col', [(c, c ^ 1) for c in range(N_Y * N_Z)])]
    ppermute x5, waiting for transfers between devices: 1.13 us -> 5.69 us  [z_group_shift(): lax.ppermute(value, ('zl', 'col'), [(i, i ^ N_Y * N_Z ^ 1) for i in range...]
    ppermute x5, waiting for transfers between devices: 5.99 us -> 2.05 us  [z_group_shift(): return lax.ppermute(value, 'col', [(c, c ^ 1) for c in range(N_Y * N_Z)])]
    ppermute x5, starting transfers between devices: 1.91 us -> 5.56 us  [z_group_shift(): return lax.ppermute(value, 'zl', [(0, 1), (1, 0)])]
  transfers between devices with their start and end apart: 38 -> 38, of which waited for: 21 -> 18; matrix products, arithmetic and copies ran while one was open for 10% -> 7% of each run, Pallas kernels for 0% -> 0%
where the time goes in v19:
time: 215 us
  waiting for transfers between devices  107 us (50%)
  starting transfers between devices  50.7 us (24%)
  matrix products  21.1 us (10%)
  local copies, waits for them, and re-layouts  16.8 us (8%)
  between operations  14.5 us (7%)
  other arithmetic  4.59 us (2%)
    all_gather x1, waiting for transfers between devices, body(): half = lax.all_gather(slab_embed, 'xc', axis=0, tiled=True)  65.7 us
    ppermute x12, waiting for transfers between devices, y_shift(): return lax.ppermute(value, 'col', pairs)  21.8 us
    dot_general x2, matrix products, similar(): lax.dot_general(left, right, (((1,), (1,)), ((), ())), precision=lax.Prec...  21.1 us
    ppermute x12, starting transfers between devices, y_shift(): return lax.ppermute(value, 'col', pairs)  17.9 us
    gather x2, local copies, waits for them, and re-layouts, lookup(): jnp.take(source, jnp.clip(position, 0, source.shape[0] - 1), axis=0)  13 us
    ppermute x5, starting transfers between devices, z_group_shift(): lax.ppermute(value, ('zl', 'col'), [(i, i ^ N_Y * N_Z ^ 1) for i in range...  8.39 us
    ppermute x5, starting transfers between devices, z_group_shift(): return lax.ppermute(value, 'col', [(c, c ^ 1) for c in range(N_Y * N_Z)])  7.05 us
    ppermute x5, waiting for transfers between devices, z_group_shift(): lax.ppermute(value, ('zl', 'col'), [(i, i ^ N_Y * N_Z ^ 1) for i in range...  5.69 us
  transfers between devices with their start and end apart: 38, of which 18 were waited for; matrix products, arithmetic and copies ran while one was open for 7% of the time, Pallas kernels for 0%

profile of v19, /device:TPU:0, one launch (start us, length us, event | category | flops | bytes accessed | tf_op | source)
XLA Modules:
  0.0 214.9 jit_solution(3422190559726917207)
XLA Ops:
  7.9 2.1 collective-permute-start.1
  10.2 3.4 %collective-permute-done = s32[128]{0:T(128)S(1)} collective-permute-done((s32[128]{0:T(128)S(1)}, s32[128]{0:T(128)S(1)}, u32[]{:S(2)}, u32[]{:S(2)}) %collective-permute-start) | collective-permute-done | bytes 544 | tf_op jit(solution)/shard_map/ppermute | solution.py:125
  13.8 65.7 %all-gather.2.cloned.1.call-done = f32[4096,768]{1,0:T(8,128)} async-done(((f32[512,768]{1,0:T(8,128)}), f32[4096,768]{1,0:T(8,128)}) %all-gather.2.cloned.1.call-update) | async-done | bytes 12582928 | tf_op jit(solution)/shard_map/all_gather | solution.py:122
  79.5 7.1 %gather_fusion = f32[384,768]{1,0:T(8,128)S(1)} fusion(f32[4096,768]{1,0:T(8,128)} %all-gather.2.cloned.1.call-done, s32[1024]{0:T(1024)S(1)} %pad_clamp_fusion.3), kind=kCustom, calls=%fused_computation | custom fusion | bytes 2360832 | tf_op jit(solution)/shard_map/jit(_take)/gather | solution.py:23
  86.8 6.0 %gather_fusion.1 = f32[256,768]{1,0:T(8,128)S(1)} fusion(f32[4096,768]{1,0:T(8,128)} %all-gather.2.cloned.1.call-done, s32[1024]{0:T(1024)S(1)} %pad_clamp_fusion.2), kind=kCustom, calls=%fused_computation.1 | custom fusion | bytes 1573888 | tf_op jit(solution)/shard_map/jit(_take)/gather | solution.py:23
  93.0 1.6 collective-permute-start.2
  94.5 2.7 %collective-permute-start.3 = (f32[64,768]{1,0:T(8,128)S(1)}, f32[64,768]{1,0:T(8,128)S(1)}, u32[]{:S(2)}, u32[]{:S(2)}) collective-permute-start(f32[64,768]{1,0:T(8,128)S(1)} %get-tuple-element.13), channel_id=1, source_target_pairs={{0,4},{1,5},{2,6},{3,7},{4,0},{5,1},{6,2},{7,3},{8,12},{9,13},{10,... | collective-permute-start | bytes 589832 | tf_op jit(solution)/shard_map/ppermute | solution.py:33
  98.7 2.6 %collective-permute-done.2 = f32[64,768]{1,0:T(8,128)S(1)} collective-permute-done((f32[64,768]{1,0:T(8,128)S(1)}, f32[64,768]{1,0:T(8,128)S(1)}, u32[]{:S(2)}, u32[]{:S(2)}) %collective-permute-start.2) | collective-permute-done | bytes 196640 | tf_op jit(solution)/shard_map/ppermute | solution.py:33
  101.3 5.2 %collective-permute-done.3 = f32[64,768]{1,0:T(8,128)S(1)} collective-permute-done((f32[64,768]{1,0:T(8,128)S(1)}, f32[64,768]{1,0:T(8,128)S(1)}, u32[]{:S(2)}, u32[]{:S(2)}) %collective-permute-start.3) | collective-permute-done | bytes 196640 | tf_op jit(solution)/shard_map/ppermute | solution.py:33
  106.6 3.2 %collective-permute-start.5 = (f32[16,768]{1,0:T(8,128)S(1)}, f32[16,768]{1,0:T(8,128)S(1)}, u32[]{:S(2)}, u32[]{:S(2)}) collective-permute-start(f32[16,768]{1,0:T(8,128)S(1)} %get-tuple-element.17), channel_id=1, source_target_pairs={{0,1},{1,0},{2,3},{3,2},{4,5},{5,4},{6,7},{7,6},{8,9},{9,8},{10,11... | collective-permute-start | bytes 147464 | tf_op jit(solution)/shard_map/ppermute | solution.py:47
  111.3 2.4 %collective-permute-start.20 = (f32[96,768]{1,0:T(8,128)S(1)}, f32[96,768]{1,0:T(8,128)S(1)}, u32[]{:S(2)}, u32[]{:S(2)}) collective-permute-start(f32[96,768]{1,0:T(8,128)S(1)} %get-tuple-element.10), channel_id=1, source_target_pairs={{0,4},{1,5},{2,6},{3,7},{4,0},{5,1},{6,2},{7,3},{8,12},{9,13},{10,... | collective-permute-start | bytes 884744 | tf_op jit(solution)/shard_map/ppermute | solution.py:33
  113.7 1.6 collective-permute-start.21
  116.7 2.7 %collective-permute-done.6 = f32[16,768]{1,0:T(8,128)S(1)} collective-permute-done((f32[16,768]{1,0:T(8,128)S(1)}, f32[16,768]{1,0:T(8,128)S(1)}, u32[]{:S(2)}, u32[]{:S(2)}) %collective-permute-start.6) | collective-permute-done | bytes 49184 | tf_op jit(solution)/shard_map/ppermute | solution.py:49
  119.3 1.9 collective-permute-done.7
  122.6 2.8 %collective-permute-start.10 = (f32[16,768]{1,0:T(8,128)S(1)}, f32[16,768]{1,0:T(8,128)S(1)}, u32[]{:S(2)}, u32[]{:S(2)}) collective-permute-start(f32[16,768]{1,0:T(8,128)S(1)} %add_add_fusion.3), channel_id=1, source_target_pairs={{0,65},{1,64},{2,67},{3,66},{4,69},{5,68},{6,71},{7,70},{64,1},{65... | collective-permute-start | bytes 147464 | tf_op jit(solution)/shard_map/ppermute | solution.py:51
  128.8 2.2 %collective-permute-start.24 = (f32[24,768]{1,0:T(8,128)S(1)}, f32[24,768]{1,0:T(8,128)S(1)}, u32[]{:S(2)}, u32[]{:S(2)}) collective-permute-start(f32[24,768]{1,0:T(8,128)S(1)} %get-tuple-element.15), channel_id=1, source_target_pairs={{0,65},{1,64},{2,67},{3,66},{4,69},{5,68},{6,71},{7,70},{64,1},{65... | collective-permute-start | bytes 221192 | tf_op jit(solution)/shard_map/ppermute | solution.py:51
  131.6 2.2 %collective-permute-start.11 = (f32[64,768]{1,0:T(8,128)S(1)}, f32[64,768]{1,0:T(8,128)S(1)}, u32[]{:S(2)}, u32[]{:S(2)}) collective-permute-start(f32[64,768]{1,0:T(8,128)S(1)} %bitcast_select_fusion.2), channel_id=1, source_target_pairs={{0,6},{1,7},{2,0},{3,1},{4,2},{5,3},{6,4},{7,5},{8,14},{9,15},{10,... | collective-permute-start | bytes 589832 | tf_op jit(solution)/shard_map/ppermute | solution.py:33
  137.4 1.8 collective-permute-start.27
  139.3 1.7 collective-permute-done.25
  143.7 4.2 %collective-permute-done.13 = f32[64,768]{1,0:T(8,128)S(1)} collective-permute-done((f32[64,768]{1,0:T(8,128)S(1)}, f32[64,768]{1,0:T(8,128)S(1)}, u32[]{:S(2)}, u32[]{:S(2)}) %collective-permute-start.13) | collective-permute-done | bytes 196640 | tf_op jit(solution)/shard_map/ppermute | solution.py:33
  148.1 10.2 %fusion.14 = f32[256,4096]{1,0:T(8,128)} fusion(f32[256,768]{1,0:T(8,128)S(1)} %bitcast.68, f32[4096,768]{1,0:T(8,128)} %all-gather.2.cloned.1.call-done), kind=kOutput, calls=%fused_computation.88 | convolution fusion | flops 4831838208 | bytes 17563648 | tf_op jit(solution)/shard_map/dot_general | solution.py:11
  158.4 2.4 %reduce_max.9 = f32[4096]{0:T(1024)S(1)} reduce(f32[256,4096]{1,0:T(8,128)} %fusion.14, f32[]{:T(128)} %constant.196.clone.1), dimensions={0}, to_apply=%region_0.1 | reduce | flops 1044480 | bytes 4210692 | tf_op jit(solution)/shard_map/reduce_max | solution.py:132
  165.5 2.2 %collective-permute-start.17 = (f32[4096]{0:T(1024)S(1)}, f32[4096]{0:T(1024)S(1)}, u32[]{:S(2)}, u32[]{:S(2)}) collective-permute-start(f32[4096]{0:T(1024)S(1)} %maximum_maximum_fusion.1), channel_id=1, source_target_pairs={{0,32},{8,40},{16,48},{24,56},{32,0},{40,8},{48,16},{56,24},{1,33}... | collective-permute-start | bytes 49160 | tf_op jit(solution)/shard_map/ppermute | solution.py:82
  167.8 3.0 %collective-permute-done.17 = f32[4096]{0:T(1024)S(1)} collective-permute-done((f32[4096]{0:T(1024)S(1)}, f32[4096]{0:T(1024)S(1)}, u32[]{:S(2)}, u32[]{:S(2)}) %collective-permute-start.17) | collective-permute-done | bytes 16416 | tf_op jit(solution)/shard_map/ppermute | solution.py:82
  172.7 2.1 collective-permute-done.29
  174.9 5.4 %collective-permute-done.30 = f32[96,768]{1,0:T(8,128)S(1)} collective-permute-done((f32[96,768]{1,0:T(8,128)S(1)}, f32[96,768]{1,0:T(8,128)S(1)}, u32[]{:S(2)}, u32[]{:S(2)}) %collective-permute-start.30) | collective-permute-done | bytes 294944 | tf_op jit(solution)/shard_map/ppermute | solution.py:33
  180.5 10.8 %maximum_reduce_fusion = f32[384]{0:T(512)S(1)} fusion(f32[384,768]{1,0:T(8,128)S(1)} %bitcast.71, f32[4096,768]{1,0:T(8,128)} %all-gather.2.cloned.1.call-done, f32[4096]{0:T(1024)S(1)} %maximum_maximum_fusion), kind=kOutput, calls=%fused_computation.6 | convolution fusion | flops 7252475392 | bytes 13780480 | tf_op jit(solution)/shard_map/dot_general | solution.py:11
  191.4 1.6 collective-permute-start.31
  196.6 2.6 %collective-permute-done.33 = f32[384]{0:T(512)S(1)} collective-permute-done((f32[384]{0:T(512)S(1)}, f32[384]{0:T(512)S(1)}, u32[]{:S(2)}, u32[]{:S(2)}) %collective-permute-start.33) | collective-permute-done | bytes 1568 | tf_op jit(solution)/shard_map/ppermute | solution.py:51
  199.8 2.1 collective-permute-start.35
  201.9 2.6 %collective-permute-start.36 = (f32[4,384]{1,0:T(4,128)S(1)}, f32[4,384]{1,0:T(4,128)S(1)}, u32[]{:S(2)}, u32[]{:S(2)}) collective-permute-start(f32[4,384]{1,0:T(4,128)S(1)} %broadcast_select_fusion), channel_id=1, source_target_pairs={{0,6},{1,7},{2,4},{3,5},{4,2},{5,3},{6,0},{7,1},{8,14},{9,15},{10,... | collective-permute-start | bytes 18440 | tf_op jit(solution)/shard_map/ppermute | solution.py:95
  205.0 1.7 collective-permute-done.36
  (121 shorter events, 30.9 us)
Async XLA Ops:
  7.2 72.3 %all-gather.2.cloned.1.call-start = ((), (), s32[]{:S(2)}) async-start(), calls=%async_computation | async-start | bytes 14155776 | tf_op jit(solution)/shard_map/all_gather | solution.py:122
  7.9 5.7 %collective-permute-start.1 = (s32[192]{0:T(256)S(1)}, s32[192]{0:T(256)S(1)}, u32[]{:S(2)}, u32[]{:S(2)}) collective-permute-start(s32[192]{0:T(256)S(1)} %copy-done.1), channel_id=1, source_target_pairs={{0,64},{64,0},{1,65},{65,1},{2,66},{66,2},{3,67},{67,3},{4,68},{68... | collective-permute-start | bytes 2312 | tf_op jit(solution)/shard_map/ppermute | solution.py:126
  93.0 8.3 %collective-permute-start.2 = (f32[64,768]{1,0:T(8,128)S(1)}, f32[64,768]{1,0:T(8,128)S(1)}, u32[]{:S(2)}, u32[]{:S(2)}) collective-permute-start(f32[64,768]{1,0:T(8,128)S(1)} %get-tuple-element.11), channel_id=1, source_target_pairs={{0,2},{1,3},{2,4},{3,5},{4,6},{5,7},{6,0},{7,1},{8,10},{9,11},{10,... | collective-permute-start | bytes 589832 | tf_op jit(solution)/shard_map/ppermute | solution.py:33
  94.5 12.0 %collective-permute-start.3 = (f32[64,768]{1,0:T(8,128)S(1)}, f32[64,768]{1,0:T(8,128)S(1)}, u32[]{:S(2)}, u32[]{:S(2)}) collective-permute-start(f32[64,768]{1,0:T(8,128)S(1)} %get-tuple-element.13), channel_id=1, source_target_pairs={{0,4},{1,5},{2,6},{3,7},{4,0},{5,1},{6,2},{7,3},{8,12},{9,13},{10,... | collective-permute-start | bytes 589832 | tf_op jit(solution)/shard_map/ppermute | solution.py:33
  97.3 9.3 %collective-permute-start.4 = (f32[64,768]{1,0:T(8,128)S(1)}, f32[64,768]{1,0:T(8,128)S(1)}, u32[]{:S(2)}, u32[]{:S(2)}) collective-permute-start(f32[64,768]{1,0:T(8,128)S(1)} %get-tuple-element.12), channel_id=1, source_target_pairs={{0,6},{1,7},{2,0},{3,1},{4,2},{5,3},{6,4},{7,5},{8,14},{9,15},{10,... | collective-permute-start | bytes 589832 | tf_op jit(solution)/shard_map/ppermute | solution.py:33
  106.6 9.3 %collective-permute-start.5 = (f32[16,768]{1,0:T(8,128)S(1)}, f32[16,768]{1,0:T(8,128)S(1)}, u32[]{:S(2)}, u32[]{:S(2)}) collective-permute-start(f32[16,768]{1,0:T(8,128)S(1)} %get-tuple-element.17), channel_id=1, source_target_pairs={{0,1},{1,0},{2,3},{3,2},{4,5},{5,4},{6,7},{7,6},{8,9},{9,8},{10,11... | collective-permute-start | bytes 147464 | tf_op jit(solution)/shard_map/ppermute | solution.py:47
  109.9 12.7 %collective-permute-start.19 = (f32[96,768]{1,0:T(8,128)S(1)}, f32[96,768]{1,0:T(8,128)S(1)}, u32[]{:S(2)}, u32[]{:S(2)}) collective-permute-start(f32[96,768]{1,0:T(8,128)S(1)} %get-tuple-element.8), channel_id=1, source_target_pairs={{0,2},{1,3},{2,4},{3,5},{4,6},{5,7},{6,0},{7,1},{8,10},{9,11},{10,... | collective-permute-start | bytes 884744 | tf_op jit(solution)/shard_map/ppermute | solution.py:33
  111.3 15.3 %collective-permute-start.20 = (f32[96,768]{1,0:T(8,128)S(1)}, f32[96,768]{1,0:T(8,128)S(1)}, u32[]{:S(2)}, u32[]{:S(2)}) collective-permute-start(f32[96,768]{1,0:T(8,128)S(1)} %get-tuple-element.10), channel_id=1, source_target_pairs={{0,4},{1,5},{2,6},{3,7},{4,0},{5,1},{6,2},{7,3},{8,12},{9,13},{10,... | collective-permute-start | bytes 884744 | tf_op jit(solution)/shard_map/ppermute | solution.py:33
  113.7 12.9 %collective-permute-start.21 = (f32[96,768]{1,0:T(8,128)S(1)}, f32[96,768]{1,0:T(8,128)S(1)}, u32[]{:S(2)}, u32[]{:S(2)}) collective-permute-start(f32[96,768]{1,0:T(8,128)S(1)} %get-tuple-element.9), channel_id=1, source_target_pairs={{0,6},{1,7},{2,0},{3,1},{4,2},{5,3},{6,4},{7,5},{8,14},{9,15},{10,... | collective-permute-start | bytes 884744 | tf_op jit(solution)/shard_map/ppermute | solution.py:33
  115.9 5.3 %collective-permute-start.7 = (f32[16,768]{1,0:T(8,128)S(1)}, f32[16,768]{1,0:T(8,128)S(1)}, u32[]{:S(2)}, u32[]{:S(2)}) collective-permute-start(f32[16,768]{1,0:T(8,128)S(1)} %get-tuple-element.18), channel_id=1, source_target_pairs={{0,65},{1,64},{2,67},{3,66},{4,69},{5,68},{6,71},{7,70},{64,1},{65... | collective-permute-start | bytes 147464 | tf_op jit(solution)/shard_map/ppermute | solution.py:51
  121.2 7.5 %collective-permute-start.8 = (f32[16,768]{1,0:T(8,128)S(1)}, f32[16,768]{1,0:T(8,128)S(1)}, u32[]{:S(2)}, u32[]{:S(2)}) collective-permute-start(f32[16,768]{1,0:T(8,128)S(1)} %add_add_fusion.3), channel_id=1, source_target_pairs={{0,1},{1,0},{2,3},{3,2},{4,5},{5,4},{6,7},{7,6},{8,9},{9,8},{10,11... | collective-permute-start | bytes 147464 | tf_op jit(solution)/shard_map/ppermute | solution.py:47
  122.0 8.9 %collective-permute-start.9 = (f32[16,768]{1,0:T(8,128)S(1)}, f32[16,768]{1,0:T(8,128)S(1)}, u32[]{:S(2)}, u32[]{:S(2)}) collective-permute-start(f32[16,768]{1,0:T(8,128)S(1)} %add_add_fusion.3), channel_id=1, source_target_pairs={{0,64},{64,0},{1,65},{65,1},{2,66},{66,2},{3,67},{67,3},{4,68},{68... | collective-permute-start | bytes 147464 | tf_op jit(solution)/shard_map/ppermute | solution.py:49
  122.6 8.3 %collective-permute-start.10 = (f32[16,768]{1,0:T(8,128)S(1)}, f32[16,768]{1,0:T(8,128)S(1)}, u32[]{:S(2)}, u32[]{:S(2)}) collective-permute-start(f32[16,768]{1,0:T(8,128)S(1)} %add_add_fusion.3), channel_id=1, source_target_pairs={{0,65},{1,64},{2,67},{3,66},{4,69},{5,68},{6,71},{7,70},{64,1},{65... | collective-permute-start | bytes 147464 | tf_op jit(solution)/shard_map/ppermute | solution.py:51
  126.7 8.2 %collective-permute-start.22 = (f32[24,768]{1,0:T(8,128)S(1)}, f32[24,768]{1,0:T(8,128)S(1)}, u32[]{:S(2)}, u32[]{:S(2)}) collective-permute-start(f32[24,768]{1,0:T(8,128)S(1)} %get-tuple-element.14), channel_id=1, source_target_pairs={{0,1},{1,0},{2,3},{3,2},{4,5},{5,4},{6,7},{7,6},{8,9},{9,8},{10,11... | collective-permute-start | bytes 221192 | tf_op jit(solution)/shard_map/ppermute | solution.py:47
  127.2 7.8 %collective-permute-start.23 = (f32[24,768]{1,0:T(8,128)S(1)}, f32[24,768]{1,0:T(8,128)S(1)}, u32[]{:S(2)}, u32[]{:S(2)}) collective-permute-start(f32[24,768]{1,0:T(8,128)S(1)} %get-tuple-element.16), channel_id=1, source_target_pairs={{0,64},{64,0},{1,65},{65,1},{2,66},{66,2},{3,67},{67,3},{4,68},{68... | collective-permute-start | bytes 221192 | tf_op jit(solution)/shard_map/ppermute | solution.py:49
  128.8 6.2 %collective-permute-start.24 = (f32[24,768]{1,0:T(8,128)S(1)}, f32[24,768]{1,0:T(8,128)S(1)}, u32[]{:S(2)}, u32[]{:S(2)}) collective-permute-start(f32[24,768]{1,0:T(8,128)S(1)} %get-tuple-element.15), channel_id=1, source_target_pairs={{0,65},{1,64},{2,67},{3,66},{4,69},{5,68},{6,71},{7,70},{64,1},{65... | collective-permute-start | bytes 221192 | tf_op jit(solution)/shard_map/ppermute | solution.py:51
  131.6 12.0 %collective-permute-start.11 = (f32[64,768]{1,0:T(8,128)S(1)}, f32[64,768]{1,0:T(8,128)S(1)}, u32[]{:S(2)}, u32[]{:S(2)}) collective-permute-start(f32[64,768]{1,0:T(8,128)S(1)} %bitcast_select_fusion.2), channel_id=1, source_target_pairs={{0,6},{1,7},{2,0},{3,1},{4,2},{5,3},{6,4},{7,5},{8,14},{9,15},{10,... | collective-permute-start | bytes 589832 | tf_op jit(solution)/shard_map/ppermute | solution.py:33
  133.9 9.8 %collective-permute-start.12 = (f32[64,768]{1,0:T(8,128)S(1)}, f32[64,768]{1,0:T(8,128)S(1)}, u32[]{:S(2)}, u32[]{:S(2)}) collective-permute-start(f32[64,768]{1,0:T(8,128)S(1)} %bitcast_select_fusion.2), channel_id=1, source_target_pairs={{0,4},{1,5},{2,6},{3,7},{4,0},{5,1},{6,2},{7,3},{8,12},{9,13},{10,... | collective-permute-start | bytes 589832 | tf_op jit(solution)/shard_map/ppermute | solution.py:33
  135.0 5.9 %collective-permute-start.25 = (f32[24,768]{1,0:T(8,128)S(1)}, f32[24,768]{1,0:T(8,128)S(1)}, u32[]{:S(2)}, u32[]{:S(2)}) collective-permute-start(f32[24,768]{1,0:T(8,128)S(1)} %add_add_fusion.2), channel_id=1, source_target_pairs={{0,1},{1,0},{2,3},{3,2},{4,5},{5,4},{6,7},{7,6},{8,9},{9,8},{10,11... | collective-permute-start | bytes 221192 | tf_op jit(solution)/shard_map/ppermute | solution.py:47
  136.1 5.7 %collective-permute-start.26 = (f32[24,768]{1,0:T(8,128)S(1)}, f32[24,768]{1,0:T(8,128)S(1)}, u32[]{:S(2)}, u32[]{:S(2)}) collective-permute-start(f32[24,768]{1,0:T(8,128)S(1)} %add_add_fusion.2), channel_id=1, source_target_pairs={{0,64},{64,0},{1,65},{65,1},{2,66},{66,2},{3,67},{67,3},{4,68},{68... | collective-permute-start | bytes 221192 | tf_op jit(solution)/shard_map/ppermute | solution.py:49
  137.4 5.6 %collective-permute-start.27 = (f32[24,768]{1,0:T(8,128)S(1)}, f32[24,768]{1,0:T(8,128)S(1)}, u32[]{:S(2)}, u32[]{:S(2)}) collective-permute-start(f32[24,768]{1,0:T(8,128)S(1)} %add_add_fusion.2), channel_id=1, source_target_pairs={{0,65},{1,64},{2,67},{3,66},{4,69},{5,68},{6,71},{7,70},{64,1},{65... | collective-permute-start | bytes 221192 | tf_op jit(solution)/shard_map/ppermute | solution.py:51
  141.0 6.9 %collective-permute-start.13 = (f32[64,768]{1,0:T(8,128)S(1)}, f32[64,768]{1,0:T(8,128)S(1)}, u32[]{:S(2)}, u32[]{:S(2)}) collective-permute-start(f32[64,768]{1,0:T(8,128)S(1)} %bitcast_select_fusion.2), channel_id=1, source_target_pairs={{0,2},{1,3},{2,4},{3,5},{4,6},{5,7},{6,0},{7,1},{8,10},{9,11},{10,... | collective-permute-start | bytes 589832 | tf_op jit(solution)/shard_map/ppermute | solution.py:33
  162.8 9.9 %collective-permute-start.28 = (f32[96,768]{1,0:T(8,128)S(1)}, f32[96,768]{1,0:T(8,128)S(1)}, u32[]{:S(2)}, u32[]{:S(2)}) collective-permute-start(f32[96,768]{1,0:T(8,128)S(1)} %bitcast_select_fusion), channel_id=1, source_target_pairs={{0,6},{1,7},{2,0},{3,1},{4,2},{5,3},{6,4},{7,5},{8,14},{9,15},{10,... | collective-permute-start | bytes 884744 | tf_op jit(solution)/shard_map/ppermute | solution.py:33
  163.4 11.4 %collective-permute-start.29 = (f32[96,768]{1,0:T(8,128)S(1)}, f32[96,768]{1,0:T(8,128)S(1)}, u32[]{:S(2)}, u32[]{:S(2)}) collective-permute-start(f32[96,768]{1,0:T(8,128)S(1)} %bitcast_select_fusion), channel_id=1, source_target_pairs={{0,4},{1,5},{2,6},{3,7},{4,0},{5,1},{6,2},{7,3},{8,12},{9,13},{10,... | collective-permute-start | bytes 884744 | tf_op jit(solution)/shard_map/ppermute | solution.py:33
  164.5 15.7 %collective-permute-start.30 = (f32[96,768]{1,0:T(8,128)S(1)}, f32[96,768]{1,0:T(8,128)S(1)}, u32[]{:S(2)}, u32[]{:S(2)}) collective-permute-start(f32[96,768]{1,0:T(8,128)S(1)} %bitcast_select_fusion), channel_id=1, source_target_pairs={{0,2},{1,3},{2,4},{3,5},{4,6},{5,7},{6,0},{7,1},{8,10},{9,11},{10,... | collective-permute-start | bytes 884744 | tf_op jit(solution)/shard_map/ppermute | solution.py:33
  165.5 5.3 %collective-permute-start.17 = (f32[4096]{0:T(1024)S(1)}, f32[4096]{0:T(1024)S(1)}, u32[]{:S(2)}, u32[]{:S(2)}) collective-permute-start(f32[4096]{0:T(1024)S(1)} %maximum_maximum_fusion.1), channel_id=1, source_target_pairs={{0,32},{8,40},{16,48},{24,56},{32,0},{40,8},{48,16},{56,24},{1,33}... | collective-permute-start | bytes 49160 | tf_op jit(solution)/shard_map/ppermute | solution.py:82
  170.8 24.7 %collective-permute-start.18 = (f32[4096]{0:T(1024)S(1)}, f32[4096]{0:T(1024)S(1)}, u32[]{:S(2)}, u32[]{:S(2)}) collective-permute-start(f32[4096]{0:T(1024)S(1)} %maximum_maximum_fusion), channel_id=1, source_target_pairs={{0,64},{64,0},{1,65},{65,1},{2,66},{66,2},{3,67},{67,3},{4,68},{68... | collective-permute-start | bytes 49160 | tf_op jit(solution)/shard_map/ppermute | solution.py:139
  191.4 5.2 %collective-permute-start.31 = (f32[384]{0:T(512)S(1)}, f32[384]{0:T(512)S(1)}, u32[]{:S(2)}, u32[]{:S(2)}) collective-permute-start(f32[384]{0:T(512)S(1)} %maximum_reduce_fusion), channel_id=1, source_target_pairs={{0,1},{1,0},{2,3},{3,2},{4,5},{5,4},{6,7},{7,6},{8,9},{9,8},{10,11... | collective-permute-start | bytes 4616 | tf_op jit(solution)/shard_map/ppermute | solution.py:47
  194.3 4.8 %collective-permute-start.33 = (f32[384]{0:T(512)S(1)}, f32[384]{0:T(512)S(1)}, u32[]{:S(2)}, u32[]{:S(2)}) collective-permute-start(f32[384]{0:T(512)S(1)} %maximum_reduce_fusion), channel_id=1, source_target_pairs={{0,65},{1,64},{2,67},{3,66},{4,69},{5,68},{6,71},{7,70},{64,1},{65... | collective-permute-start | bytes 4616 | tf_op jit(solution)/shard_map/ppermute | solution.py:51
  199.8 4.8 %collective-permute-start.34 = (f32[4,384]{1,0:T(4,128)S(1)}, f32[4,384]{1,0:T(4,128)S(1)}, u32[]{:S(2)}, u32[]{:S(2)}) collective-permute-start(f32[4,384]{1,0:T(4,128)S(1)} %broadcast_select_fusion), channel_id=1, source_target_pairs={{0,2},{1,3},{2,0},{3,1},{4,6},{5,7},{6,4},{7,5},{8,10},{9,11},{10,... | collective-permute-start | bytes 18440 | tf_op jit(solution)/shard_map/ppermute | solution.py:95
  199.8 5.2 %collective-permute-start.35 = (f32[4,384]{1,0:T(4,128)S(1)}, f32[4,384]{1,0:T(4,128)S(1)}, u32[]{:S(2)}, u32[]{:S(2)}) collective-permute-start(f32[4,384]{1,0:T(4,128)S(1)} %broadcast_select_fusion), channel_id=1, source_target_pairs={{0,4},{1,5},{2,6},{3,7},{4,0},{5,1},{6,2},{7,3},{8,12},{9,13},{10,... | collective-permute-start | bytes 18440 | tf_op jit(solution)/shard_map/ppermute | solution.py:95
  201.9 4.8 %collective-permute-start.36 = (f32[4,384]{1,0:T(4,128)S(1)}, f32[4,384]{1,0:T(4,128)S(1)}, u32[]{:S(2)}, u32[]{:S(2)}) collective-permute-start(f32[4,384]{1,0:T(4,128)S(1)} %broadcast_select_fusion), channel_id=1, source_target_pairs={{0,6},{1,7},{2,4},{3,5},{4,2},{5,3},{6,0},{7,1},{8,14},{9,15},{10,... | collective-permute-start | bytes 18440 | tf_op jit(solution)/shard_map/ppermute | solution.py:95
  (9 other events, 39.4 us)
Sparse Core Ops, SparseCore 0:
  9.7 69.7 all-gather.1

commit v20 on v18

--- a/solution.py
+++ b/solution.py
@@ -125,7 +125,9 @@
     both_sel = pair_join(sel_index, lax.ppermute(sel_index, "zl", zl_swap), zl == 0)
     both_cand = pair_join(cand_index, lax.ppermute(cand_index, "zl", zl_swap), zl == 0)
     selected = group_masked_sum(lookup(half, both_sel, first_row))
-    chosen = group_masked_sum(lookup(half, both_cand, first_row))
+    cand_rows = lookup(half, both_cand, first_row)
+    split = cand_rows.shape[0] // 2
+    chosen = jnp.concatenate([group_masked_sum(cand_rows[:split]), group_masked_sum(cand_rows[split:])])
     n_sel = both_sel.shape[0]
     sel_scores = lax.optimization_barrier(similar(selected, half))
     reached = all_max_two_rounds(jnp.max(sel_scores, axis=0), "xc", n_xc)

time: 209 us -> 237 us (1.13)
  starting transfers between devices: 44.7 us -> 72 us
    ppermute x12 -> x18, starting transfers between devices: 10.1 us -> 28.5 us  [y_shift(): return lax.ppermute(value, 'col', pairs)]
    ppermute x5 -> x7, starting transfers between devices: 8.14 us -> 16.7 us  [z_group_shift(): lax.ppermute(value, ('zl', 'col'), [(i, i ^ N_Y * N_Z ^ 1) for i in range...]
    ppermute x12 -> x18, waiting for transfers between devices: 21.3 us -> 28 us  [y_shift(): return lax.ppermute(value, 'col', pairs)]
    ppermute x5 -> x7, waiting for transfers between devices: 5.99 us -> 3.73 us  [z_group_shift(): return lax.ppermute(value, 'col', [(c, c ^ 1) for c in range(N_Y * N_Z)])]
    ppermute x5 -> x7, starting transfers between devices: 14 us -> 14.4 us  [z_group_shift(): return lax.ppermute(value, 'col', [(c, c ^ 1) for c in range(N_Y * N_Z)])]
  transfers between devices with their start and end apart: 38 -> 50, of which waited for: 21 -> 20; matrix products, arithmetic and copies ran while one was open for 10% -> 10% of each run, Pallas kernels for 0% -> 0%
where the time goes in v20:
time: 237 us
  waiting for transfers between devices  107 us (45%)
  starting transfers between devices  72 us (30%)
  matrix products  21.1 us (9%)
  local copies, waits for them, and re-layouts  17.2 us (7%)
  between operations  14.5 us (6%)
  other arithmetic  5.11 us (2%)
    all_gather x1, waiting for transfers between devices, body(): half = lax.all_gather(slab_embed, 'xc', axis=0, tiled=True)  65.7 us
    ppermute x18, starting transfers between devices, y_shift(): return lax.ppermute(value, 'col', pairs)  28.5 us
    ppermute x18, waiting for transfers between devices, y_shift(): return lax.ppermute(value, 'col', pairs)  28 us
    dot_general x2, matrix products, similar(): lax.dot_general(left, right, (((1,), (1,)), ((), ())), precision=lax.Prec...  21.1 us
    ppermute x7, starting transfers between devices, z_group_shift(): lax.ppermute(value, ('zl', 'col'), [(i, i ^ N_Y * N_Z ^ 1) for i in range...  16.7 us
    ppermute x7, starting transfers between devices, z_group_shift(): return lax.ppermute(value, 'col', [(c, c ^ 1) for c in range(N_Y * N_Z)])  14.4 us
    gather x2, local copies, waits for them, and re-layouts, lookup(): jnp.take(source, jnp.clip(position, 0, source.shape[0] - 1), axis=0)  13 us
  transfers between devices with their start and end apart: 50, of which 20 were waited for; matrix products, arithmetic and copies ran while one was open for 10% of the time, Pallas kernels for 0%

profile of v20, /device:TPU:0, one launch (start us, length us, event | category | flops | bytes accessed | tf_op | source)
XLA Modules:
  0.0 237.0 jit_solution(15190195062419330126)
XLA Ops:
  7.9 2.1 collective-permute-start
  11.6 2.0 collective-permute-done.18
  13.8 65.7 %all-gather.2.cloned.1.call-done = f32[4096,768]{1,0:T(8,128)} async-done(((f32[512,768]{1,0:T(8,128)}), f32[4096,768]{1,0:T(8,128)}) %all-gather.2.cloned.1.call-update) | async-done | bytes 12582928 | tf_op jit(solution)/shard_map/all_gather | solution.py:122
  79.5 7.1 %gather_fusion.2 = f32[384,768]{1,0:T(8,128)S(1)} fusion(f32[4096,768]{1,0:T(8,128)} %all-gather.2.cloned.1.call-done, s32[1024]{0:T(1024)S(1)} %pad_clamp_fusion.2), kind=kCustom, calls=%fused_computation.4 | custom fusion | bytes 2360832 | tf_op jit(solution)/shard_map/jit(_take)/gather | solution.py:23
  86.9 2.8 %collective-permute-start.21 = (f32[48,768]{1,0:T(8,128)S(1)}, f32[48,768]{1,0:T(8,128)S(1)}, u32[]{:S(2)}, u32[]{:S(2)}) collective-permute-start(f32[48,768]{1,0:T(8,128)S(1)} %get-tuple-element.12), channel_id=1, source_target_pairs={{0,6},{1,7},{2,0},{3,1},{4,2},{5,3},{6,4},{7,5},{8,14},{9,15},{10,... | collective-permute-start | bytes 442376 | tf_op jit(solution)/shard_map/ppermute | solution.py:33
  91.4 6.0 %gather_fusion = f32[256,768]{1,0:T(8,128)S(1)} fusion(f32[4096,768]{1,0:T(8,128)} %all-gather.2.cloned.1.call-done, s32[1024]{0:T(1024)S(1)} %pad_clamp_fusion.4), kind=kCustom, calls=%fused_computation.2 | custom fusion | bytes 1573888 | tf_op jit(solution)/shard_map/jit(_take)/gather | solution.py:23
  97.6 2.4 %collective-permute-start.3 = (f32[64,768]{1,0:T(8,128)S(1)}, f32[64,768]{1,0:T(8,128)S(1)}, u32[]{:S(2)}, u32[]{:S(2)}) collective-permute-start(f32[64,768]{1,0:T(8,128)S(1)} %get-tuple-element.9), channel_id=1, source_target_pairs={{0,6},{1,7},{2,0},{3,1},{4,2},{5,3},{6,4},{7,5},{8,14},{9,15},{10,... | collective-permute-start | bytes 589832 | tf_op jit(solution)/shard_map/ppermute | solution.py:33
  105.2 9.2 %collective-permute-done.33 = f32[48,768]{1,0:T(8,128)S(1)} collective-permute-done((f32[48,768]{1,0:T(8,128)S(1)}, f32[48,768]{1,0:T(8,128)S(1)}, u32[]{:S(2)}, u32[]{:S(2)}) %collective-permute-start.33) | collective-permute-done | bytes 147488 | tf_op jit(solution)/shard_map/ppermute | solution.py:33
  114.4 2.9 %collective-permute-start.24 = (f32[12,768]{1,0:T(8,128)S(1)}, f32[12,768]{1,0:T(8,128)S(1)}, u32[]{:S(2)}, u32[]{:S(2)}) collective-permute-start(f32[12,768]{1,0:T(8,128)S(1)} %get-tuple-element.21), channel_id=1, source_target_pairs={{0,65},{1,64},{2,67},{3,66},{4,69},{5,68},{6,71},{7,70},{64,1},{65... | collective-permute-start | bytes 110600 | tf_op jit(solution)/shard_map/ppermute | solution.py:51
  119.7 3.1 %collective-permute-start.36 = (f32[12,768]{1,0:T(8,128)S(1)}, f32[12,768]{1,0:T(8,128)S(1)}, u32[]{:S(2)}, u32[]{:S(2)}) collective-permute-start(f32[12,768]{1,0:T(8,128)S(1)} %get-tuple-element.24), channel_id=1, source_target_pairs={{0,65},{1,64},{2,67},{3,66},{4,69},{5,68},{6,71},{7,70},{64,1},{65... | collective-permute-start | bytes 110600 | tf_op jit(solution)/shard_map/ppermute | solution.py:51
  125.0 1.9 collective-permute-start.1
  127.1 2.7 %collective-permute-start.27 = (f32[12,768]{1,0:T(8,128)S(1)}, f32[12,768]{1,0:T(8,128)S(1)}, u32[]{:S(2)}, u32[]{:S(2)}) collective-permute-start(f32[12,768]{1,0:T(8,128)S(1)} %add_add_fusion.4), channel_id=1, source_target_pairs={{0,65},{1,64},{2,67},{3,66},{4,69},{5,68},{6,71},{7,70},{64,1},{65... | collective-permute-start | bytes 110600 | tf_op jit(solution)/shard_map/ppermute | solution.py:51
  131.9 2.7 %collective-permute-start.39 = (f32[12,768]{1,0:T(8,128)S(1)}, f32[12,768]{1,0:T(8,128)S(1)}, u32[]{:S(2)}, u32[]{:S(2)}) collective-permute-start(f32[12,768]{1,0:T(8,128)S(1)} %add_add_fusion.3), channel_id=1, source_target_pairs={{0,65},{1,64},{2,67},{3,66},{4,69},{5,68},{6,71},{7,70},{64,1},{65... | collective-permute-start | bytes 110600 | tf_op jit(solution)/shard_map/ppermute | solution.py:51
  134.7 2.1 collective-permute-start.37
  136.8 2.6 %collective-permute-start.6 = (f32[16,768]{1,0:T(8,128)S(1)}, f32[16,768]{1,0:T(8,128)S(1)}, u32[]{:S(2)}, u32[]{:S(2)}) collective-permute-start(f32[16,768]{1,0:T(8,128)S(1)} %get-tuple-element.18), channel_id=1, source_target_pairs={{0,65},{1,64},{2,67},{3,66},{4,69},{5,68},{6,71},{7,70},{64,1},{65... | collective-permute-start | bytes 147464 | tf_op jit(solution)/shard_map/ppermute | solution.py:51
  139.5 2.1 collective-permute-start.4
  147.4 2.6 %collective-permute-start.7 = (f32[16,768]{1,0:T(8,128)S(1)}, f32[16,768]{1,0:T(8,128)S(1)}, u32[]{:S(2)}, u32[]{:S(2)}) collective-permute-start(f32[16,768]{1,0:T(8,128)S(1)} %add_add_fusion.5), channel_id=1, source_target_pairs={{0,1},{1,0},{2,3},{3,2},{4,5},{5,4},{6,7},{7,6},{8,9},{9,8},{10,11... | collective-permute-start | bytes 147464 | tf_op jit(solution)/shard_map/ppermute | solution.py:47
  150.2 3.0 %collective-permute-start.40 = (f32[48,768]{1,0:T(8,128)S(1)}, f32[48,768]{1,0:T(8,128)S(1)}, u32[]{:S(2)}, u32[]{:S(2)}) collective-permute-start(f32[48,768]{1,0:T(8,128)S(1)} %reshape.346), channel_id=1, source_target_pairs={{0,6},{1,7},{2,0},{3,1},{4,2},{5,3},{6,4},{7,5},{8,14},{9,15},{10,... | collective-permute-start | bytes 442376 | tf_op jit(solution)/shard_map/ppermute | solution.py:33
  155.0 1.9 collective-permute-start.28
  158.3 5.5 %collective-permute-done.10 = f32[64,768]{1,0:T(8,128)S(1)} collective-permute-done((f32[64,768]{1,0:T(8,128)S(1)}, f32[64,768]{1,0:T(8,128)S(1)}, u32[]{:S(2)}, u32[]{:S(2)}) %collective-permute-start.10) | collective-permute-done | bytes 196640 | tf_op jit(solution)/shard_map/ppermute | solution.py:33
  163.8 2.1 collective-permute-start.11
  166.0 5.8 %collective-permute-done.11 = f32[64,768]{1,0:T(8,128)S(1)} collective-permute-done((f32[64,768]{1,0:T(8,128)S(1)}, f32[64,768]{1,0:T(8,128)S(1)}, u32[]{:S(2)}, u32[]{:S(2)}) %collective-permute-start.11) | collective-permute-done | bytes 196640 | tf_op jit(solution)/shard_map/ppermute | solution.py:33
  171.7 2.4 %collective-permute-start.12 = (f32[64,768]{1,0:T(8,128)S(1)}, f32[64,768]{1,0:T(8,128)S(1)}, u32[]{:S(2)}, u32[]{:S(2)}) collective-permute-start(f32[64,768]{1,0:T(8,128)S(1)} %bitcast_select_fusion), channel_id=1, source_target_pairs={{0,2},{1,3},{2,4},{3,5},{4,6},{5,7},{6,0},{7,1},{8,10},{9,11},{10,... | collective-permute-start | bytes 589832 | tf_op jit(solution)/shard_map/ppermute | solution.py:33
  174.1 5.1 %collective-permute-done.12 = f32[64,768]{1,0:T(8,128)S(1)} collective-permute-done((f32[64,768]{1,0:T(8,128)S(1)}, f32[64,768]{1,0:T(8,128)S(1)}, u32[]{:S(2)}, u32[]{:S(2)}) %collective-permute-start.12) | collective-permute-done | bytes 196640 | tf_op jit(solution)/shard_map/ppermute | solution.py:33
  180.6 10.3 %fusion.34 = f32[256,4096]{1,0:T(8,128)} fusion(f32[256,768]{1,0:T(8,128)S(1)} %bitcast.57, f32[4096,768]{1,0:T(8,128)} %all-gather.2.cloned.1.call-done), kind=kOutput, calls=%fused_computation.126 | convolution fusion | flops 4831838208 | bytes 17563648 | tf_op jit(solution)/shard_map/dot_general | solution.py:11
  190.9 2.4 %reduce_max.9 = f32[4096]{0:T(1024)S(1)} reduce(f32[256,4096]{1,0:T(8,128)} %fusion.34, f32[]{:T(128)} %constant.211.clone.1), dimensions={0}, to_apply=%region_0.1 | reduce | flops 1044480 | bytes 4210692 | tf_op jit(solution)/shard_map/reduce_max | solution.py:133
  196.6 1.8 collective-permute-start.30
  198.4 2.2 collective-permute-start.16
  200.6 2.4 %collective-permute-done.30 = f32[48,768]{1,0:T(8,128)S(1)} collective-permute-done((f32[48,768]{1,0:T(8,128)S(1)}, f32[48,768]{1,0:T(8,128)S(1)}, u32[]{:S(2)}, u32[]{:S(2)}) %collective-permute-start.30) | collective-permute-done | bytes 147488 | tf_op jit(solution)/shard_map/ppermute | solution.py:33
  203.7 10.8 %maximum_reduce_fusion = f32[384]{0:T(512)S(1)} fusion(f32[4096]{0:T(1024)S(1)} %maximum_maximum_fusion, f32[4096,768]{1,0:T(8,128)} %all-gather.2.cloned.1.call-done, f32[192,768]{1,0:T(8,128)S(1)} %bitcast.60, f32[192,768]{1,0:T(8,128)S(1)} %bitcast.61), kind=kOutput, calls=%fused_computation.7 | convolution fusion | flops 7252770304 | bytes 13780480 | tf_op jit(solution)/shard_map/dot_general | solution.py:11
  215.6 3.7 %collective-permute-start.43 = (f32[384]{0:T(512)S(1)}, f32[384]{0:T(512)S(1)}, u32[]{:S(2)}, u32[]{:S(2)}) collective-permute-start(f32[384]{0:T(512)S(1)} %maximum_reduce_fusion), channel_id=1, source_target_pairs={{0,1},{1,0},{2,3},{3,2},{4,5},{5,4},{6,7},{7,6},{8,9},{9,8},{10,11... | collective-permute-start | bytes 4616 | tf_op jit(solution)/shard_map/ppermute | solution.py:47
  226.4 1.8 collective-permute-done.47
  (149 shorter events, 41.2 us)
Async XLA Ops:
  7.2 72.3 %all-gather.2.cloned.1.call-start = ((), (), s32[]{:S(2)}) async-start(), calls=%async_computation | async-start | bytes 14155776 | tf_op jit(solution)/shard_map/all_gather | solution.py:122
  86.9 14.7 %collective-permute-start.21 = (f32[48,768]{1,0:T(8,128)S(1)}, f32[48,768]{1,0:T(8,128)S(1)}, u32[]{:S(2)}, u32[]{:S(2)}) collective-permute-start(f32[48,768]{1,0:T(8,128)S(1)} %get-tuple-element.12), channel_id=1, source_target_pairs={{0,6},{1,7},{2,0},{3,1},{4,2},{5,3},{6,4},{7,5},{8,14},{9,15},{10,... | collective-permute-start | bytes 442376 | tf_op jit(solution)/shard_map/ppermute | solution.py:33
  89.7 12.8 %collective-permute-start.20 = (f32[48,768]{1,0:T(8,128)S(1)}, f32[48,768]{1,0:T(8,128)S(1)}, u32[]{:S(2)}, u32[]{:S(2)}) collective-permute-start(f32[48,768]{1,0:T(8,128)S(1)} %get-tuple-element.13), channel_id=1, source_target_pairs={{0,4},{1,5},{2,6},{3,7},{4,0},{5,1},{6,2},{7,3},{8,12},{9,13},{10,... | collective-permute-start | bytes 442376 | tf_op jit(solution)/shard_map/ppermute | solution.py:33
  90.5 13.3 %collective-permute-start.19 = (f32[48,768]{1,0:T(8,128)S(1)}, f32[48,768]{1,0:T(8,128)S(1)}, u32[]{:S(2)}, u32[]{:S(2)}) collective-permute-start(f32[48,768]{1,0:T(8,128)S(1)} %get-tuple-element.11), channel_id=1, source_target_pairs={{0,2},{1,3},{2,4},{3,5},{4,6},{5,7},{6,0},{7,1},{8,10},{9,11},{10,... | collective-permute-start | bytes 442376 | tf_op jit(solution)/shard_map/ppermute | solution.py:33
  97.6 33.2 %collective-permute-start.3 = (f32[64,768]{1,0:T(8,128)S(1)}, f32[64,768]{1,0:T(8,128)S(1)}, u32[]{:S(2)}, u32[]{:S(2)}) collective-permute-start(f32[64,768]{1,0:T(8,128)S(1)} %get-tuple-element.9), channel_id=1, source_target_pairs={{0,6},{1,7},{2,0},{3,1},{4,2},{5,3},{6,4},{7,5},{8,14},{9,15},{10,... | collective-permute-start | bytes 589832 | tf_op jit(solution)/shard_map/ppermute | solution.py:33
  100.0 31.9 %collective-permute-start.2 = (f32[64,768]{1,0:T(8,128)S(1)}, f32[64,768]{1,0:T(8,128)S(1)}, u32[]{:S(2)}, u32[]{:S(2)}) collective-permute-start(f32[64,768]{1,0:T(8,128)S(1)} %get-tuple-element.10), channel_id=1, source_target_pairs={{0,4},{1,5},{2,6},{3,7},{4,0},{5,1},{6,2},{7,3},{8,12},{9,13},{10,... | collective-permute-start | bytes 589832 | tf_op jit(solution)/shard_map/ppermute | solution.py:33
  101.6 12.8 %collective-permute-start.33 = (f32[48,768]{1,0:T(8,128)S(1)}, f32[48,768]{1,0:T(8,128)S(1)}, u32[]{:S(2)}, u32[]{:S(2)}) collective-permute-start(f32[48,768]{1,0:T(8,128)S(1)} %get-tuple-element.15), channel_id=1, source_target_pairs={{0,6},{1,7},{2,0},{3,1},{4,2},{5,3},{6,4},{7,5},{8,14},{9,15},{10,... | collective-permute-start | bytes 442376 | tf_op jit(solution)/shard_map/ppermute | solution.py:33
  102.5 14.8 %collective-permute-start.32 = (f32[48,768]{1,0:T(8,128)S(1)}, f32[48,768]{1,0:T(8,128)S(1)}, u32[]{:S(2)}, u32[]{:S(2)}) collective-permute-start(f32[48,768]{1,0:T(8,128)S(1)} %get-tuple-element.16), channel_id=1, source_target_pairs={{0,4},{1,5},{2,6},{3,7},{4,0},{5,1},{6,2},{7,3},{8,12},{9,13},{10,... | collective-permute-start | bytes 442376 | tf_op jit(solution)/shard_map/ppermute | solution.py:33
  103.8 13.7 %collective-permute-start.31 = (f32[48,768]{1,0:T(8,128)S(1)}, f32[48,768]{1,0:T(8,128)S(1)}, u32[]{:S(2)}, u32[]{:S(2)}) collective-permute-start(f32[48,768]{1,0:T(8,128)S(1)} %get-tuple-element.14), channel_id=1, source_target_pairs={{0,2},{1,3},{2,4},{3,5},{4,6},{5,7},{6,0},{7,1},{8,10},{9,11},{10,... | collective-permute-start | bytes 442376 | tf_op jit(solution)/shard_map/ppermute | solution.py:33
  117.5 6.0 %collective-permute-start.22 = (f32[12,768]{1,0:T(8,128)S(1)}, f32[12,768]{1,0:T(8,128)S(1)}, u32[]{:S(2)}, u32[]{:S(2)}) collective-permute-start(f32[12,768]{1,0:T(8,128)S(1)} %get-tuple-element.20), channel_id=1, source_target_pairs={{0,1},{1,0},{2,3},{3,2},{4,5},{5,4},{6,7},{7,6},{8,9},{9,8},{10,11... | collective-permute-start | bytes 110600 | tf_op jit(solution)/shard_map/ppermute | solution.py:47
  123.4 6.4 %collective-permute-start.34 = (f32[12,768]{1,0:T(8,128)S(1)}, f32[12,768]{1,0:T(8,128)S(1)}, u32[]{:S(2)}, u32[]{:S(2)}) collective-permute-start(f32[12,768]{1,0:T(8,128)S(1)} %get-tuple-element.23), channel_id=1, source_target_pairs={{0,1},{1,0},{2,3},{3,2},{4,5},{5,4},{6,7},{7,6},{8,9},{9,8},{10,11... | collective-permute-start | bytes 110600 | tf_op jit(solution)/shard_map/ppermute | solution.py:47
  125.0 9.7 %collective-permute-start.1 = (f32[64,768]{1,0:T(8,128)S(1)}, f32[64,768]{1,0:T(8,128)S(1)}, u32[]{:S(2)}, u32[]{:S(2)}) collective-permute-start(f32[64,768]{1,0:T(8,128)S(1)} %get-tuple-element.8), channel_id=1, source_target_pairs={{0,2},{1,3},{2,4},{3,5},{4,6},{5,7},{6,0},{7,1},{8,10},{9,11},{10,... | collective-permute-start | bytes 589832 | tf_op jit(solution)/shard_map/ppermute | solution.py:33
  127.1 7.6 %collective-permute-start.27 = (f32[12,768]{1,0:T(8,128)S(1)}, f32[12,768]{1,0:T(8,128)S(1)}, u32[]{:S(2)}, u32[]{:S(2)}) collective-permute-start(f32[12,768]{1,0:T(8,128)S(1)} %add_add_fusion.4), channel_id=1, source_target_pairs={{0,65},{1,64},{2,67},{3,66},{4,69},{5,68},{6,71},{7,70},{64,1},{65... | collective-permute-start | bytes 110600 | tf_op jit(solution)/shard_map/ppermute | solution.py:51
  129.8 7.0 %collective-permute-start.26 = (f32[12,768]{1,0:T(8,128)S(1)}, f32[12,768]{1,0:T(8,128)S(1)}, u32[]{:S(2)}, u32[]{:S(2)}) collective-permute-start(f32[12,768]{1,0:T(8,128)S(1)} %add_add_fusion.4), channel_id=1, source_target_pairs={{0,64},{64,0},{1,65},{65,1},{2,66},{66,2},{3,67},{67,3},{4,68},{68... | collective-permute-start | bytes 110600 | tf_op jit(solution)/shard_map/ppermute | solution.py:49
  130.8 8.7 %collective-permute-start.25 = (f32[12,768]{1,0:T(8,128)S(1)}, f32[12,768]{1,0:T(8,128)S(1)}, u32[]{:S(2)}, u32[]{:S(2)}) collective-permute-start(f32[12,768]{1,0:T(8,128)S(1)} %add_add_fusion.4), channel_id=1, source_target_pairs={{0,1},{1,0},{2,3},{3,2},{4,5},{5,4},{6,7},{7,6},{8,9},{9,8},{10,11... | collective-permute-start | bytes 110600 | tf_op jit(solution)/shard_map/ppermute | solution.py:47
  131.9 7.6 %collective-permute-start.39 = (f32[12,768]{1,0:T(8,128)S(1)}, f32[12,768]{1,0:T(8,128)S(1)}, u32[]{:S(2)}, u32[]{:S(2)}) collective-permute-start(f32[12,768]{1,0:T(8,128)S(1)} %add_add_fusion.3), channel_id=1, source_target_pairs={{0,65},{1,64},{2,67},{3,66},{4,69},{5,68},{6,71},{7,70},{64,1},{65... | collective-permute-start | bytes 110600 | tf_op jit(solution)/shard_map/ppermute | solution.py:51
  134.6 7.0 %collective-permute-start.38 = (f32[12,768]{1,0:T(8,128)S(1)}, f32[12,768]{1,0:T(8,128)S(1)}, u32[]{:S(2)}, u32[]{:S(2)}) collective-permute-start(f32[12,768]{1,0:T(8,128)S(1)} %add_add_fusion.3), channel_id=1, source_target_pairs={{0,64},{64,0},{1,65},{65,1},{2,66},{66,2},{3,67},{67,3},{4,68},{68... | collective-permute-start | bytes 110600 | tf_op jit(solution)/shard_map/ppermute | solution.py:49
  134.7 7.0 %collective-permute-start.37 = (f32[12,768]{1,0:T(8,128)S(1)}, f32[12,768]{1,0:T(8,128)S(1)}, u32[]{:S(2)}, u32[]{:S(2)}) collective-permute-start(f32[12,768]{1,0:T(8,128)S(1)} %add_add_fusion.3), channel_id=1, source_target_pairs={{0,1},{1,0},{2,3},{3,2},{4,5},{5,4},{6,7},{7,6},{8,9},{9,8},{10,11... | collective-permute-start | bytes 110600 | tf_op jit(solution)/shard_map/ppermute | solution.py:47
  136.8 6.0 %collective-permute-start.6 = (f32[16,768]{1,0:T(8,128)S(1)}, f32[16,768]{1,0:T(8,128)S(1)}, u32[]{:S(2)}, u32[]{:S(2)}) collective-permute-start(f32[16,768]{1,0:T(8,128)S(1)} %get-tuple-element.18), channel_id=1, source_target_pairs={{0,65},{1,64},{2,67},{3,66},{4,69},{5,68},{6,71},{7,70},{64,1},{65... | collective-permute-start | bytes 147464 | tf_op jit(solution)/shard_map/ppermute | solution.py:51
  145.2 8.4 %collective-permute-start.9 = (f32[16,768]{1,0:T(8,128)S(1)}, f32[16,768]{1,0:T(8,128)S(1)}, u32[]{:S(2)}, u32[]{:S(2)}) collective-permute-start(f32[16,768]{1,0:T(8,128)S(1)} %add_add_fusion.5), channel_id=1, source_target_pairs={{0,65},{1,64},{2,67},{3,66},{4,69},{5,68},{6,71},{7,70},{64,1},{65... | collective-permute-start | bytes 147464 | tf_op jit(solution)/shard_map/ppermute | solution.py:51
  146.9 8.1 %collective-permute-start.8 = (f32[16,768]{1,0:T(8,128)S(1)}, f32[16,768]{1,0:T(8,128)S(1)}, u32[]{:S(2)}, u32[]{:S(2)}) collective-permute-start(f32[16,768]{1,0:T(8,128)S(1)} %add_add_fusion.5), channel_id=1, source_target_pairs={{0,64},{64,0},{1,65},{65,1},{2,66},{66,2},{3,67},{67,3},{4,68},{68... | collective-permute-start | bytes 147464 | tf_op jit(solution)/shard_map/ppermute | solution.py:49
  147.4 9.5 %collective-permute-start.7 = (f32[16,768]{1,0:T(8,128)S(1)}, f32[16,768]{1,0:T(8,128)S(1)}, u32[]{:S(2)}, u32[]{:S(2)}) collective-permute-start(f32[16,768]{1,0:T(8,128)S(1)} %add_add_fusion.5), channel_id=1, source_target_pairs={{0,1},{1,0},{2,3},{3,2},{4,5},{5,4},{6,7},{7,6},{8,9},{9,8},{10,11... | collective-permute-start | bytes 147464 | tf_op jit(solution)/shard_map/ppermute | solution.py:47
  150.2 43.2 %collective-permute-start.40 = (f32[48,768]{1,0:T(8,128)S(1)}, f32[48,768]{1,0:T(8,128)S(1)}, u32[]{:S(2)}, u32[]{:S(2)}) collective-permute-start(f32[48,768]{1,0:T(8,128)S(1)} %reshape.346), channel_id=1, source_target_pairs={{0,6},{1,7},{2,0},{3,1},{4,2},{5,3},{6,4},{7,5},{8,14},{9,15},{10,... | collective-permute-start | bytes 442376 | tf_op jit(solution)/shard_map/ppermute | solution.py:33
  153.1 40.3 %collective-permute-start.41 = (f32[48,768]{1,0:T(8,128)S(1)}, f32[48,768]{1,0:T(8,128)S(1)}, u32[]{:S(2)}, u32[]{:S(2)}) collective-permute-start(f32[48,768]{1,0:T(8,128)S(1)} %reshape.346), channel_id=1, source_target_pairs={{0,4},{1,5},{2,6},{3,7},{4,0},{5,1},{6,2},{7,3},{8,12},{9,13},{10,... | collective-permute-start | bytes 442376 | tf_op jit(solution)/shard_map/ppermute | solution.py:33
  153.6 40.8 %collective-permute-start.42 = (f32[48,768]{1,0:T(8,128)S(1)}, f32[48,768]{1,0:T(8,128)S(1)}, u32[]{:S(2)}, u32[]{:S(2)}) collective-permute-start(f32[48,768]{1,0:T(8,128)S(1)} %reshape.346), channel_id=1, source_target_pairs={{0,2},{1,3},{2,4},{3,5},{4,6},{5,7},{6,0},{7,1},{8,10},{9,11},{10,... | collective-permute-start | bytes 442376 | tf_op jit(solution)/shard_map/ppermute | solution.py:33
  155.0 45.5 %collective-permute-start.28 = (f32[48,768]{1,0:T(8,128)S(1)}, f32[48,768]{1,0:T(8,128)S(1)}, u32[]{:S(2)}, u32[]{:S(2)}) collective-permute-start(f32[48,768]{1,0:T(8,128)S(1)} %reshape.344), channel_id=1, source_target_pairs={{0,6},{1,7},{2,0},{3,1},{4,2},{5,3},{6,4},{7,5},{8,14},{9,15},{10,... | collective-permute-start | bytes 442376 | tf_op jit(solution)/shard_map/ppermute | solution.py:33
  157.6 6.2 %collective-permute-start.10 = (f32[64,768]{1,0:T(8,128)S(1)}, f32[64,768]{1,0:T(8,128)S(1)}, u32[]{:S(2)}, u32[]{:S(2)}) collective-permute-start(f32[64,768]{1,0:T(8,128)S(1)} %bitcast_select_fusion), channel_id=1, source_target_pairs={{0,6},{1,7},{2,0},{3,1},{4,2},{5,3},{6,4},{7,5},{8,14},{9,15},{10,... | collective-permute-start | bytes 589832 | tf_op jit(solution)/shard_map/ppermute | solution.py:33
  163.8 7.9 %collective-permute-start.11 = (f32[64,768]{1,0:T(8,128)S(1)}, f32[64,768]{1,0:T(8,128)S(1)}, u32[]{:S(2)}, u32[]{:S(2)}) collective-permute-start(f32[64,768]{1,0:T(8,128)S(1)} %bitcast_select_fusion), channel_id=1, source_target_pairs={{0,4},{1,5},{2,6},{3,7},{4,0},{5,1},{6,2},{7,3},{8,12},{9,13},{10,... | collective-permute-start | bytes 589832 | tf_op jit(solution)/shard_map/ppermute | solution.py:33
  171.7 7.5 %collective-permute-start.12 = (f32[64,768]{1,0:T(8,128)S(1)}, f32[64,768]{1,0:T(8,128)S(1)}, u32[]{:S(2)}, u32[]{:S(2)}) collective-permute-start(f32[64,768]{1,0:T(8,128)S(1)} %bitcast_select_fusion), channel_id=1, source_target_pairs={{0,2},{1,3},{2,4},{3,5},{4,6},{5,7},{6,0},{7,1},{8,10},{9,11},{10,... | collective-permute-start | bytes 589832 | tf_op jit(solution)/shard_map/ppermute | solution.py:33
  179.3 21.3 %collective-permute-start.29 = (f32[48,768]{1,0:T(8,128)S(1)}, f32[48,768]{1,0:T(8,128)S(1)}, u32[]{:S(2)}, u32[]{:S(2)}) collective-permute-start(f32[48,768]{1,0:T(8,128)S(1)} %reshape.344), channel_id=1, source_target_pairs={{0,4},{1,5},{2,6},{3,7},{4,0},{5,1},{6,2},{7,3},{8,12},{9,13},{10,... | collective-permute-start | bytes 442376 | tf_op jit(solution)/shard_map/ppermute | solution.py:33
  196.6 6.4 %collective-permute-start.30 = (f32[48,768]{1,0:T(8,128)S(1)}, f32[48,768]{1,0:T(8,128)S(1)}, u32[]{:S(2)}, u32[]{:S(2)}) collective-permute-start(f32[48,768]{1,0:T(8,128)S(1)} %reshape.344), channel_id=1, source_target_pairs={{0,2},{1,3},{2,4},{3,5},{4,6},{5,7},{6,0},{7,1},{8,10},{9,11},{10,... | collective-permute-start | bytes 442376 | tf_op jit(solution)/shard_map/ppermute | solution.py:33
  219.3 10.2 %collective-permute-start.17 = (f32[4096]{0:T(1024)S(1)}, f32[4096]{0:T(1024)S(1)}, u32[]{:S(2)}, u32[]{:S(2)}) collective-permute-start(f32[4096]{0:T(1024)S(1)} %maximum_maximum_fusion), channel_id=1, source_target_pairs={{0,64},{64,0},{1,65},{65,1},{2,66},{66,2},{3,67},{67,3},{4,68},{68... | collective-permute-start | bytes 49160 | tf_op jit(solution)/shard_map/ppermute | solution.py:140
  (21 other events, 96.6 us)
Sparse Core Ops, SparseCore 0:
  9.7 69.7 all-gather.1

commit v21 on v18

--- a/solution.py
+++ b/solution.py
@@ -127,8 +127,11 @@
     selected = group_masked_sum(lookup(half, both_sel, first_row))
     chosen = group_masked_sum(lookup(half, both_cand, first_row))
     n_sel = both_sel.shape[0]
-    sel_scores = lax.optimization_barrier(similar(selected, half))
-    reached = all_max_two_rounds(jnp.max(sel_scores, axis=0), "xc", n_xc)
+    width = half.shape[0] // 2
+    sel_max = [
+        jnp.max(lax.optimization_barrier(similar(selected, half[i * width:(i + 1) * width])), axis=0) for i in range(2)
+    ]
+    reached = all_max_two_rounds(jnp.concatenate(sel_max), "xc", n_xc)
     old = lax.dynamic_slice_in_dim(coverage_old, zl * half.shape[0], half.shape[0])
     coverage = jnp.maximum(old, reached)
     gain_part = jnp.sum(jnp.maximum(similar(chosen, half) - coverage[None, :], 0.0), axis=1)

time: 209 us -> 211 us (level)
  waiting for transfers between devices: 105 us -> 97.2 us
  starting transfers between devices: 44.7 us -> 50.7 us
  other arithmetic: 5.59 us -> 8.01 us
    ppermute x12, starting transfers between devices: 10.1 us -> 17.9 us  [y_shift(): return lax.ppermute(value, 'col', pairs)]
    ppermute x5, starting transfers between devices: 14 us -> 7.05 us  [z_group_shift(): return lax.ppermute(value, 'col', [(c, c ^ 1) for c in range(N_Y * N_Z)])]
    ppermute x12, waiting for transfers between devices: 21.3 us -> 14.9 us  [y_shift(): return lax.ppermute(value, 'col', pairs)]
    ppermute x5, waiting for transfers between devices: 1.13 us -> 5.67 us  [z_group_shift(): lax.ppermute(value, ('zl', 'col'), [(i, i ^ N_Y * N_Z ^ 1) for i in range...]
    ppermute x5, waiting for transfers between devices: 5.99 us -> 2.05 us  [z_group_shift(): return lax.ppermute(value, 'col', [(c, c ^ 1) for c in range(N_Y * N_Z)])]
    ppermute x5, starting transfers between devices: 1.91 us -> 5.56 us  [z_group_shift(): return lax.ppermute(value, 'zl', [(0, 1), (1, 0)])]
    all_gather x1, waiting for transfers between devices: 65.7 us -> 62.6 us  [body(): half = lax.all_gather(slab_embed, 'xc', axis=0, tiled=True)]
    ppermute x1, waiting for transfers between devices: 1.34 us -> 3.49 us  [body(): lax.ppermute(sel_index, 'zl', zl_swap)]
  transfers between devices with their start and end apart: 38 -> 38, of which waited for: 21 -> 17; matrix products, arithmetic and copies ran while one was open for 10% -> 12% of each run, Pallas kernels for 0% -> 0%
where the time goes in v21:
time: 211 us; the launch traced here: 210 us
  waiting for transfers between devices  97.2 us (46%)
  starting transfers between devices  50.7 us (24%)
  matrix products  22.5 us (11%)
  local copies, waits for them, and re-layouts  17.6 us (8%)
  between operations  14.5 us (7%)
  other arithmetic  8.01 us (4%)
    all_gather x1, waiting for transfers between devices, body(): half = lax.all_gather(slab_embed, 'xc', axis=0, tiled=True)  62.6 us
    dot_general x3, matrix products, similar(): lax.dot_general(left, right, (((1,), (1,)), ((), ())), precision=lax.Prec...  22.5 us
    ppermute x12, starting transfers between devices, y_shift(): return lax.ppermute(value, 'col', pairs)  17.9 us
    ppermute x12, waiting for transfers between devices, y_shift(): return lax.ppermute(value, 'col', pairs)  14.9 us
    gather x2, local copies, waits for them, and re-layouts, lookup(): jnp.take(source, jnp.clip(position, 0, source.shape[0] - 1), axis=0)  13 us
    ppermute x5, starting transfers between devices, z_group_shift(): lax.ppermute(value, ('zl', 'col'), [(i, i ^ N_Y * N_Z ^ 1) for i in range...  8.39 us
    ppermute x5, starting transfers between devices, z_group_shift(): return lax.ppermute(value, 'col', [(c, c ^ 1) for c in range(N_Y * N_Z)])  7.05 us
    ppermute x5, waiting for transfers between devices, z_group_shift(): lax.ppermute(value, ('zl', 'col'), [(i, i ^ N_Y * N_Z ^ 1) for i in range...  5.67 us
  transfers between devices with their start and end apart: 38, of which 17 were waited for; matrix products, arithmetic and copies ran while one was open for 12% of the time, Pallas kernels for 0%

profile of v21, /device:TPU:0, one launch (start us, length us, event | category | flops | bytes accessed | tf_op | source)
XLA Modules:
  0.0 210.5 jit_solution(6966574637064383773)
XLA Ops:
  7.9 2.1 collective-permute-start.18
  10.2 3.5 %collective-permute-done = s32[128]{0:T(128)S(1)} collective-permute-done((s32[128]{0:T(128)}, s32[128]{0:T(128)S(1)}, u32[]{:S(2)}, u32[]{:S(2)}) %collective-permute-start) | collective-permute-done | bytes 544 | tf_op jit(solution)/shard_map/ppermute | solution.py:125
  16.9 62.6 %all-gather.2.cloned.1.call-done = f32[4096,768]{1,0:T(8,128)} async-done(((f32[512,768]{1,0:T(8,128)}), f32[4096,768]{1,0:T(8,128)}) %all-gather.2.cloned.1.call-update) | async-done | bytes 12582928 | tf_op jit(solution)/shard_map/all_gather | solution.py:122
  79.5 6.0 %gather_fusion = f32[256,768]{1,0:T(8,128)S(1)} fusion(f32[4096,768]{1,0:T(8,128)} %all-gather.2.cloned.1.call-done, s32[1024]{0:T(1024)S(1)} %pad_clamp_fusion.3), kind=kCustom, calls=%fused_computation | custom fusion | bytes 1573888 | tf_op jit(solution)/shard_map/jit(_take)/gather | solution.py:23
  86.5 1.5 collective-permute-start.1
  88.0 2.7 %collective-permute-start.2 = (f32[64,768]{1,0:T(8,128)}, f32[64,768]{1,0:T(8,128)}, u32[]{:S(2)}, u32[]{:S(2)}) collective-permute-start(f32[64,768]{1,0:T(8,128)} %get-tuple-element.9), channel_id=1, source_target_pairs={{0,4},{1,5},{2,6},{3,7},{4,0},{5,1},{6,2},{7,3},{8,12},{9,13},{10,... | collective-permute-start | bytes 589832 | tf_op jit(solution)/shard_map/ppermute | solution.py:33
  92.1 7.1 %gather_fusion.2 = f32[384,768]{1,0:T(8,128)S(1)} fusion(f32[4096,768]{1,0:T(8,128)} %all-gather.2.cloned.1.call-done, s32[1024]{0:T(1024)S(1)} %pad_clamp_fusion.1), kind=kCustom, calls=%fused_computation.2 | custom fusion | bytes 2360832 | tf_op jit(solution)/shard_map/jit(_take)/gather | solution.py:23
  101.4 3.2 %collective-permute-start.4 = (f32[16,768]{1,0:T(8,128)S(1)}, f32[16,768]{1,0:T(8,128)S(1)}, u32[]{:S(2)}, u32[]{:S(2)}) collective-permute-start(f32[16,768]{1,0:T(8,128)S(1)} %get-tuple-element.13), channel_id=1, source_target_pairs={{0,1},{1,0},{2,3},{3,2},{4,5},{5,4},{6,7},{7,6},{8,9},{9,8},{10,11... | collective-permute-start | bytes 147464 | tf_op jit(solution)/shard_map/ppermute | solution.py:47
  105.9 2.6 %collective-permute-start.20 = (f32[96,768]{1,0:T(8,128)S(1)}, f32[96,768]{1,0:T(8,128)S(1)}, u32[]{:S(2)}, u32[]{:S(2)}) collective-permute-start(f32[96,768]{1,0:T(8,128)S(1)} %get-tuple-element.6), channel_id=1, source_target_pairs={{0,4},{1,5},{2,6},{3,7},{4,0},{5,1},{6,2},{7,3},{8,12},{9,13},{10,... | collective-permute-start | bytes 884744 | tf_op jit(solution)/shard_map/ppermute | solution.py:33
  108.5 1.6 collective-permute-start.21
  111.4 2.7 %collective-permute-done.5 = f32[16,768]{1,0:T(8,128)S(1)} collective-permute-done((f32[16,768]{1,0:T(8,128)S(1)}, f32[16,768]{1,0:T(8,128)S(1)}, u32[]{:S(2)}, u32[]{:S(2)}) %collective-permute-start.5) | collective-permute-done | bytes 49184 | tf_op jit(solution)/shard_map/ppermute | solution.py:49
  114.1 1.9 collective-permute-done.6
  117.4 2.8 %collective-permute-start.9 = (f32[16,768]{1,0:T(8,128)S(1)}, f32[16,768]{1,0:T(8,128)S(1)}, u32[]{:S(2)}, u32[]{:S(2)}) collective-permute-start(f32[16,768]{1,0:T(8,128)S(1)} %add_add_fusion.3), channel_id=1, source_target_pairs={{0,65},{1,64},{2,67},{3,66},{4,69},{5,68},{6,71},{7,70},{64,1},{65... | collective-permute-start | bytes 147464 | tf_op jit(solution)/shard_map/ppermute | solution.py:51
  122.0 1.6 collective-permute-start.23
  123.5 2.2 %collective-permute-start.24 = (f32[24,768]{1,0:T(8,128)S(1)}, f32[24,768]{1,0:T(8,128)S(1)}, u32[]{:S(2)}, u32[]{:S(2)}) collective-permute-start(f32[24,768]{1,0:T(8,128)S(1)} %get-tuple-element.11), channel_id=1, source_target_pairs={{0,65},{1,64},{2,67},{3,66},{4,69},{5,68},{6,71},{7,70},{64,1},{65... | collective-permute-start | bytes 221192 | tf_op jit(solution)/shard_map/ppermute | solution.py:51
  126.4 2.2 %collective-permute-start.10 = (f32[64,768]{1,0:T(8,128)S(1)}, f32[64,768]{1,0:T(8,128)S(1)}, u32[]{:S(2)}, u32[]{:S(2)}) collective-permute-start(f32[64,768]{1,0:T(8,128)S(1)} %bitcast_select_fusion.2), channel_id=1, source_target_pairs={{0,6},{1,7},{2,0},{3,1},{4,2},{5,3},{6,4},{7,5},{8,14},{9,15},{10,... | collective-permute-start | bytes 589832 | tf_op jit(solution)/shard_map/ppermute | solution.py:33
  132.2 1.8 collective-permute-start.27
  134.1 1.7 collective-permute-done.25
  138.4 4.2 %collective-permute-done.12 = f32[64,768]{1,0:T(8,128)S(1)} collective-permute-done((f32[64,768]{1,0:T(8,128)S(1)}, f32[64,768]{1,0:T(8,128)S(1)}, u32[]{:S(2)}, u32[]{:S(2)}) %collective-permute-start.12) | collective-permute-done | bytes 196640 | tf_op jit(solution)/shard_map/ppermute | solution.py:33
  142.9 6.8 %fusion.2 = f32[256,2048]{1,0:T(8,128)} fusion(f32[256,768]{1,0:T(8,128)S(1)} %bitcast.66, f32[4096,768]{1,0:T(8,128)} %all-gather.2.cloned.1.call-done), kind=kOutput, calls=%fused_computation.8 | convolution fusion | flops 2415919104 | bytes 9175040 | tf_op jit(solution)/shard_map/dot_general | solution.py:11
  149.6 4.9 %fusion = f32[256,2048]{1,0:T(8,128)S(1)} fusion(f32[256,768]{1,0:T(8,128)S(1)} %bitcast.67, f32[4096,768]{1,0:T(8,128)} %all-gather.2.cloned.1.call-done), kind=kOutput, calls=%fused_computation.6 | convolution fusion | flops 2415919104 | bytes 9175040 | tf_op jit(solution)/shard_map/dot_general | solution.py:11
  154.5 1.7 reduce_max.18
  161.1 2.2 %collective-permute-start.16 = (f32[4096]{0:T(1024)S(1)}, f32[4096]{0:T(1024)S(1)}, u32[]{:S(2)}, u32[]{:S(2)}) collective-permute-start(f32[4096]{0:T(1024)S(1)} %maximum_maximum_fusion.1), channel_id=1, source_target_pairs={{0,32},{8,40},{16,48},{24,56},{32,0},{40,8},{48,16},{56,24},{1,33}... | collective-permute-start | bytes 49160 | tf_op jit(solution)/shard_map/ppermute | solution.py:82
  163.4 3.0 %collective-permute-done.16 = f32[4096]{0:T(1024)S(1)} collective-permute-done((f32[4096]{0:T(1024)S(1)}, f32[4096]{0:T(1024)S(1)}, u32[]{:S(2)}, u32[]{:S(2)}) %collective-permute-start.16) | collective-permute-done | bytes 16416 | tf_op jit(solution)/shard_map/ppermute | solution.py:82
  168.4 2.1 %collective-permute-done.29 = f32[96,768]{1,0:T(8,128)S(1)} collective-permute-done((f32[96,768]{1,0:T(8,128)S(1)}, f32[96,768]{1,0:T(8,128)S(1)}, u32[]{:S(2)}, u32[]{:S(2)}) %collective-permute-start.29) | collective-permute-done | bytes 294944 | tf_op jit(solution)/shard_map/ppermute | solution.py:33
  170.5 5.4 %collective-permute-done.30 = f32[96,768]{1,0:T(8,128)S(1)} collective-permute-done((f32[96,768]{1,0:T(8,128)S(1)}, f32[96,768]{1,0:T(8,128)S(1)}, u32[]{:S(2)}, u32[]{:S(2)}) %collective-permute-start.30) | collective-permute-done | bytes 294944 | tf_op jit(solution)/shard_map/ppermute | solution.py:33
  176.2 10.8 %maximum_reduce_fusion = f32[384]{0:T(512)S(1)} fusion(f32[384,768]{1,0:T(8,128)S(1)} %bitcast.72, f32[4096,768]{1,0:T(8,128)} %all-gather.2.cloned.1.call-done, f32[4096]{0:T(1024)S(1)} %maximum_maximum_fusion), kind=kOutput, calls=%fused_computation.10 | convolution fusion | flops 7252475392 | bytes 13780480 | tf_op jit(solution)/shard_map/dot_general | solution.py:11
  187.0 1.6 collective-permute-start.31
  192.2 2.6 %collective-permute-done.33 = f32[384]{0:T(512)S(1)} collective-permute-done((f32[384]{0:T(512)S(1)}, f32[384]{0:T(512)S(1)}, u32[]{:S(2)}, u32[]{:S(2)}) %collective-permute-start.33) | collective-permute-done | bytes 1568 | tf_op jit(solution)/shard_map/ppermute | solution.py:51
  195.4 2.1 collective-permute-start.35
  197.5 2.6 %collective-permute-start.36 = (f32[4,384]{1,0:T(4,128)S(1)}, f32[4,384]{1,0:T(4,128)S(1)}, u32[]{:S(2)}, u32[]{:S(2)}) collective-permute-start(f32[4,384]{1,0:T(4,128)S(1)} %broadcast_select_fusion), channel_id=1, source_target_pairs={{0,6},{1,7},{2,4},{3,5},{4,2},{5,3},{6,0},{7,1},{8,14},{9,15},{10,... | collective-permute-start | bytes 18440 | tf_op jit(solution)/shard_map/ppermute | solution.py:95
  200.6 1.7 collective-permute-done.36
  (120 shorter events, 34.9 us)
Async XLA Ops:
  7.2 72.3 %all-gather.2.cloned.1.call-start = ((), (), s32[]{:S(2)}) async-start(), calls=%async_computation | async-start | bytes 14155776 | tf_op jit(solution)/shard_map/all_gather | solution.py:122
  7.9 7.3 %collective-permute-start.18 = (s32[192]{0:T(256)}, s32[192]{0:T(256)S(1)}, u32[]{:S(2)}, u32[]{:S(2)}) collective-permute-start(s32[192]{0:T(256)} %param.7), channel_id=1, source_target_pairs={{0,64},{64,0},{1,65},{65,1},{2,66},{66,2},{3,67},{67,3},{4,68},{68... | collective-permute-start | bytes 2312 | tf_op jit(solution)/shard_map/ppermute | solution.py:126
  86.5 12.9 %collective-permute-start.1 = (f32[64,768]{1,0:T(8,128)}, f32[64,768]{1,0:T(8,128)S(1)}, u32[]{:S(2)}, u32[]{:S(2)}) collective-permute-start(f32[64,768]{1,0:T(8,128)} %get-tuple-element.7), channel_id=1, source_target_pairs={{0,2},{1,3},{2,4},{3,5},{4,6},{5,7},{6,0},{7,1},{8,10},{9,11},{10,... | collective-permute-start | bytes 589832 | tf_op jit(solution)/shard_map/ppermute | solution.py:33
  88.0 12.3 %collective-permute-start.2 = (f32[64,768]{1,0:T(8,128)}, f32[64,768]{1,0:T(8,128)}, u32[]{:S(2)}, u32[]{:S(2)}) collective-permute-start(f32[64,768]{1,0:T(8,128)} %get-tuple-element.9), channel_id=1, source_target_pairs={{0,4},{1,5},{2,6},{3,7},{4,0},{5,1},{6,2},{7,3},{8,12},{9,13},{10,... | collective-permute-start | bytes 589832 | tf_op jit(solution)/shard_map/ppermute | solution.py:33
  90.7 9.6 %collective-permute-start.3 = (f32[64,768]{1,0:T(8,128)S(1)}, f32[64,768]{1,0:T(8,128)}, u32[]{:S(2)}, u32[]{:S(2)}) collective-permute-start(f32[64,768]{1,0:T(8,128)S(1)} %get-tuple-element.8), channel_id=1, source_target_pairs={{0,6},{1,7},{2,0},{3,1},{4,2},{5,3},{6,4},{7,5},{8,14},{9,15},{10,... | collective-permute-start | bytes 589832 | tf_op jit(solution)/shard_map/ppermute | solution.py:33
  101.4 9.3 %collective-permute-start.4 = (f32[16,768]{1,0:T(8,128)S(1)}, f32[16,768]{1,0:T(8,128)S(1)}, u32[]{:S(2)}, u32[]{:S(2)}) collective-permute-start(f32[16,768]{1,0:T(8,128)S(1)} %get-tuple-element.13), channel_id=1, source_target_pairs={{0,1},{1,0},{2,3},{3,2},{4,5},{5,4},{6,7},{7,6},{8,9},{9,8},{10,11... | collective-permute-start | bytes 147464 | tf_op jit(solution)/shard_map/ppermute | solution.py:47
  104.7 12.7 %collective-permute-start.19 = (f32[96,768]{1,0:T(8,128)S(1)}, f32[96,768]{1,0:T(8,128)S(1)}, u32[]{:S(2)}, u32[]{:S(2)}) collective-permute-start(f32[96,768]{1,0:T(8,128)S(1)} %get-tuple-element.4), channel_id=1, source_target_pairs={{0,2},{1,3},{2,4},{3,5},{4,6},{5,7},{6,0},{7,1},{8,10},{9,11},{10,... | collective-permute-start | bytes 884744 | tf_op jit(solution)/shard_map/ppermute | solution.py:33
  105.9 15.5 %collective-permute-start.20 = (f32[96,768]{1,0:T(8,128)S(1)}, f32[96,768]{1,0:T(8,128)S(1)}, u32[]{:S(2)}, u32[]{:S(2)}) collective-permute-start(f32[96,768]{1,0:T(8,128)S(1)} %get-tuple-element.6), channel_id=1, source_target_pairs={{0,4},{1,5},{2,6},{3,7},{4,0},{5,1},{6,2},{7,3},{8,12},{9,13},{10,... | collective-permute-start | bytes 884744 | tf_op jit(solution)/shard_map/ppermute | solution.py:33
  108.5 12.9 %collective-permute-start.21 = (f32[96,768]{1,0:T(8,128)S(1)}, f32[96,768]{1,0:T(8,128)S(1)}, u32[]{:S(2)}, u32[]{:S(2)}) collective-permute-start(f32[96,768]{1,0:T(8,128)S(1)} %get-tuple-element.5), channel_id=1, source_target_pairs={{0,6},{1,7},{2,0},{3,1},{4,2},{5,3},{6,4},{7,5},{8,14},{9,15},{10,... | collective-permute-start | bytes 884744 | tf_op jit(solution)/shard_map/ppermute | solution.py:33
  110.7 5.3 %collective-permute-start.6 = (f32[16,768]{1,0:T(8,128)S(1)}, f32[16,768]{1,0:T(8,128)S(1)}, u32[]{:S(2)}, u32[]{:S(2)}) collective-permute-start(f32[16,768]{1,0:T(8,128)S(1)} %get-tuple-element.14), channel_id=1, source_target_pairs={{0,65},{1,64},{2,67},{3,66},{4,69},{5,68},{6,71},{7,70},{64,1},{65... | collective-permute-start | bytes 147464 | tf_op jit(solution)/shard_map/ppermute | solution.py:51
  116.0 7.5 %collective-permute-start.7 = (f32[16,768]{1,0:T(8,128)S(1)}, f32[16,768]{1,0:T(8,128)S(1)}, u32[]{:S(2)}, u32[]{:S(2)}) collective-permute-start(f32[16,768]{1,0:T(8,128)S(1)} %add_add_fusion.3), channel_id=1, source_target_pairs={{0,1},{1,0},{2,3},{3,2},{4,5},{5,4},{6,7},{7,6},{8,9},{9,8},{10,11... | collective-permute-start | bytes 147464 | tf_op jit(solution)/shard_map/ppermute | solution.py:47
  116.8 8.9 %collective-permute-start.8 = (f32[16,768]{1,0:T(8,128)S(1)}, f32[16,768]{1,0:T(8,128)S(1)}, u32[]{:S(2)}, u32[]{:S(2)}) collective-permute-start(f32[16,768]{1,0:T(8,128)S(1)} %add_add_fusion.3), channel_id=1, source_target_pairs={{0,64},{64,0},{1,65},{65,1},{2,66},{66,2},{3,67},{67,3},{4,68},{68... | collective-permute-start | bytes 147464 | tf_op jit(solution)/shard_map/ppermute | solution.py:49
  117.4 8.3 %collective-permute-start.9 = (f32[16,768]{1,0:T(8,128)S(1)}, f32[16,768]{1,0:T(8,128)S(1)}, u32[]{:S(2)}, u32[]{:S(2)}) collective-permute-start(f32[16,768]{1,0:T(8,128)S(1)} %add_add_fusion.3), channel_id=1, source_target_pairs={{0,65},{1,64},{2,67},{3,66},{4,69},{5,68},{6,71},{7,70},{64,1},{65... | collective-permute-start | bytes 147464 | tf_op jit(solution)/shard_map/ppermute | solution.py:51
  121.5 8.2 %collective-permute-start.22 = (f32[24,768]{1,0:T(8,128)S(1)}, f32[24,768]{1,0:T(8,128)S(1)}, u32[]{:S(2)}, u32[]{:S(2)}) collective-permute-start(f32[24,768]{1,0:T(8,128)S(1)} %get-tuple-element.10), channel_id=1, source_target_pairs={{0,1},{1,0},{2,3},{3,2},{4,5},{5,4},{6,7},{7,6},{8,9},{9,8},{10,11... | collective-permute-start | bytes 221192 | tf_op jit(solution)/shard_map/ppermute | solution.py:47
  122.0 7.8 %collective-permute-start.23 = (f32[24,768]{1,0:T(8,128)S(1)}, f32[24,768]{1,0:T(8,128)S(1)}, u32[]{:S(2)}, u32[]{:S(2)}) collective-permute-start(f32[24,768]{1,0:T(8,128)S(1)} %get-tuple-element.12), channel_id=1, source_target_pairs={{0,64},{64,0},{1,65},{65,1},{2,66},{66,2},{3,67},{67,3},{4,68},{68... | collective-permute-start | bytes 221192 | tf_op jit(solution)/shard_map/ppermute | solution.py:49
  123.5 6.2 %collective-permute-start.24 = (f32[24,768]{1,0:T(8,128)S(1)}, f32[24,768]{1,0:T(8,128)S(1)}, u32[]{:S(2)}, u32[]{:S(2)}) collective-permute-start(f32[24,768]{1,0:T(8,128)S(1)} %get-tuple-element.11), channel_id=1, source_target_pairs={{0,65},{1,64},{2,67},{3,66},{4,69},{5,68},{6,71},{7,70},{64,1},{65... | collective-permute-start | bytes 221192 | tf_op jit(solution)/shard_map/ppermute | solution.py:51
  126.4 12.0 %collective-permute-start.10 = (f32[64,768]{1,0:T(8,128)S(1)}, f32[64,768]{1,0:T(8,128)S(1)}, u32[]{:S(2)}, u32[]{:S(2)}) collective-permute-start(f32[64,768]{1,0:T(8,128)S(1)} %bitcast_select_fusion.2), channel_id=1, source_target_pairs={{0,6},{1,7},{2,0},{3,1},{4,2},{5,3},{6,4},{7,5},{8,14},{9,15},{10,... | collective-permute-start | bytes 589832 | tf_op jit(solution)/shard_map/ppermute | solution.py:33
  128.6 9.8 %collective-permute-start.11 = (f32[64,768]{1,0:T(8,128)S(1)}, f32[64,768]{1,0:T(8,128)S(1)}, u32[]{:S(2)}, u32[]{:S(2)}) collective-permute-start(f32[64,768]{1,0:T(8,128)S(1)} %bitcast_select_fusion.2), channel_id=1, source_target_pairs={{0,4},{1,5},{2,6},{3,7},{4,0},{5,1},{6,2},{7,3},{8,12},{9,13},{10,... | collective-permute-start | bytes 589832 | tf_op jit(solution)/shard_map/ppermute | solution.py:33
  129.8 5.9 %collective-permute-start.25 = (f32[24,768]{1,0:T(8,128)S(1)}, f32[24,768]{1,0:T(8,128)S(1)}, u32[]{:S(2)}, u32[]{:S(2)}) collective-permute-start(f32[24,768]{1,0:T(8,128)S(1)} %add_add_fusion.2), channel_id=1, source_target_pairs={{0,1},{1,0},{2,3},{3,2},{4,5},{5,4},{6,7},{7,6},{8,9},{9,8},{10,11... | collective-permute-start | bytes 221192 | tf_op jit(solution)/shard_map/ppermute | solution.py:47
  130.8 5.7 %collective-permute-start.26 = (f32[24,768]{1,0:T(8,128)S(1)}, f32[24,768]{1,0:T(8,128)S(1)}, u32[]{:S(2)}, u32[]{:S(2)}) collective-permute-start(f32[24,768]{1,0:T(8,128)S(1)} %add_add_fusion.2), channel_id=1, source_target_pairs={{0,64},{64,0},{1,65},{65,1},{2,66},{66,2},{3,67},{67,3},{4,68},{68... | collective-permute-start | bytes 221192 | tf_op jit(solution)/shard_map/ppermute | solution.py:49
  132.2 5.6 %collective-permute-start.27 = (f32[24,768]{1,0:T(8,128)S(1)}, f32[24,768]{1,0:T(8,128)S(1)}, u32[]{:S(2)}, u32[]{:S(2)}) collective-permute-start(f32[24,768]{1,0:T(8,128)S(1)} %add_add_fusion.2), channel_id=1, source_target_pairs={{0,65},{1,64},{2,67},{3,66},{4,69},{5,68},{6,71},{7,70},{64,1},{65... | collective-permute-start | bytes 221192 | tf_op jit(solution)/shard_map/ppermute | solution.py:51
  135.7 6.9 %collective-permute-start.12 = (f32[64,768]{1,0:T(8,128)S(1)}, f32[64,768]{1,0:T(8,128)S(1)}, u32[]{:S(2)}, u32[]{:S(2)}) collective-permute-start(f32[64,768]{1,0:T(8,128)S(1)} %bitcast_select_fusion.2), channel_id=1, source_target_pairs={{0,2},{1,3},{2,4},{3,5},{4,6},{5,7},{6,0},{7,1},{8,10},{9,11},{10,... | collective-permute-start | bytes 589832 | tf_op jit(solution)/shard_map/ppermute | solution.py:33
  158.4 9.9 %collective-permute-start.28 = (f32[96,768]{1,0:T(8,128)S(1)}, f32[96,768]{1,0:T(8,128)S(1)}, u32[]{:S(2)}, u32[]{:S(2)}) collective-permute-start(f32[96,768]{1,0:T(8,128)S(1)} %bitcast_select_fusion), channel_id=1, source_target_pairs={{0,6},{1,7},{2,0},{3,1},{4,2},{5,3},{6,4},{7,5},{8,14},{9,15},{10,... | collective-permute-start | bytes 884744 | tf_op jit(solution)/shard_map/ppermute | solution.py:33
  159.1 11.4 %collective-permute-start.29 = (f32[96,768]{1,0:T(8,128)S(1)}, f32[96,768]{1,0:T(8,128)S(1)}, u32[]{:S(2)}, u32[]{:S(2)}) collective-permute-start(f32[96,768]{1,0:T(8,128)S(1)} %bitcast_select_fusion), channel_id=1, source_target_pairs={{0,4},{1,5},{2,6},{3,7},{4,0},{5,1},{6,2},{7,3},{8,12},{9,13},{10,... | collective-permute-start | bytes 884744 | tf_op jit(solution)/shard_map/ppermute | solution.py:33
  160.2 15.7 %collective-permute-start.30 = (f32[96,768]{1,0:T(8,128)S(1)}, f32[96,768]{1,0:T(8,128)S(1)}, u32[]{:S(2)}, u32[]{:S(2)}) collective-permute-start(f32[96,768]{1,0:T(8,128)S(1)} %bitcast_select_fusion), channel_id=1, source_target_pairs={{0,2},{1,3},{2,4},{3,5},{4,6},{5,7},{6,0},{7,1},{8,10},{9,11},{10,... | collective-permute-start | bytes 884744 | tf_op jit(solution)/shard_map/ppermute | solution.py:33
  161.1 5.3 %collective-permute-start.16 = (f32[4096]{0:T(1024)S(1)}, f32[4096]{0:T(1024)S(1)}, u32[]{:S(2)}, u32[]{:S(2)}) collective-permute-start(f32[4096]{0:T(1024)S(1)} %maximum_maximum_fusion.1), channel_id=1, source_target_pairs={{0,32},{8,40},{16,48},{24,56},{32,0},{40,8},{48,16},{56,24},{1,33}... | collective-permute-start | bytes 49160 | tf_op jit(solution)/shard_map/ppermute | solution.py:82
  166.5 24.7 %collective-permute-start.17 = (f32[4096]{0:T(1024)S(1)}, f32[4096]{0:T(1024)S(1)}, u32[]{:S(2)}, u32[]{:S(2)}) collective-permute-start(f32[4096]{0:T(1024)S(1)} %maximum_maximum_fusion), channel_id=1, source_target_pairs={{0,64},{64,0},{1,65},{65,1},{2,66},{66,2},{3,67},{67,3},{4,68},{68... | collective-permute-start | bytes 49160 | tf_op jit(solution)/shard_map/ppermute | solution.py:141
  187.0 5.2 %collective-permute-start.31 = (f32[384]{0:T(512)S(1)}, f32[384]{0:T(512)S(1)}, u32[]{:S(2)}, u32[]{:S(2)}) collective-permute-start(f32[384]{0:T(512)S(1)} %maximum_reduce_fusion), channel_id=1, source_target_pairs={{0,1},{1,0},{2,3},{3,2},{4,5},{5,4},{6,7},{7,6},{8,9},{9,8},{10,11... | collective-permute-start | bytes 4616 | tf_op jit(solution)/shard_map/ppermute | solution.py:47
  189.9 4.8 %collective-permute-start.33 = (f32[384]{0:T(512)S(1)}, f32[384]{0:T(512)S(1)}, u32[]{:S(2)}, u32[]{:S(2)}) collective-permute-start(f32[384]{0:T(512)S(1)} %maximum_reduce_fusion), channel_id=1, source_target_pairs={{0,65},{1,64},{2,67},{3,66},{4,69},{5,68},{6,71},{7,70},{64,1},{65... | collective-permute-start | bytes 4616 | tf_op jit(solution)/shard_map/ppermute | solution.py:51
  195.4 4.8 %collective-permute-start.34 = (f32[4,384]{1,0:T(4,128)S(1)}, f32[4,384]{1,0:T(4,128)S(1)}, u32[]{:S(2)}, u32[]{:S(2)}) collective-permute-start(f32[4,384]{1,0:T(4,128)S(1)} %broadcast_select_fusion), channel_id=1, source_target_pairs={{0,2},{1,3},{2,0},{3,1},{4,6},{5,7},{6,4},{7,5},{8,10},{9,11},{10,... | collective-permute-start | bytes 18440 | tf_op jit(solution)/shard_map/ppermute | solution.py:95
  195.4 5.2 %collective-permute-start.35 = (f32[4,384]{1,0:T(4,128)S(1)}, f32[4,384]{1,0:T(4,128)S(1)}, u32[]{:S(2)}, u32[]{:S(2)}) collective-permute-start(f32[4,384]{1,0:T(4,128)S(1)} %broadcast_select_fusion), channel_id=1, source_target_pairs={{0,4},{1,5},{2,6},{3,7},{4,0},{5,1},{6,2},{7,3},{8,12},{9,13},{10,... | collective-permute-start | bytes 18440 | tf_op jit(solution)/shard_map/ppermute | solution.py:95
  197.5 4.8 %collective-permute-start.36 = (f32[4,384]{1,0:T(4,128)S(1)}, f32[4,384]{1,0:T(4,128)S(1)}, u32[]{:S(2)}, u32[]{:S(2)}) collective-permute-start(f32[4,384]{1,0:T(4,128)S(1)} %broadcast_select_fusion), channel_id=1, source_target_pairs={{0,6},{1,7},{2,4},{3,5},{4,2},{5,3},{6,0},{7,1},{8,14},{9,15},{10,... | collective-permute-start | bytes 18440 | tf_op jit(solution)/shard_map/ppermute | solution.py:95
  (7 other events, 33.7 us)
Sparse Core Ops, SparseCore 0:
  9.7 69.7 all-gather.1

commit v22 on v18

--- a/solution.py
+++ b/solution.py
@@ -85,15 +85,15 @@
     return value
 
 
-def group_gather_in_order(value):
+def group_sum_in_order(value):
     here = lax.axis_index("col")
     y, z = here // N_Z, here % N_Z
     g = lax.axis_index("zl") * 2 + z
     received = jnp.stack([value] + [z_group_shift(value, k) for k in range(1, 4)])
-    z_ordered = jnp.take(received, jnp.arange(4) ^ g, axis=0)
+    z_sum = jnp.sum(jnp.take(received, jnp.arange(4) ^ g, axis=0), axis=0)
     col_pairs = [[(c, c ^ (2 * k)) for c in range(N_Y * N_Z)] for k in range(1, N_Y)]
-    received = jnp.stack([z_ordered] + [lax.ppermute(z_ordered, "col", pairs) for pairs in col_pairs])
-    return jnp.take(received, jnp.arange(N_Y) ^ y, axis=0)
+    received = jnp.stack([z_sum] + [lax.ppermute(z_sum, "col", pairs) for pairs in col_pairs])
+    return jnp.sum(jnp.take(received, jnp.arange(N_Y) ^ y, axis=0), axis=0)
 
 
 def all_max(value, axis, n):
@@ -132,8 +132,7 @@
     old = lax.dynamic_slice_in_dim(coverage_old, zl * half.shape[0], half.shape[0])
     coverage = jnp.maximum(old, reached)
     gain_part = jnp.sum(jnp.maximum(similar(chosen, half) - coverage[None, :], 0.0), axis=1)
-    parts = group_gather_in_order(gain_part)
-    total = jnp.sum(parts.reshape(-1, gain_part.shape[0]), axis=0)
+    total = group_sum_in_order(gain_part)
     total_gain = lax.dynamic_slice_in_dim(total, zl * cand_index.shape[0], cand_index.shape[0])
     full_coverage = pair_join(coverage, lax.ppermute(coverage, "zl", zl_swap), zl == 0)
     return (full_coverage, total_gain)

time: 209 us -> 209 us (level)
  transfers between devices with their start and end apart: 38 -> 38, of which waited for: 21 -> 20; matrix products, arithmetic and copies ran while one was open for 10% -> 6% of each run, Pallas kernels for 0% -> 0%
where the time goes in v22:
time: 209 us
  waiting for transfers between devices  104 us (50%)
  starting transfers between devices  44.6 us (21%)
  matrix products  21.1 us (10%)
  local copies, waits for them, and re-layouts  17.6 us (8%)
  between operations  14.5 us (7%)
  other arithmetic  6.73 us (3%)
    all_gather x1, waiting for transfers between devices, body(): half = lax.all_gather(slab_embed, 'xc', axis=0, tiled=True)  65.2 us
    dot_general x2, matrix products, similar(): lax.dot_general(left, right, (((1,), (1,)), ((), ())), precision=lax.Prec...  21.1 us
    ppermute x12, waiting for transfers between devices, y_shift(): return lax.ppermute(value, 'col', pairs)  20.7 us
    ppermute x5, starting transfers between devices, z_group_shift(): return lax.ppermute(value, 'col', [(c, c ^ 1) for c in range(N_Y * N_Z)])  14 us
    gather x2, local copies, waits for them, and re-layouts, lookup(): jnp.take(source, jnp.clip(position, 0, source.shape[0] - 1), axis=0)  13 us
    ppermute x12, starting transfers between devices, y_shift(): return lax.ppermute(value, 'col', pairs)  10.1 us
    ppermute x5, starting transfers between devices, z_group_shift(): lax.ppermute(value, ('zl', 'col'), [(i, i ^ N_Y * N_Z ^ 1) for i in range...  8.14 us
    ppermute x5, waiting for transfers between devices, z_group_shift(): return lax.ppermute(value, 'col', [(c, c ^ 1) for c in range(N_Y * N_Z)])  6.54 us
  transfers between devices with their start and end apart: 38, of which 20 were waited for; matrix products, arithmetic and copies ran while one was open for 6% of the time, Pallas kernels for 0%

profile of v22, /device:TPU:0, one launch (start us, length us, event | category | flops | bytes accessed | tf_op | source)
XLA Modules:
  0.0 208.7 jit_solution(17445739290626050738)
XLA Ops:
  7.9 2.1 collective-permute-start
  10.2 1.3 collective-permute-done
  11.6 2.0 collective-permute-done.18
  14.3 65.2 %all-gather.2.cloned.1.call-done = f32[4096,768]{1,0:T(8,128)} async-done(((f32[512,768]{1,0:T(8,128)}), f32[4096,768]{1,0:T(8,128)}) %all-gather.2.cloned.1.call-update) | async-done | bytes 12582928 | tf_op jit(solution)/shard_map/all_gather | solution.py:122
  79.5 6.0 %gather_fusion = f32[256,768]{1,0:T(8,128)S(1)} fusion(f32[4096,768]{1,0:T(8,128)} %all-gather.2.cloned.1.call-done, s32[1024]{0:T(1024)S(1)} %pad_clamp_fusion.4), kind=kCustom, calls=%fused_computation.2 | custom fusion | bytes 1573888 | tf_op jit(solution)/shard_map/jit(_take)/gather | solution.py:23
  86.5 2.7 %collective-permute-start.3 = (f32[64,768]{1,0:T(8,128)}, f32[64,768]{1,0:T(8,128)S(1)}, u32[]{:S(2)}, u32[]{:S(2)}) collective-permute-start(f32[64,768]{1,0:T(8,128)} %get-tuple-element.9), channel_id=1, source_target_pairs={{0,6},{1,7},{2,0},{3,1},{4,2},{5,3},{6,4},{7,5},{8,14},{9,15},{10,... | collective-permute-start | bytes 589832 | tf_op jit(solution)/shard_map/ppermute | solution.py:33
  90.9 7.1 %gather_fusion.2 = f32[384,768]{1,0:T(8,128)S(1)} fusion(f32[4096,768]{1,0:T(8,128)} %all-gather.2.cloned.1.call-done, s32[1024]{0:T(1024)S(1)} %pad_clamp_fusion.2), kind=kCustom, calls=%fused_computation.4 | custom fusion | bytes 2360832 | tf_op jit(solution)/shard_map/jit(_take)/gather | solution.py:23
  98.9 3.2 %collective-permute-done.1 = f32[64,768]{1,0:T(8,128)} collective-permute-done((f32[64,768]{1,0:T(8,128)S(1)}, f32[64,768]{1,0:T(8,128)}, u32[]{:S(2)}, u32[]{:S(2)}) %collective-permute-start.1) | collective-permute-done | bytes 196640 | tf_op jit(solution)/shard_map/ppermute | solution.py:33
  103.1 3.0 %collective-permute-start.6 = (f32[16,768]{1,0:T(8,128)S(1)}, f32[16,768]{1,0:T(8,128)S(1)}, u32[]{:S(2)}, u32[]{:S(2)}) collective-permute-start(f32[16,768]{1,0:T(8,128)S(1)} %get-tuple-element.15), channel_id=1, source_target_pairs={{0,65},{1,64},{2,67},{3,66},{4,69},{5,68},{6,71},{7,70},{64,1},{65... | collective-permute-start | bytes 147464 | tf_op jit(solution)/shard_map/ppermute | solution.py:51
  108.7 1.8 collective-permute-start.4
  110.8 2.0 collective-permute-done.5
  112.8 1.5 collective-permute-done.4
  114.3 2.8 %collective-permute-start.9 = (f32[16,768]{1,0:T(8,128)S(1)}, f32[16,768]{1,0:T(8,128)S(1)}, u32[]{:S(2)}, u32[]{:S(2)}) collective-permute-start(f32[16,768]{1,0:T(8,128)S(1)} %add_add_fusion.3), channel_id=1, source_target_pairs={{0,65},{1,64},{2,67},{3,66},{4,69},{5,68},{6,71},{7,70},{64,1},{65... | collective-permute-start | bytes 147464 | tf_op jit(solution)/shard_map/ppermute | solution.py:51
  117.2 1.9 collective-permute-start.7
  119.1 3.8 %collective-permute-done.19 = f32[96,768]{1,0:T(8,128)S(1)} collective-permute-done((f32[96,768]{1,0:T(8,128)S(1)}, f32[96,768]{1,0:T(8,128)S(1)}, u32[]{:S(2)}, u32[]{:S(2)}) %collective-permute-start.19) | collective-permute-done | bytes 294944 | tf_op jit(solution)/shard_map/ppermute | solution.py:33
  123.7 4.1 %collective-permute-start.22 = (f32[24,768]{1,0:T(8,128)S(1)}, f32[24,768]{1,0:T(8,128)S(1)}, u32[]{:S(2)}, u32[]{:S(2)}) collective-permute-start(f32[24,768]{1,0:T(8,128)S(1)} %get-tuple-element.11), channel_id=1, source_target_pairs={{0,1},{1,0},{2,3},{3,2},{4,5},{5,4},{6,7},{7,6},{8,9},{9,8},{10,11... | collective-permute-start | bytes 221192 | tf_op jit(solution)/shard_map/ppermute | solution.py:47
  129.9 1.3 collective-permute-done.22
  132.3 1.4 collective-permute-start.26
  133.7 2.3 %collective-permute-start.25 = (f32[24,768]{1,0:T(8,128)S(1)}, f32[24,768]{1,0:T(8,128)S(1)}, u32[]{:S(2)}, u32[]{:S(2)}) collective-permute-start(f32[24,768]{1,0:T(8,128)S(1)} %add_add_fusion.2), channel_id=1, source_target_pairs={{0,1},{1,0},{2,3},{3,2},{4,5},{5,4},{6,7},{7,6},{8,9},{9,8},{10,11... | collective-permute-start | bytes 221192 | tf_op jit(solution)/shard_map/ppermute | solution.py:47
  137.2 2.3 %collective-permute-done.25 = f32[24,768]{1,0:T(8,128)S(1)} collective-permute-done((f32[24,768]{1,0:T(8,128)S(1)}, f32[24,768]{1,0:T(8,128)S(1)}, u32[]{:S(2)}, u32[]{:S(2)}) %collective-permute-start.25) | collective-permute-done | bytes 73760 | tf_op jit(solution)/shard_map/ppermute | solution.py:47
  140.2 3.9 %collective-permute-done.12 = f32[64,768]{1,0:T(8,128)S(1)} collective-permute-done((f32[64,768]{1,0:T(8,128)S(1)}, f32[64,768]{1,0:T(8,128)S(1)}, u32[]{:S(2)}, u32[]{:S(2)}) %collective-permute-start.12) | collective-permute-done | bytes 196640 | tf_op jit(solution)/shard_map/ppermute | solution.py:33
  144.4 10.3 %fusion.13 = f32[256,4096]{1,0:T(8,128)} fusion(f32[256,768]{1,0:T(8,128)S(1)} %bitcast.61, f32[4096,768]{1,0:T(8,128)} %all-gather.2.cloned.1.call-done), kind=kOutput, calls=%fused_computation.86 | convolution fusion | flops 4831838208 | bytes 17563648 | tf_op jit(solution)/shard_map/dot_general | solution.py:11
  154.6 2.4 %reduce_max.9 = f32[4096]{0:T(1024)S(1)} reduce(f32[256,4096]{1,0:T(8,128)} %fusion.13, f32[]{:T(128)} %constant.182.clone.1), dimensions={0}, to_apply=%region_0.1 | reduce | flops 1044480 | bytes 4210692 | tf_op jit(solution)/shard_map/reduce_max | solution.py:131
  161.2 2.2 %collective-permute-start.16 = (f32[4096]{0:T(1024)S(1)}, f32[4096]{0:T(1024)S(1)}, u32[]{:S(2)}, u32[]{:S(2)}) collective-permute-start(f32[4096]{0:T(1024)S(1)} %maximum_maximum_fusion.1), channel_id=1, source_target_pairs={{0,32},{8,40},{16,48},{24,56},{32,0},{40,8},{48,16},{56,24},{1,33}... | collective-permute-start | bytes 49160 | tf_op jit(solution)/shard_map/ppermute | solution.py:82
  163.5 3.0 %collective-permute-done.16 = f32[4096]{0:T(1024)S(1)} collective-permute-done((f32[4096]{0:T(1024)S(1)}, f32[4096]{0:T(1024)S(1)}, u32[]{:S(2)}, u32[]{:S(2)}) %collective-permute-start.16) | collective-permute-done | bytes 16416 | tf_op jit(solution)/shard_map/ppermute | solution.py:82
  166.5 2.5 %collective-permute-done.28 = f32[96,768]{1,0:T(8,128)S(1)} collective-permute-done((f32[96,768]{1,0:T(8,128)S(1)}, f32[96,768]{1,0:T(8,128)S(1)}, u32[]{:S(2)}, u32[]{:S(2)}) %collective-permute-start.28) | collective-permute-done | bytes 294944 | tf_op jit(solution)/shard_map/ppermute | solution.py:33
  169.0 2.4 %collective-permute-done.29 = f32[96,768]{1,0:T(8,128)S(1)} collective-permute-done((f32[96,768]{1,0:T(8,128)S(1)}, f32[96,768]{1,0:T(8,128)S(1)}, u32[]{:S(2)}, u32[]{:S(2)}) %collective-permute-start.29) | collective-permute-done | bytes 294944 | tf_op jit(solution)/shard_map/ppermute | solution.py:33
  171.5 5.0 %collective-permute-done.30 = f32[96,768]{1,0:T(8,128)S(1)} collective-permute-done((f32[96,768]{1,0:T(8,128)S(1)}, f32[96,768]{1,0:T(8,128)S(1)}, u32[]{:S(2)}, u32[]{:S(2)}) %collective-permute-start.30) | collective-permute-done | bytes 294944 | tf_op jit(solution)/shard_map/ppermute | solution.py:33
  176.8 10.8 %maximum_reduce_fusion = f32[384]{0:T(512)S(1)} fusion(f32[384,768]{1,0:T(8,128)S(1)} %bitcast.64, f32[4096,768]{1,0:T(8,128)} %all-gather.2.cloned.1.call-done, f32[4096]{0:T(1024)S(1)} %maximum_maximum_fusion), kind=kOutput, calls=%fused_computation.6 | convolution fusion | flops 7252475392 | bytes 13780480 | tf_op jit(solution)/shard_map/dot_general | solution.py:11
  188.5 3.9 %collective-permute-start.31 = (f32[384]{0:T(512)S(1)}, f32[384]{0:T(512)S(1)}, u32[]{:S(2)}, u32[]{:S(2)}) collective-permute-start(f32[384]{0:T(512)S(1)} %maximum_reduce_fusion), channel_id=1, source_target_pairs={{0,1},{1,0},{2,3},{3,2},{4,5},{5,4},{6,7},{7,6},{8,9},{9,8},{10,11... | collective-permute-start | bytes 4616 | tf_op jit(solution)/shard_map/ppermute | solution.py:47
  192.5 1.5 collective-permute-done.31
  195.6 3.2 %collective-permute-start.34 = (f32[384]{0:T(512)S(1)}, f32[384]{0:T(512)S(1)}, u32[]{:S(2)}, u32[]{:S(2)}) collective-permute-start(f32[384]{0:T(512)S(1)} %select_reduce_fusion.1), channel_id=1, source_target_pairs={{0,2},{1,3},{2,0},{3,1},{4,6},{5,7},{6,4},{7,5},{8,10},{9,11},{10,... | collective-permute-start | bytes 4616 | tf_op jit(solution)/shard_map/ppermute | solution.py:95
  (126 shorter events, 25.3 us)
Async XLA Ops:
  7.2 72.3 %all-gather.2.cloned.1.call-start = ((), (), s32[]{:S(2)}) async-start(), calls=%async_computation | async-start | bytes 14155776 | tf_op jit(solution)/shard_map/all_gather | solution.py:122
  86.5 12.4 %collective-permute-start.3 = (f32[64,768]{1,0:T(8,128)}, f32[64,768]{1,0:T(8,128)S(1)}, u32[]{:S(2)}, u32[]{:S(2)}) collective-permute-start(f32[64,768]{1,0:T(8,128)} %get-tuple-element.9), channel_id=1, source_target_pairs={{0,6},{1,7},{2,0},{3,1},{4,2},{5,3},{6,4},{7,5},{8,14},{9,15},{10,... | collective-permute-start | bytes 589832 | tf_op jit(solution)/shard_map/ppermute | solution.py:33
  89.2 9.6 %collective-permute-start.2 = (f32[64,768]{1,0:T(8,128)}, f32[64,768]{1,0:T(8,128)}, u32[]{:S(2)}, u32[]{:S(2)}) collective-permute-start(f32[64,768]{1,0:T(8,128)} %get-tuple-element.10), channel_id=1, source_target_pairs={{0,4},{1,5},{2,6},{3,7},{4,0},{5,1},{6,2},{7,3},{8,12},{9,13},{10,... | collective-permute-start | bytes 589832 | tf_op jit(solution)/shard_map/ppermute | solution.py:33
  90.0 12.0 %collective-permute-start.1 = (f32[64,768]{1,0:T(8,128)S(1)}, f32[64,768]{1,0:T(8,128)}, u32[]{:S(2)}, u32[]{:S(2)}) collective-permute-start(f32[64,768]{1,0:T(8,128)S(1)} %get-tuple-element.8), channel_id=1, source_target_pairs={{0,2},{1,3},{2,4},{3,5},{4,6},{5,7},{6,0},{7,1},{8,10},{9,11},{10,... | collective-permute-start | bytes 589832 | tf_op jit(solution)/shard_map/ppermute | solution.py:33
  103.1 5.6 %collective-permute-start.6 = (f32[16,768]{1,0:T(8,128)S(1)}, f32[16,768]{1,0:T(8,128)S(1)}, u32[]{:S(2)}, u32[]{:S(2)}) collective-permute-start(f32[16,768]{1,0:T(8,128)S(1)} %get-tuple-element.15), channel_id=1, source_target_pairs={{0,65},{1,64},{2,67},{3,66},{4,69},{5,68},{6,71},{7,70},{64,1},{65... | collective-permute-start | bytes 147464 | tf_op jit(solution)/shard_map/ppermute | solution.py:51
  106.2 10.9 %collective-permute-start.21 = (f32[96,768]{1,0:T(8,128)S(1)}, f32[96,768]{1,0:T(8,128)S(1)}, u32[]{:S(2)}, u32[]{:S(2)}) collective-permute-start(f32[96,768]{1,0:T(8,128)S(1)} %get-tuple-element.6), channel_id=1, source_target_pairs={{0,6},{1,7},{2,0},{3,1},{4,2},{5,3},{6,4},{7,5},{8,14},{9,15},{10,... | collective-permute-start | bytes 884744 | tf_op jit(solution)/shard_map/ppermute | solution.py:33
  106.9 12.2 %collective-permute-start.20 = (f32[96,768]{1,0:T(8,128)S(1)}, f32[96,768]{1,0:T(8,128)S(1)}, u32[]{:S(2)}, u32[]{:S(2)}) collective-permute-start(f32[96,768]{1,0:T(8,128)S(1)} %get-tuple-element.7), channel_id=1, source_target_pairs={{0,4},{1,5},{2,6},{3,7},{4,0},{5,1},{6,2},{7,3},{8,12},{9,13},{10,... | collective-permute-start | bytes 884744 | tf_op jit(solution)/shard_map/ppermute | solution.py:33
  107.7 15.1 %collective-permute-start.19 = (f32[96,768]{1,0:T(8,128)S(1)}, f32[96,768]{1,0:T(8,128)S(1)}, u32[]{:S(2)}, u32[]{:S(2)}) collective-permute-start(f32[96,768]{1,0:T(8,128)S(1)} %get-tuple-element.5), channel_id=1, source_target_pairs={{0,2},{1,3},{2,4},{3,5},{4,6},{5,7},{6,0},{7,1},{8,10},{9,11},{10,... | collective-permute-start | bytes 884744 | tf_op jit(solution)/shard_map/ppermute | solution.py:33
  108.5 4.3 %collective-permute-start.5 = (f32[16,768]{1,0:T(8,128)S(1)}, f32[16,768]{1,0:T(8,128)S(1)}, u32[]{:S(2)}, u32[]{:S(2)}) collective-permute-start(f32[16,768]{1,0:T(8,128)S(1)} %get-tuple-element.16), channel_id=1, source_target_pairs={{0,64},{64,0},{1,65},{65,1},{2,66},{66,2},{3,67},{67,3},{4,68},{68... | collective-permute-start | bytes 147464 | tf_op jit(solution)/shard_map/ppermute | solution.py:49
  108.7 5.6 %collective-permute-start.4 = (f32[16,768]{1,0:T(8,128)S(1)}, f32[16,768]{1,0:T(8,128)S(1)}, u32[]{:S(2)}, u32[]{:S(2)}) collective-permute-start(f32[16,768]{1,0:T(8,128)S(1)} %get-tuple-element.14), channel_id=1, source_target_pairs={{0,1},{1,0},{2,3},{3,2},{4,5},{5,4},{6,7},{7,6},{8,9},{9,8},{10,11... | collective-permute-start | bytes 147464 | tf_op jit(solution)/shard_map/ppermute | solution.py:47
  114.3 9.4 %collective-permute-start.9 = (f32[16,768]{1,0:T(8,128)S(1)}, f32[16,768]{1,0:T(8,128)S(1)}, u32[]{:S(2)}, u32[]{:S(2)}) collective-permute-start(f32[16,768]{1,0:T(8,128)S(1)} %add_add_fusion.3), channel_id=1, source_target_pairs={{0,65},{1,64},{2,67},{3,66},{4,69},{5,68},{6,71},{7,70},{64,1},{65... | collective-permute-start | bytes 147464 | tf_op jit(solution)/shard_map/ppermute | solution.py:51
  117.2 10.6 %collective-permute-start.8 = (f32[16,768]{1,0:T(8,128)S(1)}, f32[16,768]{1,0:T(8,128)S(1)}, u32[]{:S(2)}, u32[]{:S(2)}) collective-permute-start(f32[16,768]{1,0:T(8,128)S(1)} %add_add_fusion.3), channel_id=1, source_target_pairs={{0,64},{64,0},{1,65},{65,1},{2,66},{66,2},{3,67},{67,3},{4,68},{68... | collective-permute-start | bytes 147464 | tf_op jit(solution)/shard_map/ppermute | solution.py:49
  117.2 10.6 %collective-permute-start.7 = (f32[16,768]{1,0:T(8,128)S(1)}, f32[16,768]{1,0:T(8,128)S(1)}, u32[]{:S(2)}, u32[]{:S(2)}) collective-permute-start(f32[16,768]{1,0:T(8,128)S(1)} %add_add_fusion.3), channel_id=1, source_target_pairs={{0,1},{1,0},{2,3},{3,2},{4,5},{5,4},{6,7},{7,6},{8,9},{9,8},{10,11... | collective-permute-start | bytes 147464 | tf_op jit(solution)/shard_map/ppermute | solution.py:47
  123.0 7.0 %collective-permute-start.24 = (f32[24,768]{1,0:T(8,128)S(1)}, f32[24,768]{1,0:T(8,128)S(1)}, u32[]{:S(2)}, u32[]{:S(2)}) collective-permute-start(f32[24,768]{1,0:T(8,128)S(1)} %get-tuple-element.12), channel_id=1, source_target_pairs={{0,65},{1,64},{2,67},{3,66},{4,69},{5,68},{6,71},{7,70},{64,1},{65... | collective-permute-start | bytes 221192 | tf_op jit(solution)/shard_map/ppermute | solution.py:51
  123.4 6.6 %collective-permute-start.23 = (f32[24,768]{1,0:T(8,128)S(1)}, f32[24,768]{1,0:T(8,128)S(1)}, u32[]{:S(2)}, u32[]{:S(2)}) collective-permute-start(f32[24,768]{1,0:T(8,128)S(1)} %get-tuple-element.13), channel_id=1, source_target_pairs={{0,64},{64,0},{1,65},{65,1},{2,66},{66,2},{3,67},{67,3},{4,68},{68... | collective-permute-start | bytes 221192 | tf_op jit(solution)/shard_map/ppermute | solution.py:49
  123.7 7.5 %collective-permute-start.22 = (f32[24,768]{1,0:T(8,128)S(1)}, f32[24,768]{1,0:T(8,128)S(1)}, u32[]{:S(2)}, u32[]{:S(2)}) collective-permute-start(f32[24,768]{1,0:T(8,128)S(1)} %get-tuple-element.11), channel_id=1, source_target_pairs={{0,1},{1,0},{2,3},{3,2},{4,5},{5,4},{6,7},{7,6},{8,9},{9,8},{10,11... | collective-permute-start | bytes 221192 | tf_op jit(solution)/shard_map/ppermute | solution.py:47
  128.4 11.7 %collective-permute-start.10 = (f32[64,768]{1,0:T(8,128)S(1)}, f32[64,768]{1,0:T(8,128)S(1)}, u32[]{:S(2)}, u32[]{:S(2)}) collective-permute-start(f32[64,768]{1,0:T(8,128)S(1)} %bitcast_select_fusion.2), channel_id=1, source_target_pairs={{0,6},{1,7},{2,0},{3,1},{4,2},{5,3},{6,4},{7,5},{8,14},{9,15},{10,... | collective-permute-start | bytes 589832 | tf_op jit(solution)/shard_map/ppermute | solution.py:33
  129.6 10.6 %collective-permute-start.11 = (f32[64,768]{1,0:T(8,128)S(1)}, f32[64,768]{1,0:T(8,128)S(1)}, u32[]{:S(2)}, u32[]{:S(2)}) collective-permute-start(f32[64,768]{1,0:T(8,128)S(1)} %bitcast_select_fusion.2), channel_id=1, source_target_pairs={{0,4},{1,5},{2,6},{3,7},{4,0},{5,1},{6,2},{7,3},{8,12},{9,13},{10,... | collective-permute-start | bytes 589832 | tf_op jit(solution)/shard_map/ppermute | solution.py:33
  131.2 6.0 %collective-permute-start.27 = (f32[24,768]{1,0:T(8,128)S(1)}, f32[24,768]{1,0:T(8,128)S(1)}, u32[]{:S(2)}, u32[]{:S(2)}) collective-permute-start(f32[24,768]{1,0:T(8,128)S(1)} %add_add_fusion.2), channel_id=1, source_target_pairs={{0,65},{1,64},{2,67},{3,66},{4,69},{5,68},{6,71},{7,70},{64,1},{65... | collective-permute-start | bytes 221192 | tf_op jit(solution)/shard_map/ppermute | solution.py:51
  132.3 5.0 %collective-permute-start.26 = (f32[24,768]{1,0:T(8,128)S(1)}, f32[24,768]{1,0:T(8,128)S(1)}, u32[]{:S(2)}, u32[]{:S(2)}) collective-permute-start(f32[24,768]{1,0:T(8,128)S(1)} %add_add_fusion.2), channel_id=1, source_target_pairs={{0,64},{64,0},{1,65},{65,1},{2,66},{66,2},{3,67},{67,3},{4,68},{68... | collective-permute-start | bytes 221192 | tf_op jit(solution)/shard_map/ppermute | solution.py:49
  133.7 5.9 %collective-permute-start.25 = (f32[24,768]{1,0:T(8,128)S(1)}, f32[24,768]{1,0:T(8,128)S(1)}, u32[]{:S(2)}, u32[]{:S(2)}) collective-permute-start(f32[24,768]{1,0:T(8,128)S(1)} %add_add_fusion.2), channel_id=1, source_target_pairs={{0,1},{1,0},{2,3},{3,2},{4,5},{5,4},{6,7},{7,6},{8,9},{9,8},{10,11... | collective-permute-start | bytes 221192 | tf_op jit(solution)/shard_map/ppermute | solution.py:47
  137.2 6.9 %collective-permute-start.12 = (f32[64,768]{1,0:T(8,128)S(1)}, f32[64,768]{1,0:T(8,128)S(1)}, u32[]{:S(2)}, u32[]{:S(2)}) collective-permute-start(f32[64,768]{1,0:T(8,128)S(1)} %bitcast_select_fusion.2), channel_id=1, source_target_pairs={{0,2},{1,3},{2,4},{3,5},{4,6},{5,7},{6,0},{7,1},{8,10},{9,11},{10,... | collective-permute-start | bytes 589832 | tf_op jit(solution)/shard_map/ppermute | solution.py:33
  159.1 9.9 %collective-permute-start.28 = (f32[96,768]{1,0:T(8,128)S(1)}, f32[96,768]{1,0:T(8,128)S(1)}, u32[]{:S(2)}, u32[]{:S(2)}) collective-permute-start(f32[96,768]{1,0:T(8,128)S(1)} %bitcast_select_fusion), channel_id=1, source_target_pairs={{0,6},{1,7},{2,0},{3,1},{4,2},{5,3},{6,4},{7,5},{8,14},{9,15},{10,... | collective-permute-start | bytes 884744 | tf_op jit(solution)/shard_map/ppermute | solution.py:33
  160.0 11.5 %collective-permute-start.29 = (f32[96,768]{1,0:T(8,128)S(1)}, f32[96,768]{1,0:T(8,128)S(1)}, u32[]{:S(2)}, u32[]{:S(2)}) collective-permute-start(f32[96,768]{1,0:T(8,128)S(1)} %bitcast_select_fusion), channel_id=1, source_target_pairs={{0,4},{1,5},{2,6},{3,7},{4,0},{5,1},{6,2},{7,3},{8,12},{9,13},{10,... | collective-permute-start | bytes 884744 | tf_op jit(solution)/shard_map/ppermute | solution.py:33
  160.3 16.2 %collective-permute-start.30 = (f32[96,768]{1,0:T(8,128)S(1)}, f32[96,768]{1,0:T(8,128)S(1)}, u32[]{:S(2)}, u32[]{:S(2)}) collective-permute-start(f32[96,768]{1,0:T(8,128)S(1)} %bitcast_select_fusion), channel_id=1, source_target_pairs={{0,2},{1,3},{2,4},{3,5},{4,6},{5,7},{6,0},{7,1},{8,10},{9,11},{10,... | collective-permute-start | bytes 884744 | tf_op jit(solution)/shard_map/ppermute | solution.py:33
  161.2 5.3 %collective-permute-start.16 = (f32[4096]{0:T(1024)S(1)}, f32[4096]{0:T(1024)S(1)}, u32[]{:S(2)}, u32[]{:S(2)}) collective-permute-start(f32[4096]{0:T(1024)S(1)} %maximum_maximum_fusion.1), channel_id=1, source_target_pairs={{0,32},{8,40},{16,48},{24,56},{32,0},{40,8},{48,16},{56,24},{1,33}... | collective-permute-start | bytes 49160 | tf_op jit(solution)/shard_map/ppermute | solution.py:82
  187.6 4.9 %collective-permute-start.33 = (f32[384]{0:T(512)S(1)}, f32[384]{0:T(512)S(1)}, u32[]{:S(2)}, u32[]{:S(2)}) collective-permute-start(f32[384]{0:T(512)S(1)} %maximum_reduce_fusion), channel_id=1, source_target_pairs={{0,65},{1,64},{2,67},{3,66},{4,69},{5,68},{6,71},{7,70},{64,1},{65... | collective-permute-start | bytes 4616 | tf_op jit(solution)/shard_map/ppermute | solution.py:51
  188.5 5.5 %collective-permute-start.31 = (f32[384]{0:T(512)S(1)}, f32[384]{0:T(512)S(1)}, u32[]{:S(2)}, u32[]{:S(2)}) collective-permute-start(f32[384]{0:T(512)S(1)} %maximum_reduce_fusion), channel_id=1, source_target_pairs={{0,1},{1,0},{2,3},{3,2},{4,5},{5,4},{6,7},{7,6},{8,9},{9,8},{10,11... | collective-permute-start | bytes 4616 | tf_op jit(solution)/shard_map/ppermute | solution.py:47
  192.4 6.4 %collective-permute-start.17 = (f32[4096]{0:T(1024)S(1)}, f32[4096]{0:T(1024)S(1)}, u32[]{:S(2)}, u32[]{:S(2)}) collective-permute-start(f32[4096]{0:T(1024)S(1)} %maximum_maximum_fusion), channel_id=1, source_target_pairs={{0,64},{64,0},{1,65},{65,1},{2,66},{66,2},{3,67},{67,3},{4,68},{68... | collective-permute-start | bytes 49160 | tf_op jit(solution)/shard_map/ppermute | solution.py:137
  194.6 4.8 %collective-permute-start.36 = (f32[384]{0:T(512)S(1)}, f32[384]{0:T(512)S(1)}, u32[]{:S(2)}, u32[]{:S(2)}) collective-permute-start(f32[384]{0:T(512)S(1)} %select_reduce_fusion.1), channel_id=1, source_target_pairs={{0,6},{1,7},{2,4},{3,5},{4,2},{5,3},{6,0},{7,1},{8,14},{9,15},{10,... | collective-permute-start | bytes 4616 | tf_op jit(solution)/shard_map/ppermute | solution.py:95
  195.4 5.1 %collective-permute-start.35 = (f32[384]{0:T(512)S(1)}, f32[384]{0:T(512)S(1)}, u32[]{:S(2)}, u32[]{:S(2)}) collective-permute-start(f32[384]{0:T(512)S(1)} %select_reduce_fusion.1), channel_id=1, source_target_pairs={{0,4},{1,5},{2,6},{3,7},{4,0},{5,1},{6,2},{7,3},{8,12},{9,13},{10,... | collective-permute-start | bytes 4616 | tf_op jit(solution)/shard_map/ppermute | solution.py:95
  195.6 4.9 %collective-permute-start.34 = (f32[384]{0:T(512)S(1)}, f32[384]{0:T(512)S(1)}, u32[]{:S(2)}, u32[]{:S(2)}) collective-permute-start(f32[384]{0:T(512)S(1)} %select_reduce_fusion.1), channel_id=1, source_target_pairs={{0,2},{1,3},{2,0},{3,1},{4,6},{5,7},{6,4},{7,5},{8,10},{9,11},{10,... | collective-permute-start | bytes 4616 | tf_op jit(solution)/shard_map/ppermute | solution.py:95
  (9 other events, 37.0 us)
Sparse Core Ops, SparseCore 0:
  9.7 69.7 all-gather.1

commit v23 on v18

--- a/solution.py
+++ b/solution.py
@@ -78,7 +78,7 @@
 
 
 def all_max_two_rounds(value, axis, n):
-    for bits in ((1, 2, 3), (4,)):
+    for bits in (tuple(range(1, n)),):
         received = [lax.ppermute(value, axis, [(i, i ^ k) for i in range(n)]) for k in bits]
         for other in received:
             value = jnp.maximum(value, other)

time: 209 us -> 216 us (1.033)
  starting transfers between devices: 44.7 us -> 48.9 us
  waiting for transfers between devices: 105 us -> 108 us
    ppermute x12, waiting for transfers between devices: 21.3 us -> 25.8 us  [y_shift(): return lax.ppermute(value, 'col', pairs)]
    ppermute x4 -> x7, starting transfers between devices: 4.13 us -> 8.12 us  [all_max_two_rounds(): lax.ppermute(value, axis, [(i, i ^ k) for i in range(n)])]
  transfers between devices with their start and end apart: 38 -> 41, of which waited for: 21 -> 21; matrix products, arithmetic and copies ran while one was open for 10% -> 10% of each run, Pallas kernels for 0% -> 0%
where the time goes in v23:
time: 216 us; the launch traced here: 215 us
  waiting for transfers between devices  108 us (50%)
  starting transfers between devices  48.9 us (23%)
  matrix products  21.1 us (10%)
  local copies, waits for them, and re-layouts  17.6 us (8%)
  between operations  14.5 us (7%)
  other arithmetic  5.6 us (3%)
    all_gather x1, waiting for transfers between devices, body(): half = lax.all_gather(slab_embed, 'xc', axis=0, tiled=True)  65.7 us
    ppermute x12, waiting for transfers between devices, y_shift(): return lax.ppermute(value, 'col', pairs)  25.8 us
    dot_general x2, matrix products, similar(): lax.dot_general(left, right, (((1,), (1,)), ((), ())), precision=lax.Prec...  21.1 us
    ppermute x5, starting transfers between devices, z_group_shift(): return lax.ppermute(value, 'col', [(c, c ^ 1) for c in range(N_Y * N_Z)])  14.1 us
    gather x2, local copies, waits for them, and re-layouts, lookup(): jnp.take(source, jnp.clip(position, 0, source.shape[0] - 1), axis=0)  13 us
    ppermute x12, starting transfers between devices, y_shift(): return lax.ppermute(value, 'col', pairs)  10.3 us
    ppermute x7, starting transfers between devices, all_max_two_rounds(): lax.ppermute(value, axis, [(i, i ^ k) for i in range(n)])  8.12 us
    ppermute x5, starting transfers between devices, z_group_shift(): lax.ppermute(value, ('zl', 'col'), [(i, i ^ N_Y * N_Z ^ 1) for i in range...  8.03 us
  transfers between devices with their start and end apart: 41, of which 21 were waited for; matrix products, arithmetic and copies ran while one was open for 10% of the time, Pallas kernels for 0%

profile of v23, /device:TPU:0, one launch (start us, length us, event | category | flops | bytes accessed | tf_op | source)
XLA Modules:
  0.0 215.2 jit_solution(15100742622403666364)
XLA Ops:
  7.9 2.1 collective-permute-start
  10.2 1.3 collective-permute-done
  11.6 2.0 collective-permute-done.21
  13.8 65.7 %all-gather.2.cloned.1.call-done = f32[4096,768]{1,0:T(8,128)} async-done(((f32[512,768]{1,0:T(8,128)}), f32[4096,768]{1,0:T(8,128)}) %all-gather.2.cloned.1.call-update) | async-done | bytes 12582928 | tf_op jit(solution)/shard_map/all_gather | solution.py:122
  79.5 6.0 %gather_fusion = f32[256,768]{1,0:T(8,128)S(1)} fusion(f32[4096,768]{1,0:T(8,128)} %all-gather.2.cloned.1.call-done, s32[1024]{0:T(1024)S(1)} %pad_clamp_fusion.3), kind=kCustom, calls=%fused_computation | custom fusion | bytes 1573888 | tf_op jit(solution)/shard_map/jit(_take)/gather | solution.py:23
  86.5 2.7 %collective-permute-start.3 = (f32[64,768]{1,0:T(8,128)}, f32[64,768]{1,0:T(8,128)S(1)}, u32[]{:S(2)}, u32[]{:S(2)}) collective-permute-start(f32[64,768]{1,0:T(8,128)} %get-tuple-element.8), channel_id=1, source_target_pairs={{0,6},{1,7},{2,0},{3,1},{4,2},{5,3},{6,4},{7,5},{8,14},{9,15},{10,... | collective-permute-start | bytes 589832 | tf_op jit(solution)/shard_map/ppermute | solution.py:33
  90.9 7.1 %gather_fusion.2 = f32[384,768]{1,0:T(8,128)S(1)} fusion(f32[4096,768]{1,0:T(8,128)} %all-gather.2.cloned.1.call-done, s32[1024]{0:T(1024)S(1)} %pad_clamp_fusion.1), kind=kCustom, calls=%fused_computation.2 | custom fusion | bytes 2360832 | tf_op jit(solution)/shard_map/jit(_take)/gather | solution.py:23
  98.8 3.2 %collective-permute-done.1 = f32[64,768]{1,0:T(8,128)} collective-permute-done((f32[64,768]{1,0:T(8,128)S(1)}, f32[64,768]{1,0:T(8,128)}, u32[]{:S(2)}, u32[]{:S(2)}) %collective-permute-start.1) | collective-permute-done | bytes 196640 | tf_op jit(solution)/shard_map/ppermute | solution.py:33
  103.1 3.0 %collective-permute-start.6 = (f32[16,768]{1,0:T(8,128)S(1)}, f32[16,768]{1,0:T(8,128)S(1)}, u32[]{:S(2)}, u32[]{:S(2)}) collective-permute-start(f32[16,768]{1,0:T(8,128)S(1)} %get-tuple-element.14), channel_id=1, source_target_pairs={{0,65},{1,64},{2,67},{3,66},{4,69},{5,68},{6,71},{7,70},{64,1},{65... | collective-permute-start | bytes 147464 | tf_op jit(solution)/shard_map/ppermute | solution.py:51
  108.7 1.8 collective-permute-start.4
  110.8 2.0 collective-permute-done.5
  112.8 1.5 collective-permute-done.4
  114.3 2.8 %collective-permute-start.9 = (f32[16,768]{1,0:T(8,128)S(1)}, f32[16,768]{1,0:T(8,128)S(1)}, u32[]{:S(2)}, u32[]{:S(2)}) collective-permute-start(f32[16,768]{1,0:T(8,128)S(1)} %add_add_fusion.3), channel_id=1, source_target_pairs={{0,65},{1,64},{2,67},{3,66},{4,69},{5,68},{6,71},{7,70},{64,1},{65... | collective-permute-start | bytes 147464 | tf_op jit(solution)/shard_map/ppermute | solution.py:51
  117.2 1.9 collective-permute-start.7
  119.1 3.8 %collective-permute-done.22 = f32[96,768]{1,0:T(8,128)S(1)} collective-permute-done((f32[96,768]{1,0:T(8,128)S(1)}, f32[96,768]{1,0:T(8,128)S(1)}, u32[]{:S(2)}, u32[]{:S(2)}) %collective-permute-start.22) | collective-permute-done | bytes 294944 | tf_op jit(solution)/shard_map/ppermute | solution.py:33
  123.7 4.1 %collective-permute-start.25 = (f32[24,768]{1,0:T(8,128)S(1)}, f32[24,768]{1,0:T(8,128)S(1)}, u32[]{:S(2)}, u32[]{:S(2)}) collective-permute-start(f32[24,768]{1,0:T(8,128)S(1)} %get-tuple-element.10), channel_id=1, source_target_pairs={{0,1},{1,0},{2,3},{3,2},{4,5},{5,4},{6,7},{7,6},{8,9},{9,8},{10,11... | collective-permute-start | bytes 221192 | tf_op jit(solution)/shard_map/ppermute | solution.py:47
  129.9 1.3 collective-permute-done.25
  132.2 1.4 collective-permute-start.29
  133.7 2.3 %collective-permute-start.28 = (f32[24,768]{1,0:T(8,128)S(1)}, f32[24,768]{1,0:T(8,128)S(1)}, u32[]{:S(2)}, u32[]{:S(2)}) collective-permute-start(f32[24,768]{1,0:T(8,128)S(1)} %add_add_fusion.2), channel_id=1, source_target_pairs={{0,1},{1,0},{2,3},{3,2},{4,5},{5,4},{6,7},{7,6},{8,9},{9,8},{10,11... | collective-permute-start | bytes 221192 | tf_op jit(solution)/shard_map/ppermute | solution.py:47
  137.2 2.3 %collective-permute-done.28 = f32[24,768]{1,0:T(8,128)S(1)} collective-permute-done((f32[24,768]{1,0:T(8,128)S(1)}, f32[24,768]{1,0:T(8,128)S(1)}, u32[]{:S(2)}, u32[]{:S(2)}) %collective-permute-start.28) | collective-permute-done | bytes 73760 | tf_op jit(solution)/shard_map/ppermute | solution.py:47
  140.2 3.9 %collective-permute-done.12 = f32[64,768]{1,0:T(8,128)S(1)} collective-permute-done((f32[64,768]{1,0:T(8,128)S(1)}, f32[64,768]{1,0:T(8,128)S(1)}, u32[]{:S(2)}, u32[]{:S(2)}) %collective-permute-start.12) | collective-permute-done | bytes 196640 | tf_op jit(solution)/shard_map/ppermute | solution.py:33
  144.3 10.3 %fusion.14 = f32[256,4096]{1,0:T(8,128)} fusion(f32[256,768]{1,0:T(8,128)S(1)} %bitcast.68, f32[4096,768]{1,0:T(8,128)} %all-gather.2.cloned.1.call-done), kind=kOutput, calls=%fused_computation.87 | convolution fusion | flops 4831838208 | bytes 17563648 | tf_op jit(solution)/shard_map/dot_general | solution.py:11
  154.6 2.4 %reduce_max.9 = f32[4096]{0:T(1024)S(1)} reduce(f32[256,4096]{1,0:T(8,128)} %fusion.14, f32[]{:T(128)} %constant.196.clone.1), dimensions={0}, to_apply=%region_0.1 | reduce | flops 1044480 | bytes 4210692 | tf_op jit(solution)/shard_map/reduce_max | solution.py:131
  158.4 2.3 %collective-permute-start.17 = (f32[4096]{0:T(1024)S(1)}, f32[4096]{0:T(1024)S(1)}, u32[]{:S(2)}, u32[]{:S(2)}) collective-permute-start(f32[4096]{0:T(1024)S(1)} %reduce_max.9), channel_id=1, source_target_pairs={{0,40},{8,32},{16,56},{24,48},{32,8},{40,0},{48,24},{56,16},{1,41}... | collective-permute-start | bytes 49160 | tf_op jit(solution)/shard_map/ppermute | solution.py:82
  161.7 2.6 %collective-permute-start.16 = (f32[4096]{0:T(1024)S(1)}, f32[4096]{0:T(1024)S(1)}, u32[]{:S(2)}, u32[]{:S(2)}) collective-permute-start(f32[4096]{0:T(1024)S(1)} %reduce_max.9), channel_id=1, source_target_pairs={{0,32},{8,40},{16,48},{24,56},{32,0},{40,8},{48,16},{56,24},{1,33}... | collective-permute-start | bytes 49160 | tf_op jit(solution)/shard_map/ppermute | solution.py:82
  164.4 1.8 collective-permute-start.13
  168.8 1.4 collective-permute-done.31
  170.2 8.2 %collective-permute-done.32 = f32[96,768]{1,0:T(8,128)S(1)} collective-permute-done((f32[96,768]{1,0:T(8,128)S(1)}, f32[96,768]{1,0:T(8,128)S(1)}, u32[]{:S(2)}, u32[]{:S(2)}) %collective-permute-start.32) | collective-permute-done | bytes 294944 | tf_op jit(solution)/shard_map/ppermute | solution.py:33
  178.5 4.7 %collective-permute-done.33 = f32[96,768]{1,0:T(8,128)S(1)} collective-permute-done((f32[96,768]{1,0:T(8,128)S(1)}, f32[96,768]{1,0:T(8,128)S(1)}, u32[]{:S(2)}, u32[]{:S(2)}) %collective-permute-start.33) | collective-permute-done | bytes 294944 | tf_op jit(solution)/shard_map/ppermute | solution.py:33
  183.4 10.8 %maximum_reduce_fusion = f32[384]{0:T(512)S(1)} fusion(f32[384,768]{1,0:T(8,128)S(1)} %bitcast.71, f32[4096,768]{1,0:T(8,128)} %all-gather.2.cloned.1.call-done, f32[4096]{0:T(1024)S(1)} %maximum_maximum_fusion), kind=kOutput, calls=%fused_computation.6 | convolution fusion | flops 7252475392 | bytes 13780480 | tf_op jit(solution)/shard_map/dot_general | solution.py:11
  195.0 4.0 %collective-permute-start.34 = (f32[384]{0:T(512)S(1)}, f32[384]{0:T(512)S(1)}, u32[]{:S(2)}, u32[]{:S(2)}) collective-permute-start(f32[384]{0:T(512)S(1)} %maximum_reduce_fusion), channel_id=1, source_target_pairs={{0,1},{1,0},{2,3},{3,2},{4,5},{5,4},{6,7},{7,6},{8,9},{9,8},{10,11... | collective-permute-start | bytes 4616 | tf_op jit(solution)/shard_map/ppermute | solution.py:47
  202.2 3.2 %collective-permute-start.37 = (f32[4,384]{1,0:T(4,128)S(1)}, f32[4,384]{1,0:T(4,128)S(1)}, u32[]{:S(2)}, u32[]{:S(2)}) collective-permute-start(f32[4,384]{1,0:T(4,128)S(1)} %broadcast_select_fusion), channel_id=1, source_target_pairs={{0,2},{1,3},{2,0},{3,1},{4,6},{5,7},{6,4},{7,5},{8,10},{9,11},{10,... | collective-permute-start | bytes 18440 | tf_op jit(solution)/shard_map/ppermute | solution.py:95
  (126 shorter events, 26.8 us)
Async XLA Ops:
  7.2 72.3 %all-gather.2.cloned.1.call-start = ((), (), s32[]{:S(2)}) async-start(), calls=%async_computation | async-start | bytes 14155776 | tf_op jit(solution)/shard_map/all_gather | solution.py:122
  86.5 11.9 %collective-permute-start.3 = (f32[64,768]{1,0:T(8,128)}, f32[64,768]{1,0:T(8,128)S(1)}, u32[]{:S(2)}, u32[]{:S(2)}) collective-permute-start(f32[64,768]{1,0:T(8,128)} %get-tuple-element.8), channel_id=1, source_target_pairs={{0,6},{1,7},{2,0},{3,1},{4,2},{5,3},{6,4},{7,5},{8,14},{9,15},{10,... | collective-permute-start | bytes 589832 | tf_op jit(solution)/shard_map/ppermute | solution.py:33
  89.2 9.6 %collective-permute-start.2 = (f32[64,768]{1,0:T(8,128)}, f32[64,768]{1,0:T(8,128)}, u32[]{:S(2)}, u32[]{:S(2)}) collective-permute-start(f32[64,768]{1,0:T(8,128)} %get-tuple-element.9), channel_id=1, source_target_pairs={{0,4},{1,5},{2,6},{3,7},{4,0},{5,1},{6,2},{7,3},{8,12},{9,13},{10,... | collective-permute-start | bytes 589832 | tf_op jit(solution)/shard_map/ppermute | solution.py:33
  90.0 12.0 %collective-permute-start.1 = (f32[64,768]{1,0:T(8,128)S(1)}, f32[64,768]{1,0:T(8,128)}, u32[]{:S(2)}, u32[]{:S(2)}) collective-permute-start(f32[64,768]{1,0:T(8,128)S(1)} %get-tuple-element.7), channel_id=1, source_target_pairs={{0,2},{1,3},{2,4},{3,5},{4,6},{5,7},{6,0},{7,1},{8,10},{9,11},{10,... | collective-permute-start | bytes 589832 | tf_op jit(solution)/shard_map/ppermute | solution.py:33
  103.1 5.6 %collective-permute-start.6 = (f32[16,768]{1,0:T(8,128)S(1)}, f32[16,768]{1,0:T(8,128)S(1)}, u32[]{:S(2)}, u32[]{:S(2)}) collective-permute-start(f32[16,768]{1,0:T(8,128)S(1)} %get-tuple-element.14), channel_id=1, source_target_pairs={{0,65},{1,64},{2,67},{3,66},{4,69},{5,68},{6,71},{7,70},{64,1},{65... | collective-permute-start | bytes 147464 | tf_op jit(solution)/shard_map/ppermute | solution.py:51
  106.2 10.9 %collective-permute-start.24 = (f32[96,768]{1,0:T(8,128)S(1)}, f32[96,768]{1,0:T(8,128)S(1)}, u32[]{:S(2)}, u32[]{:S(2)}) collective-permute-start(f32[96,768]{1,0:T(8,128)S(1)} %get-tuple-element.5), channel_id=1, source_target_pairs={{0,6},{1,7},{2,0},{3,1},{4,2},{5,3},{6,4},{7,5},{8,14},{9,15},{10,... | collective-permute-start | bytes 884744 | tf_op jit(solution)/shard_map/ppermute | solution.py:33
  106.9 12.2 %collective-permute-start.23 = (f32[96,768]{1,0:T(8,128)S(1)}, f32[96,768]{1,0:T(8,128)S(1)}, u32[]{:S(2)}, u32[]{:S(2)}) collective-permute-start(f32[96,768]{1,0:T(8,128)S(1)} %get-tuple-element.6), channel_id=1, source_target_pairs={{0,4},{1,5},{2,6},{3,7},{4,0},{5,1},{6,2},{7,3},{8,12},{9,13},{10,... | collective-permute-start | bytes 884744 | tf_op jit(solution)/shard_map/ppermute | solution.py:33
  107.7 15.1 %collective-permute-start.22 = (f32[96,768]{1,0:T(8,128)S(1)}, f32[96,768]{1,0:T(8,128)S(1)}, u32[]{:S(2)}, u32[]{:S(2)}) collective-permute-start(f32[96,768]{1,0:T(8,128)S(1)} %get-tuple-element.4), channel_id=1, source_target_pairs={{0,2},{1,3},{2,4},{3,5},{4,6},{5,7},{6,0},{7,1},{8,10},{9,11},{10,... | collective-permute-start | bytes 884744 | tf_op jit(solution)/shard_map/ppermute | solution.py:33
  108.7 5.6 %collective-permute-start.4 = (f32[16,768]{1,0:T(8,128)S(1)}, f32[16,768]{1,0:T(8,128)S(1)}, u32[]{:S(2)}, u32[]{:S(2)}) collective-permute-start(f32[16,768]{1,0:T(8,128)S(1)} %get-tuple-element.13), channel_id=1, source_target_pairs={{0,1},{1,0},{2,3},{3,2},{4,5},{5,4},{6,7},{7,6},{8,9},{9,8},{10,11... | collective-permute-start | bytes 147464 | tf_op jit(solution)/shard_map/ppermute | solution.py:47
  114.3 9.4 %collective-permute-start.9 = (f32[16,768]{1,0:T(8,128)S(1)}, f32[16,768]{1,0:T(8,128)S(1)}, u32[]{:S(2)}, u32[]{:S(2)}) collective-permute-start(f32[16,768]{1,0:T(8,128)S(1)} %add_add_fusion.3), channel_id=1, source_target_pairs={{0,65},{1,64},{2,67},{3,66},{4,69},{5,68},{6,71},{7,70},{64,1},{65... | collective-permute-start | bytes 147464 | tf_op jit(solution)/shard_map/ppermute | solution.py:51
  117.1 10.6 %collective-permute-start.8 = (f32[16,768]{1,0:T(8,128)S(1)}, f32[16,768]{1,0:T(8,128)S(1)}, u32[]{:S(2)}, u32[]{:S(2)}) collective-permute-start(f32[16,768]{1,0:T(8,128)S(1)} %add_add_fusion.3), channel_id=1, source_target_pairs={{0,64},{64,0},{1,65},{65,1},{2,66},{66,2},{3,67},{67,3},{4,68},{68... | collective-permute-start | bytes 147464 | tf_op jit(solution)/shard_map/ppermute | solution.py:49
  117.2 10.6 %collective-permute-start.7 = (f32[16,768]{1,0:T(8,128)S(1)}, f32[16,768]{1,0:T(8,128)S(1)}, u32[]{:S(2)}, u32[]{:S(2)}) collective-permute-start(f32[16,768]{1,0:T(8,128)S(1)} %add_add_fusion.3), channel_id=1, source_target_pairs={{0,1},{1,0},{2,3},{3,2},{4,5},{5,4},{6,7},{7,6},{8,9},{9,8},{10,11... | collective-permute-start | bytes 147464 | tf_op jit(solution)/shard_map/ppermute | solution.py:47
  123.0 7.0 %collective-permute-start.27 = (f32[24,768]{1,0:T(8,128)S(1)}, f32[24,768]{1,0:T(8,128)S(1)}, u32[]{:S(2)}, u32[]{:S(2)}) collective-permute-start(f32[24,768]{1,0:T(8,128)S(1)} %get-tuple-element.11), channel_id=1, source_target_pairs={{0,65},{1,64},{2,67},{3,66},{4,69},{5,68},{6,71},{7,70},{64,1},{65... | collective-permute-start | bytes 221192 | tf_op jit(solution)/shard_map/ppermute | solution.py:51
  123.3 6.6 %collective-permute-start.26 = (f32[24,768]{1,0:T(8,128)S(1)}, f32[24,768]{1,0:T(8,128)S(1)}, u32[]{:S(2)}, u32[]{:S(2)}) collective-permute-start(f32[24,768]{1,0:T(8,128)S(1)} %get-tuple-element.12), channel_id=1, source_target_pairs={{0,64},{64,0},{1,65},{65,1},{2,66},{66,2},{3,67},{67,3},{4,68},{68... | collective-permute-start | bytes 221192 | tf_op jit(solution)/shard_map/ppermute | solution.py:49
  123.7 7.5 %collective-permute-start.25 = (f32[24,768]{1,0:T(8,128)S(1)}, f32[24,768]{1,0:T(8,128)S(1)}, u32[]{:S(2)}, u32[]{:S(2)}) collective-permute-start(f32[24,768]{1,0:T(8,128)S(1)} %get-tuple-element.10), channel_id=1, source_target_pairs={{0,1},{1,0},{2,3},{3,2},{4,5},{5,4},{6,7},{7,6},{8,9},{9,8},{10,11... | collective-permute-start | bytes 221192 | tf_op jit(solution)/shard_map/ppermute | solution.py:47
  128.4 11.7 %collective-permute-start.10 = (f32[64,768]{1,0:T(8,128)S(1)}, f32[64,768]{1,0:T(8,128)S(1)}, u32[]{:S(2)}, u32[]{:S(2)}) collective-permute-start(f32[64,768]{1,0:T(8,128)S(1)} %bitcast_select_fusion.2), channel_id=1, source_target_pairs={{0,6},{1,7},{2,0},{3,1},{4,2},{5,3},{6,4},{7,5},{8,14},{9,15},{10,... | collective-permute-start | bytes 589832 | tf_op jit(solution)/shard_map/ppermute | solution.py:33
  129.6 10.6 %collective-permute-start.11 = (f32[64,768]{1,0:T(8,128)S(1)}, f32[64,768]{1,0:T(8,128)S(1)}, u32[]{:S(2)}, u32[]{:S(2)}) collective-permute-start(f32[64,768]{1,0:T(8,128)S(1)} %bitcast_select_fusion.2), channel_id=1, source_target_pairs={{0,4},{1,5},{2,6},{3,7},{4,0},{5,1},{6,2},{7,3},{8,12},{9,13},{10,... | collective-permute-start | bytes 589832 | tf_op jit(solution)/shard_map/ppermute | solution.py:33
  131.2 6.0 %collective-permute-start.30 = (f32[24,768]{1,0:T(8,128)S(1)}, f32[24,768]{1,0:T(8,128)S(1)}, u32[]{:S(2)}, u32[]{:S(2)}) collective-permute-start(f32[24,768]{1,0:T(8,128)S(1)} %add_add_fusion.2), channel_id=1, source_target_pairs={{0,65},{1,64},{2,67},{3,66},{4,69},{5,68},{6,71},{7,70},{64,1},{65... | collective-permute-start | bytes 221192 | tf_op jit(solution)/shard_map/ppermute | solution.py:51
  132.2 5.0 %collective-permute-start.29 = (f32[24,768]{1,0:T(8,128)S(1)}, f32[24,768]{1,0:T(8,128)S(1)}, u32[]{:S(2)}, u32[]{:S(2)}) collective-permute-start(f32[24,768]{1,0:T(8,128)S(1)} %add_add_fusion.2), channel_id=1, source_target_pairs={{0,64},{64,0},{1,65},{65,1},{2,66},{66,2},{3,67},{67,3},{4,68},{68... | collective-permute-start | bytes 221192 | tf_op jit(solution)/shard_map/ppermute | solution.py:49
  133.7 5.9 %collective-permute-start.28 = (f32[24,768]{1,0:T(8,128)S(1)}, f32[24,768]{1,0:T(8,128)S(1)}, u32[]{:S(2)}, u32[]{:S(2)}) collective-permute-start(f32[24,768]{1,0:T(8,128)S(1)} %add_add_fusion.2), channel_id=1, source_target_pairs={{0,1},{1,0},{2,3},{3,2},{4,5},{5,4},{6,7},{7,6},{8,9},{9,8},{10,11... | collective-permute-start | bytes 221192 | tf_op jit(solution)/shard_map/ppermute | solution.py:47
  137.2 6.9 %collective-permute-start.12 = (f32[64,768]{1,0:T(8,128)S(1)}, f32[64,768]{1,0:T(8,128)S(1)}, u32[]{:S(2)}, u32[]{:S(2)}) collective-permute-start(f32[64,768]{1,0:T(8,128)S(1)} %bitcast_select_fusion.2), channel_id=1, source_target_pairs={{0,2},{1,3},{2,4},{3,5},{4,6},{5,7},{6,0},{7,1},{8,10},{9,11},{10,... | collective-permute-start | bytes 589832 | tf_op jit(solution)/shard_map/ppermute | solution.py:33
  157.0 7.3 %collective-permute-start.19 = (f32[4096]{0:T(1024)S(1)}, f32[4096]{0:T(1024)S(1)}, u32[]{:S(2)}, u32[]{:S(2)}) collective-permute-start(f32[4096]{0:T(1024)S(1)} %reduce_max.9), channel_id=1, source_target_pairs={{0,56},{8,48},{16,40},{24,32},{32,24},{40,16},{48,8},{56,0},{1,57}... | collective-permute-start | bytes 49160 | tf_op jit(solution)/shard_map/ppermute | solution.py:82
  157.1 7.2 %collective-permute-start.18 = (f32[4096]{0:T(1024)S(1)}, f32[4096]{0:T(1024)S(1)}, u32[]{:S(2)}, u32[]{:S(2)}) collective-permute-start(f32[4096]{0:T(1024)S(1)} %reduce_max.9), channel_id=1, source_target_pairs={{0,48},{8,56},{16,32},{24,40},{32,16},{40,24},{48,0},{56,8},{1,49}... | collective-permute-start | bytes 49160 | tf_op jit(solution)/shard_map/ppermute | solution.py:82
  158.4 6.1 %collective-permute-start.17 = (f32[4096]{0:T(1024)S(1)}, f32[4096]{0:T(1024)S(1)}, u32[]{:S(2)}, u32[]{:S(2)}) collective-permute-start(f32[4096]{0:T(1024)S(1)} %reduce_max.9), channel_id=1, source_target_pairs={{0,40},{8,32},{16,56},{24,48},{32,8},{40,0},{48,24},{56,16},{1,41}... | collective-permute-start | bytes 49160 | tf_op jit(solution)/shard_map/ppermute | solution.py:82
  160.8 9.4 %collective-permute-start.31 = (f32[96,768]{1,0:T(8,128)S(1)}, f32[96,768]{1,0:T(8,128)S(1)}, u32[]{:S(2)}, u32[]{:S(2)}) collective-permute-start(f32[96,768]{1,0:T(8,128)S(1)} %bitcast_select_fusion), channel_id=1, source_target_pairs={{0,6},{1,7},{2,0},{3,1},{4,2},{5,3},{6,4},{7,5},{8,14},{9,15},{10,... | collective-permute-start | bytes 884744 | tf_op jit(solution)/shard_map/ppermute | solution.py:33
  161.7 5.2 %collective-permute-start.16 = (f32[4096]{0:T(1024)S(1)}, f32[4096]{0:T(1024)S(1)}, u32[]{:S(2)}, u32[]{:S(2)}) collective-permute-start(f32[4096]{0:T(1024)S(1)} %reduce_max.9), channel_id=1, source_target_pairs={{0,32},{8,40},{16,48},{24,56},{32,0},{40,8},{48,16},{56,24},{1,33}... | collective-permute-start | bytes 49160 | tf_op jit(solution)/shard_map/ppermute | solution.py:82
  166.9 11.5 %collective-permute-start.32 = (f32[96,768]{1,0:T(8,128)S(1)}, f32[96,768]{1,0:T(8,128)S(1)}, u32[]{:S(2)}, u32[]{:S(2)}) collective-permute-start(f32[96,768]{1,0:T(8,128)S(1)} %bitcast_select_fusion), channel_id=1, source_target_pairs={{0,4},{1,5},{2,6},{3,7},{4,0},{5,1},{6,2},{7,3},{8,12},{9,13},{10,... | collective-permute-start | bytes 884744 | tf_op jit(solution)/shard_map/ppermute | solution.py:33
  167.5 15.6 %collective-permute-start.33 = (f32[96,768]{1,0:T(8,128)S(1)}, f32[96,768]{1,0:T(8,128)S(1)}, u32[]{:S(2)}, u32[]{:S(2)}) collective-permute-start(f32[96,768]{1,0:T(8,128)S(1)} %bitcast_select_fusion), channel_id=1, source_target_pairs={{0,2},{1,3},{2,4},{3,5},{4,6},{5,7},{6,0},{7,1},{8,10},{9,11},{10,... | collective-permute-start | bytes 884744 | tf_op jit(solution)/shard_map/ppermute | solution.py:33
  168.7 30.4 %collective-permute-start.20 = (f32[4096]{0:T(1024)S(1)}, f32[4096]{0:T(1024)S(1)}, u32[]{:S(2)}, u32[]{:S(2)}) collective-permute-start(f32[4096]{0:T(1024)S(1)} %maximum_maximum_fusion), channel_id=1, source_target_pairs={{0,64},{64,0},{1,65},{65,1},{2,66},{66,2},{3,67},{67,3},{4,68},{68... | collective-permute-start | bytes 49160 | tf_op jit(solution)/shard_map/ppermute | solution.py:138
  194.3 5.4 %collective-permute-start.36 = (f32[384]{0:T(512)S(1)}, f32[384]{0:T(512)S(1)}, u32[]{:S(2)}, u32[]{:S(2)}) collective-permute-start(f32[384]{0:T(512)S(1)} %maximum_reduce_fusion), channel_id=1, source_target_pairs={{0,65},{1,64},{2,67},{3,66},{4,69},{5,68},{6,71},{7,70},{64,1},{65... | collective-permute-start | bytes 4616 | tf_op jit(solution)/shard_map/ppermute | solution.py:51
  195.0 5.6 %collective-permute-start.34 = (f32[384]{0:T(512)S(1)}, f32[384]{0:T(512)S(1)}, u32[]{:S(2)}, u32[]{:S(2)}) collective-permute-start(f32[384]{0:T(512)S(1)} %maximum_reduce_fusion), channel_id=1, source_target_pairs={{0,1},{1,0},{2,3},{3,2},{4,5},{5,4},{6,7},{7,6},{8,9},{9,8},{10,11... | collective-permute-start | bytes 4616 | tf_op jit(solution)/shard_map/ppermute | solution.py:47
  201.9 5.1 %collective-permute-start.38 = (f32[4,384]{1,0:T(4,128)S(1)}, f32[4,384]{1,0:T(4,128)S(1)}, u32[]{:S(2)}, u32[]{:S(2)}) collective-permute-start(f32[4,384]{1,0:T(4,128)S(1)} %broadcast_select_fusion), channel_id=1, source_target_pairs={{0,4},{1,5},{2,6},{3,7},{4,0},{5,1},{6,2},{7,3},{8,12},{9,13},{10,... | collective-permute-start | bytes 18440 | tf_op jit(solution)/shard_map/ppermute | solution.py:95
  (12 other events, 55.2 us)
Sparse Core Ops, SparseCore 0:
  9.7 69.7 all-gather.1
